TPU v7x, 32 devices: a whole 2x2x4 slice. The times are simulated.
32 devices in a mesh: groups: 2 (over x), ctx: 16 (over z, y, core).
Axes of the slice: x: 2, y: 2, z: 4, core: 2. Of those that a mesh axis runs over, the one named last changes fastest.
Arguments:
- qkv: bfloat16 [4096, 12288], P(('groups', 'ctx')), parts along dimension 0, may hold values from -6 to 6
- doc_ids: int32 [4096], P(('groups', 'ctx')), parts along dimension 0, may hold values from 0 to 7, as said below
- short_w: float32 [7, 12288], replicated, may hold values from -2 to 2
- rates: float32 [256, 16], replicated, may hold values from 0 to 1, as said below
- residues: float32 [256, 16], replicated, may hold values from -1 to 1
Outputs:
- mixed: bfloat16 [4096, 4096], P(('groups', 'ctx')), parts along dimension 0
There are 2 independent parts, one for each index of `groups`. A program takes and returns all parts, laid end to end along the dimension named above; an argument that names none is the same for every part. Nothing has to cross between parts.
Inputs may be any that keep to these rules, and one draw needn't show every extreme that they name: `doc_ids`: never falling along the tokens; every document is one nonempty run. `rates`: positive.
All inputs are finite; a program needn't handle non-finite values.
Results may differ from a plain program's by a relative error of at most 0.005.
Values may be sent and summed in bfloat16 or wider, within the bound.
No kernel may reach another device: no remote copies, remote signals or barrier semaphores. Data moves between devices by JAX's collectives and lax.ppermute only.
A program may use at most 128 MiB of HBM per device.

v0:
```python
import jax
import jax.numpy as jnp
from jax import lax
from jax.sharding import PartitionSpec as P

HIGH = lax.Precision.HIGHEST


def from_behind(shard, axis, by):
    peers = lax.axis_size(axis)
    pairs = [(i, i + by) for i in range(peers) if 0 <= i + by < peers]
    return lax.ppermute(shard, axis, pairs)


def carried_in(shard, axis, combine, identity):
    peers, mine = (lax.axis_size(axis), lax.axis_index(axis))
    everything = jax.tree.map(lambda part: lax.all_gather(part, axis), shard)
    start = jax.tree.map(
        lambda part, zero: jnp.broadcast_to(jnp.asarray(zero, part.dtype), part.shape),
        shard,
        identity,
    )

    def lap(k, before):
        reached = k < mine
        new = combine(before, jax.tree.map(lambda part: part[k], everything))
        return jax.tree.map(lambda a, b: jnp.where(reached, a, b), new, before)

    return lax.fori_loop(0, peers, lap, start)


def short_conv(extended, ext_rows, weights, length):
    tap_count = weights.shape[0]
    own_docs = ext_rows[tap_count - 1 :]
    summed = jnp.zeros((length, extended.shape[1]), jnp.float32)
    for tap_index in range(tap_count):
        begin = tap_count - 1 - tap_index
        window = extended[begin : begin + length].astype(jnp.float32)
        matching = (ext_rows[begin : begin + length] == own_docs).astype(jnp.float32)[:, None]
        summed = summed + weights[tap_index][None, :] * window * matching
    return summed


def split_dot(pattern, weights, values):
    high_part = weights.astype(jnp.bfloat16)
    low_part = (weights - lax.optimization_barrier(high_part).astype(jnp.float32)).astype(
        jnp.bfloat16
    )
    first = jnp.einsum(pattern, high_part, values, preferred_element_type=jnp.float32)
    return first + jnp.einsum(pattern, low_part, values, preferred_element_type=jnp.float32)


def lower_toeplitz(kernel):
    filters, length = kernel.shape
    wrapped = jnp.concatenate(
        [kernel[:, :1], jnp.zeros((filters, length), jnp.float32), kernel[:, :0:-1]], axis=1
    )
    tiled = jnp.tile(wrapped, (1, length))[:, : length * (2 * length - 1)]
    return tiled.reshape(filters, length, 2 * length - 1)[:, :, :length]


def block_terms(product, doc_rows, rates, residues):
    length = product.shape[0]
    filters, pole_count = rates.shape
    group_width = product.shape[1] // filters
    places = jnp.arange(length).astype(jnp.float32)
    decays = jnp.exp(-rates[:, :, None] * places[None, None, :])
    kernel = jnp.sum(residues[:, :, None] * decays, axis=1)
    offsets = jnp.arange(length)[:, None] - jnp.arange(length)[None, :]
    visible = (offsets >= 0) & (doc_rows[:, None] == doc_rows[None, :])
    toeplitz = jnp.where(visible[None], lower_toeplitz(kernel), 0.0)
    values = product.reshape(length, filters, group_width).transpose(1, 2, 0)
    local_grid = split_dot("gts,gcs->gct", toeplitz, values)
    local_part = local_grid.transpose(2, 0, 1).reshape(length, filters * group_width)
    at_tail = (doc_rows == doc_rows[length - 1]).astype(jnp.float32)
    at_head = (doc_rows == doc_rows[0]).astype(jnp.float32)
    end_weight = (
        jnp.exp(-rates[:, :, None] * (length - 1.0 - places)[None, None, :])
        * at_tail[None, None, :]
    )
    states = split_dot("gks,gcs->kgc", end_weight, values).reshape(
        pole_count, filters * group_width
    )
    passing = jnp.exp(-rates * length) * (doc_rows[0] == doc_rows[length - 1]).astype(jnp.float32)
    in_weight = (
        residues[:, :, None]
        * jnp.exp(-rates[:, :, None] * (places + 1.0)[None, None, :])
        * at_head[None, None, :]
    )
    return (local_part, states, passing.T, in_weight)


def carried(in_weight, beginning):
    filters, pole_count, length = in_weight.shape
    group_width = beginning.shape[1] // filters
    shaped = beginning.reshape(pole_count, filters, group_width).transpose(1, 2, 0)
    result = jnp.einsum("gck,gkt->gct", shaped, in_weight, precision=HIGH)
    return result.transpose(2, 0, 1).reshape(length, filters * group_width)


def local_terms(gated, doc_ids, rates, residues):
    length, channels = gated.shape
    filters, pole_count = rates.shape
    group_width = channels // filters
    per_piece = min(filters, 32, max(1, 8192 // length))
    piece_count = filters // per_piece
    pieces = gated.reshape(length, piece_count, per_piece * group_width).transpose(1, 0, 2)

    def process(members):
        return block_terms(members[0], doc_ids, members[1], members[2])

    local_part, states, passing, in_weight = lax.map(
        process,
        (
            pieces,
            rates.reshape(piece_count, per_piece, pole_count),
            residues.reshape(piece_count, per_piece, pole_count),
        ),
    )
    local_part = local_part.transpose(1, 0, 2).reshape(length, channels)
    states = states.transpose(1, 0, 2).reshape(pole_count, channels)
    passing = passing.transpose(1, 0, 2).reshape(pole_count, filters)
    in_weight = in_weight.reshape(filters, pole_count, length)
    return (local_part, states, passing, in_weight)


def on_device(qkv, doc_ids, short_w, rates, residues):
    length = qkv.shape[0]
    tap_count = short_w.shape[0]
    channels = qkv.shape[1] // 3
    filters, pole_count = rates.shape
    group_width = channels // filters
    rim_rows, rim_docs = from_behind(
        (qkv[length - (tap_count - 1) :], doc_ids[length - (tap_count - 1) :].astype(jnp.bfloat16)),
        "ctx",
        1,
    )
    extended = jnp.concatenate([rim_rows, qkv], axis=0)
    ext_rows = jnp.concatenate([rim_docs.astype(jnp.int32), doc_ids], axis=0)
    convolved = short_conv(extended, ext_rows, short_w, length)
    queries = convolved[:, :channels]
    gated = (convolved[:, channels : 2 * channels] * convolved[:, 2 * channels :]).astype(
        jnp.bfloat16
    )

    def combine(earlier, later):
        early_decay, early_state = earlier
        late_decay, late_state = later
        return (
            early_decay * late_decay,
            jnp.repeat(late_decay, group_width, axis=-1) * early_state + late_state,
        )

    local_part, states, passing, in_weight = local_terms(gated, doc_ids, rates, residues)
    joined = (ext_rows[tap_count - 2] == doc_ids[0]).astype(jnp.float32)
    passing = passing * joined
    before_decay, before_state = carried_in(
        (passing, states), "ctx", combine, (jnp.ones_like(passing), jnp.zeros_like(states))
    )
    long_part = local_part + carried(in_weight, joined * before_state)
    return (queries * long_part).astype(jnp.bfloat16)


def solution(mesh):
    return jax.shard_map(
        on_device,
        mesh=mesh,
        in_specs=(P(("groups", "ctx"), None), P(("groups", "ctx")), P(), P(), P()),
        out_specs=P(("groups", "ctx"), None),
        check_vma=False,
    )
```

profile of v0, /device:TPU:24, one launch (start us, length us, event | category | flops | bytes accessed | tf_op | source)
XLA Modules:
  0.0 369.6 jit_solution(17251351968695284969)
XLA Ops:
  7.3 1.9 collective-permute-start.1
  10.2 3.5 collective-permute-start
  15.1 2.5 fusion.22
  22.1 15.0 %multiply_add_fusion = f32[128,12288]{1,0:T(8,128)S(1)} fusion(bf16[128,12288]{1,0:T(8,128)(2,1)} %param.9, bf16[6,12288]{1,0:T(8,128)(2,1)S(1)} %collective-permute-done, f32[128]{0:T(128)S(1)} %get-tuple-element.259, f32[12288]{0:T(1024)S(1)} %bitcast.123, f32[128]{0:T(128)S(1)} %get-tuple-element.260, f32[12288]{0:T(1024)S(1)} %bitcast.124, ...), kind=kLoop, calls=%fused_computation.39 | loop fusion | flops 69206016 | bytes 9931776 | tf_op jit(solution)/shard_map/add | solution.py:40
  37.0 2.6 copy-done
  40.6 199.3 %while.31 = (s32[]{:T(128)}, f32[8,128,512]{1,2,0:T(8,128)}, f32[8,16,512]{1,2,0:T(8,128)}, f32[8,16,32]{1,2,0:T(8,128)S(1)}, f32[8,32,16,128]{3,2,1,0:T(8,128)}...) while((s32[]{:T(128)}, f32[8,128,512]{1,2,0:T(8,128)}, ...), condition=%wide.region_2.3_spmd, body=%wide.region_0.2_spmd.sunk | while | flops 41639040 | bytes 38879408 | solution.py:112
  43.4 2.4 copy.38
  45.9 2.3 slice.230
  48.2 9.5 %reshape.164 = f32[32,128,255]{2,1,0:T(8,128)} reshape(f32[32,32640]{1,0:T(8,128)} %slice.230) | data formatting | bytes 8355840 | tf_op jit(solution)/shard_map/while/body/eval_jaxpr/reshape | solution.py:59
  57.7 1.8 fusion.53
  60.3 2.3 convolution_add_fusion.4
  68.3 2.4 copy.38
  70.8 2.3 slice.230
  73.1 9.5 %reshape.164 = f32[32,128,255]{2,1,0:T(8,128)} reshape(f32[32,32640]{1,0:T(8,128)} %slice.230) | data formatting | bytes 8355840 | tf_op jit(solution)/shard_map/while/body/eval_jaxpr/reshape | solution.py:59
  82.6 1.8 fusion.53
  85.2 2.3 convolution_add_fusion.4
  93.3 2.4 copy.38
  95.7 2.3 slice.230
  98.0 9.5 %reshape.164 = f32[32,128,255]{2,1,0:T(8,128)} reshape(f32[32,32640]{1,0:T(8,128)} %slice.230) | data formatting | bytes 8355840 | tf_op jit(solution)/shard_map/while/body/eval_jaxpr/reshape | solution.py:59
  110.1 2.3 convolution_add_fusion.4
  118.2 2.4 copy.38
  120.6 2.3 slice.230
  122.9 9.5 %reshape.164 = f32[32,128,255]{2,1,0:T(8,128)} reshape(f32[32,32640]{1,0:T(8,128)} %slice.230) | data formatting | bytes 8355840 | tf_op jit(solution)/shard_map/while/body/eval_jaxpr/reshape | solution.py:59
  135.0 2.3 convolution_add_fusion.4
  143.1 2.4 copy.38
  145.6 2.3 slice.230
  147.9 9.5 %reshape.164 = f32[32,128,255]{2,1,0:T(8,128)} reshape(f32[32,32640]{1,0:T(8,128)} %slice.230) | data formatting | bytes 8355840 | tf_op jit(solution)/shard_map/while/body/eval_jaxpr/reshape | solution.py:59
  159.9 2.3 convolution_add_fusion.4
  168.0 2.4 copy.38
  170.5 2.3 slice.230
  172.8 9.5 %reshape.164 = f32[32,128,255]{2,1,0:T(8,128)} reshape(f32[32,32640]{1,0:T(8,128)} %slice.230) | data formatting | bytes 8355840 | tf_op jit(solution)/shard_map/while/body/eval_jaxpr/reshape | solution.py:59
  184.9 2.3 convolution_add_fusion.4
  192.9 2.4 copy.38
  195.4 2.3 slice.230
  197.7 9.5 %reshape.164 = f32[32,128,255]{2,1,0:T(8,128)} reshape(f32[32,32640]{1,0:T(8,128)} %slice.230) | data formatting | bytes 8355840 | tf_op jit(solution)/shard_map/while/body/eval_jaxpr/reshape | solution.py:59
  209.8 2.3 convolution_add_fusion.4
  217.9 2.4 copy.38
  220.3 2.3 slice.230
  222.6 9.5 %reshape.164 = f32[32,128,255]{2,1,0:T(8,128)} reshape(f32[32,32640]{1,0:T(8,128)} %slice.230) | data formatting | bytes 8355840 | tf_op jit(solution)/shard_map/while/body/eval_jaxpr/reshape | solution.py:59
  234.7 2.3 convolution_add_fusion.4
  239.9 3.0 copy.33
  246.9 17.0 %all_gather.7 = f32[16,16,256]{2,1,0:T(8,128)S(1)} all-gather(f32[1,16,256]{2,1,0:T(8,128)S(1)} %copy.32), channel_id=1, replica_groups=mesh['groups'=2,'ctx'=16] {'ctx'}, dimensions={0}, use_global_device_ids=true | all-gather | bytes 278528 | tf_op jit(solution)/shard_map/all_gather | solution.py:17
  263.8 29.0 %all-gather.2.cloned.1.call-done = f32[16,16,4096]{2,1,0:T(8,128)} async-done(((f32[1,16,4096]{2,1,0:T(8,128)}), f32[16,16,4096]{2,1,0:T(8,128)}) %all-gather.2.cloned.1.call-update) | async-done | bytes 4194320 | tf_op jit(solution)/shard_map/all_gather | solution.py:17
  292.9 53.7 %while.32 = (s32[]{:T(128)}, f32[16,4096]{1,0:T(8,128)S(1)}, s32[]{:T(128)}, f32[16,16,256]{2,1,0:T(8,128)S(1)}, f32[16,16,4096]{2,1,0:T(8,128)}, /*index=5*/s32[]{:T(128)}, s32[]{:T(128)}) while((s32[]{:T(128)}, f32[16,4096]{1,0:T(8,128)S(1)}, s32[]{:T(128)}, f32[16,16,256]{2,1,0:T(8,128)S(1)}, f32[16,16,4096]{2,1,0:T(8,128)}, ...), condition=%wide.region_4.5_spmd.clone, body=%wide.region_3.4_spmd.clone.sunk | while | flops 262148 | bytes 1884265 | solution.py:29
  346.6 2.1 reshape.157
  348.7 7.5 %fusion.19 = f32[256,16,128]{2,1,0:T(8,128)} fusion(f32[256,16,128]{2,1,0:T(8,128)} %bitcast.111, f32[256,16,16]{1,0,2:T(8,128)} %bitcast.108), kind=kOutput, calls=%fused_computation.53 | convolution fusion | flops 100663296 | bytes 4456448 | tf_op jit(solution)/shard_map/gck,gkt->gct/dot_general | solution.py:97
  356.3 2.9 copy.29
  359.2 3.5 fusion.18
  (278 shorter events, 126.0 us)
Async XLA Ops:
  6.5 286.3 %all-gather.2.cloned.1.call-start = ((), (), s32[]{:S(2)}) async-start(), calls=%async_computation | async-start | bytes 4456448 | tf_op jit(solution)/shard_map/all_gather | solution.py:17
  7.3 13.3 %collective-permute-start.1 = (bf16[6]{0:T(256)(128)(2,1)S(1)}, bf16[6]{0:T(256)(128)(2,1)S(1)}, u32[]{:S(2)}, u32[]{:S(2)}) collective-permute-start(bf16[6]{0:T(256)(128)(2,1)S(1)} %slice.113), channel_id=1, source_target_pairs={{0,1},{1,2},{2,3},{3,4},{4,5},{5,6},{6,7},{7,8},{8,9},{9,10},{10,1... | collective-permute-start | bytes 44 | tf_op jit(solution)/shard_map/ppermute | solution.py:12
  10.2 11.9 %collective-permute-start = (bf16[6,12288]{1,0:T(8,128)(2,1)S(1)}, bf16[6,12288]{1,0:T(8,128)(2,1)S(1)}, u32[]{:S(2)}, u32[]{:S(2)}) collective-permute-start(bf16[6,12288]{1,0:T(8,128)(2,1)S(1)} %slice.111), channel_id=1, source_target_pairs={{0,1},{1,2},{2,3},{3,4},{4,5},{5,6},{6,7},{7,8},{8,9},{9,10},{10,1... | collective-permute-start | bytes 442376 | tf_op jit(solution)/shard_map/ppermute | solution.py:12
  37.0 2.7 copy-start
  39.7 0.9 copy-start.3
  239.9 5.1 %copy-start.2 = (f32[8,128,512]{1,2,0:T(8,128)S(1)}, f32[8,128,512]{1,2,0:T(8,128)}, u32[]{:S(2)}) copy-start(f32[8,128,512]{1,2,0:T(8,128)} %get-tuple-element.190) | copy-start | bytes 6291460
  348.7 10.5 %copy-start.1 = (f32[128,4096]{1,0:T(8,128)S(1)}, f32[128,4096]{1,0:T(8,128)}, u32[]{:S(2)}) copy-start(f32[128,4096]{1,0:T(8,128)} %copy.31) | copy-start | bytes 6291460
Sparse Core Ops, SparseCore 0:
  243.1 49.7 all-gather.1
where the time goes:
time: 374 us; the launch traced here: 370 us
  local copies, waits for them, and re-layouts  190 us (51%)
  other arithmetic  75 us (20%)
  matrix products  35.4 us (9%)
  waiting for transfers between devices  29.1 us (8%)
  blocking collectives  17 us (5%)
  between operations  16.1 us (4%)
  starting transfers between devices  5.44 us (1%)
    reshape x8, local copies, waits for them, and re-layouts, lower_toeplitz(): return tiled.reshape(filters, length, 2 * length - 1)[:, :, :length]  75.7 us
    all_gather x1, waiting for transfers between devices, carried_in(): everything = jax.tree.map(lambda part: lax.all_gather(part, axis), shard)  29 us
    reshape x16, local copies, waits for them, and re-layouts, combine(): jnp.repeat(late_decay, group_width, axis=-1) * early_state + late_state  24.9 us
    dot_general x16, matrix products, split_dot(): jnp.einsum(pattern, low_part, values, preferred_element_type=jnp.float32)  20.5 us
    while x8, local copies, waits for them, and re-layouts  19.4 us
    select_n x16, other arithmetic, lap(): return jax.tree.map(lambda a, b: jnp.where(reached, a, b), new, before)  18.7 us
    slice x8, local copies, waits for them, and re-layouts, lower_toeplitz(): tiled = jnp.tile(wrapped, (1, length))[:, :length * (2 * length - 1)]  18.6 us
    all_gather x1, blocking collectives, carried_in(): everything = jax.tree.map(lambda part: lax.all_gather(part, axis), shard)  17 us
  transfers between devices with their start and end apart: 3, of which 1 were waited for; matrix products, arithmetic and copies ran while one was open for 3% of the time, Pallas kernels for 0%

commit v1 on v0

v1 whole, which is shorter than its diff:
```python
import functools

import jax
import jax.numpy as jnp
from jax import lax
from jax.experimental import pallas as pl
from jax.experimental.pallas import tpu as pltpu
from jax.sharding import PartitionSpec as P

HIGH = lax.Precision.HIGHEST
WIDTH = 256
RIM = 8


def from_behind(shard, axis, by):
    peers = lax.axis_size(axis)
    pairs = [(i, i + by) for i in range(peers) if 0 <= i + by < peers]
    return lax.ppermute(shard, axis, pairs)


def split_bf16(x):
    hi = x.astype(jnp.bfloat16)
    lo = (x - lax.optimization_barrier(hi).astype(jnp.float32)).astype(jnp.bfloat16)
    return hi, lo


def local_kernel(taps, group_width,
                 xq, xk, xv, rq, rk, rv, wq, wk, wv, masks_ref, m_ref, base_ref, ewh_ref, ewl_ref,
                 q_out, loc_out, st_out, ext_s):
    length, width = xq.shape
    groups = width // group_width
    masks = masks_ref[...]

    def conv(x_ref, r_ref, w_ref):
        ext_s[0:RIM, :] = r_ref[...].astype(jnp.float32)
        ext_s[RIM:RIM + length, :] = x_ref[...].astype(jnp.float32)
        w = w_ref[...]
        acc = (w[0:1, :] * ext_s[RIM:RIM + length, :]) * masks[:, 0:1]
        for j in range(1, taps):
            window = ext_s[pl.ds(RIM - j, length), :]
            acc = acc + (w[j:j + 1, :] * window) * masks[:, j:j + 1]
        return acc

    cq = conv(xq, rq, wq)
    ck = conv(xk, rk, wk)
    cv = conv(xv, rv, wv)
    q_out[...] = cq
    gated = (ck * cv).astype(jnp.bfloat16)

    lane_group = lax.broadcasted_iota(jnp.int32, (length, width), 1) // group_width
    zero = jnp.zeros_like(gated)
    xbd = jnp.concatenate([jnp.where(lane_group == g, gated, zero) for g in range(groups)], axis=0)

    visible = m_ref[...] > 0.5
    pieces = []
    for g in range(groups):
        row = jnp.broadcast_to(base_ref[g:g + 1, :], (length, length))
        rolled = pltpu.roll(row, 0, 1, stride=1, stride_axis=0)
        pieces.append(jnp.where(visible, rolled, 0.0))
    toeplitz = jnp.concatenate(pieces, axis=1)
    t_hi = toeplitz.astype(jnp.bfloat16)
    t_lo = (toeplitz - t_hi.astype(jnp.float32)).astype(jnp.bfloat16)
    loc = jnp.dot(t_hi, xbd, preferred_element_type=jnp.float32)
    loc = loc + jnp.dot(t_lo, xbd, preferred_element_type=jnp.float32)
    loc_out[...] = loc
    st = jnp.dot(ewh_ref[...], xbd, preferred_element_type=jnp.float32)
    st = st + jnp.dot(ewl_ref[...], xbd, preferred_element_type=jnp.float32)
    st_out[...] = st


def final_kernel(group_width, pole_count, q_ref, loc_ref, iw_ref, b_ref, o_ref):
    length, width = q_ref.shape
    groups = width // group_width
    b = b_ref[...]
    tiled = jnp.concatenate([b] * groups, axis=0)
    row_group = lax.broadcasted_iota(jnp.int32, tiled.shape, 0) // pole_count
    lane_group = lax.broadcasted_iota(jnp.int32, tiled.shape, 1) // group_width
    bbd = jnp.where(row_group == lane_group, tiled, 0.0)
    car = jnp.dot(iw_ref[...], bbd, precision=HIGH, preferred_element_type=jnp.float32)
    o_ref[...] = (q_ref[...] * (loc_ref[...] + car)).astype(o_ref.dtype)


def on_device(qkv, doc_ids, short_w, rates, residues):
    length = qkv.shape[0]
    taps = short_w.shape[0]
    channels = qkv.shape[1] // 3
    filters, pole_count = rates.shape
    group_width = channels // filters
    width = min(WIDTH, channels)
    nb = channels // width
    gpb = width // group_width
    peers = lax.axis_size("ctx")
    me = lax.axis_index("ctx")

    doc_all = lax.all_gather(doc_ids, "ctx", tiled=True)
    prev_docs = lax.dynamic_slice(doc_all, (jnp.maximum(me * length - RIM, 0),), (RIM,))
    rim = from_behind(qkv[length - RIM:], "ctx", 1)

    ext_docs = jnp.concatenate([prev_docs, doc_ids], axis=0)
    cols = [(ext_docs[RIM - j:RIM - j + length] == doc_ids) for j in range(taps)]
    cols += [jnp.zeros((length,), bool)] * (8 - taps)
    masks = jnp.stack(cols, axis=1).astype(jnp.float32)
    pos = jnp.arange(length)
    visible = ((pos[None, :] <= pos[:, None]) & (doc_ids[:, None] == doc_ids[None, :])).astype(jnp.float32)

    places = jnp.arange(length).astype(jnp.float32)
    lags = ((length - jnp.arange(length)) % length).astype(jnp.float32)
    base = jnp.sum(residues[:, :, None] * jnp.exp(-rates[:, :, None] * lags[None, None, :]), axis=1)
    at_tail = (doc_ids == doc_ids[length - 1]).astype(jnp.float32)
    at_head = (doc_ids == doc_ids[0]).astype(jnp.float32)
    end_weight = jnp.exp(-rates[:, :, None] * (length - 1.0 - places)[None, None, :]) * at_tail[None, None, :]
    end_weight = end_weight.transpose(1, 0, 2).reshape(pole_count, filters * length)
    ew_hi, ew_lo = split_bf16(end_weight)
    in_weight = (residues[:, :, None] * jnp.exp(-rates[:, :, None] * (places + 1.0)[None, None, :])
                 * at_head[None, None, :])
    in_weight = in_weight.transpose(2, 0, 1).reshape(length, filters * pole_count)

    col = lambda off: (lambda j: (0, j + off))
    fixed = lambda j: (0, 0)
    q_part, local_part, states = pl.pallas_call(
        functools.partial(local_kernel, taps, group_width),
        grid=(nb,),
        in_specs=[
            pl.BlockSpec((length, width), col(0)),
            pl.BlockSpec((length, width), col(nb)),
            pl.BlockSpec((length, width), col(2 * nb)),
            pl.BlockSpec((RIM, width), col(0)),
            pl.BlockSpec((RIM, width), col(nb)),
            pl.BlockSpec((RIM, width), col(2 * nb)),
            pl.BlockSpec((taps, width), col(0)),
            pl.BlockSpec((taps, width), col(nb)),
            pl.BlockSpec((taps, width), col(2 * nb)),
            pl.BlockSpec((length, 8), fixed),
            pl.BlockSpec((length, length), fixed),
            pl.BlockSpec((gpb, length), lambda j: (j, 0)),
            pl.BlockSpec((pole_count, gpb * length), col(0)),
            pl.BlockSpec((pole_count, gpb * length), col(0)),
        ],
        out_specs=[
            pl.BlockSpec((length, width), col(0)),
            pl.BlockSpec((length, width), col(0)),
            pl.BlockSpec((pole_count, width), col(0)),
        ],
        out_shape=[
            jax.ShapeDtypeStruct((length, channels), jnp.float32),
            jax.ShapeDtypeStruct((length, channels), jnp.float32),
            jax.ShapeDtypeStruct((pole_count, channels), jnp.float32),
        ],
        scratch_shapes=[pltpu.VMEM((RIM + length, width), jnp.float32)],
        compiler_params=pltpu.CompilerParams(dimension_semantics=("arbitrary",)),
    )(qkv, qkv, qkv, rim, rim, rim, short_w, short_w, short_w, masks, visible, base, ew_hi, ew_lo)

    rate_cols = jnp.repeat(rates.T, group_width, axis=1)
    doc_last = doc_all[length - 1::length]
    mine_last = doc_last[me]
    total = states
    offset = 1
    while offset < peers:
        got = from_behind(total, "ctx", offset)
        source = jnp.maximum(me - offset, 0)
        same = (me >= offset) & (doc_last[source] == mine_last)
        decay = jnp.exp(-rate_cols * float(length * offset))
        total = total + jnp.where(same, decay * got, 0.0)
        offset *= 2
    before = from_behind(total, "ctx", 1)
    joined = (me >= 1) & (doc_last[jnp.maximum(me - 1, 0)] == doc_ids[0])
    beginning = jnp.where(joined, before, 0.0)

    return pl.pallas_call(
        functools.partial(final_kernel, group_width, pole_count),
        grid=(nb,),
        in_specs=[
            pl.BlockSpec((length, width), col(0)),
            pl.BlockSpec((length, width), col(0)),
            pl.BlockSpec((length, gpb * pole_count), col(0)),
            pl.BlockSpec((pole_count, width), col(0)),
        ],
        out_specs=pl.BlockSpec((length, width), col(0)),
        out_shape=jax.ShapeDtypeStruct((length, channels), jnp.bfloat16),
        compiler_params=pltpu.CompilerParams(dimension_semantics=("arbitrary",)),
    )(q_part, local_part, in_weight, beginning)


def solution(mesh):
    return jax.shard_map(
        on_device,
        mesh=mesh,
        in_specs=(P(("groups", "ctx"), None), P(("groups", "ctx")), P(), P(), P()),
        out_specs=P(("groups", "ctx"), None),
        check_vma=False,
    )
```

time: 374 us -> 122 us (0.33)
  local copies, waits for them, and re-layouts: 190 us -> 14.2 us
  other arithmetic: 75 us -> 13.7 us
  Pallas kernels: 0 us -> 36.4 us
  matrix products: 35.4 us -> 0 us
  between operations: 16.1 us -> 6.66 us
  waiting for transfers between devices: 29.1 us -> 21.6 us
  starting transfers between devices: 5.44 us -> 11.1 us
    reshape x28 -> x0, local copies, waits for them, and re-layouts: 108 us -> none  [the longest x8 75.7 us: lower_toeplitz(): return tiled.reshape(filters, length, 2 * length - 1)[:, :, :length]]
    pallas_call x0 -> x2, Pallas kernels: none -> 36.4 us  [the longest x1 24.3 us: on_device(): pl.pallas_call(functools.partial(local_kernel, taps, group_width), grid=(...]
    dot_general x33 -> x0, matrix products: 35.4 us -> none  [the longest x16 20.5 us: split_dot(): jnp.einsum(pattern, low_part, values, preferred_element_type=jnp.float32)]
    all_gather x1 -> x0, waiting for transfers between devices: 29 us -> none  [carried_in(): everything = jax.tree.map(lambda part: lax.all_gather(part, axis), shard)]
    slice x29 -> x3, local copies, waits for them, and re-layouts: 29.9 us -> 2.36 us  [the longest x1 1.32 us: on_device(): at_head = (doc_ids == doc_ids[0]).astype(jnp.float32)]
    convert_element_type x36 -> x6, other arithmetic: 31 us -> 7.25 us  [the longest x1 2.37 us: split_bf16(): (x - lax.optimization_barrier(hi).astype(jnp.float32)).astype(jnp.bfloat16)]
    ppermute x2 -> x6, waiting for transfers between devices: 0.01 us -> 21.6 us  [from_behind(): return lax.ppermute(shard, axis, pairs)]
    while x8 -> x0, local copies, waits for them, and re-layouts: 19.4 us -> none
  transfers between devices with their start and end apart: 3 -> 6, of which waited for: 1 -> 5; matrix products, arithmetic and copies ran while one was open for 3% -> 21% of each run, Pallas kernels for 0% -> 0%
where the time goes in v1:
time: 122 us; the launch traced here: 121 us
  Pallas kernels  36.4 us (30%)
  waiting for transfers between devices  21.6 us (18%)
  blocking collectives  17 us (14%)
  local copies, waits for them, and re-layouts  14.2 us (12%)
  other arithmetic  13.7 us (11%)
  starting transfers between devices  11.1 us (9%)
  between operations  6.66 us (5%)
    pallas_call x1, Pallas kernels, on_device(): pl.pallas_call(functools.partial(local_kernel, taps, group_width), grid=(...  24.3 us
    ppermute x6, waiting for transfers between devices, from_behind(): return lax.ppermute(shard, axis, pairs)  21.6 us
    all_gather x1, blocking collectives, on_device(): doc_all = lax.all_gather(doc_ids, 'ctx', tiled=True)  17 us
    pallas_call x1, Pallas kernels, on_device(): pl.pallas_call(functools.partial(final_kernel, group_width, pole_count),...  12.1 us
    ppermute x6, starting transfers between devices, from_behind(): return lax.ppermute(shard, axis, pairs)  11.1 us
    exp x4, local copies, waits for them, and re-layouts, on_device(): decay = jnp.exp(-rate_cols * float(length * offset))  6.23 us
  transfers between devices with their start and end apart: 6, of which 5 were waited for; matrix products, arithmetic and copies ran while one was open for 21% of the time, Pallas kernels for 0%

profile of v1, /device:TPU:24, one launch (start us, length us, event | category | flops | bytes accessed | tf_op | source)
XLA Modules:
  0.0 120.7 jit_solution(3182566724985861510)
XLA Ops:
  0.0 0.9 slice.31
  0.9 1.9 %collective-permute-start = (bf16[8,12288]{1,0:T(8,128)(2,1)S(1)}, bf16[8,12288]{1,0:T(8,128)(2,1)S(1)}, u32[]{:S(2)}, u32[]{:S(2)}) collective-permute-start(bf16[8,12288]{1,0:T(8,128)(2,1)S(1)} %slice.31), channel_id=1, source_target_pairs={{0,1},{1,2},{2,3},{3,4},{4,5},{5,6},{6,7},{7,8},{8,9},{9,10},{10,1... | collective-permute-start | bytes 589832 | tf_op jit(solution)/shard_map/ppermute | solution.py:18
  2.9 1.3 %fusion.8 = (s32[1]{0:T(128)}, s32[1]{0:T(128)}) fusion(s32[128]{0:T(128)} %param.6), kind=kLoop, calls=%fused_computation.39 | loop fusion | bytes 16 | tf_op jit(solution)/shard_map/slice | solution.py:110
  4.2 1.4 %fusion.4.m_ref = f32[128,128]{1,0:T(8,128)} fusion(s32[128]{0:T(128)} %param.6), kind=kLoop, calls=%fused_computation.16 | loop fusion | flops 65536 | bytes 66048 | tf_op jit(solution)/shard_map/convert_element_type | solution.py:104
  5.7 17.0 %all-gather = s32[16,1,128]{2,1,0:T(1,128)S(1)} all-gather(s32[1,1,128]{2,1,0:T(1,128)} %bitcast.48), channel_id=1, replica_groups=mesh['groups'=2,'ctx'=16] {'ctx'}, dimensions={0}, use_global_device_ids=true | all-gather | bytes 8704 | tf_op jit(solution)/shard_map/all_gather | solution.py:95
  22.6 0.1 dynamic_slice.19
  22.7 0.7 pad_add_fusion
  23.4 2.1 %compare_convert_fusion = (f32[128]{0:T(128)S(1)}, f32[128]{0:T(128)S(1)}, pred[128,1]{0,1:T(4,128)(4,1)S(1)}, pred[128,1]{0,1:T(4,128)(4,1)S(1)}, pred[128,1]{0...) fusion(s32[128]{0:T(128)} %param.6, s32[]{:T(128)} %bitcast.12, ...), kind=kLoop, calls=%fused_computation.23 | loop fusion | flops 1280 | bytes 5384 | tf_op jit(solution)/shard_map/convert_element_type | solution.py:110
  25.6 0.7 copy.36.masks_ref
  26.3 0.7 exponential_bitcast_fusion
  27.1 0.6 mul.155
  27.7 1.4 %fusion.2.ewh_ref = bf16[16,32768]{1,0:T(8,128)(2,1)S(1)} fusion(f32[2,8,256,128]{3,2,1,0:T(8,128)S(1)} %bitcast.46, f32[32768]{0:T(1024)S(1)} %get-tuple-element.38, f32[32768]{0:T(1024)S(1)} %get-tuple-element.39), kind=kLoop, calls=%fused_computation.6 | loop fusion | flops 1572864 | bytes 3407872 | tf_op jit(solution)/shard_map/convert_element_type | solution.py:22
  29.0 0.0 copy-start
  29.0 0.0 copy-start.3
  29.1 2.4 %subtract_convert_fusion.ewl_ref = bf16[16,32768]{1,0:T(8,128)(2,1)} fusion(bf16[16,32768]{1,0:T(8,128)(2,1)S(1)} %fusion.2.ewh_ref, f32[2,8,256,128]{3,2,1,0:T(8,128)S(1)} %bitcast.47, f32[32768]{0:T(1024)S(1)} %get-tuple-element.38, f32[32768]{0:T(1024)S(1)} %get-tuple-element.39), kind=kLoop, calls=%fused_computation.4 | loop fusion | flops 2621440 | bytes 4456448 | tf_op jit(solution)/shard_map/convert_element_type | solution.py:23
  31.4 0.0 copy-done
  31.4 0.1 copy.35
  31.5 0.0 copy-done.3
  31.5 0.1 copy.34
  31.6 2.3 %multiply_reduce_fusion.base_ref = f32[256,128]{1,0:T(8,128)} fusion(f32[128]{0:T(128)S(1)} %fusion.5, f32[256,16]{1,0:T(8,128)S(1)} %copy.35, f32[256,16]{1,0:T(8,128)S(1)} %copy.34), kind=kLoop, calls=%fused_computation.5 | loop fusion | flops 1540096 | bytes 164352 | tf_op jit(solution)/shard_map/reduce_sum | solution.py:108
  34.0 0.0 collective-permute-done.rq.rk.rv
  34.0 0.7 copy-done.1
  34.6 24.3 %shard_map.55 = (f32[128,4096]{1,0:T(8,128)}, f32[128,4096]{1,0:T(8,128)}, f32[16,4096]{1,0:T(8,128)}) custom-call(bf16[128,12288]{1,0:T(8,128)(2,1)} %xv.1, bf16[128,12288]{1,0:T(8,128)(2,1)} %xv.1, bf16[128,12288]{1,0:T(8,128)(2,1)} %xv.1, bf16[8,12288]{1,0:T(8,128)(2,1)} %copy-done.1, bf16[8,12288]{1,0:T(8,128)(2,1)} %copy-done.1, ...), custom_call_target="tpu_custom_call" | custom-call | tf_op jit(solution)/shard_map/pallas_call | solution.py:120
  58.9 2.3 %collective-permute-start.1 = (f32[16,4096]{1,0:T(8,128)}, f32[16,4096]{1,0:T(8,128)S(1)}, u32[]{:S(2)}, u32[]{:S(2)}) collective-permute-start(f32[16,4096]{1,0:T(8,128)} %get-tuple-element.10), channel_id=1, source_target_pairs={{0,1},{1,2},{2,3},{3,4},{4,5},{5,6},{6,7},{7,8},{8,9},{9,10},{10,1... | collective-permute-start | bytes 786440 | tf_op jit(solution)/shard_map/ppermute | solution.py:18
  61.2 0.1 slice.40
  61.3 0.6 broadcast_in_dim.15
  61.9 1.6 %exp.58 = f32[16,4096]{1,0:T(8,128)S(1)} reshape(f32[16,256,16]{2,1,0:T(8,128)S(1)} %broadcast_in_dim.15) | data formatting | bytes 524288 | tf_op jit(solution)/shard_map/exp | solution.py:162
  63.5 0.7 fusion.7
  65.4 2.3 %collective-permute-done.1 = f32[16,4096]{1,0:T(8,128)S(1)} collective-permute-done((f32[16,4096]{1,0:T(8,128)}, f32[16,4096]{1,0:T(8,128)S(1)}, u32[]{:S(2)}, u32[]{:S(2)}) %collective-permute-start.1) | collective-permute-done | bytes 262176 | tf_op jit(solution)/shard_map/ppermute | solution.py:18
  67.8 2.3 %collective-permute-start.2 = (f32[16,4096]{1,0:T(8,128)S(1)}, f32[16,4096]{1,0:T(8,128)S(1)}, u32[]{:S(2)}, u32[]{:S(2)}) collective-permute-start(f32[16,4096]{1,0:T(8,128)S(1)} %select_add_fusion.3), channel_id=1, source_target_pairs={{0,2},{1,3},{2,4},{3,5},{4,6},{5,7},{6,8},{7,9},{8,10},{9,11},{10,... | collective-permute-start | bytes 786440 | tf_op jit(solution)/shard_map/ppermute | solution.py:18
  71.3 0.6 broadcast_in_dim.33
  71.9 1.6 %exp.61 = f32[16,4096]{1,0:T(8,128)S(1)} reshape(f32[16,256,16]{2,1,0:T(8,128)S(1)} %broadcast_in_dim.33) | data formatting | bytes 524288 | tf_op jit(solution)/shard_map/exp | solution.py:162
  73.5 4.0 %collective-permute-done.2 = f32[16,4096]{1,0:T(8,128)S(1)} collective-permute-done((f32[16,4096]{1,0:T(8,128)S(1)}, f32[16,4096]{1,0:T(8,128)S(1)}, u32[]{:S(2)}, u32[]{:S(2)}) %collective-permute-start.2) | collective-permute-done | bytes 262176 | tf_op jit(solution)/shard_map/ppermute | solution.py:18
  77.5 1.5 %collective-permute-start.3 = (f32[16,4096]{1,0:T(8,128)S(1)}, f32[16,4096]{1,0:T(8,128)S(1)}, u32[]{:S(2)}, u32[]{:S(2)}) collective-permute-start(f32[16,4096]{1,0:T(8,128)S(1)} %select_add_fusion.2), channel_id=1, source_target_pairs={{0,4},{1,5},{2,6},{3,7},{4,8},{5,9},{6,10},{7,11},{8,12},{9,13},{1... | collective-permute-start | bytes 786440 | tf_op jit(solution)/shard_map/ppermute | solution.py:18
  80.3 0.6 broadcast_in_dim.34
  80.9 1.6 %exp.64 = f32[16,4096]{1,0:T(8,128)S(1)} reshape(f32[16,256,16]{2,1,0:T(8,128)S(1)} %broadcast_in_dim.34) | data formatting | bytes 524288 | tf_op jit(solution)/shard_map/exp | solution.py:162
  82.5 3.3 %collective-permute-done.3 = f32[16,4096]{1,0:T(8,128)S(1)} collective-permute-done((f32[16,4096]{1,0:T(8,128)S(1)}, f32[16,4096]{1,0:T(8,128)S(1)}, u32[]{:S(2)}, u32[]{:S(2)}) %collective-permute-start.3) | collective-permute-done | bytes 262176 | tf_op jit(solution)/shard_map/ppermute | solution.py:18
  85.8 1.3 %collective-permute-start.4 = (f32[16,4096]{1,0:T(8,128)S(1)}, f32[16,4096]{1,0:T(8,128)S(1)}, u32[]{:S(2)}, u32[]{:S(2)}) collective-permute-start(f32[16,4096]{1,0:T(8,128)S(1)} %select_add_fusion.1), channel_id=1, source_target_pairs={{0,8},{1,9},{2,10},{3,11},{4,12},{5,13},{6,14},{7,15},{16,24},{17,... | collective-permute-start | bytes 786440 | tf_op jit(solution)/shard_map/ppermute | solution.py:18
  87.1 0.1 mul.167
  87.2 0.1 mul.165
  88.7 0.6 broadcast_in_dim.35
  89.3 1.6 %exp.67 = f32[16,4096]{1,0:T(8,128)S(1)} reshape(f32[16,256,16]{2,1,0:T(8,128)S(1)} %broadcast_in_dim.35) | data formatting | bytes 524288 | tf_op jit(solution)/shard_map/exp | solution.py:162
  90.8 8.3 %collective-permute-done.4 = f32[16,4096]{1,0:T(8,128)S(1)} collective-permute-done((f32[16,4096]{1,0:T(8,128)S(1)}, f32[16,4096]{1,0:T(8,128)S(1)}, u32[]{:S(2)}, u32[]{:S(2)}) %collective-permute-start.4) | collective-permute-done | bytes 262176 | tf_op jit(solution)/shard_map/ppermute | solution.py:18
  99.2 1.9 %collective-permute-start.5 = (f32[16,4096]{1,0:T(8,128)S(1)}, f32[16,4096]{1,0:T(8,128)S(1)}, u32[]{:S(2)}, u32[]{:S(2)}) collective-permute-start(f32[16,4096]{1,0:T(8,128)S(1)} %select_add_fusion), channel_id=1, source_target_pairs={{0,1},{1,2},{2,3},{3,4},{4,5},{5,6},{6,7},{7,8},{8,9},{9,10},{10,1... | collective-permute-start | bytes 786440 | tf_op jit(solution)/shard_map/ppermute | solution.py:18
  101.1 1.7 %multiply_multiply_fusion.iw_ref = f32[128,4096]{1,0:T(8,128)} fusion(f32[128]{0:T(128)S(1)} %get-tuple-element.28, f32[128]{0:T(128)S(1)} %convert_add_fusion, f32[4096]{0:T(1024)S(1)} %mul.167, f32[4096]{0:T(1024)S(1)} %mul.165), kind=kLoop, calls=%fused_computation.3 | loop fusion | flops 1572864 | bytes 2130944 | tf_op jit(solution)/shard_map/mul | solution.py:114
  104.1 3.7 %collective-permute-done.5 = f32[16,4096]{1,0:T(8,128)S(1)} collective-permute-done((f32[16,4096]{1,0:T(8,128)S(1)}, f32[16,4096]{1,0:T(8,128)S(1)}, u32[]{:S(2)}, u32[]{:S(2)}) %collective-permute-start.5) | collective-permute-done | bytes 262176 | tf_op jit(solution)/shard_map/ppermute | solution.py:18
  107.8 0.7 broadcast_select_fusion.b_ref
  108.5 12.1 %shard_map.56 = bf16[128,4096]{1,0:T(8,128)(2,1)} custom-call(f32[128,4096]{1,0:T(8,128)} %get-tuple-element.8.q_ref, f32[128,4096]{1,0:T(8,128)} %get-tuple-element.9.loc_ref, f32[128,4096]{1,0:T(8,128)} %multiply_multiply_fusion.iw_ref, f32[16,4096]{1,0:T(8,128)} %broadcast_select_fusion.b_ref), custom_call_target="tpu_custom_call" | custom-call | tf_op jit(solution)/shard_map/pallas_call | solution.py:169
  (15 shorter events, 0.3 us)
Async XLA Ops:
  0.9 33.0 %collective-permute-start = (bf16[8,12288]{1,0:T(8,128)(2,1)S(1)}, bf16[8,12288]{1,0:T(8,128)(2,1)S(1)}, u32[]{:S(2)}, u32[]{:S(2)}) collective-permute-start(bf16[8,12288]{1,0:T(8,128)(2,1)S(1)} %slice.31), channel_id=1, source_target_pairs={{0,1},{1,2},{2,3},{3,4},{4,5},{5,6},{6,7},{7,8},{8,9},{9,10},{10,1... | collective-permute-start | bytes 589832 | tf_op jit(solution)/shard_map/ppermute | solution.py:18
  29.0 2.4 %copy-start = (bf16[16,32768]{1,0:T(8,128)(2,1)}, bf16[16,32768]{1,0:T(8,128)(2,1)S(1)}, u32[]{:S(2)}) copy-start(bf16[16,32768]{1,0:T(8,128)(2,1)S(1)} %fusion.2.ewh_ref) | copy-start | bytes 3145732
  29.0 2.5 %copy-start.3 = (f32[256,16]{0,1:T(8,128)S(1)}, f32[256,16]{0,1:T(8,128)}, u32[]{:S(2)}) copy-start(f32[256,16]{0,1:T(8,128)} %param.9) | copy-start | bytes 49156
  34.0 0.7 copy-start.1
  58.9 8.8 %collective-permute-start.1 = (f32[16,4096]{1,0:T(8,128)}, f32[16,4096]{1,0:T(8,128)S(1)}, u32[]{:S(2)}, u32[]{:S(2)}) collective-permute-start(f32[16,4096]{1,0:T(8,128)} %get-tuple-element.10), channel_id=1, source_target_pairs={{0,1},{1,2},{2,3},{3,4},{4,5},{5,6},{6,7},{7,8},{8,9},{9,10},{10,1... | collective-permute-start | bytes 786440 | tf_op jit(solution)/shard_map/ppermute | solution.py:18
  61.3 6.4 %copy-start.2 = (f32[16,4096]{1,0:T(8,128)S(1)}, f32[16,4096]{1,0:T(8,128)}, u32[]{:S(2)}) copy-start(f32[16,4096]{1,0:T(8,128)} %get-tuple-element.10) | copy-start | bytes 786436
  67.8 9.7 %collective-permute-start.2 = (f32[16,4096]{1,0:T(8,128)S(1)}, f32[16,4096]{1,0:T(8,128)S(1)}, u32[]{:S(2)}, u32[]{:S(2)}) collective-permute-start(f32[16,4096]{1,0:T(8,128)S(1)} %select_add_fusion.3), channel_id=1, source_target_pairs={{0,2},{1,3},{2,4},{3,5},{4,6},{5,7},{6,8},{7,9},{8,10},{9,11},{10,... | collective-permute-start | bytes 786440 | tf_op jit(solution)/shard_map/ppermute | solution.py:18
  77.5 8.3 %collective-permute-start.3 = (f32[16,4096]{1,0:T(8,128)S(1)}, f32[16,4096]{1,0:T(8,128)S(1)}, u32[]{:S(2)}, u32[]{:S(2)}) collective-permute-start(f32[16,4096]{1,0:T(8,128)S(1)} %select_add_fusion.2), channel_id=1, source_target_pairs={{0,4},{1,5},{2,6},{3,7},{4,8},{5,9},{6,10},{7,11},{8,12},{9,13},{1... | collective-permute-start | bytes 786440 | tf_op jit(solution)/shard_map/ppermute | solution.py:18
  85.8 13.3 %collective-permute-start.4 = (f32[16,4096]{1,0:T(8,128)S(1)}, f32[16,4096]{1,0:T(8,128)S(1)}, u32[]{:S(2)}, u32[]{:S(2)}) collective-permute-start(f32[16,4096]{1,0:T(8,128)S(1)} %select_add_fusion.1), channel_id=1, source_target_pairs={{0,8},{1,9},{2,10},{3,11},{4,12},{5,13},{6,14},{7,15},{16,24},{17,... | collective-permute-start | bytes 786440 | tf_op jit(solution)/shard_map/ppermute | solution.py:18
  99.2 8.6 %collective-permute-start.5 = (f32[16,4096]{1,0:T(8,128)S(1)}, f32[16,4096]{1,0:T(8,128)S(1)}, u32[]{:S(2)}, u32[]{:S(2)}) collective-permute-start(f32[16,4096]{1,0:T(8,128)S(1)} %select_add_fusion), channel_id=1, source_target_pairs={{0,1},{1,2},{2,3},{3,4},{4,5},{5,6},{6,7},{7,8},{8,9},{9,10},{10,1... | collective-permute-start | bytes 786440 | tf_op jit(solution)/shard_map/ppermute | solution.py:18

commit v2 on v1

--- a/solution.py
+++ b/solution.py
@@ -68,7 +68,7 @@
     st_out[...] = st
 
 
-def final_kernel(group_width, pole_count, q_ref, loc_ref, iw_ref, b_ref, o_ref):
+def final_kernel(group_width, pole_count, q_ref, loc_ref, iwh_ref, iwl_ref, b_ref, o_ref):
     length, width = q_ref.shape
     groups = width // group_width
     b = b_ref[...]
@@ -76,7 +76,12 @@
     row_group = lax.broadcasted_iota(jnp.int32, tiled.shape, 0) // pole_count
     lane_group = lax.broadcasted_iota(jnp.int32, tiled.shape, 1) // group_width
     bbd = jnp.where(row_group == lane_group, tiled, 0.0)
-    car = jnp.dot(iw_ref[...], bbd, precision=HIGH, preferred_element_type=jnp.float32)
+    b_hi = bbd.astype(jnp.bfloat16)
+    b_lo = (bbd - b_hi.astype(jnp.float32)).astype(jnp.bfloat16)
+    iw_hi = iwh_ref[...]
+    car = jnp.dot(iw_hi, b_hi, preferred_element_type=jnp.float32)
+    car = car + jnp.dot(iw_hi, b_lo, preferred_element_type=jnp.float32)
+    car = car + jnp.dot(iwl_ref[...], b_hi, preferred_element_type=jnp.float32)
     o_ref[...] = (q_ref[...] * (loc_ref[...] + car)).astype(o_ref.dtype)
 
 
@@ -92,9 +97,9 @@
     peers = lax.axis_size("ctx")
     me = lax.axis_index("ctx")
 
-    doc_all = lax.all_gather(doc_ids, "ctx", tiled=True)
-    prev_docs = lax.dynamic_slice(doc_all, (jnp.maximum(me * length - RIM, 0),), (RIM,))
-    rim = from_behind(qkv[length - RIM:], "ctx", 1)
+    tail_docs = jnp.broadcast_to(doc_ids[length - RIM:, None].astype(jnp.bfloat16), (RIM, 128))
+    rim = from_behind(jnp.concatenate([qkv[length - RIM:], tail_docs], axis=1), "ctx", 1)
+    prev_docs = rim[:, 3 * channels].astype(jnp.int32)
 
     ext_docs = jnp.concatenate([prev_docs, doc_ids], axis=0)
     cols = [(ext_docs[RIM - j:RIM - j + length] == doc_ids) for j in range(taps)]
@@ -150,21 +155,27 @@
         compiler_params=pltpu.CompilerParams(dimension_semantics=("arbitrary",)),
     )(qkv, qkv, qkv, rim, rim, rim, short_w, short_w, short_w, masks, visible, base, ew_hi, ew_lo)
 
-    rate_cols = jnp.repeat(rates.T, group_width, axis=1)
-    doc_last = doc_all[length - 1::length]
-    mine_last = doc_last[me]
+    prev_last = prev_docs[RIM - 1]
+    flag = ((prev_last == doc_ids[0]) & (doc_ids[0] == doc_ids[length - 1])).astype(jnp.float32)
+    offsets = []
+    while (1 << len(offsets)) < peers:
+        offsets.append(1 << len(offsets))
+    spans = jnp.asarray([float(length * o) for o in offsets], jnp.float32)
+    decays = jnp.repeat(jnp.exp(-rates.T[None] * spans[:, None, None]), group_width, axis=2)
     total = states
-    offset = 1
-    while offset < peers:
-        got = from_behind(total, "ctx", offset)
-        source = jnp.maximum(me - offset, 0)
-        same = (me >= offset) & (doc_last[source] == mine_last)
-        decay = jnp.exp(-rate_cols * float(length * offset))
-        total = total + jnp.where(same, decay * got, 0.0)
-        offset *= 2
+    for step, offset in enumerate(offsets):
+        if step + 1 < len(offsets):
+            packed = jnp.concatenate([total, jnp.full((pole_count, 128), flag, jnp.float32)], axis=1)
+            got = from_behind(packed, "ctx", offset)
+            total = total + (flag * decays[step]) * got[:, :channels]
+            flag = flag * got[0, channels]
+        else:
+            got = from_behind(total, "ctx", offset)
+            total = total + (flag * decays[step]) * got
     before = from_behind(total, "ctx", 1)
-    joined = (me >= 1) & (doc_last[jnp.maximum(me - 1, 0)] == doc_ids[0])
+    joined = (me >= 1) & (prev_last == doc_ids[0])
     beginning = jnp.where(joined, before, 0.0)
+    iw_hi, iw_lo = split_bf16(in_weight)
 
     return pl.pallas_call(
         functools.partial(final_kernel, group_width, pole_count),
@@ -173,12 +184,13 @@
             pl.BlockSpec((length, width), col(0)),
             pl.BlockSpec((length, width), col(0)),
             pl.BlockSpec((length, gpb * pole_count), col(0)),
+            pl.BlockSpec((length, gpb * pole_count), col(0)),
             pl.BlockSpec((pole_count, width), col(0)),
         ],
         out_specs=pl.BlockSpec((length, width), col(0)),
         out_shape=jax.ShapeDtypeStruct((length, channels), jnp.bfloat16),
         compiler_params=pltpu.CompilerParams(dimension_semantics=("arbitrary",)),
-    )(q_part, local_part, in_weight, beginning)
+    )(q_part, local_part, iw_hi, iw_lo, beginning)
 
 
 def solution(mesh):

time: 122 us -> 119 us (0.975)
  blocking collectives: 17 us -> 0 us
  waiting for transfers between devices: 21.6 us -> 30.7 us
  local copies, waits for them, and re-layouts: 14.2 us -> 17.3 us
  other arithmetic: 13.7 us -> 16.2 us
  between operations: 6.66 us -> 4.78 us
  starting transfers between devices: 11.1 us -> 12.7 us
    all_gather x1 -> x0, blocking collectives: 17 us -> none  [on_device(): doc_all = lax.all_gather(doc_ids, 'ctx', tiled=True)]
    ppermute x6, waiting for transfers between devices: 21.6 us -> 30.7 us  [from_behind(): return lax.ppermute(shard, axis, pairs)]
    mul x0 -> x5, local copies, waits for them, and re-layouts: none -> 6.24 us  [the longest x3 4.67 us: on_device(): total = total + flag * decays[step] * got[:, :channels]]
    exp x4 -> x0, local copies, waits for them, and re-layouts: 6.23 us -> none  [on_device(): decay = jnp.exp(-rate_cols * float(length * offset))]
    slice x2 -> x6, local copies, waits for them, and re-layouts: 1.04 us -> 3.78 us  [the longest x3 2.22 us: on_device(): flag = flag * got[0, channels]]
    add x4, other arithmetic: 0.16 us -> 2.84 us  [the longest x3 1.78 us: on_device(): total = total + flag * decays[step] * got[:, :channels]]
    convert_element_type x1 -> x2, other arithmetic: 2.37 us -> 3.96 us  [split_bf16(): (x - lax.optimization_barrier(hi).astype(jnp.float32)).astype(jnp.bfloat16)]
    ppermute x6, starting transfers between devices: 11.1 us -> 12.7 us  [from_behind(): return lax.ppermute(shard, axis, pairs)]
  transfers between devices with their start and end apart: 6 -> 6, of which waited for: 5 -> 5; matrix products, arithmetic and copies ran while one was open for 21% -> 11% of each run, Pallas kernels for 0% -> 0%
where the time goes in v2:
time: 119 us; the launch traced here: 118 us
  Pallas kernels  36.1 us (30%)
  waiting for transfers between devices  30.7 us (26%)
  local copies, waits for them, and re-layouts  17.3 us (15%)
  other arithmetic  16.2 us (14%)
  starting transfers between devices  12.7 us (11%)
  between operations  4.78 us (4%)
    ppermute x6, waiting for transfers between devices, from_behind(): return lax.ppermute(shard, axis, pairs)  30.7 us
    pallas_call x1, Pallas kernels, on_device(): pl.pallas_call(functools.partial(local_kernel, taps, group_width), grid=(...  24.5 us
    ppermute x6, starting transfers between devices, from_behind(): return lax.ppermute(shard, axis, pairs)  12.7 us
    pallas_call x1, Pallas kernels, on_device(): pl.pallas_call(functools.partial(final_kernel, group_width, pole_count),...  11.6 us
    mul x3, local copies, waits for them, and re-layouts, on_device(): total = total + flag * decays[step] * got[:, :channels]  4.67 us
    convert_element_type x2, other arithmetic, split_bf16(): (x - lax.optimization_barrier(hi).astype(jnp.float32)).astype(jnp.bfloat16)  3.96 us
    broadcast_in_dim x4, local copies, waits for them, and re-layouts, on_device(): jnp.repeat(jnp.exp(-rates.T[None] * spans[:, None, None]), group_width, a...  2.39 us
  transfers between devices with their start and end apart: 6, of which 5 were waited for; matrix products, arithmetic and copies ran while one was open for 11% of the time, Pallas kernels for 0%

profile of v2, /device:TPU:24, one launch (start us, length us, event | category | flops | bytes accessed | tf_op | source)
XLA Modules:
  0.0 117.8 jit_solution(3947387330422515184)
XLA Ops:
  0.0 1.0 slice.80
  1.0 0.7 convert.3
  1.8 1.9 %collective-permute-start = (bf16[8,12416]{1,0:T(8,128)(2,1)S(1)}, bf16[8,12416]{1,0:T(8,128)(2,1)S(1)}, u32[]{:S(2)}, u32[]{:S(2)}) collective-permute-start(bf16[8,12416]{1,0:T(8,128)(2,1)S(1)} %pad_maximum_fusion), channel_id=1, source_target_pairs={{0,1},{1,2},{2,3},{3,4},{4,5},{5,6},{6,7},{7,8},{8,9},{9,10},{10,1... | collective-permute-start | bytes 595976 | tf_op jit(solution)/shard_map/ppermute | solution.py:18
  3.7 1.3 %fusion.16 = (s32[1]{0:T(128)}, s32[1]{0:T(128)}) fusion(s32[128]{0:T(128)} %param.7), kind=kLoop, calls=%fused_computation.51 | loop fusion | bytes 16 | tf_op jit(solution)/shard_map/slice | solution.py:115
  5.1 1.4 %fusion.8.m_ref = f32[128,128]{1,0:T(8,128)} fusion(s32[128]{0:T(128)} %param.7), kind=kLoop, calls=%fused_computation.23 | loop fusion | flops 65536 | bytes 66048 | tf_op jit(solution)/shard_map/convert_element_type | solution.py:109
  6.5 0.7 negate_bitcast_fusion
  7.2 0.1 copy.36
  7.3 0.8 copy.35
  9.4 2.3 %multiply_reduce_fusion.base_ref = f32[256,128]{1,0:T(8,128)} fusion(f32[128]{0:T(128)S(1)} %fusion.14, f32[256,16]{1,0:T(8,128)S(1)} %copy.36, f32[256,16]{1,0:T(8,128)S(1)} %copy.35), kind=kLoop, calls=%fused_computation.7 | loop fusion | flops 1540096 | bytes 164352 | tf_op jit(solution)/shard_map/reduce_sum | solution.py:113
  11.8 0.1 fusion.13
  12.0 1.4 %compare_convert_fusion = (f32[128]{0:T(128)S(1)}, f32[128]{0:T(128)S(1)}, pred[128,1]{0,1:T(4,128)(4,1)S(1)}, pred[128,1]{0,1:T(4,128)(4,1)S(1)}, pred[128,1]{0...) fusion(s32[128]{0:T(128)S(1)} %copy-done.4, s32[]{:T(128)} %bitcast.10, ...), kind=kLoop, calls=%fused_computation.35 | loop fusion | flops 1280 | bytes 5384 | tf_op jit(solution)/shard_map/convert_element_type | solution.py:115
  13.4 0.7 copy.37.masks_ref
  14.1 0.6 mul.189
  14.7 1.4 %fusion.3.ewh_ref = bf16[16,32768]{1,0:T(8,128)(2,1)S(1)} fusion(f32[2,8,256,128]{3,2,1,0:T(8,128)S(1)} %bitcast.43, f32[32768]{0:T(1024)S(1)} %broadcast_bitcast_fusion, f32[32768]{0:T(1024)S(1)} %broadcast_bitcast_fusion.1), kind=kLoop, calls=%fused_computation.8 | loop fusion | flops 1572864 | bytes 3407872 | tf_op jit(solution)/shard_map/convert_element_type | solution.py:22
  16.1 2.4 %subtract_convert_fusion.1.ewl_ref = bf16[16,32768]{1,0:T(8,128)(2,1)} fusion(bf16[16,32768]{1,0:T(8,128)(2,1)S(1)} %fusion.3.ewh_ref, f32[2,8,256,128]{3,2,1,0:T(8,128)S(1)} %bitcast.44, f32[32768]{0:T(1024)S(1)} %broadcast_bitcast_fusion, f32[32768]{0:T(1024)S(1)} %broadcast_bitcast_fusion.1), kind=kLoop, calls=%fused_computation.6 | loop fusion | flops 2621440 | bytes 4456448 | tf_op jit(solution)/shard_map/convert_element_type | solution.py:23
  18.5 0.5 slice.91
  20.3 24.5 %shard_map.64 = (f32[128,4096]{1,0:T(8,128)}, f32[128,4096]{1,0:T(8,128)}, f32[16,4096]{1,0:T(8,128)}) custom-call(bf16[128,12288]{1,0:T(8,128)(2,1)} %xv.1, bf16[128,12288]{1,0:T(8,128)(2,1)} %xv.1, bf16[128,12288]{1,0:T(8,128)(2,1)} %xv.1, bf16[8,12416]{1,0:T(8,128)(2,1)} %copy-done.2, bf16[8,12416]{1,0:T(8,128)(2,1)} %copy-done.2, ...), custom_call_target="tpu_custom_call" | custom-call | tf_op jit(solution)/shard_map/pallas_call | solution.py:125
  44.8 1.0 concatenate.17
  45.8 3.5 %collective-permute-start.1 = (f32[16,4224]{1,0:T(8,128)S(1)}, f32[16,4224]{1,0:T(8,128)S(1)}, u32[]{:S(2)}, u32[]{:S(2)}) collective-permute-start(f32[16,4224]{1,0:T(8,128)S(1)} %concatenate.17), channel_id=1, source_target_pairs={{0,1},{1,2},{2,3},{3,4},{4,5},{5,6},{6,7},{7,8},{8,9},{9,10},{10,1... | collective-permute-start | bytes 811016 | tf_op jit(solution)/shard_map/ppermute | solution.py:18
  49.4 5.0 %collective-permute-done.1 = f32[16,4224]{1,0:T(8,128)S(1)} collective-permute-done((f32[16,4224]{1,0:T(8,128)S(1)}, f32[16,4224]{1,0:T(8,128)S(1)}, u32[]{:S(2)}, u32[]{:S(2)}) %collective-permute-start.1) | collective-permute-done | bytes 270368 | tf_op jit(solution)/shard_map/ppermute | solution.py:18
  54.5 0.5 slice.105
  55.7 0.6 broadcast_in_dim.14
  56.3 1.6 %mul.214 = f32[16,4096]{1,0:T(8,128)S(1)} reshape(f32[16,256,16]{2,1,0:T(8,128)S(1)} %broadcast_in_dim.14) | data formatting | bytes 524288 | tf_op jit(solution)/shard_map/mul | solution.py:170
  57.9 2.5 %collective-permute-start.2 = (f32[16,4224]{1,0:T(8,128)S(1)}, f32[16,4224]{1,0:T(8,128)}, u32[]{:S(2)}, u32[]{:S(2)}) collective-permute-start(f32[16,4224]{1,0:T(8,128)S(1)} %concatenate.18), channel_id=1, source_target_pairs={{0,2},{1,3},{2,4},{3,5},{4,6},{5,7},{6,8},{7,9},{8,10},{9,11},{10,... | collective-permute-start | bytes 811016 | tf_op jit(solution)/shard_map/ppermute | solution.py:18
  60.4 0.6 broadcast_in_dim.15
  61.0 1.6 %mul.220 = f32[16,4096]{1,0:T(8,128)S(1)} reshape(f32[16,256,16]{2,1,0:T(8,128)S(1)} %broadcast_in_dim.15) | data formatting | bytes 524288 | tf_op jit(solution)/shard_map/mul | solution.py:170
  62.6 4.8 %collective-permute-done.2 = f32[16,4224]{1,0:T(8,128)} collective-permute-done((f32[16,4224]{1,0:T(8,128)S(1)}, f32[16,4224]{1,0:T(8,128)}, u32[]{:S(2)}, u32[]{:S(2)}) %collective-permute-start.2) | collective-permute-done | bytes 270368 | tf_op jit(solution)/shard_map/ppermute | solution.py:18
  67.4 1.2 %slice.108 = f32[1,1]{1,0:T(1,128)} slice(f32[16,4224]{1,0:T(8,128)} %collective-permute-done.2), slice={[0:1], [4096:4097]} | slice | bytes 8 | tf_op jit(solution)/shard_map/slice | solution.py:171
  69.3 1.0 fusion.5
  70.3 1.5 %collective-permute-start.3 = (f32[16,4224]{1,0:T(8,128)S(1)}, f32[16,4224]{1,0:T(8,128)S(1)}, u32[]{:S(2)}, u32[]{:S(2)}) collective-permute-start(f32[16,4224]{1,0:T(8,128)S(1)} %concatenate.19), channel_id=1, source_target_pairs={{0,4},{1,5},{2,6},{3,7},{4,8},{5,9},{6,10},{7,11},{8,12},{9,13},{1... | collective-permute-start | bytes 811016 | tf_op jit(solution)/shard_map/ppermute | solution.py:18
  71.8 0.1 mul.201
  71.9 0.1 mul.199
  72.0 6.6 %collective-permute-done.3 = f32[16,4224]{1,0:T(8,128)S(1)} collective-permute-done((f32[16,4224]{1,0:T(8,128)S(1)}, f32[16,4224]{1,0:T(8,128)S(1)}, u32[]{:S(2)}, u32[]{:S(2)}) %collective-permute-start.3) | collective-permute-done | bytes 270368 | tf_op jit(solution)/shard_map/ppermute | solution.py:18
  78.6 0.5 slice.111
  79.8 0.6 broadcast_in_dim.16
  80.4 1.6 %mul.226 = f32[16,4096]{1,0:T(8,128)S(1)} reshape(f32[16,256,16]{2,1,0:T(8,128)S(1)} %broadcast_in_dim.16) | data formatting | bytes 524288 | tf_op jit(solution)/shard_map/mul | solution.py:170
  82.0 0.7 fusion.4
  82.7 1.3 %collective-permute-start.4 = (f32[16,4096]{1,0:T(8,128)}, f32[16,4096]{1,0:T(8,128)}, u32[]{:S(2)}, u32[]{:S(2)}) collective-permute-start(f32[16,4096]{1,0:T(8,128)} %fusion.4), channel_id=1, source_target_pairs={{0,8},{1,9},{2,10},{3,11},{4,12},{5,13},{6,14},{7,15},{16,24},{17,... | collective-permute-start | bytes 786440 | tf_op jit(solution)/shard_map/ppermute | solution.py:18
  84.0 0.4 fusion.2.iwh_ref
  84.5 0.6 broadcast_in_dim.17
  85.1 1.6 %mul.232 = f32[16,4096]{1,0:T(8,128)S(1)} reshape(f32[16,256,16]{2,1,0:T(8,128)S(1)} %broadcast_in_dim.17) | data formatting | bytes 524288 | tf_op jit(solution)/shard_map/mul | solution.py:174
  86.6 9.2 %collective-permute-done.4 = f32[16,4096]{1,0:T(8,128)} collective-permute-done((f32[16,4096]{1,0:T(8,128)}, f32[16,4096]{1,0:T(8,128)}, u32[]{:S(2)}, u32[]{:S(2)}) %collective-permute-start.4) | collective-permute-done | bytes 262176 | tf_op jit(solution)/shard_map/ppermute | solution.py:18
  95.8 1.1 multiply_add_fusion
  96.9 1.9 %collective-permute-start.5 = (f32[16,4096]{1,0:T(8,128)S(1)}, f32[16,4096]{1,0:T(8,128)S(1)}, u32[]{:S(2)}, u32[]{:S(2)}) collective-permute-start(f32[16,4096]{1,0:T(8,128)S(1)} %multiply_add_fusion), channel_id=1, source_target_pairs={{0,1},{1,2},{2,3},{3,4},{4,5},{5,6},{6,7},{7,8},{8,9},{9,10},{10,1... | collective-permute-start | bytes 786440 | tf_op jit(solution)/shard_map/ppermute | solution.py:18
  98.8 1.6 %subtract_convert_fusion.iwl_ref = bf16[128,4096]{1,0:T(8,128)(2,1)} fusion(bf16[128,4096]{1,0:T(8,128)(2,1)S(1)} %fusion.2.iwh_ref, f32[128]{0:T(128)S(1)} %get-tuple-element.23, f32[128]{0:T(128)S(1)} %convert_add_fusion, f32[4096]{0:T(1024)S(1)} %mul.201, f32[4096]{0:T(1024)S(1)} %mul.199), kind=kLoop, calls=%fused_computation.3 | loop fusion | flops 3145728 | bytes 2130944 | tf_op jit(solution)/shard_map/convert_element_type | solution.py:23
  100.4 5.1 %collective-permute-done.5 = f32[16,4096]{1,0:T(8,128)S(1)} collective-permute-done((f32[16,4096]{1,0:T(8,128)S(1)}, f32[16,4096]{1,0:T(8,128)S(1)}, u32[]{:S(2)}, u32[]{:S(2)}) %collective-permute-start.5) | collective-permute-done | bytes 262176 | tf_op jit(solution)/shard_map/ppermute | solution.py:18
  105.5 0.7 broadcast_select_fusion.b_ref
  106.2 11.6 %shard_map.65 = bf16[128,4096]{1,0:T(8,128)(2,1)} custom-call(f32[128,4096]{1,0:T(8,128)} %get-tuple-element.8.q_ref, f32[128,4096]{1,0:T(8,128)} %get-tuple-element.9.loc_ref, bf16[128,4096]{1,0:T(8,128)(2,1)} %copy-done.1, bf16[128,4096]{1,0:T(8,128)(2,1)} %subtract_convert_fusion.iwl_ref, f32[16,4096]{1,0:T(8,128)} %broadcast_select_fusion.b_ref), custom_call_target="tpu_custom_call" | custom-call | tf_op jit(solution)/shard_map/pallas_call | solution.py:180
  (33 shorter events, 0.6 us)
Async XLA Ops:
  0.0 11.9 %copy-start.4 = (s32[128]{0:T(128)S(1)}, s32[128]{0:T(128)}, u32[]{:S(2)}) copy-start(s32[128]{0:T(128)} %param.7) | copy-start | bytes 1540
  1.8 10.0 %collective-permute-start = (bf16[8,12416]{1,0:T(8,128)(2,1)S(1)}, bf16[8,12416]{1,0:T(8,128)(2,1)S(1)}, u32[]{:S(2)}, u32[]{:S(2)}) collective-permute-start(bf16[8,12416]{1,0:T(8,128)(2,1)S(1)} %pad_maximum_fusion), channel_id=1, source_target_pairs={{0,1},{1,2},{2,3},{3,4},{4,5},{5,6},{6,7},{7,8},{8,9},{9,10},{10,1... | collective-permute-start | bytes 595976 | tf_op jit(solution)/shard_map/ppermute | solution.py:18
  11.8 6.7 %copy-start.2 = (bf16[8,12416]{1,0:T(8,128)(2,1)}, bf16[8,12416]{1,0:T(8,128)(2,1)S(1)}, u32[]{:S(2)}) copy-start(bf16[8,12416]{1,0:T(8,128)(2,1)S(1)} %collective-permute-done.rq.rk.rv) | copy-start | bytes 595972
  16.1 2.4 %copy-start = (bf16[16,32768]{1,0:T(8,128)(2,1)}, bf16[16,32768]{1,0:T(8,128)(2,1)S(1)}, u32[]{:S(2)}) copy-start(bf16[16,32768]{1,0:T(8,128)(2,1)S(1)} %fusion.3.ewh_ref) | copy-start | bytes 3145732
  20.3 29.0 %copy-start.5 = (f32[4]{0:T(128)S(1)}, f32[4]{0:T(128)}, u32[]{:S(2)}) copy-start(f32[4]{0:T(128)} %constant.35.clone) | copy-start | bytes 52
  45.8 8.7 %collective-permute-start.1 = (f32[16,4224]{1,0:T(8,128)S(1)}, f32[16,4224]{1,0:T(8,128)S(1)}, u32[]{:S(2)}, u32[]{:S(2)}) collective-permute-start(f32[16,4224]{1,0:T(8,128)S(1)} %concatenate.17), channel_id=1, source_target_pairs={{0,1},{1,2},{2,3},{3,4},{4,5},{5,6},{6,7},{7,8},{8,9},{9,10},{10,1... | collective-permute-start | bytes 811016 | tf_op jit(solution)/shard_map/ppermute | solution.py:18
  55.6 2.2 %copy-start.3 = (f32[16,4096]{1,0:T(8,128)S(1)}, f32[16,4096]{1,0:T(8,128)}, u32[]{:S(2)}) copy-start(f32[16,4096]{1,0:T(8,128)} %get-tuple-element.10) | copy-start | bytes 786436
  57.9 9.5 %collective-permute-start.2 = (f32[16,4224]{1,0:T(8,128)S(1)}, f32[16,4224]{1,0:T(8,128)}, u32[]{:S(2)}, u32[]{:S(2)}) collective-permute-start(f32[16,4224]{1,0:T(8,128)S(1)} %concatenate.18), channel_id=1, source_target_pairs={{0,2},{1,3},{2,4},{3,5},{4,6},{5,7},{6,8},{7,9},{8,10},{9,11},{10,... | collective-permute-start | bytes 811016 | tf_op jit(solution)/shard_map/ppermute | solution.py:18
  70.3 8.4 %collective-permute-start.3 = (f32[16,4224]{1,0:T(8,128)S(1)}, f32[16,4224]{1,0:T(8,128)S(1)}, u32[]{:S(2)}, u32[]{:S(2)}) collective-permute-start(f32[16,4224]{1,0:T(8,128)S(1)} %concatenate.19), channel_id=1, source_target_pairs={{0,4},{1,5},{2,6},{3,7},{4,8},{5,9},{6,10},{7,11},{8,12},{9,13},{1... | collective-permute-start | bytes 811016 | tf_op jit(solution)/shard_map/ppermute | solution.py:18
  82.7 13.1 %collective-permute-start.4 = (f32[16,4096]{1,0:T(8,128)}, f32[16,4096]{1,0:T(8,128)}, u32[]{:S(2)}, u32[]{:S(2)}) collective-permute-start(f32[16,4096]{1,0:T(8,128)} %fusion.4), channel_id=1, source_target_pairs={{0,8},{1,9},{2,10},{3,11},{4,12},{5,13},{6,14},{7,15},{16,24},{17,... | collective-permute-start | bytes 786440 | tf_op jit(solution)/shard_map/ppermute | solution.py:18
  84.5 14.3 %copy-start.1 = (bf16[128,4096]{1,0:T(8,128)(2,1)}, bf16[128,4096]{1,0:T(8,128)(2,1)S(1)}, u32[]{:S(2)}) copy-start(bf16[128,4096]{1,0:T(8,128)(2,1)S(1)} %fusion.2.iwh_ref) | copy-start | bytes 3145732
  96.9 8.6 %collective-permute-start.5 = (f32[16,4096]{1,0:T(8,128)S(1)}, f32[16,4096]{1,0:T(8,128)S(1)}, u32[]{:S(2)}, u32[]{:S(2)}) collective-permute-start(f32[16,4096]{1,0:T(8,128)S(1)} %multiply_add_fusion), channel_id=1, source_target_pairs={{0,1},{1,2},{2,3},{3,4},{4,5},{5,6},{6,7},{7,8},{8,9},{9,10},{10,1... | collective-permute-start | bytes 786440 | tf_op jit(solution)/shard_map/ppermute | solution.py:18

commit v3 on v1

v3 whole, which is shorter than its diff:
```python
import functools

import jax
import jax.numpy as jnp
from jax import lax
from jax.experimental import pallas as pl
from jax.experimental.pallas import tpu as pltpu
from jax.sharding import PartitionSpec as P

WIDTH = 256
FINAL_WIDTH = 1024
RIM = 8
LANES = 128


def from_behind(shard, axis, by):
    peers = lax.axis_size(axis)
    pairs = [(i, i + by) for i in range(peers) if 0 <= i + by < peers]
    return lax.ppermute(shard, axis, pairs)


def split2(x):
    hi = x.astype(jnp.bfloat16)
    lo = (x - hi.astype(jnp.float32)).astype(jnp.bfloat16)
    return hi, lo


def split3(x):
    hi = x.astype(jnp.bfloat16)
    rest = x - hi.astype(jnp.float32)
    mid = rest.astype(jnp.bfloat16)
    lo = (rest - mid.astype(jnp.float32)).astype(jnp.bfloat16)
    return hi, mid, lo


def local_kernel(taps, group_width, spans,
                 xq, xk, xv, rq, rk, rv, wq, wk, wv, masks_ref, m_ref, rt_ref, et_ref, tail_ref,
                 flag_ref, q_out, loc_out, pk_out, dec_out, ext_s):
    length, width = xq.shape
    groups = width // group_width
    pole_count = rt_ref.shape[1]
    channels = pk_out.shape[1] - LANES
    step = pl.program_id(0)
    masks = masks_ref[...]

    def conv(x_ref, r_ref, w_ref):
        ext_s[0:RIM, :] = r_ref[...].astype(jnp.float32)
        ext_s[RIM:RIM + length, :] = x_ref[...].astype(jnp.float32)
        w = w_ref[...]
        acc = (w[0:1, :] * ext_s[RIM:RIM + length, :]) * masks[:, 0:1]
        for j in range(1, taps):
            window = ext_s[pl.ds(RIM - j, length), :]
            acc = acc + (w[j:j + 1, :] * window) * masks[:, j:j + 1]
        return acc

    cq = conv(xq, rq, wq)
    ck = conv(xk, rk, wk)
    cv = conv(xv, rv, wv)
    q_out[...] = cq
    gated = (ck * cv).astype(jnp.bfloat16)

    lane_group = lax.broadcasted_iota(jnp.int32, (length, width), 1) // group_width
    zero = jnp.zeros_like(gated)
    xbd = jnp.concatenate([jnp.where(lane_group == g, gated, zero) for g in range(groups)], axis=0)

    rt = rt_ref[0]
    et = et_ref[0]
    lane = lax.broadcasted_iota(jnp.int32, (1, length), 1)
    lags = ((length - lane) % length).astype(jnp.float32)
    to_end = (length - 1 - lane).astype(jnp.float32)
    at_tail = tail_ref[0:1, :]
    visible = m_ref[...] > 0.5
    pieces = []
    ends = []
    for g in range(groups):
        a_col = rt[:, g:g + 1]
        r_col = et[:, g:g + 1]
        base = jnp.sum(r_col * jnp.exp(-a_col * lags), axis=0, keepdims=True)
        row = jnp.broadcast_to(base, (length, length))
        rolled = pltpu.roll(row, 0, 1, stride=1, stride_axis=0)
        pieces.append(jnp.where(visible, rolled, 0.0))
        ends.append(jnp.exp(-a_col * to_end) * at_tail)
    lhs = jnp.concatenate([jnp.concatenate(pieces, axis=1), jnp.concatenate(ends, axis=1)], axis=0)
    l_hi, l_lo = split2(lhs)
    rows = length + pole_count
    res = jnp.dot(jnp.concatenate([l_hi, l_lo], axis=0), xbd, preferred_element_type=jnp.float32)
    loc_out[...] = res[0:length] + res[rows:rows + length]
    st = res[length:rows] + res[rows + length:2 * rows]
    pk_out[:, pl.ds(pl.multiple_of(step * width, width), width)] = st

    @pl.when(step == 0)
    def _():
        pk_out[:, channels:channels + LANES] = jnp.broadcast_to(flag_ref[0:1, :], (pole_count, LANES))

    spread = (lax.broadcasted_iota(jnp.int32, (groups, width), 1) // group_width
              == lax.broadcasted_iota(jnp.int32, (groups, width), 0)).astype(jnp.bfloat16)
    rate_cols = None
    for piece in split3(rt):
        part = jnp.dot(piece, spread, preferred_element_type=jnp.float32)
        rate_cols = part if rate_cols is None else rate_cols + part
    for r, span in enumerate(spans):
        dec_out[r] = jnp.exp(-rate_cols * span)


def final_kernel(group_width, pole_count, sub, q_ref, loc_ref, b_ref, rf_ref, ef_ref, head_ref, join_ref, o_ref):
    length, width = q_ref.shape
    groups = sub // group_width
    tcol = (lax.broadcasted_iota(jnp.int32, (length, 1), 0) + 1).astype(jnp.float32)
    iw = ef_ref[...] * jnp.exp(-rf_ref[...] * tcol) * head_ref[...]
    iw_hi, iw_lo = split2(iw)
    b_all = b_ref[...] * join_ref[0:1, 0:1]
    shape = (groups * pole_count, sub)
    row_group = lax.broadcasted_iota(jnp.int32, shape, 0) // pole_count
    lane_group = lax.broadcasted_iota(jnp.int32, shape, 1) // group_width
    same = row_group == lane_group
    for s in range(width // sub):
        cols = slice(s * sub, (s + 1) * sub)
        tiled = jnp.concatenate([b_all[:, cols]] * groups, axis=0)
        b_hi, b_lo = split2(jnp.where(same, tiled, 0.0))
        poles = slice(s * shape[0], (s + 1) * shape[0])
        ih = iw_hi[:, poles]
        car = jnp.dot(ih, b_hi, preferred_element_type=jnp.float32)
        car = car + jnp.dot(ih, b_lo, preferred_element_type=jnp.float32)
        car = car + jnp.dot(iw_lo[:, poles], b_hi, preferred_element_type=jnp.float32)
        o_ref[:, cols] = (q_ref[:, cols] * (loc_ref[:, cols] + car)).astype(o_ref.dtype)


def on_device(qkv, doc_ids, short_w, rates, residues):
    length = qkv.shape[0]
    taps = short_w.shape[0]
    channels = qkv.shape[1] // 3
    filters, pole_count = rates.shape
    group_width = channels // filters
    width = min(WIDTH, channels)
    nb = channels // width
    gpb = width // group_width
    final_width = min(FINAL_WIDTH, channels)
    peers = lax.axis_size("ctx")
    me = lax.axis_index("ctx")

    tail_docs = jnp.broadcast_to(doc_ids[length - RIM:, None].astype(jnp.bfloat16), (RIM, LANES))
    rim = from_behind(jnp.concatenate([qkv[length - RIM:], tail_docs], axis=1), "ctx", 1)
    prev_docs = rim[:, 3 * channels].astype(jnp.int32)
    prev_last = prev_docs[RIM - 1]

    ext_docs = jnp.concatenate([prev_docs, doc_ids], axis=0)
    cols = [(ext_docs[RIM - j:RIM - j + length] == doc_ids) for j in range(taps)]
    cols += [jnp.zeros((length,), bool)] * (8 - taps)
    masks = jnp.stack(cols, axis=1).astype(jnp.float32)
    pos = jnp.arange(length)
    visible = ((pos[None, :] <= pos[:, None]) & (doc_ids[:, None] == doc_ids[None, :])).astype(jnp.float32)
    at_tail = jnp.broadcast_to((doc_ids == doc_ids[length - 1]).astype(jnp.float32)[None, :], (8, length))
    at_head = (doc_ids == doc_ids[0]).astype(jnp.float32)[:, None]
    flag = ((prev_last == doc_ids[0]) & (doc_ids[0] == doc_ids[length - 1])).astype(jnp.float32)
    flag_row = jnp.full((8, LANES), flag, jnp.float32)
    joined = ((me >= 1) & (prev_last == doc_ids[0])).astype(jnp.float32)
    join_row = jnp.full((8, LANES), joined, jnp.float32)

    rates_t = rates.reshape(nb, gpb, pole_count).transpose(0, 2, 1)
    residues_t = residues.reshape(nb, gpb, pole_count).transpose(0, 2, 1)
    offsets = []
    while (1 << len(offsets)) < peers:
        offsets.append(1 << len(offsets))
    rounds = max(len(offsets), 1)
    spans = tuple(float(length * o) for o in offsets) or (float(length),)

    col = lambda off: (lambda j: (0, j + off))
    fixed = lambda j: (0, 0)
    q_part, local_part, packed, decays = pl.pallas_call(
        functools.partial(local_kernel, taps, group_width, spans),
        grid=(nb,),
        in_specs=[
            pl.BlockSpec((length, width), col(0)),
            pl.BlockSpec((length, width), col(nb)),
            pl.BlockSpec((length, width), col(2 * nb)),
            pl.BlockSpec((RIM, width), col(0)),
            pl.BlockSpec((RIM, width), col(nb)),
            pl.BlockSpec((RIM, width), col(2 * nb)),
            pl.BlockSpec((taps, width), col(0)),
            pl.BlockSpec((taps, width), col(nb)),
            pl.BlockSpec((taps, width), col(2 * nb)),
            pl.BlockSpec((length, 8), fixed),
            pl.BlockSpec((length, length), fixed),
            pl.BlockSpec((1, pole_count, gpb), lambda j: (j, 0, 0)),
            pl.BlockSpec((1, pole_count, gpb), lambda j: (j, 0, 0)),
            pl.BlockSpec((8, length), fixed),
            pl.BlockSpec((8, LANES), fixed),
        ],
        out_specs=[
            pl.BlockSpec((length, width), col(0)),
            pl.BlockSpec((length, width), col(0)),
            pl.BlockSpec((pole_count, channels + LANES), fixed),
            pl.BlockSpec((rounds, pole_count, width), lambda j: (0, 0, j)),
        ],
        out_shape=[
            jax.ShapeDtypeStruct((length, channels), jnp.float32),
            jax.ShapeDtypeStruct((length, channels), jnp.float32),
            jax.ShapeDtypeStruct((pole_count, channels + LANES), jnp.float32),
            jax.ShapeDtypeStruct((rounds, pole_count, channels), jnp.float32),
        ],
        scratch_shapes=[pltpu.VMEM((RIM + length, width), jnp.float32)],
        compiler_params=pltpu.CompilerParams(dimension_semantics=("arbitrary",)),
    )(qkv, qkv, qkv, rim, rim, rim, short_w, short_w, short_w, masks, visible, rates_t, residues_t,
      at_tail, flag_row)

    for step, offset in enumerate(offsets):
        got = from_behind(packed, "ctx", offset)
        mine_flag = packed[:, channels:channels + 1]
        body = packed[:, :channels] + (mine_flag * decays[step]) * got[:, :channels]
        flags = jnp.broadcast_to(mine_flag * got[:, channels:channels + 1], (pole_count, LANES))
        packed = jnp.concatenate([body, flags], axis=1)
    before = from_behind(packed, "ctx", 1)

    nbf = channels // final_width
    return pl.pallas_call(
        functools.partial(final_kernel, group_width, pole_count, width),
        grid=(nbf,),
        in_specs=[
            pl.BlockSpec((length, final_width), col(0)),
            pl.BlockSpec((length, final_width), col(0)),
            pl.BlockSpec((pole_count, final_width), col(0)),
            pl.BlockSpec((1, final_width // group_width * pole_count), col(0)),
            pl.BlockSpec((1, final_width // group_width * pole_count), col(0)),
            pl.BlockSpec((length, 1), fixed),
            pl.BlockSpec((8, LANES), fixed),
        ],
        out_specs=pl.BlockSpec((length, final_width), col(0)),
        out_shape=jax.ShapeDtypeStruct((length, channels), jnp.bfloat16),
        compiler_params=pltpu.CompilerParams(dimension_semantics=("arbitrary",)),
    )(q_part, local_part, before, rates.reshape(1, filters * pole_count),
      residues.reshape(1, filters * pole_count), at_head, join_row)


def solution(mesh):
    return jax.shard_map(
        on_device,
        mesh=mesh,
        in_specs=(P(("groups", "ctx"), None), P(("groups", "ctx")), P(), P(), P()),
        out_specs=P(("groups", "ctx"), None),
        check_vma=False,
    )
```

time: 122 us -> 104 us (0.85)
  blocking collectives: 17 us -> 0 us
  waiting for transfers between devices: 21.6 us -> 35.7 us
  other arithmetic: 13.7 us -> 8.71 us
  Pallas kernels: 36.4 us -> 32.6 us
  between operations: 6.66 us -> 2.87 us
  local copies, waits for them, and re-layouts: 14.2 us -> 10.8 us
  starting transfers between devices: 11.1 us -> 12.6 us
    all_gather x1 -> x0, blocking collectives: 17 us -> none  [on_device(): doc_all = lax.all_gather(doc_ids, 'ctx', tiled=True)]
    ppermute x6, waiting for transfers between devices: 21.6 us -> 35.7 us  [from_behind(): return lax.ppermute(shard, axis, pairs)]
    exp x4 -> x0, local copies, waits for them, and re-layouts: 6.23 us -> none  [on_device(): decay = jnp.exp(-rate_cols * float(length * offset))]
    convert_element_type x4 -> x2, other arithmetic: 5.81 us -> 0.12 us  [on_device(): prev_docs = rim[:, 3 * channels].astype(jnp.int32)]
    pallas_call x2, Pallas kernels: 36.4 us -> 32.6 us  [the longest x1 27.8 us: on_device(): pl.pallas_call(functools.partial(local_kernel, taps, group_width, spans),...]
    reshape x0 -> x4, local copies, waits for them, and re-layouts: none -> 3.04 us  [the longest x1 0.81 us: on_device(): rates_t = rates.reshape(nb, gpb, pole_count).transpose(0, 2, 1)]
    reduce_sum x1 -> x0, other arithmetic: 2.33 us -> none  [on_device(): jnp.sum(residues[:, :, None] * jnp.exp(-rates[:, :, None] * lags[None, No...]
    add x5 -> x4, other arithmetic: 0.16 us -> 2.42 us  [on_device(): body = packed[:, :channels] + mine_flag * decays[step] * got[:, :channels]]
  transfers between devices with their start and end apart: 6 -> 6, of which waited for: 5 -> 5; matrix products, arithmetic and copies ran while one was open for 21% -> 7% of each run, Pallas kernels for 0% -> 0%
where the time goes in v3:
time: 104 us; the launch traced here: 103 us
  waiting for transfers between devices  35.7 us (34%)
  Pallas kernels  32.6 us (31%)
  starting transfers between devices  12.6 us (12%)
  local copies, waits for them, and re-layouts  10.8 us (10%)
  other arithmetic  8.71 us (8%)
  between operations  2.87 us (3%)
    ppermute x6, waiting for transfers between devices, from_behind(): return lax.ppermute(shard, axis, pairs)  35.7 us
    pallas_call x1, Pallas kernels, on_device(): pl.pallas_call(functools.partial(local_kernel, taps, group_width, spans),...  27.8 us
    ppermute x6, starting transfers between devices, from_behind(): return lax.ppermute(shard, axis, pairs)  12.6 us
    pallas_call x1, Pallas kernels, on_device(): pl.pallas_call(functools.partial(final_kernel, group_width, pole_count, w...  4.89 us
    add x4, other arithmetic, on_device(): body = packed[:, :channels] + mine_flag * decays[step] * got[:, :channels]  2.42 us
  transfers between devices with their start and end apart: 6, of which 5 were waited for; matrix products, arithmetic and copies ran while one was open for 7% of the time, Pallas kernels for 0%

profile of v3, /device:TPU:24, one launch (start us, length us, event | category | flops | bytes accessed | tf_op | source)
XLA Modules:
  0.0 103.3 jit_solution(13759787753626284607)
XLA Ops:
  0.0 0.7 convert.4
  0.7 0.1 slice.88
  0.7 0.9 slice.87
  1.7 0.1 broadcast_in_dim.22
  1.8 1.9 %collective-permute-start = (bf16[8,12416]{1,0:T(8,128)(2,1)S(1)}, bf16[8,12416]{1,0:T(8,128)(2,1)S(1)}, u32[]{:S(2)}, u32[]{:S(2)}) collective-permute-start(bf16[8,12416]{1,0:T(8,128)(2,1)S(1)} %pad_maximum_fusion.4), channel_id=1, source_target_pairs={{0,1},{1,2},{2,3},{3,4},{4,5},{5,6},{6,7},{7,8},{8,9},{9,10},{10,1... | collective-permute-start | bytes 595976 | tf_op jit(solution)/shard_map/ppermute | solution.py:19
  3.7 1.4 %fusion.12 = (s32[1]{0:T(128)}, s32[1]{0:T(128)}) fusion(s32[128]{0:T(128)} %param.6), kind=kLoop, calls=%fused_computation.43 | loop fusion | bytes 16 | tf_op jit(solution)/shard_map/slice | solution.py:154
  5.1 0.8 reshape.30
  5.9 0.8 reshape.29
  6.7 0.8 copy_bitcast_fusion
  8.9 1.4 %fusion.5.m_ref = f32[128,128]{1,0:T(8,128)} fusion(s32[128]{0:T(128)} %param.6), kind=kLoop, calls=%fused_computation.21 | loop fusion | flops 65536 | bytes 66048 | tf_op jit(solution)/shard_map/convert_element_type | solution.py:151
  10.3 0.1 fusion.8
  10.4 0.7 pad_add_fusion
  11.1 2.1 %fusion.9 = (f32[128,1]{0,1:T(1,128)S(1)}, f32[128]{0:T(128)S(1)}, pred[128,1]{0,1:T(4,128)(4,1)S(1)}, pred[128,1]{0,1:T(4,128)(4,1)S(1)}, pred[128,1]{0,1:T(4,1...) fusion(s32[128]{0:T(128)} %param.6, s32[]{:T(128)} %bitcast.10, ...), kind=kLoop, calls=%fused_computation.40 | loop fusion | flops 1280 | bytes 5384 | tf_op jit(solution)/shard_map/broadcast_in_dim | solution.py:153
  13.3 0.7 copy.34.masks_ref
  14.0 0.6 slice.97
  15.9 0.6 broadcast_in_dim.23.tail_ref
  16.5 0.6 broadcast_in_dim.24.flag_ref
  17.1 27.8 %shard_map.55 = (f32[128,4096]{1,0:T(8,128)}, f32[128,4096]{1,0:T(8,128)}, f32[16,4224]{1,0:T(8,128)}, f32[4,16,4096]{2,1,0:T(8,128)}) custom-call(bf16[128,12288]{1,0:T(8,128)(2,1)} %xv.1, bf16[128,12288]{1,0:T(8,128)(2,1)} %xv.1, bf16[128,12288]{1,0:T(8,128)(2,1)} %xv.1, bf16[8,12416]{1,0:T(8,128)(2,1)} %copy-done, bf16[8,12416]{1,0:T(8,128)(2,1)} %copy-done, ...), custom_call_target="tpu_custom_call" | custom-call | tf_op jit(solution)/shard_map/pallas_call | solution.py:169
  44.9 3.7 %collective-permute-start.1 = (f32[16,4224]{1,0:T(8,128)}, f32[16,4224]{1,0:T(8,128)S(1)}, u32[]{:S(2)}, u32[]{:S(2)}) collective-permute-start(f32[16,4224]{1,0:T(8,128)} %get-tuple-element.11), channel_id=1, source_target_pairs={{0,1},{1,2},{2,3},{3,4},{4,5},{5,6},{6,7},{7,8},{8,9},{9,10},{10,1... | collective-permute-start | bytes 811016 | tf_op jit(solution)/shard_map/ppermute | solution.py:19
  48.6 5.3 %collective-permute-done.1 = f32[16,4224]{1,0:T(8,128)S(1)} collective-permute-done((f32[16,4224]{1,0:T(8,128)}, f32[16,4224]{1,0:T(8,128)S(1)}, u32[]{:S(2)}, u32[]{:S(2)}) %collective-permute-start.1) | collective-permute-done | bytes 270368 | tf_op jit(solution)/shard_map/ppermute | solution.py:19
  53.9 0.8 fusion.11
  54.7 1.1 %fusion.3 = f32[16,4096]{1,0:T(8,128)S(1)} fusion(f32[16,4224]{1,0:T(8,128)S(1)} %collective-permute-done.1, f32[4,16,4096]{2,1,0:T(8,128)} %get-tuple-element.12, f32[16,4224]{1,0:T(8,128)} %get-tuple-element.11, f32[16]{0:T(128)S(1)} %get-tuple-element.15), kind=kLoop, calls=%fused_computation.11 | loop fusion | flops 196608 | bytes 1048640 | tf_op jit(solution)/shard_map/add | solution.py:209
  55.9 0.1 broadcast_in_dim.25
  56.0 2.5 %collective-permute-start.2 = (f32[16,4224]{1,0:T(8,128)S(1)}, f32[16,4224]{1,0:T(8,128)S(1)}, u32[]{:S(2)}, u32[]{:S(2)}) collective-permute-start(f32[16,4224]{1,0:T(8,128)S(1)} %pad_maximum_fusion), channel_id=1, source_target_pairs={{0,2},{1,3},{2,4},{3,5},{4,6},{5,7},{6,8},{7,9},{8,10},{9,11},{10,... | collective-permute-start | bytes 811016 | tf_op jit(solution)/shard_map/ppermute | solution.py:19
  58.5 7.0 %collective-permute-done.2 = f32[16,4224]{1,0:T(8,128)S(1)} collective-permute-done((f32[16,4224]{1,0:T(8,128)S(1)}, f32[16,4224]{1,0:T(8,128)S(1)}, u32[]{:S(2)}, u32[]{:S(2)}) %collective-permute-start.2) | collective-permute-done | bytes 270368 | tf_op jit(solution)/shard_map/ppermute | solution.py:19
  65.5 1.1 %fusion.2 = f32[16,4096]{1,0:T(8,128)S(1)} fusion(f32[16,4096]{1,0:T(8,128)S(1)} %fusion.3, f32[16,4224]{1,0:T(8,128)S(1)} %collective-permute-done.2, f32[4,16,4096]{2,1,0:T(8,128)} %get-tuple-element.12, f32[16]{0:T(128)S(1)} %get-tuple-element.13), kind=kLoop, calls=%fused_computation.9 | loop fusion | flops 196608 | bytes 1048640 | tf_op jit(solution)/shard_map/add | solution.py:209
  66.6 0.1 fusion.7
  66.7 0.1 broadcast_in_dim.26
  66.8 1.3 %collective-permute-start.3 = (f32[16,4224]{1,0:T(8,128)S(1)}, f32[16,4224]{1,0:T(8,128)S(1)}, u32[]{:S(2)}, u32[]{:S(2)}) collective-permute-start(f32[16,4224]{1,0:T(8,128)S(1)} %pad_maximum_fusion.1), channel_id=1, source_target_pairs={{0,4},{1,5},{2,6},{3,7},{4,8},{5,9},{6,10},{7,11},{8,12},{9,13},{1... | collective-permute-start | bytes 811016 | tf_op jit(solution)/shard_map/ppermute | solution.py:19
  68.1 7.1 %collective-permute-done.3 = f32[16,4224]{1,0:T(8,128)S(1)} collective-permute-done((f32[16,4224]{1,0:T(8,128)S(1)}, f32[16,4224]{1,0:T(8,128)S(1)}, u32[]{:S(2)}, u32[]{:S(2)}) %collective-permute-start.3) | collective-permute-done | bytes 270368 | tf_op jit(solution)/shard_map/ppermute | solution.py:19
  75.2 0.1 fusion.10
  75.3 0.1 fusion.1
  75.4 0.1 broadcast_in_dim.54
  75.5 1.3 %collective-permute-start.4 = (f32[16,4224]{1,0:T(8,128)S(1)}, f32[16,4224]{1,0:T(8,128)S(1)}, u32[]{:S(2)}, u32[]{:S(2)}) collective-permute-start(f32[16,4224]{1,0:T(8,128)S(1)} %pad_maximum_fusion.2), channel_id=1, source_target_pairs={{0,8},{1,9},{2,10},{3,11},{4,12},{5,13},{6,14},{7,15},{16,24},{17,... | collective-permute-start | bytes 811016 | tf_op jit(solution)/shard_map/ppermute | solution.py:19
  76.8 11.9 %collective-permute-done.4 = f32[16,4224]{1,0:T(8,128)S(1)} collective-permute-done((f32[16,4224]{1,0:T(8,128)S(1)}, f32[16,4224]{1,0:T(8,128)S(1)}, u32[]{:S(2)}, u32[]{:S(2)}) %collective-permute-start.4) | collective-permute-done | bytes 270368 | tf_op jit(solution)/shard_map/ppermute | solution.py:19
  88.7 0.1 fusion.6
  88.8 0.1 fusion
  89.0 0.1 broadcast_in_dim.56
  89.1 1.9 %collective-permute-start.5 = (f32[16,4224]{1,0:T(8,128)S(1)}, f32[16,4224]{1,0:T(8,128)S(1)}, u32[]{:S(2)}, u32[]{:S(2)}) collective-permute-start(f32[16,4224]{1,0:T(8,128)S(1)} %pad_maximum_fusion.3), channel_id=1, source_target_pairs={{0,1},{1,2},{2,3},{3,4},{4,5},{5,6},{6,7},{7,8},{8,9},{9,10},{10,1... | collective-permute-start | bytes 811016 | tf_op jit(solution)/shard_map/ppermute | solution.py:19
  91.0 0.1 copy.35
  91.1 0.1 copy.36
  91.2 0.7 reshape.31.rf_ref
  91.9 0.7 reshape.32.ef_ref
  92.6 0.7 copy.37.head_ref
  93.4 4.4 %collective-permute-done.5.b_ref = f32[16,4224]{1,0:T(8,128)S(1)} collective-permute-done((f32[16,4224]{1,0:T(8,128)S(1)}, f32[16,4224]{1,0:T(8,128)S(1)}, u32[]{:S(2)}, u32[]{:S(2)}) %collective-permute-start.5) | collective-permute-done | bytes 270368 | tf_op jit(solution)/shard_map/ppermute | solution.py:19
  97.7 0.6 broadcast_in_dim.59.join_ref
  98.4 0.1 copy-done.2
  98.4 4.9 %shard_map.56 = bf16[128,4096]{1,0:T(8,128)(2,1)} custom-call(f32[128,4096]{1,0:T(8,128)} %get-tuple-element.9.q_ref, f32[128,4096]{1,0:T(8,128)} %get-tuple-element.10.loc_ref, f32[16,4224]{1,0:T(8,128)} %copy-done.2, f32[1,4096]{1,0:T(1,128)} %reshape.31.rf_ref, f32[1,4096]{1,0:T(1,128)} %reshape.32.ef_ref, f32[128,1]{1,0:T(8,128)} %copy.37.head_ref, ...), custom_call_target="tpu_custom_call" | custom-call | tf_op jit(solution)/shard_map/pallas_call | solution.py:215
  (20 shorter events, 0.2 us)
Async XLA Ops:
  1.8 8.5 %collective-permute-start = (bf16[8,12416]{1,0:T(8,128)(2,1)S(1)}, bf16[8,12416]{1,0:T(8,128)(2,1)S(1)}, u32[]{:S(2)}, u32[]{:S(2)}) collective-permute-start(bf16[8,12416]{1,0:T(8,128)(2,1)S(1)} %pad_maximum_fusion.4), channel_id=1, source_target_pairs={{0,1},{1,2},{2,3},{3,4},{4,5},{5,6},{6,7},{7,8},{8,9},{9,10},{10,1... | collective-permute-start | bytes 595976 | tf_op jit(solution)/shard_map/ppermute | solution.py:19
  10.3 6.8 %copy-start = (bf16[8,12416]{1,0:T(8,128)(2,1)}, bf16[8,12416]{1,0:T(8,128)(2,1)S(1)}, u32[]{:S(2)}) copy-start(bf16[8,12416]{1,0:T(8,128)(2,1)S(1)} %collective-permute-done.rq.rk.rv) | copy-start | bytes 595972
  44.9 30.4 %copy-start.1 = (f32[4,16,4096]{2,1,0:T(8,128)S(1)}, f32[4,16,4096]{2,1,0:T(8,128)}, u32[]{:S(2)}) copy-start(f32[4,16,4096]{2,1,0:T(8,128)} %get-tuple-element.12) | copy-start | bytes 3145732
  44.9 9.0 %collective-permute-start.1 = (f32[16,4224]{1,0:T(8,128)}, f32[16,4224]{1,0:T(8,128)S(1)}, u32[]{:S(2)}, u32[]{:S(2)}) collective-permute-start(f32[16,4224]{1,0:T(8,128)} %get-tuple-element.11), channel_id=1, source_target_pairs={{0,1},{1,2},{2,3},{3,4},{4,5},{5,6},{6,7},{7,8},{8,9},{9,10},{10,1... | collective-permute-start | bytes 811016 | tf_op jit(solution)/shard_map/ppermute | solution.py:19
  56.0 9.5 %collective-permute-start.2 = (f32[16,4224]{1,0:T(8,128)S(1)}, f32[16,4224]{1,0:T(8,128)S(1)}, u32[]{:S(2)}, u32[]{:S(2)}) collective-permute-start(f32[16,4224]{1,0:T(8,128)S(1)} %pad_maximum_fusion), channel_id=1, source_target_pairs={{0,2},{1,3},{2,4},{3,5},{4,6},{5,7},{6,8},{7,9},{8,10},{9,11},{10,... | collective-permute-start | bytes 811016 | tf_op jit(solution)/shard_map/ppermute | solution.py:19
  66.6 24.4 %copy-start.3 = (f32[256,16]{0,1:T(8,128)S(1)}, f32[256,16]{0,1:T(8,128)}, u32[]{:S(2)}) copy-start(f32[256,16]{0,1:T(8,128)} %param.8) | copy-start | bytes 49156
  66.6 24.5 %copy-start.4 = (f32[256,16]{0,1:T(8,128)S(1)}, f32[256,16]{0,1:T(8,128)}, u32[]{:S(2)}) copy-start(f32[256,16]{0,1:T(8,128)} %param.9) | copy-start | bytes 49156
  66.8 8.4 %collective-permute-start.3 = (f32[16,4224]{1,0:T(8,128)S(1)}, f32[16,4224]{1,0:T(8,128)S(1)}, u32[]{:S(2)}, u32[]{:S(2)}) collective-permute-start(f32[16,4224]{1,0:T(8,128)S(1)} %pad_maximum_fusion.1), channel_id=1, source_target_pairs={{0,4},{1,5},{2,6},{3,7},{4,8},{5,9},{6,10},{7,11},{8,12},{9,13},{1... | collective-permute-start | bytes 811016 | tf_op jit(solution)/shard_map/ppermute | solution.py:19
  75.5 13.2 %collective-permute-start.4 = (f32[16,4224]{1,0:T(8,128)S(1)}, f32[16,4224]{1,0:T(8,128)S(1)}, u32[]{:S(2)}, u32[]{:S(2)}) collective-permute-start(f32[16,4224]{1,0:T(8,128)S(1)} %pad_maximum_fusion.2), channel_id=1, source_target_pairs={{0,8},{1,9},{2,10},{3,11},{4,12},{5,13},{6,14},{7,15},{16,24},{17,... | collective-permute-start | bytes 811016 | tf_op jit(solution)/shard_map/ppermute | solution.py:19
  89.1 8.7 %collective-permute-start.5 = (f32[16,4224]{1,0:T(8,128)S(1)}, f32[16,4224]{1,0:T(8,128)S(1)}, u32[]{:S(2)}, u32[]{:S(2)}) collective-permute-start(f32[16,4224]{1,0:T(8,128)S(1)} %pad_maximum_fusion.3), channel_id=1, source_target_pairs={{0,1},{1,2},{2,3},{3,4},{4,5},{5,6},{6,7},{7,8},{8,9},{9,10},{10,1... | collective-permute-start | bytes 811016 | tf_op jit(solution)/shard_map/ppermute | solution.py:19
  97.7 0.7 copy-start.2

commit v4 on v3

--- a/solution.py
+++ b/solution.py
@@ -34,23 +34,47 @@
 
 
 def local_kernel(taps, group_width, spans,
-                 xq, xk, xv, rq, rk, rv, wq, wk, wv, masks_ref, m_ref, rt_ref, et_ref, tail_ref,
-                 flag_ref, q_out, loc_out, pk_out, dec_out, ext_s):
+                 xq, xk, xv, rq, rk, rv, wq, wk, wv, e_ref, rt_ref, et_ref,
+                 q_out, loc_out, pk_out, dec_out, info_out, ext_s, shift_s, vis_s, tail_s):
     length, width = xq.shape
     groups = width // group_width
     pole_count = rt_ref.shape[1]
     channels = pk_out.shape[1] - LANES
+    span_r = e_ref.shape[1]
     step = pl.program_id(0)
-    masks = masks_ref[...]
+
+    @pl.when(step == 0)
+    def _():
+        e_row = e_ref[0:1, :]
+        t_col = lax.broadcasted_iota(jnp.int32, (length, span_r), 0)
+        r_row = lax.broadcasted_iota(jnp.int32, (length, span_r), 1)
+        doc_col = jnp.sum(jnp.where(r_row == t_col, e_row, 0.0), axis=1, keepdims=True)
+        eq = e_row == doc_col
+        place = jnp.where(r_row < length, r_row, r_row - length - RIM)
+        for j in range(taps):
+            hit = eq & (place == t_col - j) & (r_row < length + RIM)
+            shift_s[j * length:(j + 1) * length, :] = jnp.where(hit, 1.0, 0.0).astype(jnp.bfloat16)
+        eqf = jnp.where(eq, 1.0, 0.0)
+        causal = r_row[:, :length] <= t_col[:, :length]
+        vis_s[...] = jnp.where(causal, eqf[:, :length], 0.0)
+        tail_s[...] = jnp.broadcast_to(eqf[length - 1:length, :length], tail_s.shape)
+        into = eqf[0:1, length + RIM - 1:length + RIM]
+        flag = into * eqf[length - 1:length, 0:1]
+        pk_out[:, channels:channels + LANES] = jnp.broadcast_to(flag, (pole_count, LANES))
+        lane = lax.broadcasted_iota(jnp.int32, info_out.shape, 1)
+        info_out[...] = jnp.where(lane == 0, eqf[:, 0:1], jnp.broadcast_to(into, info_out.shape))
+        ext_s[...] = jnp.zeros_like(ext_s)
+
+    shifts = shift_s[...]
 
     def conv(x_ref, r_ref, w_ref):
-        ext_s[0:RIM, :] = r_ref[...].astype(jnp.float32)
-        ext_s[RIM:RIM + length, :] = x_ref[...].astype(jnp.float32)
+        ext_s[0:length, :] = x_ref[...]
+        ext_s[length:length + RIM, :] = r_ref[...]
+        windows = jnp.dot(shifts, ext_s[...], preferred_element_type=jnp.float32)
         w = w_ref[...]
-        acc = (w[0:1, :] * ext_s[RIM:RIM + length, :]) * masks[:, 0:1]
+        acc = w[0:1, :] * windows[0:length]
         for j in range(1, taps):
-            window = ext_s[pl.ds(RIM - j, length), :]
-            acc = acc + (w[j:j + 1, :] * window) * masks[:, j:j + 1]
+            acc = acc + w[j:j + 1, :] * windows[j * length:(j + 1) * length]
         return acc
 
     cq = conv(xq, rq, wq)
@@ -68,8 +92,8 @@
     lane = lax.broadcasted_iota(jnp.int32, (1, length), 1)
     lags = ((length - lane) % length).astype(jnp.float32)
     to_end = (length - 1 - lane).astype(jnp.float32)
-    at_tail = tail_ref[0:1, :]
-    visible = m_ref[...] > 0.5
+    at_tail = tail_s[0:1, :]
+    visible = vis_s[...] > 0.5
     pieces = []
     ends = []
     for g in range(groups):
@@ -88,10 +112,6 @@
     st = res[length:rows] + res[rows + length:2 * rows]
     pk_out[:, pl.ds(pl.multiple_of(step * width, width), width)] = st
 
-    @pl.when(step == 0)
-    def _():
-        pk_out[:, channels:channels + LANES] = jnp.broadcast_to(flag_ref[0:1, :], (pole_count, LANES))
-
     spread = (lax.broadcasted_iota(jnp.int32, (groups, width), 1) // group_width
               == lax.broadcasted_iota(jnp.int32, (groups, width), 0)).astype(jnp.bfloat16)
     rate_cols = None
@@ -102,13 +122,13 @@
         dec_out[r] = jnp.exp(-rate_cols * span)
 
 
-def final_kernel(group_width, pole_count, sub, q_ref, loc_ref, b_ref, rf_ref, ef_ref, head_ref, join_ref, o_ref):
+def final_kernel(group_width, pole_count, sub, q_ref, loc_ref, b_ref, rf_ref, ef_ref, info_ref, o_ref):
     length, width = q_ref.shape
     groups = sub // group_width
     tcol = (lax.broadcasted_iota(jnp.int32, (length, 1), 0) + 1).astype(jnp.float32)
-    iw = ef_ref[...] * jnp.exp(-rf_ref[...] * tcol) * head_ref[...]
+    iw = ef_ref[...] * jnp.exp(-rf_ref[...] * tcol) * info_ref[:, 0:1]
     iw_hi, iw_lo = split2(iw)
-    b_all = b_ref[...] * join_ref[0:1, 0:1]
+    b_all = b_ref[...] * info_ref[0:1, 1:2]
     shape = (groups * pole_count, sub)
     row_group = lax.broadcasted_iota(jnp.int32, shape, 0) // pole_count
     lane_group = lax.broadcasted_iota(jnp.int32, shape, 1) // group_width
@@ -143,18 +163,9 @@
     prev_docs = rim[:, 3 * channels].astype(jnp.int32)
     prev_last = prev_docs[RIM - 1]
 
-    ext_docs = jnp.concatenate([prev_docs, doc_ids], axis=0)
-    cols = [(ext_docs[RIM - j:RIM - j + length] == doc_ids) for j in range(taps)]
-    cols += [jnp.zeros((length,), bool)] * (8 - taps)
-    masks = jnp.stack(cols, axis=1).astype(jnp.float32)
-    pos = jnp.arange(length)
-    visible = ((pos[None, :] <= pos[:, None]) & (doc_ids[:, None] == doc_ids[None, :])).astype(jnp.float32)
-    at_tail = jnp.broadcast_to((doc_ids == doc_ids[length - 1]).astype(jnp.float32)[None, :], (8, length))
-    at_head = (doc_ids == doc_ids[0]).astype(jnp.float32)[:, None]
-    flag = ((prev_last == doc_ids[0]) & (doc_ids[0] == doc_ids[length - 1])).astype(jnp.float32)
-    flag_row = jnp.full((8, LANES), flag, jnp.float32)
-    joined = ((me >= 1) & (prev_last == doc_ids[0])).astype(jnp.float32)
-    join_row = jnp.full((8, LANES), joined, jnp.float32)
+    span_r = 2 * LANES
+    e_vec = jnp.concatenate([doc_ids, prev_docs, jnp.full((span_r - length - RIM,), -1, jnp.int32)]).astype(jnp.float32)
+    e_rows = jnp.broadcast_to(e_vec[None, :], (8, span_r))
 
     rates_t = rates.reshape(nb, gpb, pole_count).transpose(0, 2, 1)
     residues_t = residues.reshape(nb, gpb, pole_count).transpose(0, 2, 1)
@@ -166,7 +177,7 @@
 
     col = lambda off: (lambda j: (0, j + off))
     fixed = lambda j: (0, 0)
-    q_part, local_part, packed, decays = pl.pallas_call(
+    q_part, local_part, packed, decays, info = pl.pallas_call(
         functools.partial(local_kernel, taps, group_width, spans),
         grid=(nb,),
         in_specs=[
@@ -179,29 +190,32 @@
             pl.BlockSpec((taps, width), col(0)),
             pl.BlockSpec((taps, width), col(nb)),
             pl.BlockSpec((taps, width), col(2 * nb)),
-            pl.BlockSpec((length, 8), fixed),
-            pl.BlockSpec((length, length), fixed),
+            pl.BlockSpec((8, span_r), fixed),
             pl.BlockSpec((1, pole_count, gpb), lambda j: (j, 0, 0)),
             pl.BlockSpec((1, pole_count, gpb), lambda j: (j, 0, 0)),
-            pl.BlockSpec((8, length), fixed),
-            pl.BlockSpec((8, LANES), fixed),
         ],
         out_specs=[
             pl.BlockSpec((length, width), col(0)),
             pl.BlockSpec((length, width), col(0)),
             pl.BlockSpec((pole_count, channels + LANES), fixed),
             pl.BlockSpec((rounds, pole_count, width), lambda j: (0, 0, j)),
+            pl.BlockSpec((length, LANES), fixed),
         ],
         out_shape=[
             jax.ShapeDtypeStruct((length, channels), jnp.float32),
             jax.ShapeDtypeStruct((length, channels), jnp.float32),
             jax.ShapeDtypeStruct((pole_count, channels + LANES), jnp.float32),
             jax.ShapeDtypeStruct((rounds, pole_count, channels), jnp.float32),
-        ],
-        scratch_shapes=[pltpu.VMEM((RIM + length, width), jnp.float32)],
+            jax.ShapeDtypeStruct((length, LANES), jnp.float32),
+        ],
+        scratch_shapes=[
+            pltpu.VMEM((span_r, width), jnp.bfloat16),
+            pltpu.VMEM((taps * length, span_r), jnp.bfloat16),
+            pltpu.VMEM((length, length), jnp.float32),
+            pltpu.VMEM((8, length), jnp.float32),
+        ],
         compiler_params=pltpu.CompilerParams(dimension_semantics=("arbitrary",)),
-    )(qkv, qkv, qkv, rim, rim, rim, short_w, short_w, short_w, masks, visible, rates_t, residues_t,
-      at_tail, flag_row)
+    )(qkv, qkv, qkv, rim, rim, rim, short_w, short_w, short_w, e_rows, rates_t, residues_t)
 
     for step, offset in enumerate(offsets):
         got = from_behind(packed, "ctx", offset)
@@ -221,14 +235,13 @@
             pl.BlockSpec((pole_count, final_width), col(0)),
             pl.BlockSpec((1, final_width // group_width * pole_count), col(0)),
             pl.BlockSpec((1, final_width // group_width * pole_count), col(0)),
-            pl.BlockSpec((length, 1), fixed),
-            pl.BlockSpec((8, LANES), fixed),
+            pl.BlockSpec((length, LANES), fixed),
         ],
         out_specs=pl.BlockSpec((length, final_width), col(0)),
         out_shape=jax.ShapeDtypeStruct((length, channels), jnp.bfloat16),
         compiler_params=pltpu.CompilerParams(dimension_semantics=("arbitrary",)),
     )(q_part, local_part, before, rates.reshape(1, filters * pole_count),
-      residues.reshape(1, filters * pole_count), at_head, join_row)
+      residues.reshape(1, filters * pole_count), info)
 
 
 def solution(mesh):

time: 104 us -> 99.3 us (0.955)
  the two profiles are of different devices: /device:TPU:24 before, /device:TPU:28 now
where the time goes in v4:
time: 99.3 us; the launch traced here: 98.7 us
  waiting for transfers between devices  42.9 us (43%)
  Pallas kernels  33.9 us (34%)
  starting transfers between devices  9.77 us (10%)
  local copies, waits for them, and re-layouts  6.72 us (7%)
  other arithmetic  5.2 us (5%)
    ppermute x6, waiting for transfers between devices, from_behind(): return lax.ppermute(shard, axis, pairs)  42.9 us
    pallas_call x1, Pallas kernels, on_device(): pl.pallas_call(functools.partial(local_kernel, taps, group_width, spans),...  28.9 us
    ppermute x6, starting transfers between devices, from_behind(): return lax.ppermute(shard, axis, pairs)  9.77 us
    pallas_call x1, Pallas kernels, on_device(): pl.pallas_call(functools.partial(final_kernel, group_width, pole_count, w...  5.01 us
    add x4, other arithmetic, on_device(): body = packed[:, :channels] + mine_flag * decays[step] * got[:, :channels]  2.42 us
  transfers between devices with their start and end apart: 6, of which 6 were waited for; matrix products, arithmetic and copies ran while one was open for 4% of the time, Pallas kernels for 0%

profile of v4, /device:TPU:28, one launch (start us, length us, event | category | flops | bytes accessed | tf_op | source)
XLA Modules:
  0.0 98.7 jit_solution(234312595800107366)
XLA Ops:
  0.0 0.9 slice.55
  0.9 0.7 convert.4
  1.6 0.1 slice.56
  1.7 0.1 broadcast_in_dim.16
  1.8 1.9 %collective-permute-start = (bf16[8,12416]{1,0:T(8,128)(2,1)S(1)}, bf16[8,12416]{1,0:T(8,128)(2,1)S(1)}, u32[]{:S(2)}, u32[]{:S(2)}) collective-permute-start(bf16[8,12416]{1,0:T(8,128)(2,1)S(1)} %pad_maximum_fusion.4), channel_id=1, source_target_pairs={{0,1},{1,2},{2,3},{3,4},{4,5},{5,6},{6,7},{7,8},{8,9},{9,10},{10,1... | collective-permute-start | bytes 595976 | tf_op jit(solution)/shard_map/ppermute | solution.py:19
  3.7 0.8 reshape.44
  4.5 0.8 reshape.45
  5.3 0.8 copy_bitcast_fusion
  6.1 2.7 %collective-permute-done.rq.rk.rv = bf16[8,12416]{1,0:T(8,128)(2,1)S(1)} collective-permute-done((bf16[8,12416]{1,0:T(8,128)(2,1)S(1)}, bf16[8,12416]{1,0:T(8,128)(2,1)S(1)}, u32[]{:S(2)}, u32[]{:S(2)}) %collective-permute-start) | collective-permute-done | bytes 198688 | tf_op jit(solution)/shard_map/ppermute | solution.py:19
  8.8 0.1 convert_reduce_fusion
  8.9 0.7 add_convert_fusion
  9.6 0.6 broadcast_in_dim.18.e_ref
  10.3 0.0 copy-done
  10.3 28.9 %shard_map.55 = (f32[128,4096]{1,0:T(8,128)}, f32[128,4096]{1,0:T(8,128)}, f32[16,4224]{1,0:T(8,128)}, f32[4,16,4096]{2,1,0:T(8,128)}, f32[128,128]{1,0:T(8,128)}) custom-call(bf16[128,12288]{1,0:T(8,128)(2,1)} %xv.1, bf16[128,12288]{1,0:T(8,128)(2,1)} %xv.1, bf16[128,12288]{1,0:T(8,128)(2,1)} %xv.1, bf16[8,12416]{1,0:T(8,128)(2,1)} %copy-done, ...), custom_call_target="tpu_custom_call" | custom-call | tf_op jit(solution)/shard_map/pallas_call | solution.py:180
  39.1 0.0 copy-start.1
  39.1 2.1 %collective-permute-start.1 = (f32[16,4224]{1,0:T(8,128)}, f32[16,4224]{1,0:T(8,128)S(1)}, u32[]{:S(2)}, u32[]{:S(2)}) collective-permute-start(f32[16,4224]{1,0:T(8,128)} %get-tuple-element.12), channel_id=1, source_target_pairs={{0,1},{1,2},{2,3},{3,4},{4,5},{5,6},{6,7},{7,8},{8,9},{9,10},{10,1... | collective-permute-start | bytes 811016 | tf_op jit(solution)/shard_map/ppermute | solution.py:19
  41.2 6.1 %collective-permute-done.1 = f32[16,4224]{1,0:T(8,128)S(1)} collective-permute-done((f32[16,4224]{1,0:T(8,128)}, f32[16,4224]{1,0:T(8,128)S(1)}, u32[]{:S(2)}, u32[]{:S(2)}) %collective-permute-start.1) | collective-permute-done | bytes 270368 | tf_op jit(solution)/shard_map/ppermute | solution.py:19
  47.3 0.8 fusion.7
  48.1 1.1 %fusion.3 = f32[16,4096]{1,0:T(8,128)S(1)} fusion(f32[16,4224]{1,0:T(8,128)S(1)} %collective-permute-done.1, f32[4,16,4096]{2,1,0:T(8,128)} %get-tuple-element.13, f32[16,4224]{1,0:T(8,128)} %get-tuple-element.12, f32[16]{0:T(128)S(1)} %get-tuple-element.17), kind=kLoop, calls=%fused_computation.11 | loop fusion | flops 196608 | bytes 1048640 | tf_op jit(solution)/shard_map/add | solution.py:223
  49.2 0.1 broadcast_in_dim.19
  49.3 1.3 %collective-permute-start.2 = (f32[16,4224]{1,0:T(8,128)S(1)}, f32[16,4224]{1,0:T(8,128)S(1)}, u32[]{:S(2)}, u32[]{:S(2)}) collective-permute-start(f32[16,4224]{1,0:T(8,128)S(1)} %pad_maximum_fusion), channel_id=1, source_target_pairs={{0,2},{1,3},{2,4},{3,5},{4,6},{5,7},{6,8},{7,9},{8,10},{9,11},{10,... | collective-permute-start | bytes 811016 | tf_op jit(solution)/shard_map/ppermute | solution.py:19
  50.6 7.3 %collective-permute-done.2 = f32[16,4224]{1,0:T(8,128)S(1)} collective-permute-done((f32[16,4224]{1,0:T(8,128)S(1)}, f32[16,4224]{1,0:T(8,128)S(1)}, u32[]{:S(2)}, u32[]{:S(2)}) %collective-permute-start.2) | collective-permute-done | bytes 270368 | tf_op jit(solution)/shard_map/ppermute | solution.py:19
  58.0 1.1 %fusion.2 = f32[16,4096]{1,0:T(8,128)S(1)} fusion(f32[16,4096]{1,0:T(8,128)S(1)} %fusion.3, f32[16,4224]{1,0:T(8,128)S(1)} %collective-permute-done.2, f32[4,16,4096]{2,1,0:T(8,128)} %get-tuple-element.13, f32[16]{0:T(128)S(1)} %get-tuple-element.15), kind=kLoop, calls=%fused_computation.9 | loop fusion | flops 196608 | bytes 1048640 | tf_op jit(solution)/shard_map/add | solution.py:223
  59.0 0.0 copy-start.3
  59.0 0.0 copy-start.4
  59.1 0.1 fusion.5
  59.2 0.1 broadcast_in_dim.20
  59.3 1.3 %collective-permute-start.3 = (f32[16,4224]{1,0:T(8,128)S(1)}, f32[16,4224]{1,0:T(8,128)S(1)}, u32[]{:S(2)}, u32[]{:S(2)}) collective-permute-start(f32[16,4224]{1,0:T(8,128)S(1)} %pad_maximum_fusion.1), channel_id=1, source_target_pairs={{0,4},{1,5},{2,6},{3,7},{4,8},{5,9},{6,10},{7,11},{8,12},{9,13},{1... | collective-permute-start | bytes 811016 | tf_op jit(solution)/shard_map/ppermute | solution.py:19
  60.6 8.5 %collective-permute-done.3 = f32[16,4224]{1,0:T(8,128)S(1)} collective-permute-done((f32[16,4224]{1,0:T(8,128)S(1)}, f32[16,4224]{1,0:T(8,128)S(1)}, u32[]{:S(2)}, u32[]{:S(2)}) %collective-permute-start.3) | collective-permute-done | bytes 270368 | tf_op jit(solution)/shard_map/ppermute | solution.py:19
  69.1 0.0 copy-done.1
  69.1 0.1 fusion.1
  69.2 0.1 fusion.6
  69.3 0.1 broadcast_in_dim.42
  69.4 1.3 %collective-permute-start.4 = (f32[16,4224]{1,0:T(8,128)S(1)}, f32[16,4224]{1,0:T(8,128)S(1)}, u32[]{:S(2)}, u32[]{:S(2)}) collective-permute-start(f32[16,4224]{1,0:T(8,128)S(1)} %pad_maximum_fusion.2), channel_id=1, source_target_pairs={{0,8},{1,9},{2,10},{3,11},{4,12},{5,13},{6,14},{7,15},{16,24},{17,... | collective-permute-start | bytes 811016 | tf_op jit(solution)/shard_map/ppermute | solution.py:19
  70.7 14.1 %collective-permute-done.4 = f32[16,4224]{1,0:T(8,128)S(1)} collective-permute-done((f32[16,4224]{1,0:T(8,128)S(1)}, f32[16,4224]{1,0:T(8,128)S(1)}, u32[]{:S(2)}, u32[]{:S(2)}) %collective-permute-start.4) | collective-permute-done | bytes 270368 | tf_op jit(solution)/shard_map/ppermute | solution.py:19
  84.8 0.1 fusion
  84.9 0.1 fusion.4
  85.1 0.1 broadcast_in_dim.44
  85.2 1.9 %collective-permute-start.5 = (f32[16,4224]{1,0:T(8,128)S(1)}, f32[16,4224]{1,0:T(8,128)S(1)}, u32[]{:S(2)}, u32[]{:S(2)}) collective-permute-start(f32[16,4224]{1,0:T(8,128)S(1)} %pad_maximum_fusion.3), channel_id=1, source_target_pairs={{0,1},{1,2},{2,3},{3,4},{4,5},{5,6},{6,7},{7,8},{8,9},{9,10},{10,1... | collective-permute-start | bytes 811016 | tf_op jit(solution)/shard_map/ppermute | solution.py:19
  87.1 0.0 copy-done.3
  87.1 0.1 copy.10
  87.2 0.0 copy-done.4
  87.2 0.1 copy.11
  87.3 0.7 reshape.46.rf_ref
  88.0 0.7 reshape.47.ef_ref
  88.7 4.2 %collective-permute-done.5.b_ref = f32[16,4224]{1,0:T(8,128)S(1)} collective-permute-done((f32[16,4224]{1,0:T(8,128)S(1)}, f32[16,4224]{1,0:T(8,128)S(1)}, u32[]{:S(2)}, u32[]{:S(2)}) %collective-permute-start.5) | collective-permute-done | bytes 270368 | tf_op jit(solution)/shard_map/ppermute | solution.py:19
  92.9 0.7 copy-done.2
  93.6 5.0 %shard_map.56 = bf16[128,4096]{1,0:T(8,128)(2,1)} custom-call(f32[128,4096]{1,0:T(8,128)} %get-tuple-element.10.q_ref, f32[128,4096]{1,0:T(8,128)} %get-tuple-element.11.loc_ref, f32[16,4224]{1,0:T(8,128)} %copy-done.2, f32[1,4096]{1,0:T(1,128)} %reshape.46.rf_ref, f32[1,4096]{1,0:T(1,128)} %reshape.47.ef_ref, f32[128,128]{1,0:T(8,128)} %get-tuple-element.14.info_ref), custom_call_target="tpu_custom_call" | custom-call | tf_op jit(solution)/shard_map/pallas_call | solution.py:229
  (8 shorter events, 0.1 us)
Async XLA Ops:
  1.8 7.0 %collective-permute-start = (bf16[8,12416]{1,0:T(8,128)(2,1)S(1)}, bf16[8,12416]{1,0:T(8,128)(2,1)S(1)}, u32[]{:S(2)}, u32[]{:S(2)}) collective-permute-start(bf16[8,12416]{1,0:T(8,128)(2,1)S(1)} %pad_maximum_fusion.4), channel_id=1, source_target_pairs={{0,1},{1,2},{2,3},{3,4},{4,5},{5,6},{6,7},{7,8},{8,9},{9,10},{10,1... | collective-permute-start | bytes 595976 | tf_op jit(solution)/shard_map/ppermute | solution.py:19
  8.8 1.5 %copy-start = (bf16[8,12416]{1,0:T(8,128)(2,1)}, bf16[8,12416]{1,0:T(8,128)(2,1)S(1)}, u32[]{:S(2)}) copy-start(bf16[8,12416]{1,0:T(8,128)(2,1)S(1)} %collective-permute-done.rq.rk.rv) | copy-start | bytes 595972
  39.1 29.9 %copy-start.1 = (f32[4,16,4096]{2,1,0:T(8,128)S(1)}, f32[4,16,4096]{2,1,0:T(8,128)}, u32[]{:S(2)}) copy-start(f32[4,16,4096]{2,1,0:T(8,128)} %get-tuple-element.13) | copy-start | bytes 3145732
  39.1 8.1 %collective-permute-start.1 = (f32[16,4224]{1,0:T(8,128)}, f32[16,4224]{1,0:T(8,128)S(1)}, u32[]{:S(2)}, u32[]{:S(2)}) collective-permute-start(f32[16,4224]{1,0:T(8,128)} %get-tuple-element.12), channel_id=1, source_target_pairs={{0,1},{1,2},{2,3},{3,4},{4,5},{5,6},{6,7},{7,8},{8,9},{9,10},{10,1... | collective-permute-start | bytes 811016 | tf_op jit(solution)/shard_map/ppermute | solution.py:19
  49.3 8.6 %collective-permute-start.2 = (f32[16,4224]{1,0:T(8,128)S(1)}, f32[16,4224]{1,0:T(8,128)S(1)}, u32[]{:S(2)}, u32[]{:S(2)}) collective-permute-start(f32[16,4224]{1,0:T(8,128)S(1)} %pad_maximum_fusion), channel_id=1, source_target_pairs={{0,2},{1,3},{2,4},{3,5},{4,6},{5,7},{6,8},{7,9},{8,10},{9,11},{10,... | collective-permute-start | bytes 811016 | tf_op jit(solution)/shard_map/ppermute | solution.py:19
  59.0 28.1 %copy-start.3 = (f32[256,16]{0,1:T(8,128)S(1)}, f32[256,16]{0,1:T(8,128)}, u32[]{:S(2)}) copy-start(f32[256,16]{0,1:T(8,128)} %param.8) | copy-start | bytes 49156
  59.0 28.2 %copy-start.4 = (f32[256,16]{0,1:T(8,128)S(1)}, f32[256,16]{0,1:T(8,128)}, u32[]{:S(2)}) copy-start(f32[256,16]{0,1:T(8,128)} %param.9) | copy-start | bytes 49156
  59.3 9.8 %collective-permute-start.3 = (f32[16,4224]{1,0:T(8,128)S(1)}, f32[16,4224]{1,0:T(8,128)S(1)}, u32[]{:S(2)}, u32[]{:S(2)}) collective-permute-start(f32[16,4224]{1,0:T(8,128)S(1)} %pad_maximum_fusion.1), channel_id=1, source_target_pairs={{0,4},{1,5},{2,6},{3,7},{4,8},{5,9},{6,10},{7,11},{8,12},{9,13},{1... | collective-permute-start | bytes 811016 | tf_op jit(solution)/shard_map/ppermute | solution.py:19
  69.4 15.4 %collective-permute-start.4 = (f32[16,4224]{1,0:T(8,128)S(1)}, f32[16,4224]{1,0:T(8,128)S(1)}, u32[]{:S(2)}, u32[]{:S(2)}) collective-permute-start(f32[16,4224]{1,0:T(8,128)S(1)} %pad_maximum_fusion.2), channel_id=1, source_target_pairs={{0,8},{1,9},{2,10},{3,11},{4,12},{5,13},{6,14},{7,15},{16,24},{17,... | collective-permute-start | bytes 811016 | tf_op jit(solution)/shard_map/ppermute | solution.py:19
  85.2 7.8 %collective-permute-start.5 = (f32[16,4224]{1,0:T(8,128)S(1)}, f32[16,4224]{1,0:T(8,128)S(1)}, u32[]{:S(2)}, u32[]{:S(2)}) collective-permute-start(f32[16,4224]{1,0:T(8,128)S(1)} %pad_maximum_fusion.3), channel_id=1, source_target_pairs={{0,1},{1,2},{2,3},{3,4},{4,5},{5,6},{6,7},{7,8},{8,9},{9,10},{10,1... | collective-permute-start | bytes 811016 | tf_op jit(solution)/shard_map/ppermute | solution.py:19
  92.9 0.7 copy-start.2

commit v5 on v4

--- a/solution.py
+++ b/solution.py
@@ -145,6 +145,41 @@
         o_ref[:, cols] = (q_ref[:, cols] * (loc_ref[:, cols] + car)).astype(o_ref.dtype)
 
 
+def swap_cores(shard, axis):
+    peers = lax.axis_size(axis)
+    return lax.ppermute(shard, axis, [(i, i ^ 1) for i in range(peers)])
+
+
+def chip_scan(packed, decays, channels, pole_count, peers, me):
+    core = me % 2
+    odd = core == 1
+    half = channels // 2
+    mine = lambda x: lax.dynamic_slice_in_dim(x, core * half, half, axis=1)
+    got = swap_cores(packed, "ctx")
+    own_s, own_f = packed[:, :channels], packed[:, channels:channels + 1]
+    other_s, other_f = got[:, :channels], got[:, channels:channels + 1]
+    even_s = jnp.where(odd, other_s, own_s)
+    odd_s = jnp.where(odd, own_s, other_s)
+    even_f = jnp.where(odd, other_f, own_f)
+    odd_f = jnp.where(odd, own_f, other_f)
+    step_decay = decays[0]
+    total = (odd_f * mine(step_decay)) * mine(even_s) + mine(odd_s)
+    flag = even_f * odd_f
+    chips = peers // 2
+    offset = 1
+    while offset < chips:
+        rung = offset.bit_length()
+        load = jnp.concatenate([total, jnp.broadcast_to(flag, (pole_count, LANES))], axis=1)
+        got = from_behind(load, "ctx", 2 * offset)
+        total = total + (flag * mine(decays[rung])) * got[:, :half]
+        flag = flag * got[:, half:half + 1]
+        offset *= 2
+    prefix = from_behind(total, "ctx", 2)
+    partner = swap_cores(prefix, "ctx")
+    full = jnp.where(odd, jnp.concatenate([partner, prefix], axis=1), jnp.concatenate([prefix, partner], axis=1))
+    return jnp.where(odd, (even_f * step_decay) * full + even_s, full)
+
+
 def on_device(qkv, doc_ids, short_w, rates, residues):
     length = qkv.shape[0]
     taps = short_w.shape[0]
@@ -217,13 +252,7 @@
         compiler_params=pltpu.CompilerParams(dimension_semantics=("arbitrary",)),
     )(qkv, qkv, qkv, rim, rim, rim, short_w, short_w, short_w, e_rows, rates_t, residues_t)
 
-    for step, offset in enumerate(offsets):
-        got = from_behind(packed, "ctx", offset)
-        mine_flag = packed[:, channels:channels + 1]
-        body = packed[:, :channels] + (mine_flag * decays[step]) * got[:, :channels]
-        flags = jnp.broadcast_to(mine_flag * got[:, channels:channels + 1], (pole_count, LANES))
-        packed = jnp.concatenate([body, flags], axis=1)
-    before = from_behind(packed, "ctx", 1)
+    before = chip_scan(packed, decays, channels, pole_count, peers, me)
 
     nbf = channels // final_width
     return pl.pallas_call(

time: 99.3 us -> 85.5 us (0.86)
  the two profiles are of different devices: /device:TPU:28 before, /device:TPU:24 now
where the time goes in v5:
time: 85.5 us; the launch traced here: 84.3 us
  Pallas kernels  34.2 us (40%)
  waiting for transfers between devices  29.5 us (35%)
  starting transfers between devices  9.02 us (11%)
  local copies, waits for them, and re-layouts  7.21 us (8%)
  other arithmetic  4.1 us (5%)
    ppermute x5, waiting for transfers between devices, from_behind(): return lax.ppermute(shard, axis, pairs)  29.1 us
    pallas_call x1, Pallas kernels, on_device(): pl.pallas_call(functools.partial(local_kernel, taps, group_width, spans),...  28.9 us
    ppermute x5, starting transfers between devices, from_behind(): return lax.ppermute(shard, axis, pairs)  8.95 us
    pallas_call x1, Pallas kernels, on_device(): pl.pallas_call(functools.partial(final_kernel, group_width, pole_count, w...  5.32 us
    select_n x1, other arithmetic, chip_scan(): return jnp.where(odd, even_f * step_decay * full + even_s, full)  1.75 us
  transfers between devices with their start and end apart: 7, of which 6 were waited for; matrix products, arithmetic and copies ran while one was open for 6% of the time, Pallas kernels for 0%

profile of v5, /device:TPU:24, one launch (start us, length us, event | category | flops | bytes accessed | tf_op | source)
XLA Modules:
  0.0 84.3 jit_solution(10869681519431024642)
XLA Ops:
  0.0 0.9 %slice.49 = bf16[8,12288]{1,0:T(8,128)(2,1)S(1)} slice(bf16[128,12288]{1,0:T(8,128)(2,1)} %xv.1), slice={[120:128], [0:12288]} | slice | bytes 393216 | tf_op jit(solution)/shard_map/slice | solution.py:197
  0.9 0.7 convert.4
  1.6 0.1 slice.50
  1.7 0.1 broadcast_in_dim.12
  1.8 1.9 %collective-permute-start = (bf16[8,12416]{1,0:T(8,128)(2,1)S(1)}, bf16[8,12416]{1,0:T(8,128)(2,1)S(1)}, u32[]{:S(2)}, u32[]{:S(2)}) collective-permute-start(bf16[8,12416]{1,0:T(8,128)(2,1)S(1)} %pad_maximum_fusion), channel_id=1, source_target_pairs={{0,1},{1,2},{2,3},{3,4},{4,5},{5,6},{6,7},{7,8},{8,9},{9,10},{10,1... | collective-permute-start | bytes 595976 | tf_op jit(solution)/shard_map/ppermute | solution.py:19
  3.7 0.8 reshape.39
  4.5 0.8 reshape.40
  5.4 0.8 copy_bitcast_fusion
  6.1 3.5 %collective-permute-done.rq.rk.rv = bf16[8,12416]{1,0:T(8,128)(2,1)S(1)} collective-permute-done((bf16[8,12416]{1,0:T(8,128)(2,1)S(1)}, bf16[8,12416]{1,0:T(8,128)(2,1)S(1)}, u32[]{:S(2)}, u32[]{:S(2)}) %collective-permute-start) | collective-permute-done | bytes 198688 | tf_op jit(solution)/shard_map/ppermute | solution.py:19
  9.7 0.1 convert_reduce_fusion
  9.8 0.7 add_convert_fusion
  10.5 0.6 broadcast_in_dim.14.e_ref
  11.2 0.0 copy-done
  11.2 28.9 %shard_map.55 = (f32[128,4096]{1,0:T(8,128)}, f32[128,4096]{1,0:T(8,128)}, f32[16,4224]{1,0:T(8,128)}, f32[4,16,4096]{2,1,0:T(8,128)}, f32[128,128]{1,0:T(8,128)}) custom-call(bf16[128,12288]{1,0:T(8,128)(2,1)} %xv.1, bf16[128,12288]{1,0:T(8,128)(2,1)} %xv.1, bf16[128,12288]{1,0:T(8,128)(2,1)} %xv.1, bf16[8,12416]{1,0:T(8,128)(2,1)} %copy-done, ...), custom_call_target="tpu_custom_call" | custom-call | tf_op jit(solution)/shard_map/pallas_call | solution.py:215
  40.0 0.0 copy-start.1
  40.0 0.1 collective-permute-start.1
  40.1 1.3 %fusion.15 = (f32[1,16,4096]{2,1,0:T(8,128)S(1)}, f32[1,16,4096]{2,1,0:T(8,128)S(1)}, f32[1,16,4096]{2,1,0:T(8,128)S(1)}, f32[1,16,4096]{2,1,0:T(8,128)S(1)}) fusion(f32[4,16,4096]{2,1,0:T(8,128)} %get-tuple-element.13), kind=kLoop, calls=%fused_computation.37 | loop fusion | bytes 2097152 | tf_op jit(solution)/shard_map/slice | solution.py:174
  41.4 0.5 collective-permute-done.1
  41.9 0.0 copy-done.1
  41.9 0.1 fusion.13
  42.0 0.0 copy-start.3
  42.0 0.1 fusion.16
  42.1 0.1 fusion.6
  42.2 0.1 broadcast_in_dim.15
  42.3 2.5 %collective-permute-start.2 = (f32[16,2176]{1,0:T(8,128)S(1)}, f32[16,2176]{1,0:T(8,128)S(1)}, u32[]{:S(2)}, u32[]{:S(2)}) collective-permute-start(f32[16,2176]{1,0:T(8,128)S(1)} %pad_maximum_fusion.1), channel_id=1, source_target_pairs={{0,2},{1,3},{2,4},{3,5},{4,6},{5,7},{6,8},{7,9},{8,10},{9,11},{10,... | collective-permute-start | bytes 417800 | tf_op jit(solution)/shard_map/ppermute | solution.py:19
  44.8 6.0 %collective-permute-done.2 = f32[16,2176]{1,0:T(8,128)S(1)} collective-permute-done((f32[16,2176]{1,0:T(8,128)S(1)}, f32[16,2176]{1,0:T(8,128)S(1)}, u32[]{:S(2)}, u32[]{:S(2)}) %collective-permute-start.2) | collective-permute-done | bytes 139296 | tf_op jit(solution)/shard_map/ppermute | solution.py:19
  50.8 0.1 fusion.9
  50.9 0.1 fusion.5
  51.0 0.1 broadcast_in_dim.16
  51.1 1.3 %collective-permute-start.3 = (f32[16,2176]{1,0:T(8,128)S(1)}, f32[16,2176]{1,0:T(8,128)S(1)}, u32[]{:S(2)}, u32[]{:S(2)}) collective-permute-start(f32[16,2176]{1,0:T(8,128)S(1)} %pad_maximum_fusion.2), channel_id=1, source_target_pairs={{0,4},{1,5},{2,6},{3,7},{4,8},{5,9},{6,10},{7,11},{8,12},{9,13},{1... | collective-permute-start | bytes 417800 | tf_op jit(solution)/shard_map/ppermute | solution.py:19
  52.4 5.6 %collective-permute-done.3 = f32[16,2176]{1,0:T(8,128)S(1)} collective-permute-done((f32[16,2176]{1,0:T(8,128)S(1)}, f32[16,2176]{1,0:T(8,128)S(1)}, u32[]{:S(2)}, u32[]{:S(2)}) %collective-permute-start.3) | collective-permute-done | bytes 139296 | tf_op jit(solution)/shard_map/ppermute | solution.py:19
  58.0 0.1 fusion.8
  58.2 0.1 fusion.4
  58.2 0.1 broadcast_in_dim.17
  58.3 1.3 %collective-permute-start.4 = (f32[16,2176]{1,0:T(8,128)S(1)}, f32[16,2176]{1,0:T(8,128)S(1)}, u32[]{:S(2)}, u32[]{:S(2)}) collective-permute-start(f32[16,2176]{1,0:T(8,128)S(1)} %pad_maximum_fusion.3), channel_id=1, source_target_pairs={{0,8},{1,9},{2,10},{3,11},{4,12},{5,13},{6,14},{7,15},{16,24},{17,... | collective-permute-start | bytes 417800 | tf_op jit(solution)/shard_map/ppermute | solution.py:19
  59.6 8.1 %collective-permute-done.4 = f32[16,2176]{1,0:T(8,128)S(1)} collective-permute-done((f32[16,2176]{1,0:T(8,128)S(1)}, f32[16,2176]{1,0:T(8,128)S(1)}, u32[]{:S(2)}, u32[]{:S(2)}) %collective-permute-start.4) | collective-permute-done | bytes 139296 | tf_op jit(solution)/shard_map/ppermute | solution.py:19
  67.7 0.1 fusion.3
  67.8 1.9 %collective-permute-start.5 = (f32[16,2048]{1,0:T(8,128)S(1)}, f32[16,2048]{1,0:T(8,128)S(1)}, u32[]{:S(2)}, u32[]{:S(2)}) collective-permute-start(f32[16,2048]{1,0:T(8,128)S(1)} %fusion.3), channel_id=1, source_target_pairs={{0,2},{1,3},{2,4},{3,5},{4,6},{5,7},{6,8},{7,9},{8,10},{9,11},{10,... | collective-permute-start | bytes 393224 | tf_op jit(solution)/shard_map/ppermute | solution.py:19
  69.7 5.8 %collective-permute-done.5 = f32[16,2048]{1,0:T(8,128)S(1)} collective-permute-done((f32[16,2048]{1,0:T(8,128)S(1)}, f32[16,2048]{1,0:T(8,128)S(1)}, u32[]{:S(2)}, u32[]{:S(2)}) %collective-permute-start.5) | collective-permute-done | bytes 131104 | tf_op jit(solution)/shard_map/ppermute | solution.py:19
  75.6 0.0 collective-permute-start.6
  75.6 0.0 copy-done.2
  75.6 0.1 copy.10
  75.7 0.1 copy.11
  75.8 0.7 reshape.41.rf_ref
  76.5 0.7 reshape.42.ef_ref
  77.2 0.0 collective-permute-done.6
  77.2 1.7 %fusion.2.b_ref = f32[16,4096]{1,0:T(8,128)} fusion(f32[16,4096]{1,0:T(8,128)S(1)} %get-tuple-element.26, f32[16,2048]{1,0:T(8,128)S(1)} %collective-permute-done.6, f32[16,2048]{1,0:T(8,128)S(1)} %collective-permute-done.5, f32[16]{0:T(128)S(1)} %get-tuple-element.24, pred[]{:T(512)S(6)} %eq.5, f32[4,16,4096]{2,1,0:T(8,128)} %get-tuple-element.13), kind=kLoop, calls=%fused_computation.4 | loop fusion | flops 458752 | bytes 1048641 | tf_op jit(solution)/shard_map/jit(_where)/select_n | solution.py:180
  78.9 5.3 %shard_map.56 = bf16[128,4096]{1,0:T(8,128)(2,1)} custom-call(f32[128,4096]{1,0:T(8,128)} %get-tuple-element.10.q_ref, f32[128,4096]{1,0:T(8,128)} %get-tuple-element.11.loc_ref, f32[16,4096]{1,0:T(8,128)} %fusion.2.b_ref, f32[1,4096]{1,0:T(1,128)} %reshape.41.rf_ref, f32[1,4096]{1,0:T(1,128)} %reshape.42.ef_ref, f32[128,128]{1,0:T(8,128)} %get-tuple-element.14.info_ref), custom_call_target="tpu_custom_call" | custom-call | tf_op jit(solution)/shard_map/pallas_call | solution.py:258
  (8 shorter events, 0.1 us)
Async XLA Ops:
  1.8 7.9 %collective-permute-start = (bf16[8,12416]{1,0:T(8,128)(2,1)S(1)}, bf16[8,12416]{1,0:T(8,128)(2,1)S(1)}, u32[]{:S(2)}, u32[]{:S(2)}) collective-permute-start(bf16[8,12416]{1,0:T(8,128)(2,1)S(1)} %pad_maximum_fusion), channel_id=1, source_target_pairs={{0,1},{1,2},{2,3},{3,4},{4,5},{5,6},{6,7},{7,8},{8,9},{9,10},{10,1... | collective-permute-start | bytes 595976 | tf_op jit(solution)/shard_map/ppermute | solution.py:19
  9.7 1.5 %copy-start = (bf16[8,12416]{1,0:T(8,128)(2,1)}, bf16[8,12416]{1,0:T(8,128)(2,1)S(1)}, u32[]{:S(2)}) copy-start(bf16[8,12416]{1,0:T(8,128)(2,1)S(1)} %collective-permute-done.rq.rk.rv) | copy-start | bytes 595972
  40.0 1.8 %copy-start.1 = (f32[16,4224]{1,0:T(8,128)S(1)}, f32[16,4224]{1,0:T(8,128)}, u32[]{:S(2)}) copy-start(f32[16,4224]{1,0:T(8,128)} %get-tuple-element.12) | copy-start | bytes 811012
  40.0 1.8 %collective-permute-start.1 = (f32[16,4224]{1,0:T(8,128)}, f32[16,4224]{1,0:T(8,128)S(1)}, u32[]{:S(2)}, u32[]{:S(2)}) collective-permute-start(f32[16,4224]{1,0:T(8,128)} %get-tuple-element.12), channel_id=1, source_target_pairs={{0,1},{1,0},{2,3},{3,2},{4,5},{5,4},{6,7},{7,6},{8,9},{9,8},{10,11... | collective-permute-start | bytes 811016 | tf_op jit(solution)/shard_map/ppermute | solution.py:150
  42.0 33.5 %copy-start.2 = (f32[256,16]{0,1:T(8,128)S(1)}, f32[256,16]{0,1:T(8,128)}, u32[]{:S(2)}) copy-start(f32[256,16]{0,1:T(8,128)} %param.8) | copy-start | bytes 49156
  42.0 33.6 %copy-start.3 = (f32[256,16]{0,1:T(8,128)S(1)}, f32[256,16]{0,1:T(8,128)}, u32[]{:S(2)}) copy-start(f32[256,16]{0,1:T(8,128)} %param.9) | copy-start | bytes 49156
  42.3 8.5 %collective-permute-start.2 = (f32[16,2176]{1,0:T(8,128)S(1)}, f32[16,2176]{1,0:T(8,128)S(1)}, u32[]{:S(2)}, u32[]{:S(2)}) collective-permute-start(f32[16,2176]{1,0:T(8,128)S(1)} %pad_maximum_fusion.1), channel_id=1, source_target_pairs={{0,2},{1,3},{2,4},{3,5},{4,6},{5,7},{6,8},{7,9},{8,10},{9,11},{10,... | collective-permute-start | bytes 417800 | tf_op jit(solution)/shard_map/ppermute | solution.py:19
  51.1 6.9 %collective-permute-start.3 = (f32[16,2176]{1,0:T(8,128)S(1)}, f32[16,2176]{1,0:T(8,128)S(1)}, u32[]{:S(2)}, u32[]{:S(2)}) collective-permute-start(f32[16,2176]{1,0:T(8,128)S(1)} %pad_maximum_fusion.2), channel_id=1, source_target_pairs={{0,4},{1,5},{2,6},{3,7},{4,8},{5,9},{6,10},{7,11},{8,12},{9,13},{1... | collective-permute-start | bytes 417800 | tf_op jit(solution)/shard_map/ppermute | solution.py:19
  58.3 9.4 %collective-permute-start.4 = (f32[16,2176]{1,0:T(8,128)S(1)}, f32[16,2176]{1,0:T(8,128)S(1)}, u32[]{:S(2)}, u32[]{:S(2)}) collective-permute-start(f32[16,2176]{1,0:T(8,128)S(1)} %pad_maximum_fusion.3), channel_id=1, source_target_pairs={{0,8},{1,9},{2,10},{3,11},{4,12},{5,13},{6,14},{7,15},{16,24},{17,... | collective-permute-start | bytes 417800 | tf_op jit(solution)/shard_map/ppermute | solution.py:19
  67.8 7.8 %collective-permute-start.5 = (f32[16,2048]{1,0:T(8,128)S(1)}, f32[16,2048]{1,0:T(8,128)S(1)}, u32[]{:S(2)}, u32[]{:S(2)}) collective-permute-start(f32[16,2048]{1,0:T(8,128)S(1)} %fusion.3), channel_id=1, source_target_pairs={{0,2},{1,3},{2,4},{3,5},{4,6},{5,7},{6,8},{7,9},{8,10},{9,11},{10,... | collective-permute-start | bytes 393224 | tf_op jit(solution)/shard_map/ppermute | solution.py:19
  75.6 1.6 %collective-permute-start.6 = (f32[16,2048]{1,0:T(8,128)S(1)}, f32[16,2048]{1,0:T(8,128)S(1)}, u32[]{:S(2)}, u32[]{:S(2)}) collective-permute-start(f32[16,2048]{1,0:T(8,128)S(1)} %collective-permute-done.5), channel_id=1, source_target_pairs={{0,1},{1,0},{2,3},{3,2},{4,5},{5,4},{6,7},{7,6},{8,9},{9,8},{10,11... | collective-permute-start | bytes 393224 | tf_op jit(solution)/shard_map/ppermute | solution.py:150

commit v6 on v5

--- a/solution.py
+++ b/solution.py
@@ -166,17 +166,20 @@
     total = (odd_f * mine(step_decay)) * mine(even_s) + mine(odd_s)
     flag = even_f * odd_f
     chips = peers // 2
-    offset = 1
-    while offset < chips:
-        rung = offset.bit_length()
-        load = jnp.concatenate([total, jnp.broadcast_to(flag, (pole_count, LANES))], axis=1)
-        got = from_behind(load, "ctx", 2 * offset)
-        total = total + (flag * mine(decays[rung])) * got[:, :half]
-        flag = flag * got[:, half:half + 1]
-        offset *= 2
-    prefix = from_behind(total, "ctx", 2)
-    partner = swap_cores(prefix, "ctx")
-    full = jnp.where(odd, jnp.concatenate([partner, prefix], axis=1), jnp.concatenate([prefix, partner], axis=1))
+    load = jnp.concatenate([total, jnp.broadcast_to(flag, (pole_count, LANES))], axis=1)
+    every = lax.all_gather(load, "ctx")
+    chip = me // 2
+    two_step = decays[1]
+    halves = []
+    for side in range(2):
+        decay_half = two_step[:, side * half:(side + 1) * half]
+        acc = jnp.zeros((pole_count, half), jnp.float32)
+        for earlier in range(chips):
+            part = every[2 * earlier + side]
+            carry = (part[:, half:half + 1] * decay_half) * acc + part[:, :half]
+            acc = jnp.where(earlier < chip, carry, acc)
+        halves.append(acc)
+    full = jnp.concatenate(halves, axis=1)
     return jnp.where(odd, (even_f * step_decay) * full + even_s, full)
 
 

time: 85.5 us -> 114 us (1.33)
  the two profiles are of different devices: /device:TPU:24 before, /device:TPU:0 now
where the time goes in v6:
time: 114 us; the launch traced here: 113 us
  waiting for transfers between devices  43.2 us (38%)
  Pallas kernels  34.2 us (30%)
  between operations  13.5 us (12%)
  other arithmetic  8.95 us (8%)
  local copies, waits for them, and re-layouts  8.1 us (7%)
  starting transfers between devices  5.25 us (5%)
    all_gather x1, waiting for transfers between devices, chip_scan(): every = lax.all_gather(load, 'ctx')  42.9 us
    pallas_call x1, Pallas kernels, on_device(): pl.pallas_call(functools.partial(local_kernel, taps, group_width, spans),...  28.9 us
    pallas_call x1, Pallas kernels, on_device(): pl.pallas_call(functools.partial(final_kernel, group_width, pole_count, w...  5.32 us
    select_n x2, other arithmetic, chip_scan(): acc = jnp.where(earlier < chip, carry, acc)  3.05 us
    ppermute x1, starting transfers between devices, swap_cores(): return lax.ppermute(shard, axis, [(i, i ^ 1) for i in range(peers)])  2.84 us
    ppermute x1, starting transfers between devices, from_behind(): return lax.ppermute(shard, axis, pairs)  2.41 us
  transfers between devices with their start and end apart: 3, of which 2 were waited for; matrix products, arithmetic and copies ran while one was open for 4% of the time, Pallas kernels for 0%

profile of v6, /device:TPU:0, one launch (start us, length us, event | category | flops | bytes accessed | tf_op | source)
XLA Modules:
  0.0 113.3 jit_solution(3149811087372245862)
XLA Ops:
  6.5 0.0 all-gather.3.cloned.1.call-start
  6.5 0.9 slice.178
  7.5 0.7 convert.4
  8.1 0.1 slice.179
  8.2 0.1 broadcast_in_dim.10
  8.3 2.4 %collective-permute-start = (bf16[8,12416]{1,0:T(8,128)(2,1)S(1)}, bf16[8,12416]{1,0:T(8,128)(2,1)S(1)}, u32[]{:S(2)}, u32[]{:S(2)}) collective-permute-start(bf16[8,12416]{1,0:T(8,128)(2,1)S(1)} %pad_maximum_fusion.1), channel_id=1, source_target_pairs={{0,1},{1,2},{2,3},{3,4},{4,5},{5,6},{6,7},{7,8},{8,9},{9,10},{10,1... | collective-permute-start | bytes 595976 | tf_op jit(solution)/shard_map/ppermute | solution.py:19
  10.7 0.8 reshape.36
  11.6 0.8 reshape.37
  12.4 0.8 copy_bitcast_fusion
  13.2 0.0 collective-permute-done.rq.rk.rv
  13.2 0.0 copy-start
  13.2 0.1 convert_reduce_fusion
  13.3 0.7 add_convert_fusion
  14.0 0.6 broadcast_in_dim.24.e_ref
  14.6 0.0 copy-done
  14.6 28.9 %shard_map.55 = (f32[128,4096]{1,0:T(8,128)}, f32[128,4096]{1,0:T(8,128)}, f32[16,4224]{1,0:T(8,128)}, f32[4,16,4096]{2,1,0:T(8,128)}, f32[128,128]{1,0:T(8,128)}) custom-call(bf16[128,12288]{1,0:T(8,128)(2,1)} %xv.1, bf16[128,12288]{1,0:T(8,128)(2,1)} %xv.1, bf16[128,12288]{1,0:T(8,128)(2,1)} %xv.1, bf16[8,12416]{1,0:T(8,128)(2,1)} %copy-done, ...), custom_call_target="tpu_custom_call" | custom-call | tf_op jit(solution)/shard_map/pallas_call | solution.py:218
  43.5 0.0 copy-start.1
  43.5 0.0 copy-start.2
  43.6 2.8 %collective-permute-start.1 = (f32[16,4224]{1,0:T(8,128)}, f32[16,4224]{1,0:T(8,128)S(1)}, u32[]{:S(2)}, u32[]{:S(2)}) collective-permute-start(f32[16,4224]{1,0:T(8,128)} %get-tuple-element.12), channel_id=1, source_target_pairs={{0,1},{1,0},{2,3},{3,2},{4,5},{5,4},{6,7},{7,6},{8,9},{9,8},{10,11... | collective-permute-start | bytes 811016 | tf_op jit(solution)/shard_map/ppermute | solution.py:150
  46.4 1.1 slice_bitcast_fusion
  47.5 0.3 collective-permute-done.1
  47.8 0.8 fusion.21
  48.6 1.0 fusion.23
  49.6 0.1 fusion.19
  49.7 0.1 broadcast_in_dim.26
  49.8 0.7 pad_maximum_fusion.2
  50.5 0.0 all-gather.3.cloned.1.call-update
  50.5 0.0 copy-done.1
  50.5 0.1 copy.10
  50.6 0.0 copy-done.2
  50.6 0.1 copy.11
  50.7 0.7 reshape.38.rf_ref
  51.5 0.7 reshape.39.ef_ref
  52.2 42.9 %all-gather.3.cloned.1.call-done = f32[256,2176]{1,0:T(8,128)} async-done(((f32[16,2176]{1,0:T(8,128)}), f32[256,2176]{1,0:T(8,128)}) %all-gather.3.cloned.1.call-update) | async-done | bytes 2228240 | tf_op jit(solution)/shard_map/all_gather | solution.py:170
  95.0 1.2 %slice_reduce_fusion.15 = (f32[16]{0:T(128)S(1)}, f32[16]{0:T(128)S(1)}, f32[16]{0:T(128)S(1)}, f32[16]{0:T(128)S(1)}, f32[16]{0:T(128)S(1)}, /*index=5*/f32[16]...) fusion(f32[256,2176]{1,0:T(8,128)} %all-gather.3.cloned.1.call-done), kind=kLoop, calls=%fused_computation.62 | loop fusion | bytes 2048 | tf_op jit(solution)/shard_map/slice | solution.py:179
  96.3 1.5 %fusion.11 = f32[16,2048]{1,0:T(8,128)S(1)} fusion(f32[256,2176]{1,0:T(8,128)} %all-gather.3.cloned.1.call-done, f32[16,4096]{1,0:T(8,128)S(1)} %get-tuple-element.34, f32[16]{0:T(128)S(1)} %get-tuple-element.23, f32[16]{0:T(128)S(1)} %get-tuple-element.24, f32[16]{0:T(128)S(1)} %get-tuple-element.25, f32[16]{0:T(128)S(1)} %get-tuple-element.26, ...), kind=kLoop, calls=%fused_computation.25 | loop fusion | flops 1048576 | bytes 1311240 | tf_op jit(solution)/shard_map/jit(_where)/select_n | solution.py:180
  97.8 1.5 %fusion.3 = f32[16,2048]{1,0:T(8,128)S(1)} fusion(f32[256,2176]{1,0:T(8,128)} %all-gather.3.cloned.1.call-done, f32[16,4096]{1,0:T(8,128)S(1)} %get-tuple-element.34, f32[16]{0:T(128)S(1)} %get-tuple-element.30, f32[16]{0:T(128)S(1)} %get-tuple-element.17, f32[16]{0:T(128)S(1)} %get-tuple-element.18, f32[16]{0:T(128)S(1)} %get-tuple-element.19, ...), kind=kLoop, calls=%fused_computation.9 | loop fusion | flops 1048576 | bytes 1311240 | tf_op jit(solution)/shard_map/jit(_where)/select_n | solution.py:180
  99.3 1.8 %fusion.2.b_ref = f32[16,4096]{1,0:T(8,128)} fusion(f32[16,4096]{1,0:T(8,128)S(1)} %get-tuple-element.37, f32[16,2048]{1,0:T(8,128)S(1)} %fusion.3, f32[16,2048]{1,0:T(8,128)S(1)} %fusion.11, f32[16]{0:T(128)S(1)} %get-tuple-element.31, pred[]{:T(512)S(6)} %eq.5, f32[4,16,4096]{2,1,0:T(8,128)} %get-tuple-element.13), kind=kLoop, calls=%fused_computation.4 | loop fusion | flops 327680 | bytes 1048641 | tf_op jit(solution)/shard_map/jit(_where)/select_n | solution.py:183
  101.1 5.3 %shard_map.56 = bf16[128,4096]{1,0:T(8,128)(2,1)} custom-call(f32[128,4096]{1,0:T(8,128)} %get-tuple-element.10.q_ref, f32[128,4096]{1,0:T(8,128)} %get-tuple-element.11.loc_ref, f32[16,4096]{1,0:T(8,128)} %fusion.2.b_ref, f32[1,4096]{1,0:T(1,128)} %reshape.38.rf_ref, f32[1,4096]{1,0:T(1,128)} %reshape.39.ef_ref, f32[128,128]{1,0:T(8,128)} %get-tuple-element.14.info_ref), custom_call_target="tpu_custom_call" | custom-call | tf_op jit(solution)/shard_map/pallas_call | solution.py:261
  (2 shorter events, 0.0 us)
Async XLA Ops:
  6.5 88.5 %all-gather.3.cloned.1.call-start = ((), (), s32[]{:S(2)}) async-start(), calls=%async_computation | async-start | bytes 2367488 | tf_op jit(solution)/shard_map/all_gather | solution.py:170
  8.3 4.9 %collective-permute-start = (bf16[8,12416]{1,0:T(8,128)(2,1)S(1)}, bf16[8,12416]{1,0:T(8,128)(2,1)S(1)}, u32[]{:S(2)}, u32[]{:S(2)}) collective-permute-start(bf16[8,12416]{1,0:T(8,128)(2,1)S(1)} %pad_maximum_fusion.1), channel_id=1, source_target_pairs={{0,1},{1,2},{2,3},{3,4},{4,5},{5,6},{6,7},{7,8},{8,9},{9,10},{10,1... | collective-permute-start | bytes 595976 | tf_op jit(solution)/shard_map/ppermute | solution.py:19
  13.2 1.5 %copy-start = (bf16[8,12416]{1,0:T(8,128)(2,1)}, bf16[8,12416]{1,0:T(8,128)(2,1)S(1)}, u32[]{:S(2)}) copy-start(bf16[8,12416]{1,0:T(8,128)(2,1)S(1)} %collective-permute-done.rq.rk.rv) | copy-start | bytes 595972
  43.5 7.0 %copy-start.1 = (f32[256,16]{0,1:T(8,128)S(1)}, f32[256,16]{0,1:T(8,128)}, u32[]{:S(2)}) copy-start(f32[256,16]{0,1:T(8,128)} %param.8) | copy-start | bytes 49156
  43.5 7.1 %copy-start.2 = (f32[256,16]{0,1:T(8,128)S(1)}, f32[256,16]{0,1:T(8,128)}, u32[]{:S(2)}) copy-start(f32[256,16]{0,1:T(8,128)} %param.9) | copy-start | bytes 49156
  43.6 4.2 %collective-permute-start.1 = (f32[16,4224]{1,0:T(8,128)}, f32[16,4224]{1,0:T(8,128)S(1)}, u32[]{:S(2)}, u32[]{:S(2)}) collective-permute-start(f32[16,4224]{1,0:T(8,128)} %get-tuple-element.12), channel_id=1, source_target_pairs={{0,1},{1,0},{2,3},{3,2},{4,5},{5,4},{6,7},{7,6},{8,9},{9,8},{10,11... | collective-permute-start | bytes 811016 | tf_op jit(solution)/shard_map/ppermute | solution.py:150
Sparse Core Ops, SparseCore 0:
  50.6 44.3 all-gather.2

commit v7 on v5

--- a/solution.py
+++ b/solution.py
@@ -104,12 +104,11 @@
         rolled = pltpu.roll(row, 0, 1, stride=1, stride_axis=0)
         pieces.append(jnp.where(visible, rolled, 0.0))
         ends.append(jnp.exp(-a_col * to_end) * at_tail)
-    lhs = jnp.concatenate([jnp.concatenate(pieces, axis=1), jnp.concatenate(ends, axis=1)], axis=0)
-    l_hi, l_lo = split2(lhs)
-    rows = length + pole_count
-    res = jnp.dot(jnp.concatenate([l_hi, l_lo], axis=0), xbd, preferred_element_type=jnp.float32)
-    loc_out[...] = res[0:length] + res[rows:rows + length]
-    st = res[length:rows] + res[rows + length:2 * rows]
+    e_hi, e_lo = split2(jnp.concatenate(ends, axis=1))
+    t_hi = jnp.concatenate(pieces, axis=1).astype(jnp.bfloat16)
+    res = jnp.dot(jnp.concatenate([t_hi, e_hi, e_lo], axis=0), xbd, preferred_element_type=jnp.float32)
+    loc_out[...] = res[0:length]
+    st = res[length:length + pole_count] + res[length + pole_count:length + 2 * pole_count]
     pk_out[:, pl.ds(pl.multiple_of(step * width, width), width)] = st
 
     spread = (lax.broadcasted_iota(jnp.int32, (groups, width), 1) // group_width
@@ -175,7 +174,7 @@
         flag = flag * got[:, half:half + 1]
         offset *= 2
     prefix = from_behind(total, "ctx", 2)
-    partner = swap_cores(prefix, "ctx")
+    partner = lax.ppermute(total, "ctx", [(i, (i ^ 1) + 2) for i in range(peers - 2)])
     full = jnp.where(odd, jnp.concatenate([partner, prefix], axis=1), jnp.concatenate([prefix, partner], axis=1))
     return jnp.where(odd, (even_f * step_decay) * full + even_s, full)
 
@@ -202,8 +201,8 @@
     e_vec = jnp.concatenate([doc_ids, prev_docs, jnp.full((span_r - length - RIM,), -1, jnp.int32)]).astype(jnp.float32)
     e_rows = jnp.broadcast_to(e_vec[None, :], (8, span_r))
 
-    rates_t = rates.reshape(nb, gpb, pole_count).transpose(0, 2, 1)
-    residues_t = residues.reshape(nb, gpb, pole_count).transpose(0, 2, 1)
+    both_t = jnp.stack([rates, residues]).reshape(2, nb, gpb, pole_count).transpose(0, 1, 3, 2)
+    rates_t, residues_t = both_t[0], both_t[1]
     offsets = []
     while (1 << len(offsets)) < peers:
         offsets.append(1 << len(offsets))

time: 85.5 us -> 79.1 us (0.925)
  Pallas kernels: 34.2 us -> 27.9 us
  starting transfers between devices: 9.02 us -> 10.9 us
    pallas_call x1, Pallas kernels: 28.9 us -> 22.6 us  [on_device(): pl.pallas_call(functools.partial(local_kernel, taps, group_width, spans),...]
    ppermute x5, waiting for transfers between devices: 29.1 us -> 26.2 us  [from_behind(): return lax.ppermute(shard, axis, pairs)]
    ppermute x0 -> x1, waiting for transfers between devices: none -> 1.94 us  [chip_scan(): lax.ppermute(total, 'ctx', [(i, (i ^ 1) + 2) for i in range(peers - 2)])]
    ppermute x0 -> x1, starting transfers between devices: none -> 1.92 us  [chip_scan(): lax.ppermute(total, 'ctx', [(i, (i ^ 1) + 2) for i in range(peers - 2)])]
    another operation x0 -> x4, local copies, waits for them, and re-layouts: none -> 1.71 us  [on_device(): jnp.stack([rates, residues]).reshape(2, nb, gpb, pole_count)]
    reshape x2 -> x0, local copies, waits for them, and re-layouts: 1.62 us -> none  [the longest x1 0.81 us: on_device(): rates_t = rates.reshape(nb, gpb, pole_count).transpose(0, 2, 1)]
  transfers between devices with their start and end apart: 7 -> 7, of which waited for: 6 -> 7; matrix products, arithmetic and copies ran while one was open for 6% -> 7% of each run, Pallas kernels for 0% -> 0%
where the time goes in v7:
time: 79.1 us; the launch traced here: 78.5 us
  waiting for transfers between devices  28.7 us (36%)
  Pallas kernels  27.9 us (35%)
  starting transfers between devices  10.9 us (14%)
  local copies, waits for them, and re-layouts  7.26 us (9%)
  other arithmetic  3.46 us (4%)
    ppermute x5, waiting for transfers between devices, from_behind(): return lax.ppermute(shard, axis, pairs)  26.2 us
    pallas_call x1, Pallas kernels, on_device(): pl.pallas_call(functools.partial(local_kernel, taps, group_width, spans),...  22.6 us
    ppermute x5, starting transfers between devices, from_behind(): return lax.ppermute(shard, axis, pairs)  8.95 us
    pallas_call x1, Pallas kernels, on_device(): pl.pallas_call(functools.partial(final_kernel, group_width, pole_count, w...  5.32 us
    ppermute x1, waiting for transfers between devices, chip_scan(): lax.ppermute(total, 'ctx', [(i, (i ^ 1) + 2) for i in range(peers - 2)])  1.94 us
    ppermute x1, starting transfers between devices, chip_scan(): lax.ppermute(total, 'ctx', [(i, (i ^ 1) + 2) for i in range(peers - 2)])  1.92 us
    select_n x1, other arithmetic, chip_scan(): return jnp.where(odd, even_f * step_decay * full + even_s, full)  1.75 us
    another operation x4, local copies, waits for them, and re-layouts, on_device(): jnp.stack([rates, residues]).reshape(2, nb, gpb, pole_count)  1.71 us
  transfers between devices with their start and end apart: 7, of which 7 were waited for; matrix products, arithmetic and copies ran while one was open for 7% of the time, Pallas kernels for 0%

profile of v7, /device:TPU:24, one launch (start us, length us, event | category | flops | bytes accessed | tf_op | source)
XLA Modules:
  0.0 78.5 jit_solution(632991681724905340)
XLA Ops:
  0.0 1.0 %slice.55 = bf16[8,12288]{1,0:T(8,128)(2,1)S(1)} slice(bf16[128,12288]{1,0:T(8,128)(2,1)} %xv.1), slice={[120:128], [0:12288]} | slice | bytes 393216 | tf_op jit(solution)/shard_map/slice | solution.py:196
  1.0 0.7 convert.4
  1.6 0.1 slice.56
  1.7 0.1 broadcast_in_dim.12
  1.8 1.9 %collective-permute-start = (bf16[8,12416]{1,0:T(8,128)(2,1)S(1)}, bf16[8,12416]{1,0:T(8,128)(2,1)S(1)}, u32[]{:S(2)}, u32[]{:S(2)}) collective-permute-start(bf16[8,12416]{1,0:T(8,128)(2,1)S(1)} %pad_maximum_fusion), channel_id=1, source_target_pairs={{0,1},{1,2},{2,3},{3,4},{4,5},{5,6},{6,7},{7,8},{8,9},{9,10},{10,1... | collective-permute-start | bytes 595976 | tf_op jit(solution)/shard_map/ppermute | solution.py:19
  3.7 0.8 %stack.9 = f32[1,16,16,16]{2,1,3,0:T(8,128)S(1)} reshape(f32[256,16]{0,1:T(8,128)} %param.8) | data formatting | bytes 32768 | tf_op jit(solution)/shard_map/stack | solution.py:204
  4.6 0.8 %stack.10 = f32[1,16,16,16]{2,1,3,0:T(8,128)S(1)} reshape(f32[256,16]{0,1:T(8,128)} %param.9) | data formatting | bytes 32768 | tf_op jit(solution)/shard_map/stack | solution.py:204
  5.5 0.7 slice_bitcast_fusion
  6.2 3.5 %collective-permute-done.rq.rk.rv = bf16[8,12416]{1,0:T(8,128)(2,1)S(1)} collective-permute-done((bf16[8,12416]{1,0:T(8,128)(2,1)S(1)}, bf16[8,12416]{1,0:T(8,128)(2,1)S(1)}, u32[]{:S(2)}, u32[]{:S(2)}) %collective-permute-start) | collective-permute-done | bytes 198688 | tf_op jit(solution)/shard_map/ppermute | solution.py:19
  9.7 0.1 convert_reduce_fusion
  9.8 0.0 copy-done.4
  9.8 0.1 add_convert_fusion
  9.9 0.6 broadcast_in_dim.14.e_ref
  10.5 0.0 copy-done
  10.5 22.6 %shard_map.55 = (f32[128,4096]{1,0:T(8,128)}, f32[128,4096]{1,0:T(8,128)}, f32[16,4224]{1,0:T(8,128)}, f32[4,16,4096]{2,1,0:T(8,128)}, f32[128,128]{1,0:T(8,128)}) custom-call(bf16[128,12288]{1,0:T(8,128)(2,1)} %xv.1, bf16[128,12288]{1,0:T(8,128)(2,1)} %xv.1, bf16[128,12288]{1,0:T(8,128)(2,1)} %xv.1, bf16[8,12416]{1,0:T(8,128)(2,1)} %copy-done, ...), custom_call_target="tpu_custom_call" | custom-call | tf_op jit(solution)/shard_map/pallas_call | solution.py:214
  33.1 0.0 copy-start.1
  33.2 0.1 collective-permute-start.1
  33.2 1.3 %fusion.15 = (f32[1,16,4096]{2,1,0:T(8,128)S(1)}, f32[1,16,4096]{2,1,0:T(8,128)S(1)}, f32[1,16,4096]{2,1,0:T(8,128)S(1)}, f32[1,16,4096]{2,1,0:T(8,128)S(1)}) fusion(f32[4,16,4096]{2,1,0:T(8,128)} %get-tuple-element.13), kind=kLoop, calls=%fused_computation.38 | loop fusion | bytes 2097152 | tf_op jit(solution)/shard_map/slice | solution.py:173
  34.5 0.5 collective-permute-done.1
  35.0 0.0 copy-done.1
  35.0 0.1 fusion.13
  35.1 0.0 copy-start.3
  35.2 0.1 fusion.16
  35.2 0.1 fusion.6
  35.3 0.1 broadcast_in_dim.15
  35.4 2.5 %collective-permute-start.2 = (f32[16,2176]{1,0:T(8,128)S(1)}, f32[16,2176]{1,0:T(8,128)S(1)}, u32[]{:S(2)}, u32[]{:S(2)}) collective-permute-start(f32[16,2176]{1,0:T(8,128)S(1)} %pad_maximum_fusion.1), channel_id=1, source_target_pairs={{0,2},{1,3},{2,4},{3,5},{4,6},{5,7},{6,8},{7,9},{8,10},{9,11},{10,... | collective-permute-start | bytes 417800 | tf_op jit(solution)/shard_map/ppermute | solution.py:19
  37.9 6.0 %collective-permute-done.2 = f32[16,2176]{1,0:T(8,128)S(1)} collective-permute-done((f32[16,2176]{1,0:T(8,128)S(1)}, f32[16,2176]{1,0:T(8,128)S(1)}, u32[]{:S(2)}, u32[]{:S(2)}) %collective-permute-start.2) | collective-permute-done | bytes 139296 | tf_op jit(solution)/shard_map/ppermute | solution.py:19
  43.9 0.1 fusion.9
  44.0 0.1 fusion.5
  44.1 0.1 broadcast_in_dim.16
  44.2 1.3 %collective-permute-start.3 = (f32[16,2176]{1,0:T(8,128)S(1)}, f32[16,2176]{1,0:T(8,128)S(1)}, u32[]{:S(2)}, u32[]{:S(2)}) collective-permute-start(f32[16,2176]{1,0:T(8,128)S(1)} %pad_maximum_fusion.2), channel_id=1, source_target_pairs={{0,4},{1,5},{2,6},{3,7},{4,8},{5,9},{6,10},{7,11},{8,12},{9,13},{1... | collective-permute-start | bytes 417800 | tf_op jit(solution)/shard_map/ppermute | solution.py:19
  45.5 5.6 %collective-permute-done.3 = f32[16,2176]{1,0:T(8,128)S(1)} collective-permute-done((f32[16,2176]{1,0:T(8,128)S(1)}, f32[16,2176]{1,0:T(8,128)S(1)}, u32[]{:S(2)}, u32[]{:S(2)}) %collective-permute-start.3) | collective-permute-done | bytes 139296 | tf_op jit(solution)/shard_map/ppermute | solution.py:19
  51.1 0.1 fusion.8
  51.3 0.1 fusion.4
  51.4 0.1 broadcast_in_dim.17
  51.4 1.3 %collective-permute-start.4 = (f32[16,2176]{1,0:T(8,128)S(1)}, f32[16,2176]{1,0:T(8,128)S(1)}, u32[]{:S(2)}, u32[]{:S(2)}) collective-permute-start(f32[16,2176]{1,0:T(8,128)S(1)} %pad_maximum_fusion.3), channel_id=1, source_target_pairs={{0,8},{1,9},{2,10},{3,11},{4,12},{5,13},{6,14},{7,15},{16,24},{17,... | collective-permute-start | bytes 417800 | tf_op jit(solution)/shard_map/ppermute | solution.py:19
  52.7 8.1 %collective-permute-done.4 = f32[16,2176]{1,0:T(8,128)S(1)} collective-permute-done((f32[16,2176]{1,0:T(8,128)S(1)}, f32[16,2176]{1,0:T(8,128)S(1)}, u32[]{:S(2)}, u32[]{:S(2)}) %collective-permute-start.4) | collective-permute-done | bytes 139296 | tf_op jit(solution)/shard_map/ppermute | solution.py:19
  60.8 0.1 fusion.3
  60.9 1.9 %collective-permute-start.5 = (f32[16,2048]{1,0:T(8,128)S(1)}, f32[16,2048]{1,0:T(8,128)S(1)}, u32[]{:S(2)}, u32[]{:S(2)}) collective-permute-start(f32[16,2048]{1,0:T(8,128)S(1)} %fusion.3), channel_id=1, source_target_pairs={{0,3},{1,2},{2,5},{3,4},{4,7},{5,6},{6,9},{7,8},{8,11},{9,10},{10,... | collective-permute-start | bytes 393224 | tf_op jit(solution)/shard_map/ppermute | solution.py:177
  62.8 1.9 %collective-permute-start.6 = (f32[16,2048]{1,0:T(8,128)S(1)}, f32[16,2048]{1,0:T(8,128)S(1)}, u32[]{:S(2)}, u32[]{:S(2)}) collective-permute-start(f32[16,2048]{1,0:T(8,128)S(1)} %fusion.3), channel_id=1, source_target_pairs={{0,2},{1,3},{2,4},{3,5},{4,6},{5,7},{6,8},{7,9},{8,10},{9,11},{10,... | collective-permute-start | bytes 393224 | tf_op jit(solution)/shard_map/ppermute | solution.py:19
  64.8 0.1 copy.10
  64.9 0.1 copy.11
  65.0 0.7 reshape.38.rf_ref
  65.7 0.7 reshape.39.ef_ref
  66.4 1.9 %collective-permute-done.5 = f32[16,2048]{1,0:T(8,128)S(1)} collective-permute-done((f32[16,2048]{1,0:T(8,128)S(1)}, f32[16,2048]{1,0:T(8,128)S(1)}, u32[]{:S(2)}, u32[]{:S(2)}) %collective-permute-start.5) | collective-permute-done | bytes 131104 | tf_op jit(solution)/shard_map/ppermute | solution.py:177
  68.3 3.1 %collective-permute-done.6 = f32[16,2048]{1,0:T(8,128)S(1)} collective-permute-done((f32[16,2048]{1,0:T(8,128)S(1)}, f32[16,2048]{1,0:T(8,128)S(1)}, u32[]{:S(2)}, u32[]{:S(2)}) %collective-permute-start.6) | collective-permute-done | bytes 131104 | tf_op jit(solution)/shard_map/ppermute | solution.py:19
  71.4 1.7 %fusion.2.b_ref = f32[16,4096]{1,0:T(8,128)} fusion(f32[16,4096]{1,0:T(8,128)S(1)} %get-tuple-element.26, f32[16,2048]{1,0:T(8,128)S(1)} %collective-permute-done.5, f32[16,2048]{1,0:T(8,128)S(1)} %collective-permute-done.6, f32[16]{0:T(128)S(1)} %get-tuple-element.24, pred[]{:T(512)S(6)} %eq.5, f32[4,16,4096]{2,1,0:T(8,128)} %get-tuple-element.13), kind=kLoop, calls=%fused_computation.5 | loop fusion | flops 458752 | bytes 1048641 | tf_op jit(solution)/shard_map/jit(_where)/select_n | solution.py:179
  73.2 5.3 %shard_map.56 = bf16[128,4096]{1,0:T(8,128)(2,1)} custom-call(f32[128,4096]{1,0:T(8,128)} %get-tuple-element.10.q_ref, f32[128,4096]{1,0:T(8,128)} %get-tuple-element.11.loc_ref, f32[16,4096]{1,0:T(8,128)} %fusion.2.b_ref, f32[1,4096]{1,0:T(1,128)} %reshape.38.rf_ref, f32[1,4096]{1,0:T(1,128)} %reshape.39.ef_ref, f32[128,128]{1,0:T(8,128)} %get-tuple-element.14.info_ref), custom_call_target="tpu_custom_call" | custom-call | tf_op jit(solution)/shard_map/pallas_call | solution.py:257
  (13 shorter events, 0.2 us)
Async XLA Ops:
  0.0 9.8 %copy-start.4 = (s32[128]{0:T(128)S(1)}, s32[128]{0:T(128)}, u32[]{:S(2)}) copy-start(s32[128]{0:T(128)} %param.6) | copy-start | bytes 1540
  1.8 7.9 %collective-permute-start = (bf16[8,12416]{1,0:T(8,128)(2,1)S(1)}, bf16[8,12416]{1,0:T(8,128)(2,1)S(1)}, u32[]{:S(2)}, u32[]{:S(2)}) collective-permute-start(bf16[8,12416]{1,0:T(8,128)(2,1)S(1)} %pad_maximum_fusion), channel_id=1, source_target_pairs={{0,1},{1,2},{2,3},{3,4},{4,5},{5,6},{6,7},{7,8},{8,9},{9,10},{10,1... | collective-permute-start | bytes 595976 | tf_op jit(solution)/shard_map/ppermute | solution.py:19
  9.7 0.8 %copy-start = (bf16[8,12416]{1,0:T(8,128)(2,1)}, bf16[8,12416]{1,0:T(8,128)(2,1)S(1)}, u32[]{:S(2)}) copy-start(bf16[8,12416]{1,0:T(8,128)(2,1)S(1)} %collective-permute-done.rq.rk.rv) | copy-start | bytes 595972
  33.1 1.8 %copy-start.1 = (f32[16,4224]{1,0:T(8,128)S(1)}, f32[16,4224]{1,0:T(8,128)}, u32[]{:S(2)}) copy-start(f32[16,4224]{1,0:T(8,128)} %get-tuple-element.12) | copy-start | bytes 811012
  33.2 1.8 %collective-permute-start.1 = (f32[16,4224]{1,0:T(8,128)}, f32[16,4224]{1,0:T(8,128)S(1)}, u32[]{:S(2)}, u32[]{:S(2)}) collective-permute-start(f32[16,4224]{1,0:T(8,128)} %get-tuple-element.12), channel_id=1, source_target_pairs={{0,1},{1,0},{2,3},{3,2},{4,5},{5,4},{6,7},{7,6},{8,9},{9,8},{10,11... | collective-permute-start | bytes 811016 | tf_op jit(solution)/shard_map/ppermute | solution.py:149
  35.1 29.6 %copy-start.2 = (f32[256,16]{0,1:T(8,128)S(1)}, f32[256,16]{0,1:T(8,128)}, u32[]{:S(2)}) copy-start(f32[256,16]{0,1:T(8,128)} %param.8) | copy-start | bytes 49156
  35.1 29.7 %copy-start.3 = (f32[256,16]{0,1:T(8,128)S(1)}, f32[256,16]{0,1:T(8,128)}, u32[]{:S(2)}) copy-start(f32[256,16]{0,1:T(8,128)} %param.9) | copy-start | bytes 49156
  35.4 8.5 %collective-permute-start.2 = (f32[16,2176]{1,0:T(8,128)S(1)}, f32[16,2176]{1,0:T(8,128)S(1)}, u32[]{:S(2)}, u32[]{:S(2)}) collective-permute-start(f32[16,2176]{1,0:T(8,128)S(1)} %pad_maximum_fusion.1), channel_id=1, source_target_pairs={{0,2},{1,3},{2,4},{3,5},{4,6},{5,7},{6,8},{7,9},{8,10},{9,11},{10,... | collective-permute-start | bytes 417800 | tf_op jit(solution)/shard_map/ppermute | solution.py:19
  44.2 6.9 %collective-permute-start.3 = (f32[16,2176]{1,0:T(8,128)S(1)}, f32[16,2176]{1,0:T(8,128)S(1)}, u32[]{:S(2)}, u32[]{:S(2)}) collective-permute-start(f32[16,2176]{1,0:T(8,128)S(1)} %pad_maximum_fusion.2), channel_id=1, source_target_pairs={{0,4},{1,5},{2,6},{3,7},{4,8},{5,9},{6,10},{7,11},{8,12},{9,13},{1... | collective-permute-start | bytes 417800 | tf_op jit(solution)/shard_map/ppermute | solution.py:19
  51.4 9.4 %collective-permute-start.4 = (f32[16,2176]{1,0:T(8,128)S(1)}, f32[16,2176]{1,0:T(8,128)S(1)}, u32[]{:S(2)}, u32[]{:S(2)}) collective-permute-start(f32[16,2176]{1,0:T(8,128)S(1)} %pad_maximum_fusion.3), channel_id=1, source_target_pairs={{0,8},{1,9},{2,10},{3,11},{4,12},{5,13},{6,14},{7,15},{16,24},{17,... | collective-permute-start | bytes 417800 | tf_op jit(solution)/shard_map/ppermute | solution.py:19
  60.9 7.4 %collective-permute-start.5 = (f32[16,2048]{1,0:T(8,128)S(1)}, f32[16,2048]{1,0:T(8,128)S(1)}, u32[]{:S(2)}, u32[]{:S(2)}) collective-permute-start(f32[16,2048]{1,0:T(8,128)S(1)} %fusion.3), channel_id=1, source_target_pairs={{0,3},{1,2},{2,5},{3,4},{4,7},{5,6},{6,9},{7,8},{8,11},{9,10},{10,... | collective-permute-start | bytes 393224 | tf_op jit(solution)/shard_map/ppermute | solution.py:177
  62.8 8.6 %collective-permute-start.6 = (f32[16,2048]{1,0:T(8,128)S(1)}, f32[16,2048]{1,0:T(8,128)S(1)}, u32[]{:S(2)}, u32[]{:S(2)}) collective-permute-start(f32[16,2048]{1,0:T(8,128)S(1)} %fusion.3), channel_id=1, source_target_pairs={{0,2},{1,3},{2,4},{3,5},{4,6},{5,7},{6,8},{7,9},{8,10},{9,11},{10,... | collective-permute-start | bytes 393224 | tf_op jit(solution)/shard_map/ppermute | solution.py:19

commit v8 on v7

--- a/solution.py
+++ b/solution.py
@@ -121,13 +121,21 @@
         dec_out[r] = jnp.exp(-rate_cols * span)
 
 
-def final_kernel(group_width, pole_count, sub, q_ref, loc_ref, b_ref, rf_ref, ef_ref, info_ref, o_ref):
+def final_kernel(group_width, pole_count, sub, hb, q_ref, loc_ref, zo_ref, zp_ref, pk_ref, gt_ref, pf_ref, gf_ref,
+                 d1_ref, rr_ref, info_ref, o_ref):
     length, width = q_ref.shape
     groups = sub // group_width
+    core = lax.axis_index("ctx") % 2
+    odd = core == 1
+    mine_half = (pl.program_id(0) // hb) == core
+    full = jnp.where(mine_half, zo_ref[...], zp_ref[...])
+    even_s = jnp.where(odd, gt_ref[...], pk_ref[...])
+    even_f = jnp.where(odd, gf_ref[:, 0:1], pf_ref[:, 0:1])
+    joined = jnp.where(odd, (even_f * d1_ref[0]) * full + even_s, full)
+    b_all = joined * info_ref[0:1, 1:2]
     tcol = (lax.broadcasted_iota(jnp.int32, (length, 1), 0) + 1).astype(jnp.float32)
-    iw = ef_ref[...] * jnp.exp(-rf_ref[...] * tcol) * info_ref[:, 0:1]
+    iw = rr_ref[1] * jnp.exp(-rr_ref[0] * tcol) * info_ref[:, 0:1]
     iw_hi, iw_lo = split2(iw)
-    b_all = b_ref[...] * info_ref[0:1, 1:2]
     shape = (groups * pole_count, sub)
     row_group = lax.broadcasted_iota(jnp.int32, shape, 0) // pole_count
     lane_group = lax.broadcasted_iota(jnp.int32, shape, 1) // group_width
@@ -149,7 +157,7 @@
     return lax.ppermute(shard, axis, [(i, i ^ 1) for i in range(peers)])
 
 
-def chip_scan(packed, decays, channels, pole_count, peers, me):
+def chip_scan(packed, decays, span_of, channels, pole_count, peers, me):
     core = me % 2
     odd = core == 1
     half = channels // 2
@@ -161,22 +169,39 @@
     odd_s = jnp.where(odd, own_s, other_s)
     even_f = jnp.where(odd, other_f, own_f)
     odd_f = jnp.where(odd, own_f, other_f)
-    step_decay = decays[0]
-    total = (odd_f * mine(step_decay)) * mine(even_s) + mine(odd_s)
+    total = (odd_f * mine(decays[span_of[1]])) * mine(even_s) + mine(odd_s)
     flag = even_f * odd_f
     chips = peers // 2
+    prefix = jnp.zeros_like(total)
+    prefix_flag = jnp.ones_like(flag)
     offset = 1
     while offset < chips:
-        rung = offset.bit_length()
         load = jnp.concatenate([total, jnp.broadcast_to(flag, (pole_count, LANES))], axis=1)
-        got = from_behind(load, "ctx", 2 * offset)
-        total = total + (flag * mine(decays[rung])) * got[:, :half]
-        flag = flag * got[:, half:half + 1]
+        got_load = from_behind(load, "ctx", 2 * offset)
+        came, came_flag = got_load[:, :half], got_load[:, half:half + 1]
+        if offset == 1:
+            prefix = prefix + prefix_flag * came
+        else:
+            prefix = prefix + (prefix_flag * mine(decays[span_of[2 * offset - 2]])) * came
+        prefix_flag = prefix_flag * came_flag
+        if 2 * offset < chips:
+            total = total + (flag * mine(decays[span_of[2 * offset]])) * came
+            flag = flag * came_flag
         offset *= 2
-    prefix = from_behind(total, "ctx", 2)
-    partner = lax.ppermute(total, "ctx", [(i, (i ^ 1) + 2) for i in range(peers - 2)])
-    full = jnp.where(odd, jnp.concatenate([partner, prefix], axis=1), jnp.concatenate([prefix, partner], axis=1))
-    return jnp.where(odd, (even_f * step_decay) * full + even_s, full)
+    return prefix, swap_cores(prefix, "ctx"), got
+
+
+def scan_spans(peers):
+    chips = peers // 2
+    spans = {1}
+    offset = 1
+    while offset < chips:
+        if offset > 1:
+            spans.add(2 * offset - 2)
+        if 2 * offset < chips:
+            spans.add(2 * offset)
+        offset *= 2
+    return sorted(spans)
 
 
 def on_device(qkv, doc_ids, short_w, rates, residues):
@@ -203,11 +228,10 @@
 
     both_t = jnp.stack([rates, residues]).reshape(2, nb, gpb, pole_count).transpose(0, 1, 3, 2)
     rates_t, residues_t = both_t[0], both_t[1]
-    offsets = []
-    while (1 << len(offsets)) < peers:
-        offsets.append(1 << len(offsets))
-    rounds = max(len(offsets), 1)
-    spans = tuple(float(length * o) for o in offsets) or (float(length),)
+    span_list = scan_spans(peers)
+    span_of = {v: i for i, v in enumerate(span_list)}
+    rounds = len(span_list)
+    spans = tuple(float(length * v) for v in span_list)
 
     col = lambda off: (lambda j: (0, j + off))
     fixed = lambda j: (0, 0)
@@ -251,25 +275,34 @@
         compiler_params=pltpu.CompilerParams(dimension_semantics=("arbitrary",)),
     )(qkv, qkv, qkv, rim, rim, rim, short_w, short_w, short_w, e_rows, rates_t, residues_t)
 
-    before = chip_scan(packed, decays, channels, pole_count, peers, me)
+    prefix, partner, got = chip_scan(packed, decays, span_of, channels, pole_count, peers, me)
+    half = channels // 2
+    hb = max(half // final_width, 1)
+    flag_block = channels // LANES
+    rate_rows = jnp.stack([rates, residues]).reshape(2, 1, filters * pole_count)
 
     nbf = channels // final_width
+    iw_width = final_width // group_width * pole_count
     return pl.pallas_call(
-        functools.partial(final_kernel, group_width, pole_count, width),
+        functools.partial(final_kernel, group_width, pole_count, width, hb),
         grid=(nbf,),
         in_specs=[
             pl.BlockSpec((length, final_width), col(0)),
             pl.BlockSpec((length, final_width), col(0)),
+            pl.BlockSpec((pole_count, final_width), lambda j: (0, j % hb)),
+            pl.BlockSpec((pole_count, final_width), lambda j: (0, j % hb)),
             pl.BlockSpec((pole_count, final_width), col(0)),
-            pl.BlockSpec((1, final_width // group_width * pole_count), col(0)),
-            pl.BlockSpec((1, final_width // group_width * pole_count), col(0)),
+            pl.BlockSpec((pole_count, final_width), col(0)),
+            pl.BlockSpec((pole_count, LANES), lambda j: (0, flag_block)),
+            pl.BlockSpec((pole_count, LANES), lambda j: (0, flag_block)),
+            pl.BlockSpec((1, pole_count, final_width), lambda j: (span_of[1], 0, j)),
+            pl.BlockSpec((2, 1, iw_width), lambda j: (0, 0, j)),
             pl.BlockSpec((length, LANES), fixed),
         ],
         out_specs=pl.BlockSpec((length, final_width), col(0)),
         out_shape=jax.ShapeDtypeStruct((length, channels), jnp.bfloat16),
         compiler_params=pltpu.CompilerParams(dimension_semantics=("arbitrary",)),
-    )(q_part, local_part, before, rates.reshape(1, filters * pole_count),
-      residues.reshape(1, filters * pole_count), info)
+    )(q_part, local_part, prefix, partner, packed, got, packed, got, decays, rate_rows, info)
 
 
 def solution(mesh):

time: 79.1 us -> 69 us (0.87)
  waiting for transfers between devices: 28.7 us -> 23.8 us
  starting transfers between devices: 10.9 us -> 7.17 us
  other arithmetic: 3.46 us -> 2.28 us
    ppermute x5 -> x4, waiting for transfers between devices: 26.2 us -> 22.7 us  [from_behind(): return lax.ppermute(shard, axis, pairs)]
    ppermute x1 -> x0, waiting for transfers between devices: 1.94 us -> none  [chip_scan(): lax.ppermute(total, 'ctx', [(i, (i ^ 1) + 2) for i in range(peers - 2)])]
    ppermute x5 -> x4, starting transfers between devices: 8.95 us -> 7.03 us  [from_behind(): return lax.ppermute(shard, axis, pairs)]
    ppermute x1 -> x0, starting transfers between devices: 1.92 us -> none  [chip_scan(): lax.ppermute(total, 'ctx', [(i, (i ^ 1) + 2) for i in range(peers - 2)])]
    select_n x1 -> x0, other arithmetic: 1.75 us -> none  [chip_scan(): return jnp.where(odd, even_f * step_decay * full + even_s, full)]
    reshape x2 -> x0, local copies, waits for them, and re-layouts: 1.42 us -> none  [the longest x1 0.71 us: on_device(): rates.reshape(1, filters * pole_count)]
    another operation x4 -> x6, local copies, waits for them, and re-layouts: 1.71 us -> 1.93 us  [on_device(): jnp.stack([rates, residues]).reshape(2, nb, gpb, pole_count)]
  transfers between devices with their start and end apart: 7 -> 6, of which waited for: 7 -> 6; matrix products, arithmetic and copies ran while one was open for 7% -> 7% of each run, Pallas kernels for 0% -> 0%
where the time goes in v8:
time: 69 us; the launch traced here: 68.2 us
  Pallas kernels  27.9 us (40%)
  waiting for transfers between devices  23.8 us (34%)
  starting transfers between devices  7.17 us (10%)
  local copies, waits for them, and re-layouts  6.76 us (10%)
  other arithmetic  2.28 us (3%)
    ppermute x4, waiting for transfers between devices, from_behind(): return lax.ppermute(shard, axis, pairs)  22.7 us
    pallas_call x1, Pallas kernels, on_device(): pl.pallas_call(functools.partial(local_kernel, taps, group_width, spans),...  22.7 us
    ppermute x4, starting transfers between devices, from_behind(): return lax.ppermute(shard, axis, pairs)  7.03 us
    pallas_call x1, Pallas kernels, on_device(): pl.pallas_call(functools.partial(final_kernel, group_width, pole_count, w...  5.25 us
    another operation x6, local copies, waits for them, and re-layouts, on_device(): jnp.stack([rates, residues]).reshape(2, nb, gpb, pole_count)  1.93 us
  transfers between devices with their start and end apart: 6, of which 6 were waited for; matrix products, arithmetic and copies ran while one was open for 7% of the time, Pallas kernels for 0%

profile of v8, /device:TPU:24, one launch (start us, length us, event | category | flops | bytes accessed | tf_op | source)
XLA Modules:
  0.0 68.2 jit_solution(3281078958940685760)
XLA Ops:
  0.0 1.0 %slice.56 = bf16[8,12288]{1,0:T(8,128)(2,1)S(1)} slice(bf16[128,12288]{1,0:T(8,128)(2,1)} %xv.1), slice={[120:128], [0:12288]} | slice | bytes 393216 | tf_op jit(solution)/shard_map/slice | solution.py:221
  1.0 0.7 convert.4
  1.6 0.1 slice.57
  1.7 0.1 broadcast_in_dim.36
  1.8 1.9 %collective-permute-start = (bf16[8,12416]{1,0:T(8,128)(2,1)S(1)}, bf16[8,12416]{1,0:T(8,128)(2,1)S(1)}, u32[]{:S(2)}, u32[]{:S(2)}) collective-permute-start(bf16[8,12416]{1,0:T(8,128)(2,1)S(1)} %pad_maximum_fusion), channel_id=1, source_target_pairs={{0,1},{1,2},{2,3},{3,4},{4,5},{5,6},{6,7},{7,8},{8,9},{9,10},{10,1... | collective-permute-start | bytes 595976 | tf_op jit(solution)/shard_map/ppermute | solution.py:19
  3.7 0.8 %stack.18 = f32[1,16,16,16]{2,1,3,0:T(8,128)S(1)} reshape(f32[256,16]{0,1:T(8,128)} %param.8) | data formatting | bytes 32768 | tf_op jit(solution)/shard_map/stack | solution.py:229
  4.6 0.8 %stack.19 = f32[1,16,16,16]{2,1,3,0:T(8,128)S(1)} reshape(f32[256,16]{0,1:T(8,128)} %param.9) | data formatting | bytes 32768 | tf_op jit(solution)/shard_map/stack | solution.py:229
  5.5 0.7 %slice_bitcast_fusion = (f32[16,16,16]{2,1,0:T(8,128)}, f32[16,16,16]{2,1,0:T(8,128)}) fusion(f32[2,16,16,16]{3,2,1,0:T(8,128)S(1)} %maximum_bitcast_fusion), kind=kLoop, calls=%fused_computation.7 | loop fusion | bytes 65536 | tf_op jit(solution)/shard_map/squeeze | solution.py:230
  6.3 3.4 %collective-permute-done.rq.rk.rv = bf16[8,12416]{1,0:T(8,128)(2,1)S(1)} collective-permute-done((bf16[8,12416]{1,0:T(8,128)(2,1)S(1)}, bf16[8,12416]{1,0:T(8,128)(2,1)S(1)}, u32[]{:S(2)}, u32[]{:S(2)}) %collective-permute-start) | collective-permute-done | bytes 198688 | tf_op jit(solution)/shard_map/ppermute | solution.py:19
  9.7 0.1 convert_reduce_fusion
  9.8 0.0 copy-done.7
  9.8 0.1 add_convert_fusion
  9.9 0.6 broadcast_in_dim.38.e_ref
  10.5 0.0 copy-done.2
  10.5 22.7 %shard_map.55 = (f32[128,4096]{1,0:T(8,128)}, f32[128,4096]{1,0:T(8,128)}, f32[16,4224]{1,0:T(8,128)}, f32[4,16,4096]{2,1,0:T(8,128)}, f32[128,128]{1,0:T(8,128)}) custom-call(bf16[128,12288]{1,0:T(8,128)(2,1)} %xv.1, bf16[128,12288]{1,0:T(8,128)(2,1)} %xv.1, bf16[128,12288]{1,0:T(8,128)(2,1)} %xv.1, bf16[8,12416]{1,0:T(8,128)(2,1)} %copy-done.2, ...), custom_call_target="tpu_custom_call" | custom-call | tf_op jit(solution)/shard_map/pallas_call | solution.py:238
  33.2 0.0 copy-start
  33.2 0.1 collective-permute-start.1
  33.3 1.3 %fusion.12 = (f32[1,16,4096]{2,1,0:T(8,128)S(1)}, f32[1,16,4096]{2,1,0:T(8,128)S(1)}, f32[1,16,4096]{2,1,0:T(8,128)S(1)}, f32[1,16,4096]{2,1,0:T(8,128)S(1)}) fusion(f32[4,16,4096]{2,1,0:T(8,128)} %get-tuple-element.13.d1_ref), kind=kLoop, calls=%fused_computation.34 | loop fusion | bytes 2097152 | tf_op jit(solution)/shard_map/slice | solution.py:185
  34.5 0.0 copy-done
  34.5 0.0 copy-start.5
  34.6 0.0 copy-start.6
  34.6 0.4 collective-permute-done.1.gt_ref.gf_ref
  35.0 0.1 fusion.11
  35.2 0.1 fusion.8
  35.2 0.1 broadcast_in_dim.40
  35.3 2.5 %collective-permute-start.2 = (f32[16,2176]{1,0:T(8,128)S(1)}, f32[16,2176]{1,0:T(8,128)S(1)}, u32[]{:S(2)}, u32[]{:S(2)}) collective-permute-start(f32[16,2176]{1,0:T(8,128)S(1)} %pad_maximum_fusion.1), channel_id=1, source_target_pairs={{0,2},{1,3},{2,4},{3,5},{4,6},{5,7},{6,8},{7,9},{8,10},{9,11},{10,... | collective-permute-start | bytes 417800 | tf_op jit(solution)/shard_map/ppermute | solution.py:19
  37.9 6.0 %collective-permute-done.2 = f32[16,2176]{1,0:T(8,128)S(1)} collective-permute-done((f32[16,2176]{1,0:T(8,128)S(1)}, f32[16,2176]{1,0:T(8,128)S(1)}, u32[]{:S(2)}, u32[]{:S(2)}) %collective-permute-start.2) | collective-permute-done | bytes 139296 | tf_op jit(solution)/shard_map/ppermute | solution.py:19
  43.8 0.1 fusion.6
  43.9 0.1 slice_reduce_fusion
  44.0 0.1 broadcast_in_dim.42
  44.1 1.3 %collective-permute-start.3 = (f32[16,2176]{1,0:T(8,128)S(1)}, f32[16,2176]{1,0:T(8,128)S(1)}, u32[]{:S(2)}, u32[]{:S(2)}) collective-permute-start(f32[16,2176]{1,0:T(8,128)S(1)} %pad_maximum_fusion.2), channel_id=1, source_target_pairs={{0,4},{1,5},{2,6},{3,7},{4,8},{5,9},{6,10},{7,11},{8,12},{9,13},{1... | collective-permute-start | bytes 417800 | tf_op jit(solution)/shard_map/ppermute | solution.py:19
  45.4 5.6 %collective-permute-done.3 = f32[16,2176]{1,0:T(8,128)S(1)} collective-permute-done((f32[16,2176]{1,0:T(8,128)S(1)}, f32[16,2176]{1,0:T(8,128)S(1)}, u32[]{:S(2)}, u32[]{:S(2)}) %collective-permute-start.3) | collective-permute-done | bytes 139296 | tf_op jit(solution)/shard_map/ppermute | solution.py:19
  51.1 0.1 multiply_reduce_fusion.1
  51.2 0.1 fusion.2
  51.3 0.1 broadcast_in_dim.44
  51.4 1.3 %collective-permute-start.4 = (f32[16,2176]{1,0:T(8,128)S(1)}, f32[16,2176]{1,0:T(8,128)S(1)}, u32[]{:S(2)}, u32[]{:S(2)}) collective-permute-start(f32[16,2176]{1,0:T(8,128)S(1)} %pad_maximum_fusion.3), channel_id=1, source_target_pairs={{0,8},{1,9},{2,10},{3,11},{4,12},{5,13},{6,14},{7,15},{16,24},{17,... | collective-permute-start | bytes 417800 | tf_op jit(solution)/shard_map/ppermute | solution.py:19
  52.7 0.0 copy-done.5
  52.7 0.1 copy.10
  52.8 0.1 copy.11
  52.9 0.1 stack.21
  53.0 0.1 stack.22
  53.1 7.6 %collective-permute-done.4 = f32[16,2176]{1,0:T(8,128)S(1)} collective-permute-done((f32[16,2176]{1,0:T(8,128)S(1)}, f32[16,2176]{1,0:T(8,128)S(1)}, u32[]{:S(2)}, u32[]{:S(2)}) %collective-permute-start.4) | collective-permute-done | bytes 139296 | tf_op jit(solution)/shard_map/ppermute | solution.py:19
  60.8 0.1 fusion.zo_ref
  60.9 0.1 collective-permute-start.5
  61.0 0.6 pad_maximum_fusion.4.rr_ref
  61.6 0.7 %collective-permute-done.5.zp_ref = f32[16,2048]{1,0:T(8,128)S(1)} collective-permute-done((f32[16,2048]{1,0:T(8,128)S(1)}, f32[16,2048]{1,0:T(8,128)S(1)}, u32[]{:S(2)}, u32[]{:S(2)}) %collective-permute-start.5) | collective-permute-done | bytes 131104 | tf_op jit(solution)/shard_map/ppermute | solution.py:157
  62.3 0.6 copy-done.4
  63.0 5.2 %shard_map.56 = bf16[128,4096]{1,0:T(8,128)(2,1)} custom-call(f32[128,4096]{1,0:T(8,128)} %get-tuple-element.10.q_ref, f32[128,4096]{1,0:T(8,128)} %get-tuple-element.11.loc_ref, f32[16,2048]{1,0:T(8,128)} %copy-done.3, f32[16,2048]{1,0:T(8,128)} %copy-done.4, f32[16,4224]{1,0:T(8,128)} %get-tuple-element.12.pk_ref.pf_ref, f32[16,4224]{1,0:T(8,128)} %copy-done.1, ...), custom_call_target="tpu_custom_call" | custom-call | tf_op jit(solution)/shard_map/pallas_call | solution.py:286
  (18 shorter events, 0.2 us)
Async XLA Ops:
  0.0 9.8 %copy-start.7 = (s32[128]{0:T(128)S(1)}, s32[128]{0:T(128)}, u32[]{:S(2)}) copy-start(s32[128]{0:T(128)} %param.6) | copy-start | bytes 1540
  1.8 7.9 %collective-permute-start = (bf16[8,12416]{1,0:T(8,128)(2,1)S(1)}, bf16[8,12416]{1,0:T(8,128)(2,1)S(1)}, u32[]{:S(2)}, u32[]{:S(2)}) collective-permute-start(bf16[8,12416]{1,0:T(8,128)(2,1)S(1)} %pad_maximum_fusion), channel_id=1, source_target_pairs={{0,1},{1,2},{2,3},{3,4},{4,5},{5,6},{6,7},{7,8},{8,9},{9,10},{10,1... | collective-permute-start | bytes 595976 | tf_op jit(solution)/shard_map/ppermute | solution.py:19
  9.7 0.8 %copy-start.2 = (bf16[8,12416]{1,0:T(8,128)(2,1)}, bf16[8,12416]{1,0:T(8,128)(2,1)S(1)}, u32[]{:S(2)}) copy-start(bf16[8,12416]{1,0:T(8,128)(2,1)S(1)} %collective-permute-done.rq.rk.rv) | copy-start | bytes 595972
  33.2 1.4 %copy-start = (f32[16,4224]{1,0:T(8,128)S(1)}, f32[16,4224]{1,0:T(8,128)}, u32[]{:S(2)}) copy-start(f32[16,4224]{1,0:T(8,128)} %get-tuple-element.12.pk_ref.pf_ref) | copy-start | bytes 811012
  33.2 1.8 %collective-permute-start.1 = (f32[16,4224]{1,0:T(8,128)}, f32[16,4224]{1,0:T(8,128)S(1)}, u32[]{:S(2)}, u32[]{:S(2)}) collective-permute-start(f32[16,4224]{1,0:T(8,128)} %get-tuple-element.12.pk_ref.pf_ref), channel_id=1, source_target_pairs={{0,1},{1,0},{2,3},{3,2},{4,5},{5,4},{6,7},{7,6},{8,9},{9,8},{10,11... | collective-permute-start | bytes 811016 | tf_op jit(solution)/shard_map/ppermute | solution.py:157
  34.5 18.2 %copy-start.5 = (f32[256,16]{0,1:T(8,128)S(1)}, f32[256,16]{0,1:T(8,128)}, u32[]{:S(2)}) copy-start(f32[256,16]{0,1:T(8,128)} %param.8) | copy-start | bytes 49156
  34.6 18.3 %copy-start.6 = (f32[256,16]{0,1:T(8,128)S(1)}, f32[256,16]{0,1:T(8,128)}, u32[]{:S(2)}) copy-start(f32[256,16]{0,1:T(8,128)} %param.9) | copy-start | bytes 49156
  35.0 25.9 %copy-start.1 = (f32[16,4224]{1,0:T(8,128)}, f32[16,4224]{1,0:T(8,128)S(1)}, u32[]{:S(2)}) copy-start(f32[16,4224]{1,0:T(8,128)S(1)} %collective-permute-done.1.gt_ref.gf_ref) | copy-start | bytes 811012
  35.3 8.5 %collective-permute-start.2 = (f32[16,2176]{1,0:T(8,128)S(1)}, f32[16,2176]{1,0:T(8,128)S(1)}, u32[]{:S(2)}, u32[]{:S(2)}) collective-permute-start(f32[16,2176]{1,0:T(8,128)S(1)} %pad_maximum_fusion.1), channel_id=1, source_target_pairs={{0,2},{1,3},{2,4},{3,5},{4,6},{5,7},{6,8},{7,9},{8,10},{9,11},{10,... | collective-permute-start | bytes 417800 | tf_op jit(solution)/shard_map/ppermute | solution.py:19
  44.1 6.9 %collective-permute-start.3 = (f32[16,2176]{1,0:T(8,128)S(1)}, f32[16,2176]{1,0:T(8,128)S(1)}, u32[]{:S(2)}, u32[]{:S(2)}) collective-permute-start(f32[16,2176]{1,0:T(8,128)S(1)} %pad_maximum_fusion.2), channel_id=1, source_target_pairs={{0,4},{1,5},{2,6},{3,7},{4,8},{5,9},{6,10},{7,11},{8,12},{9,13},{1... | collective-permute-start | bytes 417800 | tf_op jit(solution)/shard_map/ppermute | solution.py:19
  51.4 9.4 %collective-permute-start.4 = (f32[16,2176]{1,0:T(8,128)S(1)}, f32[16,2176]{1,0:T(8,128)S(1)}, u32[]{:S(2)}, u32[]{:S(2)}) collective-permute-start(f32[16,2176]{1,0:T(8,128)S(1)} %pad_maximum_fusion.3), channel_id=1, source_target_pairs={{0,8},{1,9},{2,10},{3,11},{4,12},{5,13},{6,14},{7,15},{16,24},{17,... | collective-permute-start | bytes 417800 | tf_op jit(solution)/shard_map/ppermute | solution.py:19
  60.9 1.4 %copy-start.3 = (f32[16,2048]{1,0:T(8,128)}, f32[16,2048]{1,0:T(8,128)S(1)}, u32[]{:S(2)}) copy-start(f32[16,2048]{1,0:T(8,128)S(1)} %fusion.zo_ref) | copy-start | bytes 393220
  60.9 1.4 %collective-permute-start.5 = (f32[16,2048]{1,0:T(8,128)S(1)}, f32[16,2048]{1,0:T(8,128)S(1)}, u32[]{:S(2)}, u32[]{:S(2)}) collective-permute-start(f32[16,2048]{1,0:T(8,128)S(1)} %fusion.zo_ref), channel_id=1, source_target_pairs={{0,1},{1,0},{2,3},{3,2},{4,5},{5,4},{6,7},{7,6},{8,9},{9,8},{10,11... | collective-permute-start | bytes 393224 | tf_op jit(solution)/shard_map/ppermute | solution.py:157
  62.3 0.7 copy-start.4

commit v9 on v8

--- a/solution.py
+++ b/solution.py
@@ -65,16 +65,16 @@
         info_out[...] = jnp.where(lane == 0, eqf[:, 0:1], jnp.broadcast_to(into, info_out.shape))
         ext_s[...] = jnp.zeros_like(ext_s)
 
-    shifts = shift_s[...]
 
     def conv(x_ref, r_ref, w_ref):
         ext_s[0:length, :] = x_ref[...]
         ext_s[length:length + RIM, :] = r_ref[...]
-        windows = jnp.dot(shifts, ext_s[...], preferred_element_type=jnp.float32)
+        ext = ext_s[...]
         w = w_ref[...]
-        acc = w[0:1, :] * windows[0:length]
+        acc = w[0:1, :] * x_ref[...].astype(jnp.float32)
         for j in range(1, taps):
-            acc = acc + w[j:j + 1, :] * windows[j * length:(j + 1) * length]
+            window = jnp.dot(shift_s[j * length:(j + 1) * length, :], ext, preferred_element_type=jnp.float32)
+            acc = acc + w[j:j + 1, :] * window
         return acc
 
     cq = conv(xq, rq, wq)
@@ -100,12 +100,12 @@
         a_col = rt[:, g:g + 1]
         r_col = et[:, g:g + 1]
         base = jnp.sum(r_col * jnp.exp(-a_col * lags), axis=0, keepdims=True)
-        row = jnp.broadcast_to(base, (length, length))
+        row = jnp.broadcast_to(base.astype(jnp.bfloat16), (length, length))
         rolled = pltpu.roll(row, 0, 1, stride=1, stride_axis=0)
-        pieces.append(jnp.where(visible, rolled, 0.0))
+        pieces.append(jnp.where(visible, rolled, jnp.zeros_like(rolled)))
         ends.append(jnp.exp(-a_col * to_end) * at_tail)
     e_hi, e_lo = split2(jnp.concatenate(ends, axis=1))
-    t_hi = jnp.concatenate(pieces, axis=1).astype(jnp.bfloat16)
+    t_hi = jnp.concatenate(pieces, axis=1)
     res = jnp.dot(jnp.concatenate([t_hi, e_hi, e_lo], axis=0), xbd, preferred_element_type=jnp.float32)
     loc_out[...] = res[0:length]
     st = res[length:length + pole_count] + res[length + pole_count:length + 2 * pole_count]

time: 69 us -> 64.8 us (0.939)
  Pallas kernels: 27.9 us -> 23.7 us
    pallas_call x1, Pallas kernels: 22.7 us -> 18.4 us  [on_device(): pl.pallas_call(functools.partial(local_kernel, taps, group_width, spans),...]
  transfers between devices with their start and end apart: 6 -> 6, of which waited for: 6 -> 6; matrix products, arithmetic and copies ran while one was open for 7% -> 8% of each run, Pallas kernels for 0% -> 0%
where the time goes in v9:
time: 64.8 us; the launch traced here: 64 us
  waiting for transfers between devices  23.8 us (37%)
  Pallas kernels  23.7 us (37%)
  starting transfers between devices  7.16 us (11%)
  local copies, waits for them, and re-layouts  6.76 us (10%)
  other arithmetic  2.28 us (4%)
    ppermute x4, waiting for transfers between devices, from_behind(): return lax.ppermute(shard, axis, pairs)  22.7 us
    pallas_call x1, Pallas kernels, on_device(): pl.pallas_call(functools.partial(local_kernel, taps, group_width, spans),...  18.4 us
    ppermute x4, starting transfers between devices, from_behind(): return lax.ppermute(shard, axis, pairs)  7.02 us
    pallas_call x1, Pallas kernels, on_device(): pl.pallas_call(functools.partial(final_kernel, group_width, pole_count, w...  5.24 us
    another operation x6, local copies, waits for them, and re-layouts, on_device(): jnp.stack([rates, residues]).reshape(2, nb, gpb, pole_count)  1.93 us
  transfers between devices with their start and end apart: 6, of which 6 were waited for; matrix products, arithmetic and copies ran while one was open for 8% of the time, Pallas kernels for 0%

profile of v9, /device:TPU:24, one launch (start us, length us, event | category | flops | bytes accessed | tf_op | source)
XLA Modules:
  0.0 64.0 jit_solution(16303793680698925292)
XLA Ops:
  0.0 1.0 %slice.56 = bf16[8,12288]{1,0:T(8,128)(2,1)S(1)} slice(bf16[128,12288]{1,0:T(8,128)(2,1)} %xv.1), slice={[120:128], [0:12288]} | slice | bytes 393216 | tf_op jit(solution)/shard_map/slice | solution.py:221
  1.0 0.7 %convert.4 = bf16[128]{0:T(256)(128)(2,1)S(1)} convert(s32[128]{0:T(128)} %param.6) | non-fusion elementwise | flops 128 | bytes 768 | tf_op jit(solution)/shard_map/convert.1
  1.6 0.1 slice.57
  1.7 0.1 broadcast_in_dim.36
  1.8 1.9 %collective-permute-start = (bf16[8,12416]{1,0:T(8,128)(2,1)S(1)}, bf16[8,12416]{1,0:T(8,128)(2,1)S(1)}, u32[]{:S(2)}, u32[]{:S(2)}) collective-permute-start(bf16[8,12416]{1,0:T(8,128)(2,1)S(1)} %pad_maximum_fusion), channel_id=1, source_target_pairs={{0,1},{1,2},{2,3},{3,4},{4,5},{5,6},{6,7},{7,8},{8,9},{9,10},{10,1... | collective-permute-start | bytes 595976 | tf_op jit(solution)/shard_map/ppermute | solution.py:19
  3.7 0.8 %stack.18 = f32[1,16,16,16]{2,1,3,0:T(8,128)S(1)} reshape(f32[256,16]{0,1:T(8,128)} %param.8) | data formatting | bytes 32768 | tf_op jit(solution)/shard_map/stack | solution.py:229
  4.6 0.8 %stack.19 = f32[1,16,16,16]{2,1,3,0:T(8,128)S(1)} reshape(f32[256,16]{0,1:T(8,128)} %param.9) | data formatting | bytes 32768 | tf_op jit(solution)/shard_map/stack | solution.py:229
  5.5 0.7 %slice_bitcast_fusion = (f32[16,16,16]{2,1,0:T(8,128)}, f32[16,16,16]{2,1,0:T(8,128)}) fusion(f32[2,16,16,16]{3,2,1,0:T(8,128)S(1)} %maximum_bitcast_fusion), kind=kLoop, calls=%fused_computation.7 | loop fusion | bytes 65536 | tf_op jit(solution)/shard_map/squeeze | solution.py:230
  6.3 3.4 %collective-permute-done.rq.rk.rv = bf16[8,12416]{1,0:T(8,128)(2,1)S(1)} collective-permute-done((bf16[8,12416]{1,0:T(8,128)(2,1)S(1)}, bf16[8,12416]{1,0:T(8,128)(2,1)S(1)}, u32[]{:S(2)}, u32[]{:S(2)}) %collective-permute-start) | collective-permute-done | bytes 198688 | tf_op jit(solution)/shard_map/ppermute | solution.py:19
  9.7 0.1 convert_reduce_fusion
  9.8 0.0 copy-done.7
  9.8 0.1 add_convert_fusion
  9.9 0.6 broadcast_in_dim.38.e_ref
  10.5 0.0 copy-done.2
  10.5 18.4 %shard_map.55 = (f32[128,4096]{1,0:T(8,128)}, f32[128,4096]{1,0:T(8,128)}, f32[16,4224]{1,0:T(8,128)}, f32[4,16,4096]{2,1,0:T(8,128)}, f32[128,128]{1,0:T(8,128)}) custom-call(bf16[128,12288]{1,0:T(8,128)(2,1)} %xv.1, bf16[128,12288]{1,0:T(8,128)(2,1)} %xv.1, bf16[128,12288]{1,0:T(8,128)(2,1)} %xv.1, bf16[8,12416]{1,0:T(8,128)(2,1)} %copy-done.2, ...), custom_call_target="tpu_custom_call" | custom-call | tf_op jit(solution)/shard_map/pallas_call | solution.py:238
  28.9 0.0 copy-start
  29.0 0.1 collective-permute-start.1
  29.0 1.3 %fusion.12 = (f32[1,16,4096]{2,1,0:T(8,128)S(1)}, f32[1,16,4096]{2,1,0:T(8,128)S(1)}, f32[1,16,4096]{2,1,0:T(8,128)S(1)}, f32[1,16,4096]{2,1,0:T(8,128)S(1)}) fusion(f32[4,16,4096]{2,1,0:T(8,128)} %get-tuple-element.13.d1_ref), kind=kLoop, calls=%fused_computation.34 | loop fusion | bytes 2097152 | tf_op jit(solution)/shard_map/slice | solution.py:185
  30.3 0.0 copy-done
  30.3 0.0 copy-start.5
  30.3 0.0 copy-start.6
  30.4 0.4 collective-permute-done.1.gt_ref.gf_ref
  30.8 0.1 fusion.11
  30.9 0.1 fusion.8
  31.0 0.1 broadcast_in_dim.40
  31.1 2.5 %collective-permute-start.2 = (f32[16,2176]{1,0:T(8,128)S(1)}, f32[16,2176]{1,0:T(8,128)S(1)}, u32[]{:S(2)}, u32[]{:S(2)}) collective-permute-start(f32[16,2176]{1,0:T(8,128)S(1)} %pad_maximum_fusion.1), channel_id=1, source_target_pairs={{0,2},{1,3},{2,4},{3,5},{4,6},{5,7},{6,8},{7,9},{8,10},{9,11},{10,... | collective-permute-start | bytes 417800 | tf_op jit(solution)/shard_map/ppermute | solution.py:19
  33.6 6.0 %collective-permute-done.2 = f32[16,2176]{1,0:T(8,128)S(1)} collective-permute-done((f32[16,2176]{1,0:T(8,128)S(1)}, f32[16,2176]{1,0:T(8,128)S(1)}, u32[]{:S(2)}, u32[]{:S(2)}) %collective-permute-start.2) | collective-permute-done | bytes 139296 | tf_op jit(solution)/shard_map/ppermute | solution.py:19
  39.6 0.1 fusion.6
  39.7 0.1 slice_reduce_fusion
  39.8 0.1 broadcast_in_dim.42
  39.9 1.3 %collective-permute-start.3 = (f32[16,2176]{1,0:T(8,128)S(1)}, f32[16,2176]{1,0:T(8,128)S(1)}, u32[]{:S(2)}, u32[]{:S(2)}) collective-permute-start(f32[16,2176]{1,0:T(8,128)S(1)} %pad_maximum_fusion.2), channel_id=1, source_target_pairs={{0,4},{1,5},{2,6},{3,7},{4,8},{5,9},{6,10},{7,11},{8,12},{9,13},{1... | collective-permute-start | bytes 417800 | tf_op jit(solution)/shard_map/ppermute | solution.py:19
  41.2 5.6 %collective-permute-done.3 = f32[16,2176]{1,0:T(8,128)S(1)} collective-permute-done((f32[16,2176]{1,0:T(8,128)S(1)}, f32[16,2176]{1,0:T(8,128)S(1)}, u32[]{:S(2)}, u32[]{:S(2)}) %collective-permute-start.3) | collective-permute-done | bytes 139296 | tf_op jit(solution)/shard_map/ppermute | solution.py:19
  46.9 0.1 multiply_reduce_fusion.1
  47.0 0.1 fusion.2
  47.1 0.1 broadcast_in_dim.44
  47.2 1.3 %collective-permute-start.4 = (f32[16,2176]{1,0:T(8,128)S(1)}, f32[16,2176]{1,0:T(8,128)S(1)}, u32[]{:S(2)}, u32[]{:S(2)}) collective-permute-start(f32[16,2176]{1,0:T(8,128)S(1)} %pad_maximum_fusion.3), channel_id=1, source_target_pairs={{0,8},{1,9},{2,10},{3,11},{4,12},{5,13},{6,14},{7,15},{16,24},{17,... | collective-permute-start | bytes 417800 | tf_op jit(solution)/shard_map/ppermute | solution.py:19
  48.5 0.0 copy-done.5
  48.5 0.1 copy.10
  48.6 0.1 copy.11
  48.7 0.1 stack.21
  48.8 0.1 stack.22
  48.9 7.6 %collective-permute-done.4 = f32[16,2176]{1,0:T(8,128)S(1)} collective-permute-done((f32[16,2176]{1,0:T(8,128)S(1)}, f32[16,2176]{1,0:T(8,128)S(1)}, u32[]{:S(2)}, u32[]{:S(2)}) %collective-permute-start.4) | collective-permute-done | bytes 139296 | tf_op jit(solution)/shard_map/ppermute | solution.py:19
  56.5 0.1 fusion.zo_ref
  56.7 0.1 collective-permute-start.5
  56.7 0.6 pad_maximum_fusion.4.rr_ref
  57.4 0.7 %collective-permute-done.5.zp_ref = f32[16,2048]{1,0:T(8,128)S(1)} collective-permute-done((f32[16,2048]{1,0:T(8,128)S(1)}, f32[16,2048]{1,0:T(8,128)S(1)}, u32[]{:S(2)}, u32[]{:S(2)}) %collective-permute-start.5) | collective-permute-done | bytes 131104 | tf_op jit(solution)/shard_map/ppermute | solution.py:157
  58.1 0.6 %copy-done.4 = f32[16,2048]{1,0:T(8,128)} copy-done((f32[16,2048]{1,0:T(8,128)}, f32[16,2048]{1,0:T(8,128)S(1)}, u32[]{:S(2)}) %copy-start.4) | copy-done | bytes 131096
  58.7 5.2 %shard_map.56 = bf16[128,4096]{1,0:T(8,128)(2,1)} custom-call(f32[128,4096]{1,0:T(8,128)} %get-tuple-element.10.q_ref, f32[128,4096]{1,0:T(8,128)} %get-tuple-element.11.loc_ref, f32[16,2048]{1,0:T(8,128)} %copy-done.3, f32[16,2048]{1,0:T(8,128)} %copy-done.4, f32[16,4224]{1,0:T(8,128)} %get-tuple-element.12.pk_ref.pf_ref, f32[16,4224]{1,0:T(8,128)} %copy-done.1, ...), custom_call_target="tpu_custom_call" | custom-call | tf_op jit(solution)/shard_map/pallas_call | solution.py:286
  (18 shorter events, 0.2 us)
Async XLA Ops:
  0.0 9.8 %copy-start.7 = (s32[128]{0:T(128)S(1)}, s32[128]{0:T(128)}, u32[]{:S(2)}) copy-start(s32[128]{0:T(128)} %param.6) | copy-start | bytes 1540
  1.8 7.9 %collective-permute-start = (bf16[8,12416]{1,0:T(8,128)(2,1)S(1)}, bf16[8,12416]{1,0:T(8,128)(2,1)S(1)}, u32[]{:S(2)}, u32[]{:S(2)}) collective-permute-start(bf16[8,12416]{1,0:T(8,128)(2,1)S(1)} %pad_maximum_fusion), channel_id=1, source_target_pairs={{0,1},{1,2},{2,3},{3,4},{4,5},{5,6},{6,7},{7,8},{8,9},{9,10},{10,1... | collective-permute-start | bytes 595976 | tf_op jit(solution)/shard_map/ppermute | solution.py:19
  9.7 0.8 %copy-start.2 = (bf16[8,12416]{1,0:T(8,128)(2,1)}, bf16[8,12416]{1,0:T(8,128)(2,1)S(1)}, u32[]{:S(2)}) copy-start(bf16[8,12416]{1,0:T(8,128)(2,1)S(1)} %collective-permute-done.rq.rk.rv) | copy-start | bytes 595972
  28.9 1.4 %copy-start = (f32[16,4224]{1,0:T(8,128)S(1)}, f32[16,4224]{1,0:T(8,128)}, u32[]{:S(2)}) copy-start(f32[16,4224]{1,0:T(8,128)} %get-tuple-element.12.pk_ref.pf_ref) | copy-start | bytes 811012
  29.0 1.8 %collective-permute-start.1 = (f32[16,4224]{1,0:T(8,128)}, f32[16,4224]{1,0:T(8,128)S(1)}, u32[]{:S(2)}, u32[]{:S(2)}) collective-permute-start(f32[16,4224]{1,0:T(8,128)} %get-tuple-element.12.pk_ref.pf_ref), channel_id=1, source_target_pairs={{0,1},{1,0},{2,3},{3,2},{4,5},{5,4},{6,7},{7,6},{8,9},{9,8},{10,11... | collective-permute-start | bytes 811016 | tf_op jit(solution)/shard_map/ppermute | solution.py:157
  30.3 18.2 %copy-start.5 = (f32[256,16]{0,1:T(8,128)S(1)}, f32[256,16]{0,1:T(8,128)}, u32[]{:S(2)}) copy-start(f32[256,16]{0,1:T(8,128)} %param.8) | copy-start | bytes 49156
  30.3 18.3 %copy-start.6 = (f32[256,16]{0,1:T(8,128)S(1)}, f32[256,16]{0,1:T(8,128)}, u32[]{:S(2)}) copy-start(f32[256,16]{0,1:T(8,128)} %param.9) | copy-start | bytes 49156
  30.8 25.9 %copy-start.1 = (f32[16,4224]{1,0:T(8,128)}, f32[16,4224]{1,0:T(8,128)S(1)}, u32[]{:S(2)}) copy-start(f32[16,4224]{1,0:T(8,128)S(1)} %collective-permute-done.1.gt_ref.gf_ref) | copy-start | bytes 811012
  31.1 8.5 %collective-permute-start.2 = (f32[16,2176]{1,0:T(8,128)S(1)}, f32[16,2176]{1,0:T(8,128)S(1)}, u32[]{:S(2)}, u32[]{:S(2)}) collective-permute-start(f32[16,2176]{1,0:T(8,128)S(1)} %pad_maximum_fusion.1), channel_id=1, source_target_pairs={{0,2},{1,3},{2,4},{3,5},{4,6},{5,7},{6,8},{7,9},{8,10},{9,11},{10,... | collective-permute-start | bytes 417800 | tf_op jit(solution)/shard_map/ppermute | solution.py:19
  39.9 6.9 %collective-permute-start.3 = (f32[16,2176]{1,0:T(8,128)S(1)}, f32[16,2176]{1,0:T(8,128)S(1)}, u32[]{:S(2)}, u32[]{:S(2)}) collective-permute-start(f32[16,2176]{1,0:T(8,128)S(1)} %pad_maximum_fusion.2), channel_id=1, source_target_pairs={{0,4},{1,5},{2,6},{3,7},{4,8},{5,9},{6,10},{7,11},{8,12},{9,13},{1... | collective-permute-start | bytes 417800 | tf_op jit(solution)/shard_map/ppermute | solution.py:19
  47.2 9.4 %collective-permute-start.4 = (f32[16,2176]{1,0:T(8,128)S(1)}, f32[16,2176]{1,0:T(8,128)S(1)}, u32[]{:S(2)}, u32[]{:S(2)}) collective-permute-start(f32[16,2176]{1,0:T(8,128)S(1)} %pad_maximum_fusion.3), channel_id=1, source_target_pairs={{0,8},{1,9},{2,10},{3,11},{4,12},{5,13},{6,14},{7,15},{16,24},{17,... | collective-permute-start | bytes 417800 | tf_op jit(solution)/shard_map/ppermute | solution.py:19
  56.6 1.4 %copy-start.3 = (f32[16,2048]{1,0:T(8,128)}, f32[16,2048]{1,0:T(8,128)S(1)}, u32[]{:S(2)}) copy-start(f32[16,2048]{1,0:T(8,128)S(1)} %fusion.zo_ref) | copy-start | bytes 393220
  56.7 1.4 %collective-permute-start.5 = (f32[16,2048]{1,0:T(8,128)S(1)}, f32[16,2048]{1,0:T(8,128)S(1)}, u32[]{:S(2)}, u32[]{:S(2)}) collective-permute-start(f32[16,2048]{1,0:T(8,128)S(1)} %fusion.zo_ref), channel_id=1, source_target_pairs={{0,1},{1,0},{2,3},{3,2},{4,5},{5,4},{6,7},{7,6},{8,9},{9,8},{10,11... | collective-permute-start | bytes 393224 | tf_op jit(solution)/shard_map/ppermute | solution.py:157
  58.1 0.7 %copy-start.4 = (f32[16,2048]{1,0:T(8,128)}, f32[16,2048]{1,0:T(8,128)S(1)}, u32[]{:S(2)}) copy-start(f32[16,2048]{1,0:T(8,128)S(1)} %collective-permute-done.5.zp_ref) | copy-start | bytes 393220

commit v10 on v9

--- a/solution.py
+++ b/solution.py
@@ -7,9 +7,11 @@
 from jax.experimental.pallas import tpu as pltpu
 from jax.sharding import PartitionSpec as P
 
+
 WIDTH = 256
 FINAL_WIDTH = 1024
 RIM = 8
+PIECES = 4
 LANES = 128
 
 
@@ -33,31 +35,57 @@
     return hi, mid, lo
 
 
-def local_kernel(taps, group_width, spans,
-                 xq, xk, xv, rq, rk, rv, wq, wk, wv, e_ref, rt_ref, et_ref,
-                 q_out, loc_out, pk_out, dec_out, info_out, ext_s, shift_s, vis_s, tail_s):
-    length, width = xq.shape
+def doc_tables(taps, e_ref, shift_ref, vis_ref, tail_ref):
+    length = vis_ref.shape[0]
+    span_r = e_ref.shape[1]
+    e_row = e_ref[0:1, :]
+    t_col = lax.broadcasted_iota(jnp.int32, (length, span_r), 0)
+    r_row = lax.broadcasted_iota(jnp.int32, (length, span_r), 1)
+    doc_col = jnp.sum(jnp.where(r_row == t_col, e_row, 0.0), axis=1, keepdims=True)
+    eq = e_row == doc_col
+    place = jnp.where(r_row < length, r_row, r_row - length - RIM)
+    for j in range(taps):
+        hit = eq & (place == t_col - j) & (r_row < length + RIM)
+        shift_ref[j * length:(j + 1) * length, :] = jnp.where(hit, 1.0, 0.0).astype(jnp.bfloat16)
+    eqf = jnp.where(eq, 1.0, 0.0)
+    causal = r_row[:, :length] <= t_col[:, :length]
+    vis_ref[...] = jnp.where(causal, eqf[:, :length], 0.0)
+    tail_ref[...] = jnp.broadcast_to(eqf[length - 1:length, :length], tail_ref.shape)
+    return eqf
+
+
+def short_conv(taps, ext_s, shift_ref, x_ref, r_ref, w_ref):
+    length = x_ref.shape[0]
+    ext_s[0:length, :] = x_ref[...]
+    ext_s[length:length + RIM, :] = r_ref[...]
+    ext = ext_s[...]
+    w = w_ref[...]
+    acc = w[0:1, :] * x_ref[...].astype(jnp.float32)
+    for j in range(1, taps):
+        window = jnp.dot(shift_ref[j * length:(j + 1) * length, :], ext, preferred_element_type=jnp.float32)
+        acc = acc + w[j:j + 1, :] * window
+    return acc
+
+
+def block_diagonal(gated, group_width):
+    length, width = gated.shape
+    lane_group = lax.broadcasted_iota(jnp.int32, (length, width), 1) // group_width
+    zero = jnp.zeros_like(gated)
+    return jnp.concatenate([jnp.where(lane_group == g, gated, zero) for g in range(width // group_width)], axis=0)
+
+
+def states_kernel(taps, group_width, spans,
+                  xk, xv, rk, rv, wk, wv, e_ref, rt_ref,
+                  g_out, pk_out, dec_out, info_out, shift_out, vis_out, ext_s, tail_s):
+    length, width = xk.shape
     groups = width // group_width
     pole_count = rt_ref.shape[1]
     channels = pk_out.shape[1] - LANES
-    span_r = e_ref.shape[1]
     step = pl.program_id(0)
 
     @pl.when(step == 0)
     def _():
-        e_row = e_ref[0:1, :]
-        t_col = lax.broadcasted_iota(jnp.int32, (length, span_r), 0)
-        r_row = lax.broadcasted_iota(jnp.int32, (length, span_r), 1)
-        doc_col = jnp.sum(jnp.where(r_row == t_col, e_row, 0.0), axis=1, keepdims=True)
-        eq = e_row == doc_col
-        place = jnp.where(r_row < length, r_row, r_row - length - RIM)
-        for j in range(taps):
-            hit = eq & (place == t_col - j) & (r_row < length + RIM)
-            shift_s[j * length:(j + 1) * length, :] = jnp.where(hit, 1.0, 0.0).astype(jnp.bfloat16)
-        eqf = jnp.where(eq, 1.0, 0.0)
-        causal = r_row[:, :length] <= t_col[:, :length]
-        vis_s[...] = jnp.where(causal, eqf[:, :length], 0.0)
-        tail_s[...] = jnp.broadcast_to(eqf[length - 1:length, :length], tail_s.shape)
+        eqf = doc_tables(taps, e_ref, shift_out, vis_out, tail_s)
         into = eqf[0:1, length + RIM - 1:length + RIM]
         flag = into * eqf[length - 1:length, 0:1]
         pk_out[:, channels:channels + LANES] = jnp.broadcast_to(flag, (pole_count, LANES))
@@ -65,50 +93,20 @@
         info_out[...] = jnp.where(lane == 0, eqf[:, 0:1], jnp.broadcast_to(into, info_out.shape))
         ext_s[...] = jnp.zeros_like(ext_s)
 
-
-    def conv(x_ref, r_ref, w_ref):
-        ext_s[0:length, :] = x_ref[...]
-        ext_s[length:length + RIM, :] = r_ref[...]
-        ext = ext_s[...]
-        w = w_ref[...]
-        acc = w[0:1, :] * x_ref[...].astype(jnp.float32)
-        for j in range(1, taps):
-            window = jnp.dot(shift_s[j * length:(j + 1) * length, :], ext, preferred_element_type=jnp.float32)
-            acc = acc + w[j:j + 1, :] * window
-        return acc
-
-    cq = conv(xq, rq, wq)
-    ck = conv(xk, rk, wk)
-    cv = conv(xv, rv, wv)
-    q_out[...] = cq
+    ck = short_conv(taps, ext_s, shift_out, xk, rk, wk)
+    cv = short_conv(taps, ext_s, shift_out, xv, rv, wv)
     gated = (ck * cv).astype(jnp.bfloat16)
-
-    lane_group = lax.broadcasted_iota(jnp.int32, (length, width), 1) // group_width
-    zero = jnp.zeros_like(gated)
-    xbd = jnp.concatenate([jnp.where(lane_group == g, gated, zero) for g in range(groups)], axis=0)
+    g_out[...] = gated
+    xbd = block_diagonal(gated, group_width)
 
     rt = rt_ref[0]
-    et = et_ref[0]
     lane = lax.broadcasted_iota(jnp.int32, (1, length), 1)
-    lags = ((length - lane) % length).astype(jnp.float32)
     to_end = (length - 1 - lane).astype(jnp.float32)
     at_tail = tail_s[0:1, :]
-    visible = vis_s[...] > 0.5
-    pieces = []
-    ends = []
-    for g in range(groups):
-        a_col = rt[:, g:g + 1]
-        r_col = et[:, g:g + 1]
-        base = jnp.sum(r_col * jnp.exp(-a_col * lags), axis=0, keepdims=True)
-        row = jnp.broadcast_to(base.astype(jnp.bfloat16), (length, length))
-        rolled = pltpu.roll(row, 0, 1, stride=1, stride_axis=0)
-        pieces.append(jnp.where(visible, rolled, jnp.zeros_like(rolled)))
-        ends.append(jnp.exp(-a_col * to_end) * at_tail)
+    ends = [jnp.exp(-rt[:, g:g + 1] * to_end) * at_tail for g in range(groups)]
     e_hi, e_lo = split2(jnp.concatenate(ends, axis=1))
-    t_hi = jnp.concatenate(pieces, axis=1)
-    res = jnp.dot(jnp.concatenate([t_hi, e_hi, e_lo], axis=0), xbd, preferred_element_type=jnp.float32)
-    loc_out[...] = res[0:length]
-    st = res[length:length + pole_count] + res[length + pole_count:length + 2 * pole_count]
+    res = jnp.dot(jnp.concatenate([e_hi, e_lo], axis=0), xbd, preferred_element_type=jnp.float32)
+    st = res[0:pole_count] + res[pole_count:2 * pole_count]
     pk_out[:, pl.ds(pl.multiple_of(step * width, width), width)] = st
 
     spread = (lax.broadcasted_iota(jnp.int32, (groups, width), 1) // group_width
@@ -119,6 +117,34 @@
         rate_cols = part if rate_cols is None else rate_cols + part
     for r, span in enumerate(spans):
         dec_out[r] = jnp.exp(-rate_cols * span)
+
+
+def toeplitz_kernel(taps, group_width, aliased, *refs):
+    if aliased:
+        xq, rq, wq, g_ref, shift_ref, vis_ref, rt_ref, et_ref, _, _, q_out, loc_out, ext_s = refs
+    else:
+        xq, rq, wq, g_ref, shift_ref, vis_ref, rt_ref, et_ref, q_out, loc_out, ext_s = refs
+    length, width = xq.shape
+    groups = width // group_width
+
+    @pl.when(pl.program_id(0) == 0)
+    def _():
+        ext_s[...] = jnp.zeros_like(ext_s)
+
+    q_out[...] = short_conv(taps, ext_s, shift_ref, xq, rq, wq)
+    xbd = block_diagonal(g_ref[...], group_width)
+    rt = rt_ref[0]
+    et = et_ref[0]
+    lane = lax.broadcasted_iota(jnp.int32, (1, length), 1)
+    lags = ((length - lane) % length).astype(jnp.float32)
+    visible = vis_ref[...] > 0.5
+    pieces = []
+    for g in range(groups):
+        base = jnp.sum(et[:, g:g + 1] * jnp.exp(-rt[:, g:g + 1] * lags), axis=0, keepdims=True)
+        row = jnp.broadcast_to(base.astype(jnp.bfloat16), (length, length))
+        rolled = pltpu.roll(row, 0, 1, stride=1, stride_axis=0)
+        pieces.append(jnp.where(visible, rolled, jnp.zeros_like(rolled)))
+    loc_out[...] = jnp.dot(jnp.concatenate(pieces, axis=1), xbd, preferred_element_type=jnp.float32)
 
 
 def final_kernel(group_width, pole_count, sub, hb, q_ref, loc_ref, zo_ref, zp_ref, pk_ref, gt_ref, pf_ref, gf_ref,
@@ -204,7 +230,7 @@
     return sorted(spans)
 
 
-def on_device(qkv, doc_ids, short_w, rates, residues):
+def device_body(qkv, doc_ids, short_w, rates, residues):
     length = qkv.shape[0]
     taps = short_w.shape[0]
     channels = qkv.shape[1] // 3
@@ -220,7 +246,6 @@
     tail_docs = jnp.broadcast_to(doc_ids[length - RIM:, None].astype(jnp.bfloat16), (RIM, LANES))
     rim = from_behind(jnp.concatenate([qkv[length - RIM:], tail_docs], axis=1), "ctx", 1)
     prev_docs = rim[:, 3 * channels].astype(jnp.int32)
-    prev_last = prev_docs[RIM - 1]
 
     span_r = 2 * LANES
     e_vec = jnp.concatenate([doc_ids, prev_docs, jnp.full((span_r - length - RIM,), -1, jnp.int32)]).astype(jnp.float32)
@@ -235,45 +260,73 @@
 
     col = lambda off: (lambda j: (0, j + off))
     fixed = lambda j: (0, 0)
-    q_part, local_part, packed, decays, info = pl.pallas_call(
-        functools.partial(local_kernel, taps, group_width, spans),
+    span_r = 2 * LANES
+    gated, packed, decays, info, shift_tbl, vis_tbl = pl.pallas_call(
+        functools.partial(states_kernel, taps, group_width, spans),
         grid=(nb,),
         in_specs=[
-            pl.BlockSpec((length, width), col(0)),
             pl.BlockSpec((length, width), col(nb)),
             pl.BlockSpec((length, width), col(2 * nb)),
-            pl.BlockSpec((RIM, width), col(0)),
             pl.BlockSpec((RIM, width), col(nb)),
             pl.BlockSpec((RIM, width), col(2 * nb)),
-            pl.BlockSpec((taps, width), col(0)),
             pl.BlockSpec((taps, width), col(nb)),
             pl.BlockSpec((taps, width), col(2 * nb)),
             pl.BlockSpec((8, span_r), fixed),
             pl.BlockSpec((1, pole_count, gpb), lambda j: (j, 0, 0)),
-            pl.BlockSpec((1, pole_count, gpb), lambda j: (j, 0, 0)),
         ],
         out_specs=[
-            pl.BlockSpec((length, width), col(0)),
             pl.BlockSpec((length, width), col(0)),
             pl.BlockSpec((pole_count, channels + LANES), fixed),
             pl.BlockSpec((rounds, pole_count, width), lambda j: (0, 0, j)),
             pl.BlockSpec((length, LANES), fixed),
+            pl.BlockSpec((taps * length, span_r), fixed),
+            pl.BlockSpec((length, length), fixed),
         ],
         out_shape=[
-            jax.ShapeDtypeStruct((length, channels), jnp.float32),
-            jax.ShapeDtypeStruct((length, channels), jnp.float32),
+            jax.ShapeDtypeStruct((length, channels), jnp.bfloat16),
             jax.ShapeDtypeStruct((pole_count, channels + LANES), jnp.float32),
             jax.ShapeDtypeStruct((rounds, pole_count, channels), jnp.float32),
             jax.ShapeDtypeStruct((length, LANES), jnp.float32),
+            jax.ShapeDtypeStruct((taps * length, span_r), jnp.bfloat16),
+            jax.ShapeDtypeStruct((length, length), jnp.float32),
         ],
-        scratch_shapes=[
-            pltpu.VMEM((span_r, width), jnp.bfloat16),
-            pltpu.VMEM((taps * length, span_r), jnp.bfloat16),
-            pltpu.VMEM((length, length), jnp.float32),
-            pltpu.VMEM((8, length), jnp.float32),
-        ],
+        scratch_shapes=[pltpu.VMEM((span_r, width), jnp.bfloat16), pltpu.VMEM((8, length), jnp.float32)],
         compiler_params=pltpu.CompilerParams(dimension_semantics=("arbitrary",)),
-    )(qkv, qkv, qkv, rim, rim, rim, short_w, short_w, short_w, e_rows, rates_t, residues_t)
+    )(qkv, qkv, rim, rim, short_w, short_w, e_rows, rates_t)
+
+    per_piece = max(nb // PIECES, 1)
+    q_part = local_part = None
+    for first in range(0, nb, per_piece):
+        count = min(per_piece, nb - first)
+        at = lambda off, first=first: (lambda j: (0, j + first + off))
+        specs = [
+            pl.BlockSpec((length, width), at(0)),
+            pl.BlockSpec((RIM, width), at(0)),
+            pl.BlockSpec((taps, width), at(0)),
+            pl.BlockSpec((length, width), at(0)),
+            pl.BlockSpec((taps * length, span_r), fixed),
+            pl.BlockSpec((length, length), fixed),
+            pl.BlockSpec((1, pole_count, gpb), lambda j, first=first: (j + first, 0, 0)),
+            pl.BlockSpec((1, pole_count, gpb), lambda j, first=first: (j + first, 0, 0)),
+        ]
+        args = [qkv, rim, short_w, gated, shift_tbl, vis_tbl, rates_t, residues_t]
+        aliased = q_part is not None
+        if aliased:
+            specs += [pl.BlockSpec(memory_space=pl.ANY)] * 2
+            args += [q_part, local_part]
+        q_part, local_part = pl.pallas_call(
+            functools.partial(toeplitz_kernel, taps, group_width, aliased),
+            grid=(count,),
+            in_specs=specs,
+            out_specs=[pl.BlockSpec((length, width), at(0)), pl.BlockSpec((length, width), at(0))],
+            out_shape=[
+                jax.ShapeDtypeStruct((length, channels), jnp.float32),
+                jax.ShapeDtypeStruct((length, channels), jnp.float32),
+            ],
+            scratch_shapes=[pltpu.VMEM((span_r, width), jnp.bfloat16)],
+            input_output_aliases={8: 0, 9: 1} if aliased else {},
+            compiler_params=pltpu.CompilerParams(dimension_semantics=("arbitrary",)),
+        )(*args)
 
     prefix, partner, got = chip_scan(packed, decays, span_of, channels, pole_count, peers, me)
     half = channels // 2
@@ -307,7 +360,7 @@
 
 def solution(mesh):
     return jax.shard_map(
-        on_device,
+        device_body,
         mesh=mesh,
         in_specs=(P(("groups", "ctx"), None), P(("groups", "ctx")), P(), P(), P()),
         out_specs=P(("groups", "ctx"), None),

time: 64.8 us -> 83 us (1.28)
  the two profiles are of different devices: /device:TPU:24 before, /device:TPU:27 now
where the time goes in v10:
time: 83 us; the launch traced here: 81.7 us
  Pallas kernels  41.3 us (50%)
  waiting for transfers between devices  18.2 us (22%)
  starting transfers between devices  12.8 us (15%)
  local copies, waits for them, and re-layouts  6.74 us (8%)
  other arithmetic  2.36 us (3%)
    pallas_call x4, Pallas kernels, device_body(): pl.pallas_call(functools.partial(toeplitz_kernel, taps, group_width, alia...  19.5 us
    ppermute x4, waiting for transfers between devices, from_behind(): return lax.ppermute(shard, axis, pairs)  18.1 us
    pallas_call x1, Pallas kernels, device_body(): pl.pallas_call(functools.partial(states_kernel, taps, group_width, spans)...  16.6 us
    ppermute x4, starting transfers between devices, from_behind(): return lax.ppermute(shard, axis, pairs)  8.54 us
    pallas_call x1, Pallas kernels, device_body(): pl.pallas_call(functools.partial(final_kernel, group_width, pole_count, w...  5.25 us
    ppermute x2, starting transfers between devices, swap_cores(): return lax.ppermute(shard, axis, [(i, i ^ 1) for i in range(peers)])  4.23 us
    another operation x6, local copies, waits for them, and re-layouts, device_body(): jnp.stack([rates, residues]).reshape(2, nb, gpb, pole_count)  1.93 us
  transfers between devices with their start and end apart: 6, of which 5 were waited for; matrix products, arithmetic and copies ran while one was open for 6% of the time, Pallas kernels for 24%

profile of v10, /device:TPU:27, one launch (start us, length us, event | category | flops | bytes accessed | tf_op | source)
XLA Modules:
  0.0 81.7 jit_solution(10639862957412789776)
XLA Ops:
  0.0 0.7 convert.4
  0.7 0.1 slice.57
  0.8 0.9 %slice.56 = bf16[8,12288]{1,0:T(8,128)(2,1)S(1)} slice(bf16[128,12288]{1,0:T(8,128)(2,1)} %refs_0_.7), slice={[120:128], [0:12288]} | slice | bytes 393216 | tf_op jit(solution)/shard_map/slice | solution.py:247
  1.8 0.1 broadcast_in_dim.36
  1.8 3.7 %collective-permute-start = (bf16[8,12416]{1,0:T(8,128)(2,1)S(1)}, bf16[8,12416]{1,0:T(8,128)(2,1)S(1)}, u32[]{:S(2)}, u32[]{:S(2)}) collective-permute-start(bf16[8,12416]{1,0:T(8,128)(2,1)S(1)} %pad_maximum_fusion), channel_id=1, source_target_pairs={{0,1},{1,2},{2,3},{3,4},{4,5},{5,6},{6,7},{7,8},{8,9},{9,10},{10,1... | collective-permute-start | bytes 595976 | tf_op jit(solution)/shard_map/ppermute | solution.py:21
  5.6 0.8 stack.19
  6.4 0.8 stack.18
  7.4 0.7 slice_bitcast_fusion
  8.1 0.1 collective-permute-done.rk.rv.refs_1_
  8.2 0.1 convert_reduce_fusion
  8.3 0.0 copy-done.7
  8.3 0.1 add_convert_fusion
  8.4 0.6 broadcast_in_dim.38.e_ref
  9.0 16.6 %shard_map.55 = (bf16[128,4096]{1,0:T(8,128)(2,1)}, f32[16,4224]{1,0:T(8,128)}, f32[4,16,4096]{2,1,0:T(8,128)}, f32[128,128]{1,0:T(8,128)}, bf16[896,256]{1,0:T(8,128)(2,1)}, /*index=5*/f32[128,128]{1,0:T(8,128)}) custom-call(bf16[128,12288]{1,0:T(8,128)(2,1)} %refs_0_.7, bf16[128,12288]{1,0:T(8,128)(2,1)} %refs_0_.7, bf16[8,12416]{1,0:T(8,128)(2,1)} %copy-done, ...), custom_call_target="tpu_custom_call" | custom-call | tf_op jit(solution)/shard_map/pallas_call | solution.py:264
  25.6 2.3 %collective-permute-start.1 = (f32[16,4224]{1,0:T(8,128)}, f32[16,4224]{1,0:T(8,128)S(1)}, u32[]{:S(2)}, u32[]{:S(2)}) collective-permute-start(f32[16,4224]{1,0:T(8,128)} %get-tuple-element.30.pk_ref.pf_ref), channel_id=1, source_target_pairs={{0,1},{1,0},{2,3},{3,2},{4,5},{5,4},{6,7},{7,6},{8,9},{9,8},{10,11... | collective-permute-start | bytes 811016 | tf_op jit(solution)/shard_map/ppermute | solution.py:183
  27.9 1.3 %fusion.12 = (f32[1,16,4096]{2,1,0:T(8,128)S(1)}, f32[1,16,4096]{2,1,0:T(8,128)S(1)}, f32[1,16,4096]{2,1,0:T(8,128)S(1)}, f32[1,16,4096]{2,1,0:T(8,128)S(1)}) fusion(f32[4,16,4096]{2,1,0:T(8,128)} %get-tuple-element.31.d1_ref), kind=kLoop, calls=%fused_computation.34 | loop fusion | bytes 2097152 | tf_op jit(solution)/shard_map/slice | solution.py:211
  29.2 0.0 copy-start.5
  29.2 0.0 copy-start.6
  29.3 0.1 collective-permute-done.1.gt_ref.gf_ref
  29.4 0.1 fusion.11
  29.5 0.1 fusion.8
  29.6 0.1 broadcast_in_dim.40
  29.7 2.2 %collective-permute-start.2 = (f32[16,2176]{1,0:T(8,128)S(1)}, f32[16,2176]{1,0:T(8,128)S(1)}, u32[]{:S(2)}, u32[]{:S(2)}) collective-permute-start(f32[16,2176]{1,0:T(8,128)S(1)} %pad_maximum_fusion.1), channel_id=1, source_target_pairs={{0,2},{1,3},{2,4},{3,5},{4,6},{5,7},{6,8},{7,9},{8,10},{9,11},{10,... | collective-permute-start | bytes 417800 | tf_op jit(solution)/shard_map/ppermute | solution.py:21
  31.9 5.4 %collective-permute-done.2 = f32[16,2176]{1,0:T(8,128)S(1)} collective-permute-done((f32[16,2176]{1,0:T(8,128)S(1)}, f32[16,2176]{1,0:T(8,128)S(1)}, u32[]{:S(2)}, u32[]{:S(2)}) %collective-permute-start.2) | collective-permute-done | bytes 139296 | tf_op jit(solution)/shard_map/ppermute | solution.py:21
  37.3 0.1 slice_reduce_fusion
  37.4 0.1 fusion.6
  37.5 0.1 broadcast_in_dim.42
  37.6 1.3 %collective-permute-start.3 = (f32[16,2176]{1,0:T(8,128)S(1)}, f32[16,2176]{1,0:T(8,128)S(1)}, u32[]{:S(2)}, u32[]{:S(2)}) collective-permute-start(f32[16,2176]{1,0:T(8,128)S(1)} %pad_maximum_fusion.2), channel_id=1, source_target_pairs={{0,4},{1,5},{2,6},{3,7},{4,8},{5,9},{6,10},{7,11},{8,12},{9,13},{1... | collective-permute-start | bytes 417800 | tf_op jit(solution)/shard_map/ppermute | solution.py:21
  38.9 4.5 %collective-permute-done.3 = f32[16,2176]{1,0:T(8,128)S(1)} collective-permute-done((f32[16,2176]{1,0:T(8,128)S(1)}, f32[16,2176]{1,0:T(8,128)S(1)}, u32[]{:S(2)}, u32[]{:S(2)}) %collective-permute-start.3) | collective-permute-done | bytes 139296 | tf_op jit(solution)/shard_map/ppermute | solution.py:21
  43.4 0.1 multiply_reduce_fusion.1
  43.5 0.1 fusion.2
  43.6 0.1 broadcast_in_dim.44
  43.7 1.3 %collective-permute-start.4 = (f32[16,2176]{1,0:T(8,128)S(1)}, f32[16,2176]{1,0:T(8,128)S(1)}, u32[]{:S(2)}, u32[]{:S(2)}) collective-permute-start(f32[16,2176]{1,0:T(8,128)S(1)} %pad_maximum_fusion.3), channel_id=1, source_target_pairs={{0,8},{1,9},{2,10},{3,11},{4,12},{5,13},{6,14},{7,15},{16,24},{17,... | collective-permute-start | bytes 417800 | tf_op jit(solution)/shard_map/ppermute | solution.py:21
  45.0 0.1 copy.17
  45.1 0.1 copy.16
  45.2 0.1 stack.22
  45.3 0.1 stack.21
  45.5 8.2 %collective-permute-done.4 = f32[16,2176]{1,0:T(8,128)S(1)} collective-permute-done((f32[16,2176]{1,0:T(8,128)S(1)}, f32[16,2176]{1,0:T(8,128)S(1)}, u32[]{:S(2)}, u32[]{:S(2)}) %collective-permute-start.4) | collective-permute-done | bytes 139296 | tf_op jit(solution)/shard_map/ppermute | solution.py:21
  53.6 0.1 fusion.zo_ref
  53.7 1.9 %collective-permute-start.5 = (f32[16,2048]{1,0:T(8,128)S(1)}, f32[16,2048]{1,0:T(8,128)S(1)}, u32[]{:S(2)}, u32[]{:S(2)}) collective-permute-start(f32[16,2048]{1,0:T(8,128)S(1)} %fusion.zo_ref), channel_id=1, source_target_pairs={{0,1},{1,0},{2,3},{3,2},{4,5},{5,4},{6,7},{7,6},{8,9},{9,8},{10,11... | collective-permute-start | bytes 393224 | tf_op jit(solution)/shard_map/ppermute | solution.py:183
  55.6 0.6 pad_maximum_fusion.4.rr_ref
  56.3 4.8 %shard_map.56 = (f32[128,4096]{1,0:T(8,128)}, f32[128,4096]{1,0:T(8,128)}) custom-call(bf16[128,12288]{1,0:T(8,128)(2,1)} %refs_0_.7, bf16[8,12416]{1,0:T(8,128)(2,1)} %copy-done, f32[7,12288]{1,0:T(8,128)} %refs_2_.7, bf16[128,4096]{1,0:T(8,128)(2,1)} %get-tuple-element.19.refs_3_, bf16[896,256]{1,0:T(8,128)(2,1)} %get-tuple-element.20.refs_4_, ...), custom_call_target="tpu_custom_call" | custom-call | tf_op jit(solution)/shard_map/pallas_call | solution.py:317
  61.1 4.9 %shard_map.57 = (f32[128,4096]{1,0:T(8,128)}, f32[128,4096]{1,0:T(8,128)}) custom-call(bf16[128,12288]{1,0:T(8,128)(2,1)} %refs_0_.7, bf16[8,12416]{1,0:T(8,128)(2,1)} %copy-done, f32[7,12288]{1,0:T(8,128)} %refs_2_.7, bf16[128,4096]{1,0:T(8,128)(2,1)} %get-tuple-element.19.refs_3_, ...), custom_call_target="tpu_custom_call", output_to_operand_aliasing={{0}: (8, {}), {1}: (9, {})} | custom-call | tf_op jit(solution)/shard_map/pallas_call | solution.py:317
  66.0 4.9 %shard_map.58 = (f32[128,4096]{1,0:T(8,128)}, f32[128,4096]{1,0:T(8,128)}) custom-call(bf16[128,12288]{1,0:T(8,128)(2,1)} %refs_0_.7, bf16[8,12416]{1,0:T(8,128)(2,1)} %copy-done, f32[7,12288]{1,0:T(8,128)} %refs_2_.7, bf16[128,4096]{1,0:T(8,128)(2,1)} %get-tuple-element.19.refs_3_, ...), custom_call_target="tpu_custom_call", output_to_operand_aliasing={{0}: (8, {}), {1}: (9, {})} | custom-call | tf_op jit(solution)/shard_map/pallas_call | solution.py:317
  70.9 4.9 %shard_map.59 = (f32[128,4096]{1,0:T(8,128)}, f32[128,4096]{1,0:T(8,128)}) custom-call(bf16[128,12288]{1,0:T(8,128)(2,1)} %refs_0_.7, bf16[8,12416]{1,0:T(8,128)(2,1)} %copy-done, f32[7,12288]{1,0:T(8,128)} %refs_2_.7, bf16[128,4096]{1,0:T(8,128)(2,1)} %get-tuple-element.19.refs_3_, ...), custom_call_target="tpu_custom_call", output_to_operand_aliasing={{0}: (8, {}), {1}: (9, {})} | custom-call | tf_op jit(solution)/shard_map/pallas_call | solution.py:317
  75.8 0.0 collective-permute-done.5.zp_ref
  75.8 0.6 copy-done.4
  76.4 5.2 %shard_map.60 = bf16[128,4096]{1,0:T(8,128)(2,1)} custom-call(f32[128,4096]{1,0:T(8,128)} %get-tuple-element.28.q_ref, f32[128,4096]{1,0:T(8,128)} %get-tuple-element.29.loc_ref, f32[16,2048]{1,0:T(8,128)} %copy-done.3, f32[16,2048]{1,0:T(8,128)} %copy-done.4, f32[16,4224]{1,0:T(8,128)} %get-tuple-element.30.pk_ref.pf_ref, f32[16,4224]{1,0:T(8,128)} %copy-done.2, ...), custom_call_target="tpu_custom_call" | custom-call | tf_op jit(solution)/shard_map/pallas_call | solution.py:339
  (22 shorter events, 0.2 us)
Async XLA Ops:
  0.0 8.3 %copy-start.7 = (s32[128]{0:T(128)S(1)}, s32[128]{0:T(128)}, u32[]{:S(2)}) copy-start(s32[128]{0:T(128)} %param.6) | copy-start | bytes 1540
  1.8 6.3 %collective-permute-start = (bf16[8,12416]{1,0:T(8,128)(2,1)S(1)}, bf16[8,12416]{1,0:T(8,128)(2,1)S(1)}, u32[]{:S(2)}, u32[]{:S(2)}) collective-permute-start(bf16[8,12416]{1,0:T(8,128)(2,1)S(1)} %pad_maximum_fusion), channel_id=1, source_target_pairs={{0,1},{1,2},{2,3},{3,4},{4,5},{5,6},{6,7},{7,8},{8,9},{9,10},{10,1... | collective-permute-start | bytes 595976 | tf_op jit(solution)/shard_map/ppermute | solution.py:21
  8.2 0.8 copy-start
  25.6 3.6 %copy-start.1 = (f32[16,4224]{1,0:T(8,128)S(1)}, f32[16,4224]{1,0:T(8,128)}, u32[]{:S(2)}) copy-start(f32[16,4224]{1,0:T(8,128)} %get-tuple-element.30.pk_ref.pf_ref) | copy-start | bytes 811012
  25.6 3.7 %collective-permute-start.1 = (f32[16,4224]{1,0:T(8,128)}, f32[16,4224]{1,0:T(8,128)S(1)}, u32[]{:S(2)}, u32[]{:S(2)}) collective-permute-start(f32[16,4224]{1,0:T(8,128)} %get-tuple-element.30.pk_ref.pf_ref), channel_id=1, source_target_pairs={{0,1},{1,0},{2,3},{3,2},{4,5},{5,4},{6,7},{7,6},{8,9},{9,8},{10,11... | collective-permute-start | bytes 811016 | tf_op jit(solution)/shard_map/ppermute | solution.py:183
  29.2 15.8 %copy-start.5 = (f32[256,16]{0,1:T(8,128)S(1)}, f32[256,16]{0,1:T(8,128)}, u32[]{:S(2)}) copy-start(f32[256,16]{0,1:T(8,128)} %param.9) | copy-start | bytes 49156
  29.2 15.9 %copy-start.6 = (f32[256,16]{0,1:T(8,128)S(1)}, f32[256,16]{0,1:T(8,128)}, u32[]{:S(2)}) copy-start(f32[256,16]{0,1:T(8,128)} %param.8) | copy-start | bytes 49156
  29.3 24.4 %copy-start.2 = (f32[16,4224]{1,0:T(8,128)}, f32[16,4224]{1,0:T(8,128)S(1)}, u32[]{:S(2)}) copy-start(f32[16,4224]{1,0:T(8,128)S(1)} %collective-permute-done.1.gt_ref.gf_ref) | copy-start | bytes 811012
  29.7 7.7 %collective-permute-start.2 = (f32[16,2176]{1,0:T(8,128)S(1)}, f32[16,2176]{1,0:T(8,128)S(1)}, u32[]{:S(2)}, u32[]{:S(2)}) collective-permute-start(f32[16,2176]{1,0:T(8,128)S(1)} %pad_maximum_fusion.1), channel_id=1, source_target_pairs={{0,2},{1,3},{2,4},{3,5},{4,6},{5,7},{6,8},{7,9},{8,10},{9,11},{10,... | collective-permute-start | bytes 417800 | tf_op jit(solution)/shard_map/ppermute | solution.py:21
  37.6 5.8 %collective-permute-start.3 = (f32[16,2176]{1,0:T(8,128)S(1)}, f32[16,2176]{1,0:T(8,128)S(1)}, u32[]{:S(2)}, u32[]{:S(2)}) collective-permute-start(f32[16,2176]{1,0:T(8,128)S(1)} %pad_maximum_fusion.2), channel_id=1, source_target_pairs={{0,4},{1,5},{2,6},{3,7},{4,8},{5,9},{6,10},{7,11},{8,12},{9,13},{1... | collective-permute-start | bytes 417800 | tf_op jit(solution)/shard_map/ppermute | solution.py:21
  43.7 9.9 %collective-permute-start.4 = (f32[16,2176]{1,0:T(8,128)S(1)}, f32[16,2176]{1,0:T(8,128)S(1)}, u32[]{:S(2)}, u32[]{:S(2)}) collective-permute-start(f32[16,2176]{1,0:T(8,128)S(1)} %pad_maximum_fusion.3), channel_id=1, source_target_pairs={{0,8},{1,9},{2,10},{3,11},{4,12},{5,13},{6,14},{7,15},{16,24},{17,... | collective-permute-start | bytes 417800 | tf_op jit(solution)/shard_map/ppermute | solution.py:21
  53.7 7.4 %copy-start.3 = (f32[16,2048]{1,0:T(8,128)}, f32[16,2048]{1,0:T(8,128)S(1)}, u32[]{:S(2)}) copy-start(f32[16,2048]{1,0:T(8,128)S(1)} %fusion.zo_ref) | copy-start | bytes 393220
  53.7 22.0 %collective-permute-start.5 = (f32[16,2048]{1,0:T(8,128)S(1)}, f32[16,2048]{1,0:T(8,128)S(1)}, u32[]{:S(2)}, u32[]{:S(2)}) collective-permute-start(f32[16,2048]{1,0:T(8,128)S(1)} %fusion.zo_ref), channel_id=1, source_target_pairs={{0,1},{1,0},{2,3},{3,2},{4,5},{5,4},{6,7},{7,6},{8,9},{9,8},{10,11... | collective-permute-start | bytes 393224 | tf_op jit(solution)/shard_map/ppermute | solution.py:183
  75.8 0.7 copy-start.4

commit v11 on v9

--- a/solution.py
+++ b/solution.py
@@ -33,19 +33,43 @@
     return hi, mid, lo
 
 
+def exact_transpose(x):
+    n = x.shape[1]
+    eye = (lax.broadcasted_iota(jnp.int32, (n, n), 0) == lax.broadcasted_iota(jnp.int32, (n, n), 1))
+    eye = eye.astype(jnp.bfloat16)
+    out = None
+    for piece in split3(x):
+        part = lax.dot_general(eye, piece, (((1,), (1,)), ((), ())), preferred_element_type=jnp.float32)
+        out = part if out is None else out + part
+    return out
+
+
+def exact_spread(x, spread):
+    out = None
+    for piece in split3(x):
+        part = jnp.dot(piece, spread, preferred_element_type=jnp.float32)
+        out = part if out is None else out + part
+    return out
+
+
 def local_kernel(taps, group_width, spans,
-                 xq, xk, xv, rq, rk, rv, wq, wk, wv, e_ref, rt_ref, et_ref,
-                 q_out, loc_out, pk_out, dec_out, info_out, ext_s, shift_s, vis_s, tail_s):
+                 xq, xk, xv, rq, rk, rv, wq, wk, wv, doc_ref, rimdoc_ref, ra_ref, re_ref,
+                 q_out, loc_out, pk_out, dec_out, info_out, rr_out, ext_s, shift_s, vis_s, tail_s):
     length, width = xq.shape
     groups = width // group_width
-    pole_count = rt_ref.shape[1]
+    pole_count = ra_ref.shape[1]
     channels = pk_out.shape[1] - LANES
-    span_r = e_ref.shape[1]
+    span_r = 2 * LANES
     step = pl.program_id(0)
 
     @pl.when(step == 0)
     def _():
-        e_row = e_ref[0:1, :]
+        rim_docs = rimdoc_ref[...].astype(jnp.float32)
+        diag = (lax.broadcasted_iota(jnp.int32, rim_docs.shape, 0)
+                == lax.broadcasted_iota(jnp.int32, rim_docs.shape, 1))
+        prev_row = jnp.sum(jnp.where(diag, rim_docs, 0.0), axis=0, keepdims=True)
+        lane8 = lax.broadcasted_iota(jnp.int32, prev_row.shape, 1)
+        e_row = jnp.concatenate([doc_ref[...].astype(jnp.float32), jnp.where(lane8 < RIM, prev_row, -1.0)], axis=1)
         t_col = lax.broadcasted_iota(jnp.int32, (length, span_r), 0)
         r_row = lax.broadcasted_iota(jnp.int32, (length, span_r), 1)
         doc_col = jnp.sum(jnp.where(r_row == t_col, e_row, 0.0), axis=1, keepdims=True)
@@ -87,8 +111,8 @@
     zero = jnp.zeros_like(gated)
     xbd = jnp.concatenate([jnp.where(lane_group == g, gated, zero) for g in range(groups)], axis=0)
 
-    rt = rt_ref[0]
-    et = et_ref[0]
+    rt = exact_transpose(ra_ref[...])
+    et = exact_transpose(re_ref[...])
     lane = lax.broadcasted_iota(jnp.int32, (1, length), 1)
     lags = ((length - lane) % length).astype(jnp.float32)
     to_end = (length - 1 - lane).astype(jnp.float32)
@@ -113,12 +137,17 @@
 
     spread = (lax.broadcasted_iota(jnp.int32, (groups, width), 1) // group_width
               == lax.broadcasted_iota(jnp.int32, (groups, width), 0)).astype(jnp.bfloat16)
-    rate_cols = None
-    for piece in split3(rt):
-        part = jnp.dot(piece, spread, preferred_element_type=jnp.float32)
-        rate_cols = part if rate_cols is None else rate_cols + part
+    rate_cols = exact_spread(rt, spread)
     for r, span in enumerate(spans):
         dec_out[r] = jnp.exp(-rate_cols * span)
+    flat = groups * pole_count
+    to_pairs = (lax.broadcasted_iota(jnp.int32, (groups, flat), 1) // pole_count
+                == lax.broadcasted_iota(jnp.int32, (groups, flat), 0)).astype(jnp.bfloat16)
+    pick = (lax.broadcasted_iota(jnp.int32, (pole_count, flat), 0)
+            == lax.broadcasted_iota(jnp.int32, (pole_count, flat), 1) % pole_count)
+    for plane, table in enumerate((rt, et)):
+        row = jnp.sum(jnp.where(pick, exact_spread(table, to_pairs), 0.0), axis=0, keepdims=True)
+        rr_out[plane] = jnp.broadcast_to(row, (8, flat))
 
 
 def final_kernel(group_width, pole_count, sub, hb, q_ref, loc_ref, zo_ref, zp_ref, pk_ref, gt_ref, pf_ref, gf_ref,
@@ -134,7 +163,7 @@
     joined = jnp.where(odd, (even_f * d1_ref[0]) * full + even_s, full)
     b_all = joined * info_ref[0:1, 1:2]
     tcol = (lax.broadcasted_iota(jnp.int32, (length, 1), 0) + 1).astype(jnp.float32)
-    iw = rr_ref[1] * jnp.exp(-rr_ref[0] * tcol) * info_ref[:, 0:1]
+    iw = rr_ref[1, 0:1, :] * jnp.exp(-rr_ref[0, 0:1, :] * tcol) * info_ref[:, 0:1]
     iw_hi, iw_lo = split2(iw)
     shape = (groups * pole_count, sub)
     row_group = lax.broadcasted_iota(jnp.int32, shape, 0) // pole_count
@@ -219,15 +248,8 @@
 
     tail_docs = jnp.broadcast_to(doc_ids[length - RIM:, None].astype(jnp.bfloat16), (RIM, LANES))
     rim = from_behind(jnp.concatenate([qkv[length - RIM:], tail_docs], axis=1), "ctx", 1)
-    prev_docs = rim[:, 3 * channels].astype(jnp.int32)
-    prev_last = prev_docs[RIM - 1]
-
     span_r = 2 * LANES
-    e_vec = jnp.concatenate([doc_ids, prev_docs, jnp.full((span_r - length - RIM,), -1, jnp.int32)]).astype(jnp.float32)
-    e_rows = jnp.broadcast_to(e_vec[None, :], (8, span_r))
-
-    both_t = jnp.stack([rates, residues]).reshape(2, nb, gpb, pole_count).transpose(0, 1, 3, 2)
-    rates_t, residues_t = both_t[0], both_t[1]
+
     span_list = scan_spans(peers)
     span_of = {v: i for i, v in enumerate(span_list)}
     rounds = len(span_list)
@@ -235,7 +257,7 @@
 
     col = lambda off: (lambda j: (0, j + off))
     fixed = lambda j: (0, 0)
-    q_part, local_part, packed, decays, info = pl.pallas_call(
+    q_part, local_part, packed, decays, info, rate_rows = pl.pallas_call(
         functools.partial(local_kernel, taps, group_width, spans),
         grid=(nb,),
         in_specs=[
@@ -248,9 +270,10 @@
             pl.BlockSpec((taps, width), col(0)),
             pl.BlockSpec((taps, width), col(nb)),
             pl.BlockSpec((taps, width), col(2 * nb)),
-            pl.BlockSpec((8, span_r), fixed),
-            pl.BlockSpec((1, pole_count, gpb), lambda j: (j, 0, 0)),
-            pl.BlockSpec((1, pole_count, gpb), lambda j: (j, 0, 0)),
+            pl.BlockSpec((1, length), fixed),
+            pl.BlockSpec((RIM, LANES), lambda j: (0, 3 * channels // LANES)),
+            pl.BlockSpec((gpb, pole_count), lambda j: (j, 0)),
+            pl.BlockSpec((gpb, pole_count), lambda j: (j, 0)),
         ],
         out_specs=[
             pl.BlockSpec((length, width), col(0)),
@@ -258,6 +281,7 @@
             pl.BlockSpec((pole_count, channels + LANES), fixed),
             pl.BlockSpec((rounds, pole_count, width), lambda j: (0, 0, j)),
             pl.BlockSpec((length, LANES), fixed),
+            pl.BlockSpec((2, 8, gpb * pole_count), lambda j: (0, 0, j)),
         ],
         out_shape=[
             jax.ShapeDtypeStruct((length, channels), jnp.float32),
@@ -265,6 +289,7 @@
             jax.ShapeDtypeStruct((pole_count, channels + LANES), jnp.float32),
             jax.ShapeDtypeStruct((rounds, pole_count, channels), jnp.float32),
             jax.ShapeDtypeStruct((length, LANES), jnp.float32),
+            jax.ShapeDtypeStruct((2, 8, filters * pole_count), jnp.float32),
         ],
         scratch_shapes=[
             pltpu.VMEM((span_r, width), jnp.bfloat16),
@@ -273,13 +298,12 @@
             pltpu.VMEM((8, length), jnp.float32),
         ],
         compiler_params=pltpu.CompilerParams(dimension_semantics=("arbitrary",)),
-    )(qkv, qkv, qkv, rim, rim, rim, short_w, short_w, short_w, e_rows, rates_t, residues_t)
+    )(qkv, qkv, qkv, rim, rim, rim, short_w, short_w, short_w, doc_ids.reshape(1, length), rim, rates, residues)
 
     prefix, partner, got = chip_scan(packed, decays, span_of, channels, pole_count, peers, me)
     half = channels // 2
     hb = max(half // final_width, 1)
     flag_block = channels // LANES
-    rate_rows = jnp.stack([rates, residues]).reshape(2, 1, filters * pole_count)
 
     nbf = channels // final_width
     iw_width = final_width // group_width * pole_count
@@ -296,7 +320,7 @@
             pl.BlockSpec((pole_count, LANES), lambda j: (0, flag_block)),
             pl.BlockSpec((pole_count, LANES), lambda j: (0, flag_block)),
             pl.BlockSpec((1, pole_count, final_width), lambda j: (span_of[1], 0, j)),
-            pl.BlockSpec((2, 1, iw_width), lambda j: (0, 0, j)),
+            pl.BlockSpec((2, 8, iw_width), lambda j: (0, 0, j)),
             pl.BlockSpec((length, LANES), fixed),
         ],
         out_specs=pl.BlockSpec((length, final_width), col(0)),

time: 64.8 us -> 66.8 us (1.031)
  Pallas kernels: 23.7 us -> 25.9 us
  other arithmetic: 2.28 us -> 1.44 us
  waiting for transfers between devices: 23.8 us -> 24.5 us
    unnamed x18 -> x12, local copies, waits for them, and re-layouts: 0.88 us -> 4.3 us
    pallas_call x1, Pallas kernels: 18.4 us -> 20.6 us  [on_device(): pl.pallas_call(functools.partial(local_kernel, taps, group_width, spans),...]
    another operation x6 -> x0, local copies, waits for them, and re-layouts: 1.93 us -> none  [on_device(): jnp.stack([rates, residues]).reshape(2, nb, gpb, pole_count)]
    squeeze x1 -> x0, local copies, waits for them, and re-layouts: 0.74 us -> none  [on_device(): rates_t, residues_t = (both_t[0], both_t[1])]
  transfers between devices with their start and end apart: 6 -> 6, of which waited for: 6 -> 6; matrix products, arithmetic and copies ran while one was open for 8% -> 6% of each run, Pallas kernels for 0% -> 0%
where the time goes in v11:
time: 66.8 us; the launch traced here: 66 us
  Pallas kernels  25.9 us (39%)
  waiting for transfers between devices  24.5 us (37%)
  starting transfers between devices  7.18 us (11%)
  local copies, waits for them, and re-layouts  6.9 us (10%)
  other arithmetic  1.44 us (2%)
    ppermute x4, waiting for transfers between devices, from_behind(): return lax.ppermute(shard, axis, pairs)  22.7 us
    pallas_call x1, Pallas kernels, on_device(): pl.pallas_call(functools.partial(local_kernel, taps, group_width, spans),...  20.6 us
    ppermute x4, starting transfers between devices, from_behind(): return lax.ppermute(shard, axis, pairs)  7.04 us
    pallas_call x1, Pallas kernels, on_device(): pl.pallas_call(functools.partial(final_kernel, group_width, pole_count, w...  5.3 us
    unnamed x12, local copies, waits for them, and re-layouts  4.3 us
    ppermute x2, waiting for transfers between devices, swap_cores(): return lax.ppermute(shard, axis, [(i, i ^ 1) for i in range(peers)])  1.77 us
  transfers between devices with their start and end apart: 6, of which 6 were waited for; matrix products, arithmetic and copies ran while one was open for 6% of the time, Pallas kernels for 0%

profile of v11, /device:TPU:24, one launch (start us, length us, event | category | flops | bytes accessed | tf_op | source)
XLA Modules:
  0.0 66.0 jit_solution(10909145785340173387)
XLA Ops:
  0.0 0.9 %slice.47 = bf16[8,12288]{1,0:T(8,128)(2,1)S(1)} slice(bf16[128,12288]{1,0:T(8,128)(2,1)} %xv.1), slice={[120:128], [0:12288]} | slice | bytes 393216 | tf_op jit(solution)/shard_map/slice | solution.py:250
  0.9 0.7 %convert.3 = bf16[128]{0:T(256)(128)(2,1)S(1)} convert(s32[128]{0:T(128)} %param.6) | non-fusion elementwise | flops 128 | bytes 768 | tf_op jit(solution)/shard_map/convert
  1.6 0.1 slice.48
  1.7 0.1 broadcast_in_dim.27
  1.8 1.9 %collective-permute-start = (bf16[8,12416]{1,0:T(8,128)(2,1)S(1)}, bf16[8,12416]{1,0:T(8,128)(2,1)S(1)}, u32[]{:S(2)}, u32[]{:S(2)}) collective-permute-start(bf16[8,12416]{1,0:T(8,128)(2,1)S(1)} %pad_maximum_fusion), channel_id=1, source_target_pairs={{0,1},{1,2},{2,3},{3,4},{4,5},{5,6},{6,7},{7,8},{8,9},{9,10},{10,1... | collective-permute-start | bytes 595976 | tf_op jit(solution)/shard_map/ppermute | solution.py:19
  3.7 1.5 %copy.8.ra_ref = f32[256,16]{1,0:T(8,128)} copy(f32[256,16]{0,1:T(8,128)} %param.8) | data formatting | bytes 32768 | tf_op args[3]
  5.2 1.5 %copy.9.re_ref = f32[256,16]{1,0:T(8,128)} copy(f32[256,16]{0,1:T(8,128)} %param.9) | data formatting | bytes 32768 | tf_op args[4]
  6.7 3.0 %collective-permute-done.rq.rk.rv.rimdoc_ref = bf16[8,12416]{1,0:T(8,128)(2,1)S(1)} collective-permute-done((bf16[8,12416]{1,0:T(8,128)(2,1)S(1)}, bf16[8,12416]{1,0:T(8,128)(2,1)S(1)}, u32[]{:S(2)}, u32[]{:S(2)}) %collective-permute-start) | collective-permute-done | bytes 198688 | tf_op jit(solution)/shard_map/ppermute | solution.py:19
  9.7 0.0 copy-start
  9.7 0.7 %copy-done = bf16[8,12416]{1,0:T(8,128)(2,1)} copy-done((bf16[8,12416]{1,0:T(8,128)(2,1)}, bf16[8,12416]{1,0:T(8,128)(2,1)S(1)}, u32[]{:S(2)}) %copy-start) | copy-done | bytes 198680
  10.4 20.6 %shard_map.55 = (f32[128,4096]{1,0:T(8,128)}, f32[128,4096]{1,0:T(8,128)}, f32[16,4224]{1,0:T(8,128)}, f32[4,16,4096]{2,1,0:T(8,128)}, f32[128,128]{1,0:T(8,128)}, /*index=5*/f32[2,8,4096]{2,1,0:T(8,128)}) custom-call(bf16[128,12288]{1,0:T(8,128)(2,1)} %xv.1, bf16[128,12288]{1,0:T(8,128)(2,1)} %xv.1, bf16[128,12288]{1,0:T(8,128)(2,1)} %xv.1, ...), custom_call_target="tpu_custom_call" | custom-call | tf_op jit(solution)/shard_map/pallas_call | solution.py:260
  30.9 0.0 copy-start.1
  31.0 0.1 collective-permute-start.1
  31.0 1.3 %fusion.12 = (f32[1,16,4096]{2,1,0:T(8,128)S(1)}, f32[1,16,4096]{2,1,0:T(8,128)S(1)}, f32[1,16,4096]{2,1,0:T(8,128)S(1)}, f32[1,16,4096]{2,1,0:T(8,128)S(1)}) fusion(f32[4,16,4096]{2,1,0:T(8,128)} %get-tuple-element.14.d1_ref), kind=kLoop, calls=%fused_computation.28 | loop fusion | bytes 2097152 | tf_op jit(solution)/shard_map/slice | solution.py:214
  32.3 0.0 copy-done.1
  32.3 0.4 collective-permute-done.1.gt_ref.gf_ref
  32.8 0.0 copy-start.2
  32.8 0.1 fusion.11
  32.9 0.1 fusion.8
  33.0 0.1 broadcast_in_dim.29
  33.1 2.5 %collective-permute-start.2 = (f32[16,2176]{1,0:T(8,128)S(1)}, f32[16,2176]{1,0:T(8,128)S(1)}, u32[]{:S(2)}, u32[]{:S(2)}) collective-permute-start(f32[16,2176]{1,0:T(8,128)S(1)} %pad_maximum_fusion.1), channel_id=1, source_target_pairs={{0,2},{1,3},{2,4},{3,5},{4,6},{5,7},{6,8},{7,9},{8,10},{9,11},{10,... | collective-permute-start | bytes 417800 | tf_op jit(solution)/shard_map/ppermute | solution.py:19
  35.6 6.0 %collective-permute-done.2 = f32[16,2176]{1,0:T(8,128)S(1)} collective-permute-done((f32[16,2176]{1,0:T(8,128)S(1)}, f32[16,2176]{1,0:T(8,128)S(1)}, u32[]{:S(2)}, u32[]{:S(2)}) %collective-permute-start.2) | collective-permute-done | bytes 139296 | tf_op jit(solution)/shard_map/ppermute | solution.py:19
  41.6 0.1 fusion.6
  41.7 0.1 slice_reduce_fusion
  41.8 0.1 broadcast_in_dim.31
  41.9 1.3 %collective-permute-start.3 = (f32[16,2176]{1,0:T(8,128)S(1)}, f32[16,2176]{1,0:T(8,128)S(1)}, u32[]{:S(2)}, u32[]{:S(2)}) collective-permute-start(f32[16,2176]{1,0:T(8,128)S(1)} %pad_maximum_fusion.2), channel_id=1, source_target_pairs={{0,4},{1,5},{2,6},{3,7},{4,8},{5,9},{6,10},{7,11},{8,12},{9,13},{1... | collective-permute-start | bytes 417800 | tf_op jit(solution)/shard_map/ppermute | solution.py:19
  43.2 5.6 %collective-permute-done.3 = f32[16,2176]{1,0:T(8,128)S(1)} collective-permute-done((f32[16,2176]{1,0:T(8,128)S(1)}, f32[16,2176]{1,0:T(8,128)S(1)}, u32[]{:S(2)}, u32[]{:S(2)}) %collective-permute-start.3) | collective-permute-done | bytes 139296 | tf_op jit(solution)/shard_map/ppermute | solution.py:19
  48.9 0.1 multiply_reduce_fusion.1
  49.0 0.1 fusion.2
  49.1 0.1 broadcast_in_dim.33
  49.2 1.3 %collective-permute-start.4 = (f32[16,2176]{1,0:T(8,128)S(1)}, f32[16,2176]{1,0:T(8,128)S(1)}, u32[]{:S(2)}, u32[]{:S(2)}) collective-permute-start(f32[16,2176]{1,0:T(8,128)S(1)} %pad_maximum_fusion.3), channel_id=1, source_target_pairs={{0,8},{1,9},{2,10},{3,11},{4,12},{5,13},{6,14},{7,15},{16,24},{17,... | collective-permute-start | bytes 417800 | tf_op jit(solution)/shard_map/ppermute | solution.py:19
  50.5 8.1 %collective-permute-done.4 = f32[16,2176]{1,0:T(8,128)S(1)} collective-permute-done((f32[16,2176]{1,0:T(8,128)S(1)}, f32[16,2176]{1,0:T(8,128)S(1)}, u32[]{:S(2)}, u32[]{:S(2)}) %collective-permute-start.4) | collective-permute-done | bytes 139296 | tf_op jit(solution)/shard_map/ppermute | solution.py:19
  58.5 0.1 fusion.zo_ref
  58.7 0.0 copy-start.3
  58.7 0.1 collective-permute-start.5
  58.7 1.3 %collective-permute-done.5.zp_ref = f32[16,2048]{1,0:T(8,128)S(1)} collective-permute-done((f32[16,2048]{1,0:T(8,128)S(1)}, f32[16,2048]{1,0:T(8,128)S(1)}, u32[]{:S(2)}, u32[]{:S(2)}) %collective-permute-start.5) | collective-permute-done | bytes 131104 | tf_op jit(solution)/shard_map/ppermute | solution.py:186
  60.1 0.0 copy-start.4
  60.1 0.0 copy-done.2
  60.1 0.0 copy-done.3
  60.1 0.6 copy-done.4
  60.7 5.3 %shard_map.56 = bf16[128,4096]{1,0:T(8,128)(2,1)} custom-call(f32[128,4096]{1,0:T(8,128)} %get-tuple-element.11.q_ref, f32[128,4096]{1,0:T(8,128)} %get-tuple-element.12.loc_ref, f32[16,2048]{1,0:T(8,128)} %copy-done.3, f32[16,2048]{1,0:T(8,128)} %copy-done.4, f32[16,4224]{1,0:T(8,128)} %get-tuple-element.13.pk_ref.pf_ref, f32[16,4224]{1,0:T(8,128)} %copy-done.2, ...), custom_call_target="tpu_custom_call" | custom-call | tf_op jit(solution)/shard_map/pallas_call | solution.py:310
  (6 shorter events, 0.1 us)
Async XLA Ops:
  1.8 7.9 %collective-permute-start = (bf16[8,12416]{1,0:T(8,128)(2,1)S(1)}, bf16[8,12416]{1,0:T(8,128)(2,1)S(1)}, u32[]{:S(2)}, u32[]{:S(2)}) collective-permute-start(bf16[8,12416]{1,0:T(8,128)(2,1)S(1)} %pad_maximum_fusion), channel_id=1, source_target_pairs={{0,1},{1,2},{2,3},{3,4},{4,5},{5,6},{6,7},{7,8},{8,9},{9,10},{10,1... | collective-permute-start | bytes 595976 | tf_op jit(solution)/shard_map/ppermute | solution.py:19
  9.7 0.7 %copy-start = (bf16[8,12416]{1,0:T(8,128)(2,1)}, bf16[8,12416]{1,0:T(8,128)(2,1)S(1)}, u32[]{:S(2)}) copy-start(bf16[8,12416]{1,0:T(8,128)(2,1)S(1)} %collective-permute-done.rq.rk.rv.rimdoc_ref) | copy-start | bytes 595972
  30.9 1.4 %copy-start.1 = (f32[16,4224]{1,0:T(8,128)S(1)}, f32[16,4224]{1,0:T(8,128)}, u32[]{:S(2)}) copy-start(f32[16,4224]{1,0:T(8,128)} %get-tuple-element.13.pk_ref.pf_ref) | copy-start | bytes 811012
  31.0 1.8 %collective-permute-start.1 = (f32[16,4224]{1,0:T(8,128)}, f32[16,4224]{1,0:T(8,128)S(1)}, u32[]{:S(2)}, u32[]{:S(2)}) collective-permute-start(f32[16,4224]{1,0:T(8,128)} %get-tuple-element.13.pk_ref.pf_ref), channel_id=1, source_target_pairs={{0,1},{1,0},{2,3},{3,2},{4,5},{5,4},{6,7},{7,6},{8,9},{9,8},{10,11... | collective-permute-start | bytes 811016 | tf_op jit(solution)/shard_map/ppermute | solution.py:186
  32.8 27.3 %copy-start.2 = (f32[16,4224]{1,0:T(8,128)}, f32[16,4224]{1,0:T(8,128)S(1)}, u32[]{:S(2)}) copy-start(f32[16,4224]{1,0:T(8,128)S(1)} %collective-permute-done.1.gt_ref.gf_ref) | copy-start | bytes 811012
  33.1 8.5 %collective-permute-start.2 = (f32[16,2176]{1,0:T(8,128)S(1)}, f32[16,2176]{1,0:T(8,128)S(1)}, u32[]{:S(2)}, u32[]{:S(2)}) collective-permute-start(f32[16,2176]{1,0:T(8,128)S(1)} %pad_maximum_fusion.1), channel_id=1, source_target_pairs={{0,2},{1,3},{2,4},{3,5},{4,6},{5,7},{6,8},{7,9},{8,10},{9,11},{10,... | collective-permute-start | bytes 417800 | tf_op jit(solution)/shard_map/ppermute | solution.py:19
  41.9 6.9 %collective-permute-start.3 = (f32[16,2176]{1,0:T(8,128)S(1)}, f32[16,2176]{1,0:T(8,128)S(1)}, u32[]{:S(2)}, u32[]{:S(2)}) collective-permute-start(f32[16,2176]{1,0:T(8,128)S(1)} %pad_maximum_fusion.2), channel_id=1, source_target_pairs={{0,4},{1,5},{2,6},{3,7},{4,8},{5,9},{6,10},{7,11},{8,12},{9,13},{1... | collective-permute-start | bytes 417800 | tf_op jit(solution)/shard_map/ppermute | solution.py:19
  49.2 9.4 %collective-permute-start.4 = (f32[16,2176]{1,0:T(8,128)S(1)}, f32[16,2176]{1,0:T(8,128)S(1)}, u32[]{:S(2)}, u32[]{:S(2)}) collective-permute-start(f32[16,2176]{1,0:T(8,128)S(1)} %pad_maximum_fusion.3), channel_id=1, source_target_pairs={{0,8},{1,9},{2,10},{3,11},{4,12},{5,13},{6,14},{7,15},{16,24},{17,... | collective-permute-start | bytes 417800 | tf_op jit(solution)/shard_map/ppermute | solution.py:19
  58.7 1.4 %copy-start.3 = (f32[16,2048]{1,0:T(8,128)}, f32[16,2048]{1,0:T(8,128)S(1)}, u32[]{:S(2)}) copy-start(f32[16,2048]{1,0:T(8,128)S(1)} %fusion.zo_ref) | copy-start | bytes 393220
  58.7 1.4 %collective-permute-start.5 = (f32[16,2048]{1,0:T(8,128)S(1)}, f32[16,2048]{1,0:T(8,128)S(1)}, u32[]{:S(2)}, u32[]{:S(2)}) collective-permute-start(f32[16,2048]{1,0:T(8,128)S(1)} %fusion.zo_ref), channel_id=1, source_target_pairs={{0,1},{1,0},{2,3},{3,2},{4,5},{5,4},{6,7},{7,6},{8,9},{9,8},{10,11... | collective-permute-start | bytes 393224 | tf_op jit(solution)/shard_map/ppermute | solution.py:186
  60.1 0.6 copy-start.4

commit v12 on v9

--- a/solution.py
+++ b/solution.py
@@ -8,7 +8,7 @@
 from jax.sharding import PartitionSpec as P
 
 WIDTH = 256
-FINAL_WIDTH = 1024
+FINAL_WIDTH = 2048
 RIM = 8
 LANES = 128
 

time: 64.8 us -> 64 us (0.988)
  Pallas kernels: 23.7 us -> 23 us
    pallas_call x1, Pallas kernels: 5.24 us -> 4.58 us  [on_device(): pl.pallas_call(functools.partial(final_kernel, group_width, pole_count, w...]
where the time goes in v12:
time: 64 us; the launch traced here: 63.3 us
  waiting for transfers between devices  23.8 us (37%)
  Pallas kernels  23 us (36%)
  starting transfers between devices  7.16 us (11%)
  local copies, waits for them, and re-layouts  6.76 us (11%)
  other arithmetic  2.28 us (4%)
    ppermute x4, waiting for transfers between devices, from_behind(): return lax.ppermute(shard, axis, pairs)  22.7 us
    pallas_call x1, Pallas kernels, on_device(): pl.pallas_call(functools.partial(local_kernel, taps, group_width, spans),...  18.4 us
    ppermute x4, starting transfers between devices, from_behind(): return lax.ppermute(shard, axis, pairs)  7.02 us
    pallas_call x1, Pallas kernels, on_device(): pl.pallas_call(functools.partial(final_kernel, group_width, pole_count, w...  4.58 us
    another operation x6, local copies, waits for them, and re-layouts, on_device(): jnp.stack([rates, residues]).reshape(2, nb, gpb, pole_count)  1.93 us
  transfers between devices with their start and end apart: 6, of which 6 were waited for; matrix products, arithmetic and copies ran while one was open for 8% of the time, Pallas kernels for 0%

profile of v12, /device:TPU:24, one launch (start us, length us, event | category | flops | bytes accessed | tf_op | source)
XLA Modules:
  0.0 63.3 jit_solution(11481793012477960650)
XLA Ops:
  0.0 1.0 %slice.56 = bf16[8,12288]{1,0:T(8,128)(2,1)S(1)} slice(bf16[128,12288]{1,0:T(8,128)(2,1)} %xv.1), slice={[120:128], [0:12288]} | slice | bytes 393216 | tf_op jit(solution)/shard_map/slice | solution.py:221
  1.0 0.7 %convert.4 = bf16[128]{0:T(256)(128)(2,1)S(1)} convert(s32[128]{0:T(128)} %param.6) | non-fusion elementwise | flops 128 | bytes 768 | tf_op jit(solution)/shard_map/convert.1
  1.6 0.1 slice.57
  1.7 0.1 broadcast_in_dim.36
  1.8 1.9 %collective-permute-start = (bf16[8,12416]{1,0:T(8,128)(2,1)S(1)}, bf16[8,12416]{1,0:T(8,128)(2,1)S(1)}, u32[]{:S(2)}, u32[]{:S(2)}) collective-permute-start(bf16[8,12416]{1,0:T(8,128)(2,1)S(1)} %pad_maximum_fusion), channel_id=1, source_target_pairs={{0,1},{1,2},{2,3},{3,4},{4,5},{5,6},{6,7},{7,8},{8,9},{9,10},{10,1... | collective-permute-start | bytes 595976 | tf_op jit(solution)/shard_map/ppermute | solution.py:19
  3.7 0.8 %stack.18 = f32[1,16,16,16]{2,1,3,0:T(8,128)S(1)} reshape(f32[256,16]{0,1:T(8,128)} %param.8) | data formatting | bytes 32768 | tf_op jit(solution)/shard_map/stack | solution.py:229
  4.6 0.8 %stack.19 = f32[1,16,16,16]{2,1,3,0:T(8,128)S(1)} reshape(f32[256,16]{0,1:T(8,128)} %param.9) | data formatting | bytes 32768 | tf_op jit(solution)/shard_map/stack | solution.py:229
  5.5 0.7 %slice_bitcast_fusion = (f32[16,16,16]{2,1,0:T(8,128)}, f32[16,16,16]{2,1,0:T(8,128)}) fusion(f32[2,16,16,16]{3,2,1,0:T(8,128)S(1)} %maximum_bitcast_fusion), kind=kLoop, calls=%fused_computation.7 | loop fusion | bytes 65536 | tf_op jit(solution)/shard_map/squeeze | solution.py:230
  6.3 3.4 %collective-permute-done.rq.rk.rv = bf16[8,12416]{1,0:T(8,128)(2,1)S(1)} collective-permute-done((bf16[8,12416]{1,0:T(8,128)(2,1)S(1)}, bf16[8,12416]{1,0:T(8,128)(2,1)S(1)}, u32[]{:S(2)}, u32[]{:S(2)}) %collective-permute-start) | collective-permute-done | bytes 198688 | tf_op jit(solution)/shard_map/ppermute | solution.py:19
  9.7 0.1 convert_reduce_fusion
  9.8 0.0 copy-done.7
  9.8 0.1 add_convert_fusion
  9.9 0.6 broadcast_in_dim.38.e_ref
  10.5 0.0 copy-done.2
  10.5 18.4 %shard_map.55 = (f32[128,4096]{1,0:T(8,128)}, f32[128,4096]{1,0:T(8,128)}, f32[16,4224]{1,0:T(8,128)}, f32[4,16,4096]{2,1,0:T(8,128)}, f32[128,128]{1,0:T(8,128)}) custom-call(bf16[128,12288]{1,0:T(8,128)(2,1)} %xv.1, bf16[128,12288]{1,0:T(8,128)(2,1)} %xv.1, bf16[128,12288]{1,0:T(8,128)(2,1)} %xv.1, bf16[8,12416]{1,0:T(8,128)(2,1)} %copy-done.2, ...), custom_call_target="tpu_custom_call" | custom-call | tf_op jit(solution)/shard_map/pallas_call | solution.py:238
  28.9 0.0 copy-start
  29.0 0.1 collective-permute-start.1
  29.0 1.3 %fusion.12 = (f32[1,16,4096]{2,1,0:T(8,128)S(1)}, f32[1,16,4096]{2,1,0:T(8,128)S(1)}, f32[1,16,4096]{2,1,0:T(8,128)S(1)}, f32[1,16,4096]{2,1,0:T(8,128)S(1)}) fusion(f32[4,16,4096]{2,1,0:T(8,128)} %get-tuple-element.13.d1_ref), kind=kLoop, calls=%fused_computation.34 | loop fusion | bytes 2097152 | tf_op jit(solution)/shard_map/slice | solution.py:185
  30.3 0.0 copy-done
  30.3 0.0 copy-start.5
  30.3 0.0 copy-start.6
  30.4 0.4 collective-permute-done.1.gt_ref.gf_ref
  30.8 0.1 fusion.11
  30.9 0.1 fusion.8
  31.0 0.1 broadcast_in_dim.40
  31.1 2.5 %collective-permute-start.2 = (f32[16,2176]{1,0:T(8,128)S(1)}, f32[16,2176]{1,0:T(8,128)S(1)}, u32[]{:S(2)}, u32[]{:S(2)}) collective-permute-start(f32[16,2176]{1,0:T(8,128)S(1)} %pad_maximum_fusion.1), channel_id=1, source_target_pairs={{0,2},{1,3},{2,4},{3,5},{4,6},{5,7},{6,8},{7,9},{8,10},{9,11},{10,... | collective-permute-start | bytes 417800 | tf_op jit(solution)/shard_map/ppermute | solution.py:19
  33.6 6.0 %collective-permute-done.2 = f32[16,2176]{1,0:T(8,128)S(1)} collective-permute-done((f32[16,2176]{1,0:T(8,128)S(1)}, f32[16,2176]{1,0:T(8,128)S(1)}, u32[]{:S(2)}, u32[]{:S(2)}) %collective-permute-start.2) | collective-permute-done | bytes 139296 | tf_op jit(solution)/shard_map/ppermute | solution.py:19
  39.6 0.1 fusion.6
  39.7 0.1 slice_reduce_fusion
  39.8 0.1 broadcast_in_dim.42
  39.9 1.3 %collective-permute-start.3 = (f32[16,2176]{1,0:T(8,128)S(1)}, f32[16,2176]{1,0:T(8,128)S(1)}, u32[]{:S(2)}, u32[]{:S(2)}) collective-permute-start(f32[16,2176]{1,0:T(8,128)S(1)} %pad_maximum_fusion.2), channel_id=1, source_target_pairs={{0,4},{1,5},{2,6},{3,7},{4,8},{5,9},{6,10},{7,11},{8,12},{9,13},{1... | collective-permute-start | bytes 417800 | tf_op jit(solution)/shard_map/ppermute | solution.py:19
  41.2 5.6 %collective-permute-done.3 = f32[16,2176]{1,0:T(8,128)S(1)} collective-permute-done((f32[16,2176]{1,0:T(8,128)S(1)}, f32[16,2176]{1,0:T(8,128)S(1)}, u32[]{:S(2)}, u32[]{:S(2)}) %collective-permute-start.3) | collective-permute-done | bytes 139296 | tf_op jit(solution)/shard_map/ppermute | solution.py:19
  46.9 0.1 multiply_reduce_fusion.1
  47.0 0.1 fusion.2
  47.1 0.1 broadcast_in_dim.44
  47.2 1.3 %collective-permute-start.4 = (f32[16,2176]{1,0:T(8,128)S(1)}, f32[16,2176]{1,0:T(8,128)S(1)}, u32[]{:S(2)}, u32[]{:S(2)}) collective-permute-start(f32[16,2176]{1,0:T(8,128)S(1)} %pad_maximum_fusion.3), channel_id=1, source_target_pairs={{0,8},{1,9},{2,10},{3,11},{4,12},{5,13},{6,14},{7,15},{16,24},{17,... | collective-permute-start | bytes 417800 | tf_op jit(solution)/shard_map/ppermute | solution.py:19
  48.5 0.0 copy-done.5
  48.5 0.1 copy.10
  48.6 0.1 copy.11
  48.7 0.1 stack.21
  48.8 0.1 stack.22
  48.9 7.6 %collective-permute-done.4 = f32[16,2176]{1,0:T(8,128)S(1)} collective-permute-done((f32[16,2176]{1,0:T(8,128)S(1)}, f32[16,2176]{1,0:T(8,128)S(1)}, u32[]{:S(2)}, u32[]{:S(2)}) %collective-permute-start.4) | collective-permute-done | bytes 139296 | tf_op jit(solution)/shard_map/ppermute | solution.py:19
  56.5 0.1 fusion.zo_ref
  56.7 0.1 collective-permute-start.5
  56.7 0.6 %pad_maximum_fusion.4.rr_ref = f32[2,1,4096]{2,1,0:T(1,128)} fusion(f32[1,1,4096]{2,1,0:T(1,128)S(1)} %stack.22, f32[1,1,4096]{2,1,0:T(1,128)S(1)} %stack.21), kind=kLoop, calls=%fused_computation.22 | loop fusion | flops 8192 | bytes 65536 | tf_op jit(solution)/shard_map/stack | solution.py:229
  57.4 0.7 %collective-permute-done.5.zp_ref = f32[16,2048]{1,0:T(8,128)S(1)} collective-permute-done((f32[16,2048]{1,0:T(8,128)S(1)}, f32[16,2048]{1,0:T(8,128)S(1)}, u32[]{:S(2)}, u32[]{:S(2)}) %collective-permute-start.5) | collective-permute-done | bytes 131104 | tf_op jit(solution)/shard_map/ppermute | solution.py:157
  58.1 0.6 %copy-done.4 = f32[16,2048]{1,0:T(8,128)} copy-done((f32[16,2048]{1,0:T(8,128)}, f32[16,2048]{1,0:T(8,128)S(1)}, u32[]{:S(2)}) %copy-start.4) | copy-done | bytes 131096
  58.7 4.6 %shard_map.56 = bf16[128,4096]{1,0:T(8,128)(2,1)} custom-call(f32[128,4096]{1,0:T(8,128)} %get-tuple-element.10.q_ref, f32[128,4096]{1,0:T(8,128)} %get-tuple-element.11.loc_ref, f32[16,2048]{1,0:T(8,128)} %copy-done.3, f32[16,2048]{1,0:T(8,128)} %copy-done.4, f32[16,4224]{1,0:T(8,128)} %get-tuple-element.12.pk_ref.pf_ref, f32[16,4224]{1,0:T(8,128)} %copy-done.1, ...), custom_call_target="tpu_custom_call" | custom-call | tf_op jit(solution)/shard_map/pallas_call | solution.py:286
  (18 shorter events, 0.2 us)
Async XLA Ops:
  0.0 9.8 %copy-start.7 = (s32[128]{0:T(128)S(1)}, s32[128]{0:T(128)}, u32[]{:S(2)}) copy-start(s32[128]{0:T(128)} %param.6) | copy-start | bytes 1540
  1.8 7.9 %collective-permute-start = (bf16[8,12416]{1,0:T(8,128)(2,1)S(1)}, bf16[8,12416]{1,0:T(8,128)(2,1)S(1)}, u32[]{:S(2)}, u32[]{:S(2)}) collective-permute-start(bf16[8,12416]{1,0:T(8,128)(2,1)S(1)} %pad_maximum_fusion), channel_id=1, source_target_pairs={{0,1},{1,2},{2,3},{3,4},{4,5},{5,6},{6,7},{7,8},{8,9},{9,10},{10,1... | collective-permute-start | bytes 595976 | tf_op jit(solution)/shard_map/ppermute | solution.py:19
  9.7 0.8 %copy-start.2 = (bf16[8,12416]{1,0:T(8,128)(2,1)}, bf16[8,12416]{1,0:T(8,128)(2,1)S(1)}, u32[]{:S(2)}) copy-start(bf16[8,12416]{1,0:T(8,128)(2,1)S(1)} %collective-permute-done.rq.rk.rv) | copy-start | bytes 595972
  28.9 1.4 %copy-start = (f32[16,4224]{1,0:T(8,128)S(1)}, f32[16,4224]{1,0:T(8,128)}, u32[]{:S(2)}) copy-start(f32[16,4224]{1,0:T(8,128)} %get-tuple-element.12.pk_ref.pf_ref) | copy-start | bytes 811012
  29.0 1.8 %collective-permute-start.1 = (f32[16,4224]{1,0:T(8,128)}, f32[16,4224]{1,0:T(8,128)S(1)}, u32[]{:S(2)}, u32[]{:S(2)}) collective-permute-start(f32[16,4224]{1,0:T(8,128)} %get-tuple-element.12.pk_ref.pf_ref), channel_id=1, source_target_pairs={{0,1},{1,0},{2,3},{3,2},{4,5},{5,4},{6,7},{7,6},{8,9},{9,8},{10,11... | collective-permute-start | bytes 811016 | tf_op jit(solution)/shard_map/ppermute | solution.py:157
  30.3 18.2 %copy-start.5 = (f32[256,16]{0,1:T(8,128)S(1)}, f32[256,16]{0,1:T(8,128)}, u32[]{:S(2)}) copy-start(f32[256,16]{0,1:T(8,128)} %param.8) | copy-start | bytes 49156
  30.3 18.3 %copy-start.6 = (f32[256,16]{0,1:T(8,128)S(1)}, f32[256,16]{0,1:T(8,128)}, u32[]{:S(2)}) copy-start(f32[256,16]{0,1:T(8,128)} %param.9) | copy-start | bytes 49156
  30.8 25.9 %copy-start.1 = (f32[16,4224]{1,0:T(8,128)}, f32[16,4224]{1,0:T(8,128)S(1)}, u32[]{:S(2)}) copy-start(f32[16,4224]{1,0:T(8,128)S(1)} %collective-permute-done.1.gt_ref.gf_ref) | copy-start | bytes 811012
  31.1 8.5 %collective-permute-start.2 = (f32[16,2176]{1,0:T(8,128)S(1)}, f32[16,2176]{1,0:T(8,128)S(1)}, u32[]{:S(2)}, u32[]{:S(2)}) collective-permute-start(f32[16,2176]{1,0:T(8,128)S(1)} %pad_maximum_fusion.1), channel_id=1, source_target_pairs={{0,2},{1,3},{2,4},{3,5},{4,6},{5,7},{6,8},{7,9},{8,10},{9,11},{10,... | collective-permute-start | bytes 417800 | tf_op jit(solution)/shard_map/ppermute | solution.py:19
  39.9 6.9 %collective-permute-start.3 = (f32[16,2176]{1,0:T(8,128)S(1)}, f32[16,2176]{1,0:T(8,128)S(1)}, u32[]{:S(2)}, u32[]{:S(2)}) collective-permute-start(f32[16,2176]{1,0:T(8,128)S(1)} %pad_maximum_fusion.2), channel_id=1, source_target_pairs={{0,4},{1,5},{2,6},{3,7},{4,8},{5,9},{6,10},{7,11},{8,12},{9,13},{1... | collective-permute-start | bytes 417800 | tf_op jit(solution)/shard_map/ppermute | solution.py:19
  47.2 9.4 %collective-permute-start.4 = (f32[16,2176]{1,0:T(8,128)S(1)}, f32[16,2176]{1,0:T(8,128)S(1)}, u32[]{:S(2)}, u32[]{:S(2)}) collective-permute-start(f32[16,2176]{1,0:T(8,128)S(1)} %pad_maximum_fusion.3), channel_id=1, source_target_pairs={{0,8},{1,9},{2,10},{3,11},{4,12},{5,13},{6,14},{7,15},{16,24},{17,... | collective-permute-start | bytes 417800 | tf_op jit(solution)/shard_map/ppermute | solution.py:19
  56.6 1.4 %copy-start.3 = (f32[16,2048]{1,0:T(8,128)}, f32[16,2048]{1,0:T(8,128)S(1)}, u32[]{:S(2)}) copy-start(f32[16,2048]{1,0:T(8,128)S(1)} %fusion.zo_ref) | copy-start | bytes 393220
  56.7 1.4 %collective-permute-start.5 = (f32[16,2048]{1,0:T(8,128)S(1)}, f32[16,2048]{1,0:T(8,128)S(1)}, u32[]{:S(2)}, u32[]{:S(2)}) collective-permute-start(f32[16,2048]{1,0:T(8,128)S(1)} %fusion.zo_ref), channel_id=1, source_target_pairs={{0,1},{1,0},{2,3},{3,2},{4,5},{5,4},{6,7},{7,6},{8,9},{9,8},{10,11... | collective-permute-start | bytes 393224 | tf_op jit(solution)/shard_map/ppermute | solution.py:157
  58.1 0.7 %copy-start.4 = (f32[16,2048]{1,0:T(8,128)}, f32[16,2048]{1,0:T(8,128)S(1)}, u32[]{:S(2)}) copy-start(f32[16,2048]{1,0:T(8,128)S(1)} %collective-permute-done.5.zp_ref) | copy-start | bytes 393220

commit v13 on v12

--- a/solution.py
+++ b/solution.py
@@ -7,7 +7,7 @@
 from jax.experimental.pallas import tpu as pltpu
 from jax.sharding import PartitionSpec as P
 
-WIDTH = 256
+WIDTH = 512
 FINAL_WIDTH = 2048
 RIM = 8
 LANES = 128
@@ -284,7 +284,7 @@
     nbf = channels // final_width
     iw_width = final_width // group_width * pole_count
     return pl.pallas_call(
-        functools.partial(final_kernel, group_width, pole_count, width, hb),
+        functools.partial(final_kernel, group_width, pole_count, min(256, width), hb),
         grid=(nbf,),
         in_specs=[
             pl.BlockSpec((length, final_width), col(0)),

time: 64 us -> 63.3 us (0.989)
  Pallas kernels: 23 us -> 21.7 us
  other arithmetic: 2.28 us -> 2.93 us
    pallas_call x1, Pallas kernels: 18.4 us -> 17.1 us  [on_device(): pl.pallas_call(functools.partial(local_kernel, taps, group_width, spans),...]
    convert_element_type x1, other arithmetic: 0.08 us -> 0.73 us  [on_device(): jnp.concatenate([doc_ids, prev_docs, jnp.full((span_r - length - RIM,), -...]
  transfers between devices with their start and end apart: 6 -> 6, of which waited for: 6 -> 6; matrix products, arithmetic and copies ran while one was open for 8% -> 7% of each run, Pallas kernels for 0% -> 0%
where the time goes in v13:
time: 63.3 us; the launch traced here: 62.6 us
  waiting for transfers between devices  24 us (38%)
  Pallas kernels  21.7 us (34%)
  starting transfers between devices  7.18 us (11%)
  local copies, waits for them, and re-layouts  6.61 us (10%)
  other arithmetic  2.93 us (5%)
    ppermute x4, waiting for transfers between devices, from_behind(): return lax.ppermute(shard, axis, pairs)  22.8 us
    pallas_call x1, Pallas kernels, on_device(): pl.pallas_call(functools.partial(local_kernel, taps, group_width, spans),...  17.1 us
    ppermute x4, starting transfers between devices, from_behind(): return lax.ppermute(shard, axis, pairs)  7.04 us
    pallas_call x1, Pallas kernels, on_device(): pl.pallas_call(functools.partial(final_kernel, group_width, pole_count, m...  4.59 us
    another operation x6, local copies, waits for them, and re-layouts, on_device(): jnp.stack([rates, residues]).reshape(2, nb, gpb, pole_count)  1.84 us
  transfers between devices with their start and end apart: 6, of which 6 were waited for; matrix products, arithmetic and copies ran while one was open for 7% of the time, Pallas kernels for 0%

profile of v13, /device:TPU:24, one launch (start us, length us, event | category | flops | bytes accessed | tf_op | source)
XLA Modules:
  0.0 62.6 jit_solution(3249883282863038452)
XLA Ops:
  0.0 0.9 %slice.56 = bf16[8,12288]{1,0:T(8,128)(2,1)S(1)} slice(bf16[128,12288]{1,0:T(8,128)(2,1)} %xv.1), slice={[120:128], [0:12288]} | slice | bytes 393216 | tf_op jit(solution)/shard_map/slice | solution.py:221
  0.9 0.7 %convert.4 = bf16[128]{0:T(256)(128)(2,1)S(1)} convert(s32[128]{0:T(128)} %param.6) | non-fusion elementwise | flops 128 | bytes 768 | tf_op jit(solution)/shard_map/convert.1
  1.6 0.1 slice.57
  1.7 0.1 broadcast_in_dim.36
  1.8 1.9 %collective-permute-start = (bf16[8,12416]{1,0:T(8,128)(2,1)S(1)}, bf16[8,12416]{1,0:T(8,128)(2,1)S(1)}, u32[]{:S(2)}, u32[]{:S(2)}) collective-permute-start(bf16[8,12416]{1,0:T(8,128)(2,1)S(1)} %pad_maximum_fusion), channel_id=1, source_target_pairs={{0,1},{1,2},{2,3},{3,4},{4,5},{5,6},{6,7},{7,8},{8,9},{9,10},{10,1... | collective-permute-start | bytes 595976 | tf_op jit(solution)/shard_map/ppermute | solution.py:19
  3.7 0.8 %stack.18 = f32[1,8,32,16]{2,1,3,0:T(8,128)S(1)} reshape(f32[256,16]{0,1:T(8,128)} %param.8) | data formatting | bytes 32768 | tf_op jit(solution)/shard_map/stack | solution.py:229
  4.5 0.8 %stack.19 = f32[1,8,32,16]{2,1,3,0:T(8,128)S(1)} reshape(f32[256,16]{0,1:T(8,128)} %param.9) | data formatting | bytes 32768 | tf_op jit(solution)/shard_map/stack | solution.py:229
  5.4 0.7 %slice_bitcast_fusion = (f32[8,16,32]{2,1,0:T(8,128)}, f32[8,16,32]{2,1,0:T(8,128)}) fusion(f32[2,8,16,32]{3,2,1,0:T(8,128)S(1)} %maximum_bitcast_fusion), kind=kLoop, calls=%fused_computation.20 | loop fusion | bytes 65536 | tf_op jit(solution)/shard_map/squeeze | solution.py:230
  6.1 3.6 %collective-permute-done.rq.rk.rv = bf16[8,12416]{1,0:T(8,128)(2,1)S(1)} collective-permute-done((bf16[8,12416]{1,0:T(8,128)(2,1)S(1)}, bf16[8,12416]{1,0:T(8,128)(2,1)S(1)}, u32[]{:S(2)}, u32[]{:S(2)}) %collective-permute-start) | collective-permute-done | bytes 198688 | tf_op jit(solution)/shard_map/ppermute | solution.py:19
  9.7 0.1 convert_reduce_fusion
  9.8 0.7 %add_convert_fusion = f32[256]{0:T(256)S(1)} fusion(s32[120]{0:T(128)S(1)} %broadcast_in_dim.37, s32[8]{0:T(128)S(1)} %convert_reduce_fusion, s32[128]{0:T(128)} %param.6), kind=kLoop, calls=%fused_computation.32 | loop fusion | flops 768 | bytes 2048 | tf_op jit(solution)/shard_map/convert_element_type | solution.py:226
  10.5 0.6 broadcast_in_dim.38.e_ref
  11.1 0.0 copy-done.2
  11.1 17.1 %shard_map.55 = (f32[128,4096]{1,0:T(8,128)}, f32[128,4096]{1,0:T(8,128)}, f32[16,4224]{1,0:T(8,128)}, f32[4,16,4096]{2,1,0:T(8,128)}, f32[128,128]{1,0:T(8,128)}) custom-call(bf16[128,12288]{1,0:T(8,128)(2,1)} %xv.1, bf16[128,12288]{1,0:T(8,128)(2,1)} %xv.1, bf16[128,12288]{1,0:T(8,128)(2,1)} %xv.1, bf16[8,12416]{1,0:T(8,128)(2,1)} %copy-done.2, ...), custom_call_target="tpu_custom_call" | custom-call | tf_op jit(solution)/shard_map/pallas_call | solution.py:238
  28.2 0.0 copy-start
  28.2 0.1 collective-permute-start.1
  28.3 1.3 %fusion.12 = (f32[1,16,4096]{2,1,0:T(8,128)S(1)}, f32[1,16,4096]{2,1,0:T(8,128)S(1)}, f32[1,16,4096]{2,1,0:T(8,128)S(1)}, f32[1,16,4096]{2,1,0:T(8,128)S(1)}) fusion(f32[4,16,4096]{2,1,0:T(8,128)} %get-tuple-element.13.d1_ref), kind=kLoop, calls=%fused_computation.34 | loop fusion | bytes 2097152 | tf_op jit(solution)/shard_map/slice | solution.py:185
  29.6 0.0 copy-done
  29.6 0.0 copy-start.5
  29.6 0.0 copy-start.6
  29.7 0.4 collective-permute-done.1.gt_ref.gf_ref
  30.1 0.1 fusion.11
  30.2 0.1 fusion.8
  30.3 0.1 broadcast_in_dim.40
  30.4 2.5 %collective-permute-start.2 = (f32[16,2176]{1,0:T(8,128)S(1)}, f32[16,2176]{1,0:T(8,128)S(1)}, u32[]{:S(2)}, u32[]{:S(2)}) collective-permute-start(f32[16,2176]{1,0:T(8,128)S(1)} %pad_maximum_fusion.1), channel_id=1, source_target_pairs={{0,2},{1,3},{2,4},{3,5},{4,6},{5,7},{6,8},{7,9},{8,10},{9,11},{10,... | collective-permute-start | bytes 417800 | tf_op jit(solution)/shard_map/ppermute | solution.py:19
  32.9 6.0 %collective-permute-done.2 = f32[16,2176]{1,0:T(8,128)S(1)} collective-permute-done((f32[16,2176]{1,0:T(8,128)S(1)}, f32[16,2176]{1,0:T(8,128)S(1)}, u32[]{:S(2)}, u32[]{:S(2)}) %collective-permute-start.2) | collective-permute-done | bytes 139296 | tf_op jit(solution)/shard_map/ppermute | solution.py:19
  38.9 0.1 fusion.6
  39.0 0.1 slice_reduce_fusion
  39.1 0.1 broadcast_in_dim.42
  39.2 1.3 %collective-permute-start.3 = (f32[16,2176]{1,0:T(8,128)S(1)}, f32[16,2176]{1,0:T(8,128)S(1)}, u32[]{:S(2)}, u32[]{:S(2)}) collective-permute-start(f32[16,2176]{1,0:T(8,128)S(1)} %pad_maximum_fusion.2), channel_id=1, source_target_pairs={{0,4},{1,5},{2,6},{3,7},{4,8},{5,9},{6,10},{7,11},{8,12},{9,13},{1... | collective-permute-start | bytes 417800 | tf_op jit(solution)/shard_map/ppermute | solution.py:19
  40.5 5.6 %collective-permute-done.3 = f32[16,2176]{1,0:T(8,128)S(1)} collective-permute-done((f32[16,2176]{1,0:T(8,128)S(1)}, f32[16,2176]{1,0:T(8,128)S(1)}, u32[]{:S(2)}, u32[]{:S(2)}) %collective-permute-start.3) | collective-permute-done | bytes 139296 | tf_op jit(solution)/shard_map/ppermute | solution.py:19
  46.1 0.1 multiply_reduce_fusion.1
  46.3 0.1 fusion.2
  46.4 0.1 broadcast_in_dim.44
  46.5 1.3 %collective-permute-start.4 = (f32[16,2176]{1,0:T(8,128)S(1)}, f32[16,2176]{1,0:T(8,128)S(1)}, u32[]{:S(2)}, u32[]{:S(2)}) collective-permute-start(f32[16,2176]{1,0:T(8,128)S(1)} %pad_maximum_fusion.3), channel_id=1, source_target_pairs={{0,8},{1,9},{2,10},{3,11},{4,12},{5,13},{6,14},{7,15},{16,24},{17,... | collective-permute-start | bytes 417800 | tf_op jit(solution)/shard_map/ppermute | solution.py:19
  47.8 0.0 copy-done.5
  47.8 0.1 copy.10
  47.9 0.0 copy-done.6
  47.9 0.1 copy.11
  48.0 0.1 stack.21
  48.1 0.1 stack.22
  48.2 7.6 %collective-permute-done.4 = f32[16,2176]{1,0:T(8,128)S(1)} collective-permute-done((f32[16,2176]{1,0:T(8,128)S(1)}, f32[16,2176]{1,0:T(8,128)S(1)}, u32[]{:S(2)}, u32[]{:S(2)}) %collective-permute-start.4) | collective-permute-done | bytes 139296 | tf_op jit(solution)/shard_map/ppermute | solution.py:19
  55.8 0.1 fusion.zo_ref
  56.0 0.1 collective-permute-start.5
  56.0 0.6 %pad_maximum_fusion.4.rr_ref = f32[2,1,4096]{2,1,0:T(1,128)} fusion(f32[1,1,4096]{2,1,0:T(1,128)S(1)} %stack.22, f32[1,1,4096]{2,1,0:T(1,128)S(1)} %stack.21), kind=kLoop, calls=%fused_computation.22 | loop fusion | flops 8192 | bytes 65536 | tf_op jit(solution)/shard_map/stack | solution.py:229
  56.7 0.7 %collective-permute-done.5.zp_ref = f32[16,2048]{1,0:T(8,128)S(1)} collective-permute-done((f32[16,2048]{1,0:T(8,128)S(1)}, f32[16,2048]{1,0:T(8,128)S(1)}, u32[]{:S(2)}, u32[]{:S(2)}) %collective-permute-start.5) | collective-permute-done | bytes 131104 | tf_op jit(solution)/shard_map/ppermute | solution.py:157
  57.4 0.6 %copy-done.4 = f32[16,2048]{1,0:T(8,128)} copy-done((f32[16,2048]{1,0:T(8,128)}, f32[16,2048]{1,0:T(8,128)S(1)}, u32[]{:S(2)}) %copy-start.4) | copy-done | bytes 131096
  58.0 4.6 %shard_map.56 = bf16[128,4096]{1,0:T(8,128)(2,1)} custom-call(f32[128,4096]{1,0:T(8,128)} %get-tuple-element.10.q_ref, f32[128,4096]{1,0:T(8,128)} %get-tuple-element.11.loc_ref, f32[16,2048]{1,0:T(8,128)} %copy-done.3, f32[16,2048]{1,0:T(8,128)} %copy-done.4, f32[16,4224]{1,0:T(8,128)} %get-tuple-element.12.pk_ref.pf_ref, f32[16,4224]{1,0:T(8,128)} %copy-done.1, ...), custom_call_target="tpu_custom_call" | custom-call | tf_op jit(solution)/shard_map/pallas_call | solution.py:286
  (16 shorter events, 0.2 us)
Async XLA Ops:
  1.8 7.9 %collective-permute-start = (bf16[8,12416]{1,0:T(8,128)(2,1)S(1)}, bf16[8,12416]{1,0:T(8,128)(2,1)S(1)}, u32[]{:S(2)}, u32[]{:S(2)}) collective-permute-start(bf16[8,12416]{1,0:T(8,128)(2,1)S(1)} %pad_maximum_fusion), channel_id=1, source_target_pairs={{0,1},{1,2},{2,3},{3,4},{4,5},{5,6},{6,7},{7,8},{8,9},{9,10},{10,1... | collective-permute-start | bytes 595976 | tf_op jit(solution)/shard_map/ppermute | solution.py:19
  9.7 1.5 %copy-start.2 = (bf16[8,12416]{1,0:T(8,128)(2,1)}, bf16[8,12416]{1,0:T(8,128)(2,1)S(1)}, u32[]{:S(2)}) copy-start(bf16[8,12416]{1,0:T(8,128)(2,1)S(1)} %collective-permute-done.rq.rk.rv) | copy-start | bytes 595972
  28.2 1.4 %copy-start = (f32[16,4224]{1,0:T(8,128)S(1)}, f32[16,4224]{1,0:T(8,128)}, u32[]{:S(2)}) copy-start(f32[16,4224]{1,0:T(8,128)} %get-tuple-element.12.pk_ref.pf_ref) | copy-start | bytes 811012
  28.2 1.8 %collective-permute-start.1 = (f32[16,4224]{1,0:T(8,128)}, f32[16,4224]{1,0:T(8,128)S(1)}, u32[]{:S(2)}, u32[]{:S(2)}) collective-permute-start(f32[16,4224]{1,0:T(8,128)} %get-tuple-element.12.pk_ref.pf_ref), channel_id=1, source_target_pairs={{0,1},{1,0},{2,3},{3,2},{4,5},{5,4},{6,7},{7,6},{8,9},{9,8},{10,11... | collective-permute-start | bytes 811016 | tf_op jit(solution)/shard_map/ppermute | solution.py:157
  29.6 18.2 %copy-start.5 = (f32[256,16]{0,1:T(8,128)S(1)}, f32[256,16]{0,1:T(8,128)}, u32[]{:S(2)}) copy-start(f32[256,16]{0,1:T(8,128)} %param.8) | copy-start | bytes 49156
  29.6 18.3 %copy-start.6 = (f32[256,16]{0,1:T(8,128)S(1)}, f32[256,16]{0,1:T(8,128)}, u32[]{:S(2)}) copy-start(f32[256,16]{0,1:T(8,128)} %param.9) | copy-start | bytes 49156
  30.1 25.9 %copy-start.1 = (f32[16,4224]{1,0:T(8,128)}, f32[16,4224]{1,0:T(8,128)S(1)}, u32[]{:S(2)}) copy-start(f32[16,4224]{1,0:T(8,128)S(1)} %collective-permute-done.1.gt_ref.gf_ref) | copy-start | bytes 811012
  30.4 8.5 %collective-permute-start.2 = (f32[16,2176]{1,0:T(8,128)S(1)}, f32[16,2176]{1,0:T(8,128)S(1)}, u32[]{:S(2)}, u32[]{:S(2)}) collective-permute-start(f32[16,2176]{1,0:T(8,128)S(1)} %pad_maximum_fusion.1), channel_id=1, source_target_pairs={{0,2},{1,3},{2,4},{3,5},{4,6},{5,7},{6,8},{7,9},{8,10},{9,11},{10,... | collective-permute-start | bytes 417800 | tf_op jit(solution)/shard_map/ppermute | solution.py:19
  39.2 6.9 %collective-permute-start.3 = (f32[16,2176]{1,0:T(8,128)S(1)}, f32[16,2176]{1,0:T(8,128)S(1)}, u32[]{:S(2)}, u32[]{:S(2)}) collective-permute-start(f32[16,2176]{1,0:T(8,128)S(1)} %pad_maximum_fusion.2), channel_id=1, source_target_pairs={{0,4},{1,5},{2,6},{3,7},{4,8},{5,9},{6,10},{7,11},{8,12},{9,13},{1... | collective-permute-start | bytes 417800 | tf_op jit(solution)/shard_map/ppermute | solution.py:19
  46.5 9.4 %collective-permute-start.4 = (f32[16,2176]{1,0:T(8,128)S(1)}, f32[16,2176]{1,0:T(8,128)S(1)}, u32[]{:S(2)}, u32[]{:S(2)}) collective-permute-start(f32[16,2176]{1,0:T(8,128)S(1)} %pad_maximum_fusion.3), channel_id=1, source_target_pairs={{0,8},{1,9},{2,10},{3,11},{4,12},{5,13},{6,14},{7,15},{16,24},{17,... | collective-permute-start | bytes 417800 | tf_op jit(solution)/shard_map/ppermute | solution.py:19
  55.9 1.4 %copy-start.3 = (f32[16,2048]{1,0:T(8,128)}, f32[16,2048]{1,0:T(8,128)S(1)}, u32[]{:S(2)}) copy-start(f32[16,2048]{1,0:T(8,128)S(1)} %fusion.zo_ref) | copy-start | bytes 393220
  56.0 1.4 %collective-permute-start.5 = (f32[16,2048]{1,0:T(8,128)S(1)}, f32[16,2048]{1,0:T(8,128)S(1)}, u32[]{:S(2)}, u32[]{:S(2)}) collective-permute-start(f32[16,2048]{1,0:T(8,128)S(1)} %fusion.zo_ref), channel_id=1, source_target_pairs={{0,1},{1,0},{2,3},{3,2},{4,5},{5,4},{6,7},{7,6},{8,9},{9,8},{10,11... | collective-permute-start | bytes 393224 | tf_op jit(solution)/shard_map/ppermute | solution.py:157
  57.4 0.7 %copy-start.4 = (f32[16,2048]{1,0:T(8,128)}, f32[16,2048]{1,0:T(8,128)S(1)}, u32[]{:S(2)}) copy-start(f32[16,2048]{1,0:T(8,128)S(1)} %collective-permute-done.5.zp_ref) | copy-start | bytes 393220

commit v14 on v13

--- a/solution.py
+++ b/solution.py
@@ -10,6 +10,7 @@
 WIDTH = 512
 FINAL_WIDTH = 2048
 RIM = 8
+SUB = 256
 LANES = 128
 
 
@@ -83,10 +84,6 @@
     q_out[...] = cq
     gated = (ck * cv).astype(jnp.bfloat16)
 
-    lane_group = lax.broadcasted_iota(jnp.int32, (length, width), 1) // group_width
-    zero = jnp.zeros_like(gated)
-    xbd = jnp.concatenate([jnp.where(lane_group == g, gated, zero) for g in range(groups)], axis=0)
-
     rt = rt_ref[0]
     et = et_ref[0]
     lane = lax.broadcasted_iota(jnp.int32, (1, length), 1)
@@ -94,22 +91,29 @@
     to_end = (length - 1 - lane).astype(jnp.float32)
     at_tail = tail_s[0:1, :]
     visible = vis_s[...] > 0.5
-    pieces = []
-    ends = []
-    for g in range(groups):
-        a_col = rt[:, g:g + 1]
-        r_col = et[:, g:g + 1]
-        base = jnp.sum(r_col * jnp.exp(-a_col * lags), axis=0, keepdims=True)
-        row = jnp.broadcast_to(base.astype(jnp.bfloat16), (length, length))
-        rolled = pltpu.roll(row, 0, 1, stride=1, stride_axis=0)
-        pieces.append(jnp.where(visible, rolled, jnp.zeros_like(rolled)))
-        ends.append(jnp.exp(-a_col * to_end) * at_tail)
-    e_hi, e_lo = split2(jnp.concatenate(ends, axis=1))
-    t_hi = jnp.concatenate(pieces, axis=1)
-    res = jnp.dot(jnp.concatenate([t_hi, e_hi, e_lo], axis=0), xbd, preferred_element_type=jnp.float32)
-    loc_out[...] = res[0:length]
-    st = res[length:length + pole_count] + res[length + pole_count:length + 2 * pole_count]
-    pk_out[:, pl.ds(pl.multiple_of(step * width, width), width)] = st
+    sub = min(SUB, width)
+    sub_groups = sub // group_width
+    lane_group = lax.broadcasted_iota(jnp.int32, (length, sub), 1) // group_width
+    for h in range(width // sub):
+        part = gated[:, h * sub:(h + 1) * sub]
+        zero = jnp.zeros_like(part)
+        xbd = jnp.concatenate([jnp.where(lane_group == g, part, zero) for g in range(sub_groups)], axis=0)
+        pieces = []
+        ends = []
+        for g in range(h * sub_groups, (h + 1) * sub_groups):
+            a_col = rt[:, g:g + 1]
+            r_col = et[:, g:g + 1]
+            base = jnp.sum(r_col * jnp.exp(-a_col * lags), axis=0, keepdims=True)
+            row = jnp.broadcast_to(base.astype(jnp.bfloat16), (length, length))
+            rolled = pltpu.roll(row, 0, 1, stride=1, stride_axis=0)
+            pieces.append(jnp.where(visible, rolled, jnp.zeros_like(rolled)))
+            ends.append(jnp.exp(-a_col * to_end) * at_tail)
+        e_hi, e_lo = split2(jnp.concatenate(ends, axis=1))
+        t_hi = jnp.concatenate(pieces, axis=1)
+        res = jnp.dot(jnp.concatenate([t_hi, e_hi, e_lo], axis=0), xbd, preferred_element_type=jnp.float32)
+        loc_out[:, h * sub:(h + 1) * sub] = res[0:length]
+        st = res[length:length + pole_count] + res[length + pole_count:length + 2 * pole_count]
+        pk_out[:, pl.ds(pl.multiple_of(step * width + h * sub, sub), sub)] = st
 
     spread = (lax.broadcasted_iota(jnp.int32, (groups, width), 1) // group_width
               == lax.broadcasted_iota(jnp.int32, (groups, width), 0)).astype(jnp.bfloat16)

time: 63.3 us -> 60.3 us (0.953)
  Pallas kernels: 21.7 us -> 18.7 us
    pallas_call x1, Pallas kernels: 17.1 us -> 14.1 us  [on_device(): pl.pallas_call(functools.partial(local_kernel, taps, group_width, spans),...]
  transfers between devices with their start and end apart: 6 -> 6, of which waited for: 6 -> 6; matrix products, arithmetic and copies ran while one was open for 7% -> 8% of each run, Pallas kernels for 0% -> 0%
where the time goes in v14:
time: 60.3 us; the launch traced here: 59.6 us
  waiting for transfers between devices  24 us (40%)
  Pallas kernels  18.7 us (31%)
  starting transfers between devices  7.15 us (12%)
  local copies, waits for them, and re-layouts  6.61 us (11%)
  other arithmetic  2.93 us (5%)
    ppermute x4, waiting for transfers between devices, from_behind(): return lax.ppermute(shard, axis, pairs)  22.8 us
    pallas_call x1, Pallas kernels, on_device(): pl.pallas_call(functools.partial(local_kernel, taps, group_width, spans),...  14.1 us
    ppermute x4, starting transfers between devices, from_behind(): return lax.ppermute(shard, axis, pairs)  7 us
    pallas_call x1, Pallas kernels, on_device(): pl.pallas_call(functools.partial(final_kernel, group_width, pole_count, m...  4.58 us
    another operation x6, local copies, waits for them, and re-layouts, on_device(): jnp.stack([rates, residues]).reshape(2, nb, gpb, pole_count)  1.84 us
    slice x1, local copies, waits for them, and re-layouts, chip_scan(): prefix = prefix + prefix_flag * mine(decays[span_of[2 * offset - 2]]) * came  1.26 us
  transfers between devices with their start and end apart: 6, of which 6 were waited for; matrix products, arithmetic and copies ran while one was open for 8% of the time, Pallas kernels for 0%

profile of v14, /device:TPU:24, one launch (start us, length us, event | category | flops | bytes accessed | tf_op | source)
XLA Modules:
  0.0 59.6 jit_solution(6496970026631365295)
XLA Ops:
  0.0 0.9 %slice.56 = bf16[8,12288]{1,0:T(8,128)(2,1)S(1)} slice(bf16[128,12288]{1,0:T(8,128)(2,1)} %xv.1), slice={[120:128], [0:12288]} | slice | bytes 393216 | tf_op jit(solution)/shard_map/slice | solution.py:225
  0.9 0.7 %convert.4 = bf16[128]{0:T(256)(128)(2,1)S(1)} convert(s32[128]{0:T(128)} %param.6) | non-fusion elementwise | flops 128 | bytes 768 | tf_op jit(solution)/shard_map/convert.1
  1.6 0.1 slice.57
  1.7 0.1 broadcast_in_dim.36
  1.8 1.9 %collective-permute-start = (bf16[8,12416]{1,0:T(8,128)(2,1)S(1)}, bf16[8,12416]{1,0:T(8,128)(2,1)S(1)}, u32[]{:S(2)}, u32[]{:S(2)}) collective-permute-start(bf16[8,12416]{1,0:T(8,128)(2,1)S(1)} %pad_maximum_fusion), channel_id=1, source_target_pairs={{0,1},{1,2},{2,3},{3,4},{4,5},{5,6},{6,7},{7,8},{8,9},{9,10},{10,1... | collective-permute-start | bytes 595976 | tf_op jit(solution)/shard_map/ppermute | solution.py:20
  3.7 0.8 %stack.18 = f32[1,8,32,16]{2,1,3,0:T(8,128)S(1)} reshape(f32[256,16]{0,1:T(8,128)} %param.8) | data formatting | bytes 32768 | tf_op jit(solution)/shard_map/stack | solution.py:233
  4.5 0.8 %stack.19 = f32[1,8,32,16]{2,1,3,0:T(8,128)S(1)} reshape(f32[256,16]{0,1:T(8,128)} %param.9) | data formatting | bytes 32768 | tf_op jit(solution)/shard_map/stack | solution.py:233
  5.4 0.7 %slice_bitcast_fusion = (f32[8,16,32]{2,1,0:T(8,128)}, f32[8,16,32]{2,1,0:T(8,128)}) fusion(f32[2,8,16,32]{3,2,1,0:T(8,128)S(1)} %maximum_bitcast_fusion), kind=kLoop, calls=%fused_computation.20 | loop fusion | bytes 65536 | tf_op jit(solution)/shard_map/squeeze | solution.py:234
  6.1 3.6 %collective-permute-done.rq.rk.rv = bf16[8,12416]{1,0:T(8,128)(2,1)S(1)} collective-permute-done((bf16[8,12416]{1,0:T(8,128)(2,1)S(1)}, bf16[8,12416]{1,0:T(8,128)(2,1)S(1)}, u32[]{:S(2)}, u32[]{:S(2)}) %collective-permute-start) | collective-permute-done | bytes 198688 | tf_op jit(solution)/shard_map/ppermute | solution.py:20
  9.7 0.1 convert_reduce_fusion
  9.8 0.7 %add_convert_fusion = f32[256]{0:T(256)S(1)} fusion(s32[120]{0:T(128)S(1)} %broadcast_in_dim.37, s32[8]{0:T(128)S(1)} %convert_reduce_fusion, s32[128]{0:T(128)} %param.6), kind=kLoop, calls=%fused_computation.32 | loop fusion | flops 768 | bytes 2048 | tf_op jit(solution)/shard_map/convert_element_type | solution.py:230
  10.5 0.6 %broadcast_in_dim.38.e_ref = f32[8,256]{1,0:T(8,128)} broadcast(f32[256]{0:T(256)S(1)} %add_convert_fusion), dimensions={1} | broadcast | bytes 9216 | tf_op jit(solution)/shard_map/broadcast_in_dim | solution.py:231
  11.1 0.0 copy-done.2
  11.1 14.1 %shard_map.55 = (f32[128,4096]{1,0:T(8,128)}, f32[128,4096]{1,0:T(8,128)}, f32[16,4224]{1,0:T(8,128)}, f32[4,16,4096]{2,1,0:T(8,128)}, f32[128,128]{1,0:T(8,128)}) custom-call(bf16[128,12288]{1,0:T(8,128)(2,1)} %xv.1, bf16[128,12288]{1,0:T(8,128)(2,1)} %xv.1, bf16[128,12288]{1,0:T(8,128)(2,1)} %xv.1, bf16[8,12416]{1,0:T(8,128)(2,1)} %copy-done.2, ...), custom_call_target="tpu_custom_call" | custom-call | tf_op jit(solution)/shard_map/pallas_call | solution.py:242
  25.3 0.0 copy-start
  25.3 0.1 collective-permute-start.1
  25.4 1.3 %fusion.12 = (f32[1,16,4096]{2,1,0:T(8,128)S(1)}, f32[1,16,4096]{2,1,0:T(8,128)S(1)}, f32[1,16,4096]{2,1,0:T(8,128)S(1)}, f32[1,16,4096]{2,1,0:T(8,128)S(1)}) fusion(f32[4,16,4096]{2,1,0:T(8,128)} %get-tuple-element.13.d1_ref), kind=kLoop, calls=%fused_computation.34 | loop fusion | bytes 2097152 | tf_op jit(solution)/shard_map/slice | solution.py:189
  26.6 0.0 copy-done
  26.6 0.0 copy-start.5
  26.7 0.0 copy-start.6
  26.7 0.4 collective-permute-done.1.gt_ref.gf_ref
  27.1 0.1 fusion.11
  27.2 0.1 fusion.8
  27.3 0.1 broadcast_in_dim.40
  27.4 2.5 %collective-permute-start.2 = (f32[16,2176]{1,0:T(8,128)S(1)}, f32[16,2176]{1,0:T(8,128)S(1)}, u32[]{:S(2)}, u32[]{:S(2)}) collective-permute-start(f32[16,2176]{1,0:T(8,128)S(1)} %pad_maximum_fusion.1), channel_id=1, source_target_pairs={{0,2},{1,3},{2,4},{3,5},{4,6},{5,7},{6,8},{7,9},{8,10},{9,11},{10,... | collective-permute-start | bytes 417800 | tf_op jit(solution)/shard_map/ppermute | solution.py:20
  29.9 6.0 %collective-permute-done.2 = f32[16,2176]{1,0:T(8,128)S(1)} collective-permute-done((f32[16,2176]{1,0:T(8,128)S(1)}, f32[16,2176]{1,0:T(8,128)S(1)}, u32[]{:S(2)}, u32[]{:S(2)}) %collective-permute-start.2) | collective-permute-done | bytes 139296 | tf_op jit(solution)/shard_map/ppermute | solution.py:20
  35.9 0.1 fusion.6
  36.0 0.1 slice_reduce_fusion
  36.1 0.1 broadcast_in_dim.42
  36.2 1.3 %collective-permute-start.3 = (f32[16,2176]{1,0:T(8,128)S(1)}, f32[16,2176]{1,0:T(8,128)S(1)}, u32[]{:S(2)}, u32[]{:S(2)}) collective-permute-start(f32[16,2176]{1,0:T(8,128)S(1)} %pad_maximum_fusion.2), channel_id=1, source_target_pairs={{0,4},{1,5},{2,6},{3,7},{4,8},{5,9},{6,10},{7,11},{8,12},{9,13},{1... | collective-permute-start | bytes 417800 | tf_op jit(solution)/shard_map/ppermute | solution.py:20
  37.5 5.6 %collective-permute-done.3 = f32[16,2176]{1,0:T(8,128)S(1)} collective-permute-done((f32[16,2176]{1,0:T(8,128)S(1)}, f32[16,2176]{1,0:T(8,128)S(1)}, u32[]{:S(2)}, u32[]{:S(2)}) %collective-permute-start.3) | collective-permute-done | bytes 139296 | tf_op jit(solution)/shard_map/ppermute | solution.py:20
  43.2 0.1 multiply_reduce_fusion.1
  43.3 0.1 fusion.2
  43.4 0.1 broadcast_in_dim.44
  43.5 1.3 %collective-permute-start.4 = (f32[16,2176]{1,0:T(8,128)S(1)}, f32[16,2176]{1,0:T(8,128)S(1)}, u32[]{:S(2)}, u32[]{:S(2)}) collective-permute-start(f32[16,2176]{1,0:T(8,128)S(1)} %pad_maximum_fusion.3), channel_id=1, source_target_pairs={{0,8},{1,9},{2,10},{3,11},{4,12},{5,13},{6,14},{7,15},{16,24},{17,... | collective-permute-start | bytes 417800 | tf_op jit(solution)/shard_map/ppermute | solution.py:20
  44.8 0.1 copy.10
  44.9 0.1 copy.11
  45.0 0.1 stack.21
  45.1 0.1 stack.22
  45.2 7.6 %collective-permute-done.4 = f32[16,2176]{1,0:T(8,128)S(1)} collective-permute-done((f32[16,2176]{1,0:T(8,128)S(1)}, f32[16,2176]{1,0:T(8,128)S(1)}, u32[]{:S(2)}, u32[]{:S(2)}) %collective-permute-start.4) | collective-permute-done | bytes 139296 | tf_op jit(solution)/shard_map/ppermute | solution.py:20
  52.9 0.1 fusion.zo_ref
  53.0 0.0 copy-done.1
  53.0 0.0 copy-start.3
  53.0 0.1 collective-permute-start.5
  53.1 0.6 %pad_maximum_fusion.4.rr_ref = f32[2,1,4096]{2,1,0:T(1,128)} fusion(f32[1,1,4096]{2,1,0:T(1,128)S(1)} %stack.22, f32[1,1,4096]{2,1,0:T(1,128)S(1)} %stack.21), kind=kLoop, calls=%fused_computation.22 | loop fusion | flops 8192 | bytes 65536 | tf_op jit(solution)/shard_map/stack | solution.py:233
  53.7 0.7 %collective-permute-done.5.zp_ref = f32[16,2048]{1,0:T(8,128)S(1)} collective-permute-done((f32[16,2048]{1,0:T(8,128)S(1)}, f32[16,2048]{1,0:T(8,128)S(1)}, u32[]{:S(2)}, u32[]{:S(2)}) %collective-permute-start.5) | collective-permute-done | bytes 131104 | tf_op jit(solution)/shard_map/ppermute | solution.py:161
  54.4 0.6 %copy-done.4 = f32[16,2048]{1,0:T(8,128)} copy-done((f32[16,2048]{1,0:T(8,128)}, f32[16,2048]{1,0:T(8,128)S(1)}, u32[]{:S(2)}) %copy-start.4) | copy-done | bytes 131096
  55.0 4.6 %shard_map.56 = bf16[128,4096]{1,0:T(8,128)(2,1)} custom-call(f32[128,4096]{1,0:T(8,128)} %get-tuple-element.10.q_ref, f32[128,4096]{1,0:T(8,128)} %get-tuple-element.11.loc_ref, f32[16,2048]{1,0:T(8,128)} %copy-done.3, f32[16,2048]{1,0:T(8,128)} %copy-done.4, f32[16,4224]{1,0:T(8,128)} %get-tuple-element.12.pk_ref.pf_ref, f32[16,4224]{1,0:T(8,128)} %copy-done.1, ...), custom_call_target="tpu_custom_call" | custom-call | tf_op jit(solution)/shard_map/pallas_call | solution.py:290
  (16 shorter events, 0.2 us)
Async XLA Ops:
  1.8 7.9 %collective-permute-start = (bf16[8,12416]{1,0:T(8,128)(2,1)S(1)}, bf16[8,12416]{1,0:T(8,128)(2,1)S(1)}, u32[]{:S(2)}, u32[]{:S(2)}) collective-permute-start(bf16[8,12416]{1,0:T(8,128)(2,1)S(1)} %pad_maximum_fusion), channel_id=1, source_target_pairs={{0,1},{1,2},{2,3},{3,4},{4,5},{5,6},{6,7},{7,8},{8,9},{9,10},{10,1... | collective-permute-start | bytes 595976 | tf_op jit(solution)/shard_map/ppermute | solution.py:20
  9.7 1.5 %copy-start.2 = (bf16[8,12416]{1,0:T(8,128)(2,1)}, bf16[8,12416]{1,0:T(8,128)(2,1)S(1)}, u32[]{:S(2)}) copy-start(bf16[8,12416]{1,0:T(8,128)(2,1)S(1)} %collective-permute-done.rq.rk.rv) | copy-start | bytes 595972
  25.3 1.4 %copy-start = (f32[16,4224]{1,0:T(8,128)S(1)}, f32[16,4224]{1,0:T(8,128)}, u32[]{:S(2)}) copy-start(f32[16,4224]{1,0:T(8,128)} %get-tuple-element.12.pk_ref.pf_ref) | copy-start | bytes 811012
  25.3 1.8 %collective-permute-start.1 = (f32[16,4224]{1,0:T(8,128)}, f32[16,4224]{1,0:T(8,128)S(1)}, u32[]{:S(2)}, u32[]{:S(2)}) collective-permute-start(f32[16,4224]{1,0:T(8,128)} %get-tuple-element.12.pk_ref.pf_ref), channel_id=1, source_target_pairs={{0,1},{1,0},{2,3},{3,2},{4,5},{5,4},{6,7},{7,6},{8,9},{9,8},{10,11... | collective-permute-start | bytes 811016 | tf_op jit(solution)/shard_map/ppermute | solution.py:161
  26.6 18.2 %copy-start.5 = (f32[256,16]{0,1:T(8,128)S(1)}, f32[256,16]{0,1:T(8,128)}, u32[]{:S(2)}) copy-start(f32[256,16]{0,1:T(8,128)} %param.8) | copy-start | bytes 49156
  26.7 18.3 %copy-start.6 = (f32[256,16]{0,1:T(8,128)S(1)}, f32[256,16]{0,1:T(8,128)}, u32[]{:S(2)}) copy-start(f32[256,16]{0,1:T(8,128)} %param.9) | copy-start | bytes 49156
  27.1 25.8 %copy-start.1 = (f32[16,4224]{1,0:T(8,128)}, f32[16,4224]{1,0:T(8,128)S(1)}, u32[]{:S(2)}) copy-start(f32[16,4224]{1,0:T(8,128)S(1)} %collective-permute-done.1.gt_ref.gf_ref) | copy-start | bytes 811012
  27.4 8.5 %collective-permute-start.2 = (f32[16,2176]{1,0:T(8,128)S(1)}, f32[16,2176]{1,0:T(8,128)S(1)}, u32[]{:S(2)}, u32[]{:S(2)}) collective-permute-start(f32[16,2176]{1,0:T(8,128)S(1)} %pad_maximum_fusion.1), channel_id=1, source_target_pairs={{0,2},{1,3},{2,4},{3,5},{4,6},{5,7},{6,8},{7,9},{8,10},{9,11},{10,... | collective-permute-start | bytes 417800 | tf_op jit(solution)/shard_map/ppermute | solution.py:20
  36.2 6.9 %collective-permute-start.3 = (f32[16,2176]{1,0:T(8,128)S(1)}, f32[16,2176]{1,0:T(8,128)S(1)}, u32[]{:S(2)}, u32[]{:S(2)}) collective-permute-start(f32[16,2176]{1,0:T(8,128)S(1)} %pad_maximum_fusion.2), channel_id=1, source_target_pairs={{0,4},{1,5},{2,6},{3,7},{4,8},{5,9},{6,10},{7,11},{8,12},{9,13},{1... | collective-permute-start | bytes 417800 | tf_op jit(solution)/shard_map/ppermute | solution.py:20
  43.5 9.4 %collective-permute-start.4 = (f32[16,2176]{1,0:T(8,128)S(1)}, f32[16,2176]{1,0:T(8,128)S(1)}, u32[]{:S(2)}, u32[]{:S(2)}) collective-permute-start(f32[16,2176]{1,0:T(8,128)S(1)} %pad_maximum_fusion.3), channel_id=1, source_target_pairs={{0,8},{1,9},{2,10},{3,11},{4,12},{5,13},{6,14},{7,15},{16,24},{17,... | collective-permute-start | bytes 417800 | tf_op jit(solution)/shard_map/ppermute | solution.py:20
  53.0 1.4 %copy-start.3 = (f32[16,2048]{1,0:T(8,128)}, f32[16,2048]{1,0:T(8,128)S(1)}, u32[]{:S(2)}) copy-start(f32[16,2048]{1,0:T(8,128)S(1)} %fusion.zo_ref) | copy-start | bytes 393220
  53.0 1.4 %collective-permute-start.5 = (f32[16,2048]{1,0:T(8,128)S(1)}, f32[16,2048]{1,0:T(8,128)S(1)}, u32[]{:S(2)}, u32[]{:S(2)}) collective-permute-start(f32[16,2048]{1,0:T(8,128)S(1)} %fusion.zo_ref), channel_id=1, source_target_pairs={{0,1},{1,0},{2,3},{3,2},{4,5},{5,4},{6,7},{7,6},{8,9},{9,8},{10,11... | collective-permute-start | bytes 393224 | tf_op jit(solution)/shard_map/ppermute | solution.py:161
  54.4 0.7 %copy-start.4 = (f32[16,2048]{1,0:T(8,128)}, f32[16,2048]{1,0:T(8,128)S(1)}, u32[]{:S(2)}) copy-start(f32[16,2048]{1,0:T(8,128)S(1)} %collective-permute-done.5.zp_ref) | copy-start | bytes 393220

commit v15 on v14

--- a/solution.py
+++ b/solution.py
@@ -7,7 +7,7 @@
 from jax.experimental.pallas import tpu as pltpu
 from jax.sharding import PartitionSpec as P
 
-WIDTH = 512
+WIDTH = 1024
 FINAL_WIDTH = 2048
 RIM = 8
 SUB = 256

time: 60.3 us -> 59.3 us (0.983)
  Pallas kernels: 18.7 us -> 17.7 us
    pallas_call x1, Pallas kernels: 14.1 us -> 13.1 us  [on_device(): pl.pallas_call(functools.partial(local_kernel, taps, group_width, spans),...]
where the time goes in v15:
time: 59.3 us; the launch traced here: 58.6 us
  waiting for transfers between devices  24.1 us (41%)
  Pallas kernels  17.7 us (30%)
  starting transfers between devices  7.17 us (12%)
  local copies, waits for them, and re-layouts  6.54 us (11%)
  other arithmetic  2.93 us (5%)
    ppermute x4, waiting for transfers between devices, from_behind(): return lax.ppermute(shard, axis, pairs)  22.9 us
    pallas_call x1, Pallas kernels, on_device(): pl.pallas_call(functools.partial(local_kernel, taps, group_width, spans),...  13.1 us
    ppermute x4, starting transfers between devices, from_behind(): return lax.ppermute(shard, axis, pairs)  7.03 us
    pallas_call x1, Pallas kernels, on_device(): pl.pallas_call(functools.partial(final_kernel, group_width, pole_count, m...  4.58 us
    another operation x6, local copies, waits for them, and re-layouts, on_device(): jnp.stack([rates, residues]).reshape(2, nb, gpb, pole_count)  1.83 us
    slice x1, local copies, waits for them, and re-layouts, chip_scan(): prefix = prefix + prefix_flag * mine(decays[span_of[2 * offset - 2]]) * came  1.26 us
  transfers between devices with their start and end apart: 6, of which 6 were waited for; matrix products, arithmetic and copies ran while one was open for 8% of the time, Pallas kernels for 0%

profile of v15, /device:TPU:24, one launch (start us, length us, event | category | flops | bytes accessed | tf_op | source)
XLA Modules:
  0.0 58.6 jit_solution(3014059041213214732)
XLA Ops:
  0.0 0.9 %slice.56 = bf16[8,12288]{1,0:T(8,128)(2,1)S(1)} slice(bf16[128,12288]{1,0:T(8,128)(2,1)} %xv.1), slice={[120:128], [0:12288]} | slice | bytes 393216 | tf_op jit(solution)/shard_map/slice | solution.py:225
  0.9 0.7 %convert.4 = bf16[128]{0:T(256)(128)(2,1)S(1)} convert(s32[128]{0:T(128)} %param.6) | non-fusion elementwise | flops 128 | bytes 768 | tf_op jit(solution)/shard_map/convert.1
  1.6 0.1 slice.57
  1.7 0.1 broadcast_in_dim.36
  1.8 1.9 %collective-permute-start = (bf16[8,12416]{1,0:T(8,128)(2,1)S(1)}, bf16[8,12416]{1,0:T(8,128)(2,1)S(1)}, u32[]{:S(2)}, u32[]{:S(2)}) collective-permute-start(bf16[8,12416]{1,0:T(8,128)(2,1)S(1)} %pad_maximum_fusion), channel_id=1, source_target_pairs={{0,1},{1,2},{2,3},{3,4},{4,5},{5,6},{6,7},{7,8},{8,9},{9,10},{10,1... | collective-permute-start | bytes 595976 | tf_op jit(solution)/shard_map/ppermute | solution.py:20
  3.7 0.8 %stack.18 = f32[1,4,64,16]{2,1,3,0:T(4,128)S(1)} reshape(f32[256,16]{0,1:T(8,128)} %param.8) | data formatting | bytes 32768 | tf_op jit(solution)/shard_map/stack | solution.py:233
  4.5 0.8 %stack.19 = f32[1,4,64,16]{2,1,3,0:T(4,128)S(1)} reshape(f32[256,16]{0,1:T(8,128)} %param.9) | data formatting | bytes 32768 | tf_op jit(solution)/shard_map/stack | solution.py:233
  5.4 0.6 %slice_bitcast_fusion = (f32[4,16,64]{2,1,0:T(8,128)}, f32[4,16,64]{2,1,0:T(8,128)}) fusion(f32[2,4,16,64]{3,2,1,0:T(8,128)S(1)} %maximum_bitcast_fusion), kind=kLoop, calls=%fused_computation.20 | loop fusion | bytes 65536 | tf_op jit(solution)/shard_map/squeeze | solution.py:234
  6.0 3.7 %collective-permute-done.rq.rk.rv = bf16[8,12416]{1,0:T(8,128)(2,1)S(1)} collective-permute-done((bf16[8,12416]{1,0:T(8,128)(2,1)S(1)}, bf16[8,12416]{1,0:T(8,128)(2,1)S(1)}, u32[]{:S(2)}, u32[]{:S(2)}) %collective-permute-start) | collective-permute-done | bytes 198688 | tf_op jit(solution)/shard_map/ppermute | solution.py:20
  9.7 0.1 convert_reduce_fusion
  9.8 0.7 %add_convert_fusion = f32[256]{0:T(256)S(1)} fusion(s32[120]{0:T(128)S(1)} %broadcast_in_dim.37, s32[8]{0:T(128)S(1)} %convert_reduce_fusion, s32[128]{0:T(128)} %param.6), kind=kLoop, calls=%fused_computation.32 | loop fusion | flops 768 | bytes 2048 | tf_op jit(solution)/shard_map/convert_element_type | solution.py:230
  10.5 0.6 %broadcast_in_dim.38.e_ref = f32[8,256]{1,0:T(8,128)} broadcast(f32[256]{0:T(256)S(1)} %add_convert_fusion), dimensions={1} | broadcast | bytes 9216 | tf_op jit(solution)/shard_map/broadcast_in_dim | solution.py:231
  11.1 0.0 copy-done.2
  11.1 13.1 %shard_map.55 = (f32[128,4096]{1,0:T(8,128)}, f32[128,4096]{1,0:T(8,128)}, f32[16,4224]{1,0:T(8,128)}, f32[4,16,4096]{2,1,0:T(8,128)}, f32[128,128]{1,0:T(8,128)}) custom-call(bf16[128,12288]{1,0:T(8,128)(2,1)} %xv.1, bf16[128,12288]{1,0:T(8,128)(2,1)} %xv.1, bf16[128,12288]{1,0:T(8,128)(2,1)} %xv.1, bf16[8,12416]{1,0:T(8,128)(2,1)} %copy-done.2, ...), custom_call_target="tpu_custom_call" | custom-call | tf_op jit(solution)/shard_map/pallas_call | solution.py:242
  24.2 0.0 copy-start
  24.2 0.1 collective-permute-start.1
  24.3 1.3 %fusion.12 = (f32[1,16,4096]{2,1,0:T(8,128)S(1)}, f32[1,16,4096]{2,1,0:T(8,128)S(1)}, f32[1,16,4096]{2,1,0:T(8,128)S(1)}, f32[1,16,4096]{2,1,0:T(8,128)S(1)}) fusion(f32[4,16,4096]{2,1,0:T(8,128)} %get-tuple-element.13.d1_ref), kind=kLoop, calls=%fused_computation.34 | loop fusion | bytes 2097152 | tf_op jit(solution)/shard_map/slice | solution.py:189
  25.6 0.0 copy-done
  25.6 0.0 copy-start.5
  25.6 0.0 copy-start.6
  25.6 0.4 collective-permute-done.1.gt_ref.gf_ref
  26.1 0.1 fusion.11
  26.2 0.1 fusion.8
  26.3 0.1 broadcast_in_dim.40
  26.4 2.5 %collective-permute-start.2 = (f32[16,2176]{1,0:T(8,128)S(1)}, f32[16,2176]{1,0:T(8,128)S(1)}, u32[]{:S(2)}, u32[]{:S(2)}) collective-permute-start(f32[16,2176]{1,0:T(8,128)S(1)} %pad_maximum_fusion.1), channel_id=1, source_target_pairs={{0,2},{1,3},{2,4},{3,5},{4,6},{5,7},{6,8},{7,9},{8,10},{9,11},{10,... | collective-permute-start | bytes 417800 | tf_op jit(solution)/shard_map/ppermute | solution.py:20
  28.9 6.0 %collective-permute-done.2 = f32[16,2176]{1,0:T(8,128)S(1)} collective-permute-done((f32[16,2176]{1,0:T(8,128)S(1)}, f32[16,2176]{1,0:T(8,128)S(1)}, u32[]{:S(2)}, u32[]{:S(2)}) %collective-permute-start.2) | collective-permute-done | bytes 139296 | tf_op jit(solution)/shard_map/ppermute | solution.py:20
  34.9 0.1 fusion.6
  35.0 0.1 slice_reduce_fusion
  35.1 0.1 broadcast_in_dim.42
  35.2 1.3 %collective-permute-start.3 = (f32[16,2176]{1,0:T(8,128)S(1)}, f32[16,2176]{1,0:T(8,128)S(1)}, u32[]{:S(2)}, u32[]{:S(2)}) collective-permute-start(f32[16,2176]{1,0:T(8,128)S(1)} %pad_maximum_fusion.2), channel_id=1, source_target_pairs={{0,4},{1,5},{2,6},{3,7},{4,8},{5,9},{6,10},{7,11},{8,12},{9,13},{1... | collective-permute-start | bytes 417800 | tf_op jit(solution)/shard_map/ppermute | solution.py:20
  36.5 5.6 %collective-permute-done.3 = f32[16,2176]{1,0:T(8,128)S(1)} collective-permute-done((f32[16,2176]{1,0:T(8,128)S(1)}, f32[16,2176]{1,0:T(8,128)S(1)}, u32[]{:S(2)}, u32[]{:S(2)}) %collective-permute-start.3) | collective-permute-done | bytes 139296 | tf_op jit(solution)/shard_map/ppermute | solution.py:20
  42.1 0.1 multiply_reduce_fusion.1
  42.3 0.1 fusion.2
  42.4 0.1 broadcast_in_dim.44
  42.4 1.3 %collective-permute-start.4 = (f32[16,2176]{1,0:T(8,128)S(1)}, f32[16,2176]{1,0:T(8,128)S(1)}, u32[]{:S(2)}, u32[]{:S(2)}) collective-permute-start(f32[16,2176]{1,0:T(8,128)S(1)} %pad_maximum_fusion.3), channel_id=1, source_target_pairs={{0,8},{1,9},{2,10},{3,11},{4,12},{5,13},{6,14},{7,15},{16,24},{17,... | collective-permute-start | bytes 417800 | tf_op jit(solution)/shard_map/ppermute | solution.py:20
  43.7 0.0 copy-done.5
  43.8 0.1 copy.10
  43.9 0.0 copy-done.6
  43.9 0.1 copy.11
  44.0 0.1 stack.21
  44.1 0.1 stack.22
  44.2 7.6 %collective-permute-done.4 = f32[16,2176]{1,0:T(8,128)S(1)} collective-permute-done((f32[16,2176]{1,0:T(8,128)S(1)}, f32[16,2176]{1,0:T(8,128)S(1)}, u32[]{:S(2)}, u32[]{:S(2)}) %collective-permute-start.4) | collective-permute-done | bytes 139296 | tf_op jit(solution)/shard_map/ppermute | solution.py:20
  51.8 0.1 fusion.zo_ref
  52.0 0.1 collective-permute-start.5
  52.0 0.6 %pad_maximum_fusion.4.rr_ref = f32[2,1,4096]{2,1,0:T(1,128)} fusion(f32[1,1,4096]{2,1,0:T(1,128)S(1)} %stack.22, f32[1,1,4096]{2,1,0:T(1,128)S(1)} %stack.21), kind=kLoop, calls=%fused_computation.22 | loop fusion | flops 8192 | bytes 65536 | tf_op jit(solution)/shard_map/stack | solution.py:233
  52.7 0.7 %collective-permute-done.5.zp_ref = f32[16,2048]{1,0:T(8,128)S(1)} collective-permute-done((f32[16,2048]{1,0:T(8,128)S(1)}, f32[16,2048]{1,0:T(8,128)S(1)}, u32[]{:S(2)}, u32[]{:S(2)}) %collective-permute-start.5) | collective-permute-done | bytes 131104 | tf_op jit(solution)/shard_map/ppermute | solution.py:161
  53.4 0.6 %copy-done.4 = f32[16,2048]{1,0:T(8,128)} copy-done((f32[16,2048]{1,0:T(8,128)}, f32[16,2048]{1,0:T(8,128)S(1)}, u32[]{:S(2)}) %copy-start.4) | copy-done | bytes 131096
  54.0 4.6 %shard_map.56 = bf16[128,4096]{1,0:T(8,128)(2,1)} custom-call(f32[128,4096]{1,0:T(8,128)} %get-tuple-element.10.q_ref, f32[128,4096]{1,0:T(8,128)} %get-tuple-element.11.loc_ref, f32[16,2048]{1,0:T(8,128)} %copy-done.3, f32[16,2048]{1,0:T(8,128)} %copy-done.4, f32[16,4224]{1,0:T(8,128)} %get-tuple-element.12.pk_ref.pf_ref, f32[16,4224]{1,0:T(8,128)} %copy-done.1, ...), custom_call_target="tpu_custom_call" | custom-call | tf_op jit(solution)/shard_map/pallas_call | solution.py:290
  (16 shorter events, 0.1 us)
Async XLA Ops:
  1.8 7.9 %collective-permute-start = (bf16[8,12416]{1,0:T(8,128)(2,1)S(1)}, bf16[8,12416]{1,0:T(8,128)(2,1)S(1)}, u32[]{:S(2)}, u32[]{:S(2)}) collective-permute-start(bf16[8,12416]{1,0:T(8,128)(2,1)S(1)} %pad_maximum_fusion), channel_id=1, source_target_pairs={{0,1},{1,2},{2,3},{3,4},{4,5},{5,6},{6,7},{7,8},{8,9},{9,10},{10,1... | collective-permute-start | bytes 595976 | tf_op jit(solution)/shard_map/ppermute | solution.py:20
  9.7 1.5 %copy-start.2 = (bf16[8,12416]{1,0:T(8,128)(2,1)}, bf16[8,12416]{1,0:T(8,128)(2,1)S(1)}, u32[]{:S(2)}) copy-start(bf16[8,12416]{1,0:T(8,128)(2,1)S(1)} %collective-permute-done.rq.rk.rv) | copy-start | bytes 595972
  24.2 1.4 %copy-start = (f32[16,4224]{1,0:T(8,128)S(1)}, f32[16,4224]{1,0:T(8,128)}, u32[]{:S(2)}) copy-start(f32[16,4224]{1,0:T(8,128)} %get-tuple-element.12.pk_ref.pf_ref) | copy-start | bytes 811012
  24.2 1.8 %collective-permute-start.1 = (f32[16,4224]{1,0:T(8,128)}, f32[16,4224]{1,0:T(8,128)S(1)}, u32[]{:S(2)}, u32[]{:S(2)}) collective-permute-start(f32[16,4224]{1,0:T(8,128)} %get-tuple-element.12.pk_ref.pf_ref), channel_id=1, source_target_pairs={{0,1},{1,0},{2,3},{3,2},{4,5},{5,4},{6,7},{7,6},{8,9},{9,8},{10,11... | collective-permute-start | bytes 811016 | tf_op jit(solution)/shard_map/ppermute | solution.py:161
  25.6 18.2 %copy-start.5 = (f32[256,16]{0,1:T(8,128)S(1)}, f32[256,16]{0,1:T(8,128)}, u32[]{:S(2)}) copy-start(f32[256,16]{0,1:T(8,128)} %param.8) | copy-start | bytes 49156
  25.6 18.3 %copy-start.6 = (f32[256,16]{0,1:T(8,128)S(1)}, f32[256,16]{0,1:T(8,128)}, u32[]{:S(2)}) copy-start(f32[256,16]{0,1:T(8,128)} %param.9) | copy-start | bytes 49156
  26.1 25.9 %copy-start.1 = (f32[16,4224]{1,0:T(8,128)}, f32[16,4224]{1,0:T(8,128)S(1)}, u32[]{:S(2)}) copy-start(f32[16,4224]{1,0:T(8,128)S(1)} %collective-permute-done.1.gt_ref.gf_ref) | copy-start | bytes 811012
  26.4 8.5 %collective-permute-start.2 = (f32[16,2176]{1,0:T(8,128)S(1)}, f32[16,2176]{1,0:T(8,128)S(1)}, u32[]{:S(2)}, u32[]{:S(2)}) collective-permute-start(f32[16,2176]{1,0:T(8,128)S(1)} %pad_maximum_fusion.1), channel_id=1, source_target_pairs={{0,2},{1,3},{2,4},{3,5},{4,6},{5,7},{6,8},{7,9},{8,10},{9,11},{10,... | collective-permute-start | bytes 417800 | tf_op jit(solution)/shard_map/ppermute | solution.py:20
  35.2 6.9 %collective-permute-start.3 = (f32[16,2176]{1,0:T(8,128)S(1)}, f32[16,2176]{1,0:T(8,128)S(1)}, u32[]{:S(2)}, u32[]{:S(2)}) collective-permute-start(f32[16,2176]{1,0:T(8,128)S(1)} %pad_maximum_fusion.2), channel_id=1, source_target_pairs={{0,4},{1,5},{2,6},{3,7},{4,8},{5,9},{6,10},{7,11},{8,12},{9,13},{1... | collective-permute-start | bytes 417800 | tf_op jit(solution)/shard_map/ppermute | solution.py:20
  42.4 9.4 %collective-permute-start.4 = (f32[16,2176]{1,0:T(8,128)S(1)}, f32[16,2176]{1,0:T(8,128)S(1)}, u32[]{:S(2)}, u32[]{:S(2)}) collective-permute-start(f32[16,2176]{1,0:T(8,128)S(1)} %pad_maximum_fusion.3), channel_id=1, source_target_pairs={{0,8},{1,9},{2,10},{3,11},{4,12},{5,13},{6,14},{7,15},{16,24},{17,... | collective-permute-start | bytes 417800 | tf_op jit(solution)/shard_map/ppermute | solution.py:20
  51.9 1.4 %copy-start.3 = (f32[16,2048]{1,0:T(8,128)}, f32[16,2048]{1,0:T(8,128)S(1)}, u32[]{:S(2)}) copy-start(f32[16,2048]{1,0:T(8,128)S(1)} %fusion.zo_ref) | copy-start | bytes 393220
  52.0 1.4 %collective-permute-start.5 = (f32[16,2048]{1,0:T(8,128)S(1)}, f32[16,2048]{1,0:T(8,128)S(1)}, u32[]{:S(2)}, u32[]{:S(2)}) collective-permute-start(f32[16,2048]{1,0:T(8,128)S(1)} %fusion.zo_ref), channel_id=1, source_target_pairs={{0,1},{1,0},{2,3},{3,2},{4,5},{5,4},{6,7},{7,6},{8,9},{9,8},{10,11... | collective-permute-start | bytes 393224 | tf_op jit(solution)/shard_map/ppermute | solution.py:161
  53.4 0.7 %copy-start.4 = (f32[16,2048]{1,0:T(8,128)}, f32[16,2048]{1,0:T(8,128)S(1)}, u32[]{:S(2)}) copy-start(f32[16,2048]{1,0:T(8,128)S(1)} %collective-permute-done.5.zp_ref) | copy-start | bytes 393220

commit v16 on v15

--- a/solution.py
+++ b/solution.py
@@ -228,7 +228,7 @@
 
     span_r = 2 * LANES
     e_vec = jnp.concatenate([doc_ids, prev_docs, jnp.full((span_r - length - RIM,), -1, jnp.int32)]).astype(jnp.float32)
-    e_rows = jnp.broadcast_to(e_vec[None, :], (8, span_r))
+    e_rows = e_vec.reshape(1, span_r)
 
     both_t = jnp.stack([rates, residues]).reshape(2, nb, gpb, pole_count).transpose(0, 1, 3, 2)
     rates_t, residues_t = both_t[0], both_t[1]
@@ -252,7 +252,7 @@
             pl.BlockSpec((taps, width), col(0)),
             pl.BlockSpec((taps, width), col(nb)),
             pl.BlockSpec((taps, width), col(2 * nb)),
-            pl.BlockSpec((8, span_r), fixed),
+            pl.BlockSpec((1, span_r), fixed),
             pl.BlockSpec((1, pole_count, gpb), lambda j: (j, 0, 0)),
             pl.BlockSpec((1, pole_count, gpb), lambda j: (j, 0, 0)),
         ],

time: 59.3 us -> 59.3 us (level)
    broadcast_in_dim x1 -> x0, local copies, waits for them, and re-layouts: 0.6 us -> none  [on_device(): e_rows = jnp.broadcast_to(e_vec[None, :], (8, span_r))]
where the time goes in v16:
time: 59.3 us; the launch traced here: 58.6 us
  waiting for transfers between devices  24 us (40%)
  Pallas kernels  17.7 us (30%)
  starting transfers between devices  7.16 us (12%)
  local copies, waits for them, and re-layouts  6.02 us (10%)
  other arithmetic  3.45 us (6%)
    ppermute x4, waiting for transfers between devices, from_behind(): return lax.ppermute(shard, axis, pairs)  22.8 us
    pallas_call x1, Pallas kernels, on_device(): pl.pallas_call(functools.partial(local_kernel, taps, group_width, spans),...  13.1 us
    ppermute x4, starting transfers between devices, from_behind(): return lax.ppermute(shard, axis, pairs)  7.01 us
    pallas_call x1, Pallas kernels, on_device(): pl.pallas_call(functools.partial(final_kernel, group_width, pole_count, m...  4.58 us
    another operation x6, local copies, waits for them, and re-layouts, on_device(): jnp.stack([rates, residues]).reshape(2, nb, gpb, pole_count)  1.83 us
    slice x1, local copies, waits for them, and re-layouts, chip_scan(): prefix = prefix + prefix_flag * mine(decays[span_of[2 * offset - 2]]) * came  1.26 us
    convert_element_type x1, other arithmetic, on_device(): jnp.concatenate([doc_ids, prev_docs, jnp.full((span_r - length - RIM,), -...  1.25 us
  transfers between devices with their start and end apart: 6, of which 6 were waited for; matrix products, arithmetic and copies ran while one was open for 8% of the time, Pallas kernels for 0%

profile of v16, /device:TPU:24, one launch (start us, length us, event | category | flops | bytes accessed | tf_op | source)
XLA Modules:
  0.0 58.6 jit_solution(3391389202657837971)
XLA Ops:
  0.0 0.9 %slice.56 = bf16[8,12288]{1,0:T(8,128)(2,1)S(1)} slice(bf16[128,12288]{1,0:T(8,128)(2,1)} %xv.1), slice={[120:128], [0:12288]} | slice | bytes 393216 | tf_op jit(solution)/shard_map/slice | solution.py:225
  0.9 0.7 %convert.4 = bf16[128]{0:T(256)(128)(2,1)S(1)} convert(s32[128]{0:T(128)} %param.6) | non-fusion elementwise | flops 128 | bytes 768 | tf_op jit(solution)/shard_map/convert.1
  1.6 0.1 slice.57
  1.7 0.1 broadcast_in_dim.30
  1.8 1.9 %collective-permute-start = (bf16[8,12416]{1,0:T(8,128)(2,1)S(1)}, bf16[8,12416]{1,0:T(8,128)(2,1)S(1)}, u32[]{:S(2)}, u32[]{:S(2)}) collective-permute-start(bf16[8,12416]{1,0:T(8,128)(2,1)S(1)} %pad_maximum_fusion), channel_id=1, source_target_pairs={{0,1},{1,2},{2,3},{3,4},{4,5},{5,6},{6,7},{7,8},{8,9},{9,10},{10,1... | collective-permute-start | bytes 595976 | tf_op jit(solution)/shard_map/ppermute | solution.py:20
  3.7 0.1 pad.12.clone
  3.8 0.8 %stack.18 = f32[1,4,64,16]{2,1,3,0:T(4,128)S(1)} reshape(f32[256,16]{0,1:T(8,128)} %param.8) | data formatting | bytes 32768 | tf_op jit(solution)/shard_map/stack | solution.py:233
  4.6 0.8 %stack.19 = f32[1,4,64,16]{2,1,3,0:T(4,128)S(1)} reshape(f32[256,16]{0,1:T(8,128)} %param.9) | data formatting | bytes 32768 | tf_op jit(solution)/shard_map/stack | solution.py:233
  5.5 0.6 %slice_bitcast_fusion = (f32[4,16,64]{2,1,0:T(8,128)}, f32[4,16,64]{2,1,0:T(8,128)}) fusion(f32[2,4,16,64]{3,2,1,0:T(8,128)S(1)} %maximum_bitcast_fusion), kind=kLoop, calls=%fused_computation.20 | loop fusion | bytes 65536 | tf_op jit(solution)/shard_map/squeeze | solution.py:234
  6.1 3.6 %collective-permute-done.rq.rk.rv = bf16[8,12416]{1,0:T(8,128)(2,1)S(1)} collective-permute-done((bf16[8,12416]{1,0:T(8,128)(2,1)S(1)}, bf16[8,12416]{1,0:T(8,128)(2,1)S(1)}, u32[]{:S(2)}, u32[]{:S(2)}) %collective-permute-start) | collective-permute-done | bytes 198688 | tf_op jit(solution)/shard_map/ppermute | solution.py:20
  9.7 0.1 convert_reduce_fusion
  9.8 1.3 %add_convert_fusion.e_ref = f32[1,256]{1,0:T(1,128)} fusion(s32[1,256]{1,0:T(1,128)S(1)} %bitcast.42, s32[1,8]{1,0:T(1,128)S(1)} %bitcast.43, s32[1,128]{1,0:T(1,128)} %bitcast.44), kind=kLoop, calls=%fused_computation.32 | loop fusion | flops 768 | bytes 2592 | tf_op jit(solution)/shard_map/convert_element_type | solution.py:230
  11.1 0.0 copy-done.2
  11.1 13.1 %shard_map.55 = (f32[128,4096]{1,0:T(8,128)}, f32[128,4096]{1,0:T(8,128)}, f32[16,4224]{1,0:T(8,128)}, f32[4,16,4096]{2,1,0:T(8,128)}, f32[128,128]{1,0:T(8,128)}) custom-call(bf16[128,12288]{1,0:T(8,128)(2,1)} %xv.1, bf16[128,12288]{1,0:T(8,128)(2,1)} %xv.1, bf16[128,12288]{1,0:T(8,128)(2,1)} %xv.1, bf16[8,12416]{1,0:T(8,128)(2,1)} %copy-done.2, ...), custom_call_target="tpu_custom_call" | custom-call | tf_op jit(solution)/shard_map/pallas_call | solution.py:242
  24.2 0.0 copy-start
  24.2 0.1 collective-permute-start.1
  24.3 1.3 %fusion.12 = (f32[1,16,4096]{2,1,0:T(8,128)S(1)}, f32[1,16,4096]{2,1,0:T(8,128)S(1)}, f32[1,16,4096]{2,1,0:T(8,128)S(1)}, f32[1,16,4096]{2,1,0:T(8,128)S(1)}) fusion(f32[4,16,4096]{2,1,0:T(8,128)} %get-tuple-element.13.d1_ref), kind=kLoop, calls=%fused_computation.34 | loop fusion | bytes 2097152 | tf_op jit(solution)/shard_map/slice | solution.py:189
  25.6 0.0 copy-done
  25.6 0.0 copy-start.5
  25.6 0.0 copy-start.6
  25.6 0.4 collective-permute-done.1.gt_ref.gf_ref
  26.1 0.1 fusion.11
  26.2 0.1 fusion.8
  26.3 0.1 broadcast_in_dim.33
  26.4 2.5 %collective-permute-start.2 = (f32[16,2176]{1,0:T(8,128)S(1)}, f32[16,2176]{1,0:T(8,128)S(1)}, u32[]{:S(2)}, u32[]{:S(2)}) collective-permute-start(f32[16,2176]{1,0:T(8,128)S(1)} %pad_maximum_fusion.1), channel_id=1, source_target_pairs={{0,2},{1,3},{2,4},{3,5},{4,6},{5,7},{6,8},{7,9},{8,10},{9,11},{10,... | collective-permute-start | bytes 417800 | tf_op jit(solution)/shard_map/ppermute | solution.py:20
  28.9 6.0 %collective-permute-done.2 = f32[16,2176]{1,0:T(8,128)S(1)} collective-permute-done((f32[16,2176]{1,0:T(8,128)S(1)}, f32[16,2176]{1,0:T(8,128)S(1)}, u32[]{:S(2)}, u32[]{:S(2)}) %collective-permute-start.2) | collective-permute-done | bytes 139296 | tf_op jit(solution)/shard_map/ppermute | solution.py:20
  34.9 0.1 fusion.6
  35.0 0.1 slice_reduce_fusion
  35.1 0.1 broadcast_in_dim.35
  35.2 1.3 %collective-permute-start.3 = (f32[16,2176]{1,0:T(8,128)S(1)}, f32[16,2176]{1,0:T(8,128)S(1)}, u32[]{:S(2)}, u32[]{:S(2)}) collective-permute-start(f32[16,2176]{1,0:T(8,128)S(1)} %pad_maximum_fusion.2), channel_id=1, source_target_pairs={{0,4},{1,5},{2,6},{3,7},{4,8},{5,9},{6,10},{7,11},{8,12},{9,13},{1... | collective-permute-start | bytes 417800 | tf_op jit(solution)/shard_map/ppermute | solution.py:20
  36.5 5.6 %collective-permute-done.3 = f32[16,2176]{1,0:T(8,128)S(1)} collective-permute-done((f32[16,2176]{1,0:T(8,128)S(1)}, f32[16,2176]{1,0:T(8,128)S(1)}, u32[]{:S(2)}, u32[]{:S(2)}) %collective-permute-start.3) | collective-permute-done | bytes 139296 | tf_op jit(solution)/shard_map/ppermute | solution.py:20
  42.1 0.1 multiply_reduce_fusion.1
  42.2 0.1 fusion.2
  42.3 0.1 broadcast_in_dim.37
  42.4 1.3 %collective-permute-start.4 = (f32[16,2176]{1,0:T(8,128)S(1)}, f32[16,2176]{1,0:T(8,128)S(1)}, u32[]{:S(2)}, u32[]{:S(2)}) collective-permute-start(f32[16,2176]{1,0:T(8,128)S(1)} %pad_maximum_fusion.3), channel_id=1, source_target_pairs={{0,8},{1,9},{2,10},{3,11},{4,12},{5,13},{6,14},{7,15},{16,24},{17,... | collective-permute-start | bytes 417800 | tf_op jit(solution)/shard_map/ppermute | solution.py:20
  43.7 0.0 copy-done.5
  43.7 0.1 copy.10
  43.8 0.0 copy-done.6
  43.8 0.1 copy.11
  43.9 0.1 stack.21
  44.1 0.1 stack.22
  44.2 7.6 %collective-permute-done.4 = f32[16,2176]{1,0:T(8,128)S(1)} collective-permute-done((f32[16,2176]{1,0:T(8,128)S(1)}, f32[16,2176]{1,0:T(8,128)S(1)}, u32[]{:S(2)}, u32[]{:S(2)}) %collective-permute-start.4) | collective-permute-done | bytes 139296 | tf_op jit(solution)/shard_map/ppermute | solution.py:20
  51.8 0.1 fusion.zo_ref
  51.9 0.1 collective-permute-start.5
  52.0 0.6 %pad_maximum_fusion.4.rr_ref = f32[2,1,4096]{2,1,0:T(1,128)} fusion(f32[1,1,4096]{2,1,0:T(1,128)S(1)} %stack.22, f32[1,1,4096]{2,1,0:T(1,128)S(1)} %stack.21), kind=kLoop, calls=%fused_computation.22 | loop fusion | flops 8192 | bytes 65536 | tf_op jit(solution)/shard_map/stack | solution.py:233
  52.6 0.7 %collective-permute-done.5.zp_ref = f32[16,2048]{1,0:T(8,128)S(1)} collective-permute-done((f32[16,2048]{1,0:T(8,128)S(1)}, f32[16,2048]{1,0:T(8,128)S(1)}, u32[]{:S(2)}, u32[]{:S(2)}) %collective-permute-start.5) | collective-permute-done | bytes 131104 | tf_op jit(solution)/shard_map/ppermute | solution.py:161
  53.3 0.6 %copy-done.4 = f32[16,2048]{1,0:T(8,128)} copy-done((f32[16,2048]{1,0:T(8,128)}, f32[16,2048]{1,0:T(8,128)S(1)}, u32[]{:S(2)}) %copy-start.4) | copy-done | bytes 131096
  54.0 4.6 %shard_map.56 = bf16[128,4096]{1,0:T(8,128)(2,1)} custom-call(f32[128,4096]{1,0:T(8,128)} %get-tuple-element.10.q_ref, f32[128,4096]{1,0:T(8,128)} %get-tuple-element.11.loc_ref, f32[16,2048]{1,0:T(8,128)} %copy-done.3, f32[16,2048]{1,0:T(8,128)} %copy-done.4, f32[16,4224]{1,0:T(8,128)} %get-tuple-element.12.pk_ref.pf_ref, f32[16,4224]{1,0:T(8,128)} %copy-done.1, ...), custom_call_target="tpu_custom_call" | custom-call | tf_op jit(solution)/shard_map/pallas_call | solution.py:290
  (16 shorter events, 0.1 us)
Async XLA Ops:
  1.8 7.9 %collective-permute-start = (bf16[8,12416]{1,0:T(8,128)(2,1)S(1)}, bf16[8,12416]{1,0:T(8,128)(2,1)S(1)}, u32[]{:S(2)}, u32[]{:S(2)}) collective-permute-start(bf16[8,12416]{1,0:T(8,128)(2,1)S(1)} %pad_maximum_fusion), channel_id=1, source_target_pairs={{0,1},{1,2},{2,3},{3,4},{4,5},{5,6},{6,7},{7,8},{8,9},{9,10},{10,1... | collective-permute-start | bytes 595976 | tf_op jit(solution)/shard_map/ppermute | solution.py:20
  9.7 1.4 %copy-start.2 = (bf16[8,12416]{1,0:T(8,128)(2,1)}, bf16[8,12416]{1,0:T(8,128)(2,1)S(1)}, u32[]{:S(2)}) copy-start(bf16[8,12416]{1,0:T(8,128)(2,1)S(1)} %collective-permute-done.rq.rk.rv) | copy-start | bytes 595972
  24.2 1.4 %copy-start = (f32[16,4224]{1,0:T(8,128)S(1)}, f32[16,4224]{1,0:T(8,128)}, u32[]{:S(2)}) copy-start(f32[16,4224]{1,0:T(8,128)} %get-tuple-element.12.pk_ref.pf_ref) | copy-start | bytes 811012
  24.2 1.8 %collective-permute-start.1 = (f32[16,4224]{1,0:T(8,128)}, f32[16,4224]{1,0:T(8,128)S(1)}, u32[]{:S(2)}, u32[]{:S(2)}) collective-permute-start(f32[16,4224]{1,0:T(8,128)} %get-tuple-element.12.pk_ref.pf_ref), channel_id=1, source_target_pairs={{0,1},{1,0},{2,3},{3,2},{4,5},{5,4},{6,7},{7,6},{8,9},{9,8},{10,11... | collective-permute-start | bytes 811016 | tf_op jit(solution)/shard_map/ppermute | solution.py:161
  25.6 18.2 %copy-start.5 = (f32[256,16]{0,1:T(8,128)S(1)}, f32[256,16]{0,1:T(8,128)}, u32[]{:S(2)}) copy-start(f32[256,16]{0,1:T(8,128)} %param.8) | copy-start | bytes 49156
  25.6 18.3 %copy-start.6 = (f32[256,16]{0,1:T(8,128)S(1)}, f32[256,16]{0,1:T(8,128)}, u32[]{:S(2)}) copy-start(f32[256,16]{0,1:T(8,128)} %param.9) | copy-start | bytes 49156
  26.0 25.9 %copy-start.1 = (f32[16,4224]{1,0:T(8,128)}, f32[16,4224]{1,0:T(8,128)S(1)}, u32[]{:S(2)}) copy-start(f32[16,4224]{1,0:T(8,128)S(1)} %collective-permute-done.1.gt_ref.gf_ref) | copy-start | bytes 811012
  26.4 8.5 %collective-permute-start.2 = (f32[16,2176]{1,0:T(8,128)S(1)}, f32[16,2176]{1,0:T(8,128)S(1)}, u32[]{:S(2)}, u32[]{:S(2)}) collective-permute-start(f32[16,2176]{1,0:T(8,128)S(1)} %pad_maximum_fusion.1), channel_id=1, source_target_pairs={{0,2},{1,3},{2,4},{3,5},{4,6},{5,7},{6,8},{7,9},{8,10},{9,11},{10,... | collective-permute-start | bytes 417800 | tf_op jit(solution)/shard_map/ppermute | solution.py:20
  35.2 6.9 %collective-permute-start.3 = (f32[16,2176]{1,0:T(8,128)S(1)}, f32[16,2176]{1,0:T(8,128)S(1)}, u32[]{:S(2)}, u32[]{:S(2)}) collective-permute-start(f32[16,2176]{1,0:T(8,128)S(1)} %pad_maximum_fusion.2), channel_id=1, source_target_pairs={{0,4},{1,5},{2,6},{3,7},{4,8},{5,9},{6,10},{7,11},{8,12},{9,13},{1... | collective-permute-start | bytes 417800 | tf_op jit(solution)/shard_map/ppermute | solution.py:20
  42.4 9.4 %collective-permute-start.4 = (f32[16,2176]{1,0:T(8,128)S(1)}, f32[16,2176]{1,0:T(8,128)S(1)}, u32[]{:S(2)}, u32[]{:S(2)}) collective-permute-start(f32[16,2176]{1,0:T(8,128)S(1)} %pad_maximum_fusion.3), channel_id=1, source_target_pairs={{0,8},{1,9},{2,10},{3,11},{4,12},{5,13},{6,14},{7,15},{16,24},{17,... | collective-permute-start | bytes 417800 | tf_op jit(solution)/shard_map/ppermute | solution.py:20
  51.9 1.4 %copy-start.3 = (f32[16,2048]{1,0:T(8,128)}, f32[16,2048]{1,0:T(8,128)S(1)}, u32[]{:S(2)}) copy-start(f32[16,2048]{1,0:T(8,128)S(1)} %fusion.zo_ref) | copy-start | bytes 393220
  51.9 1.4 %collective-permute-start.5 = (f32[16,2048]{1,0:T(8,128)S(1)}, f32[16,2048]{1,0:T(8,128)S(1)}, u32[]{:S(2)}, u32[]{:S(2)}) collective-permute-start(f32[16,2048]{1,0:T(8,128)S(1)} %fusion.zo_ref), channel_id=1, source_target_pairs={{0,1},{1,0},{2,3},{3,2},{4,5},{5,4},{6,7},{7,6},{8,9},{9,8},{10,11... | collective-permute-start | bytes 393224 | tf_op jit(solution)/shard_map/ppermute | solution.py:161
  53.3 0.7 %copy-start.4 = (f32[16,2048]{1,0:T(8,128)}, f32[16,2048]{1,0:T(8,128)S(1)}, u32[]{:S(2)}) copy-start(f32[16,2048]{1,0:T(8,128)S(1)} %collective-permute-done.5.zp_ref) | copy-start | bytes 393220

commit v17 on v15

--- a/solution.py
+++ b/solution.py
@@ -70,13 +70,17 @@
     def conv(x_ref, r_ref, w_ref):
         ext_s[0:length, :] = x_ref[...]
         ext_s[length:length + RIM, :] = r_ref[...]
-        ext = ext_s[...]
         w = w_ref[...]
-        acc = w[0:1, :] * x_ref[...].astype(jnp.float32)
-        for j in range(1, taps):
-            window = jnp.dot(shift_s[j * length:(j + 1) * length, :], ext, preferred_element_type=jnp.float32)
-            acc = acc + w[j:j + 1, :] * window
-        return acc
+        outs = []
+        for c0 in range(0, width, 2 * SUB):
+            cols = slice(c0, c0 + 2 * SUB)
+            ext = ext_s[:, cols]
+            acc = w[0:1, cols] * x_ref[:, cols].astype(jnp.float32)
+            for j in range(1, taps):
+                window = jnp.dot(shift_s[j * length:(j + 1) * length, :], ext, preferred_element_type=jnp.float32)
+                acc = acc + w[j:j + 1, cols] * window
+            outs.append(acc)
+        return jnp.concatenate(outs, axis=1)
 
     cq = conv(xq, rq, wq)
     ck = conv(xk, rk, wk)

time: 59.3 us -> 58.7 us (0.990)
  Pallas kernels: 17.7 us -> 17 us
    pallas_call x1, Pallas kernels: 13.1 us -> 12.4 us  [on_device(): pl.pallas_call(functools.partial(local_kernel, taps, group_width, spans),...]
where the time goes in v17:
time: 58.7 us; the launch traced here: 58 us
  waiting for transfers between devices  24 us (41%)
  Pallas kernels  17 us (29%)
  starting transfers between devices  7.18 us (12%)
  local copies, waits for them, and re-layouts  6.54 us (11%)
  other arithmetic  2.93 us (5%)
    ppermute x4, waiting for transfers between devices, from_behind(): return lax.ppermute(shard, axis, pairs)  22.9 us
    pallas_call x1, Pallas kernels, on_device(): pl.pallas_call(functools.partial(local_kernel, taps, group_width, spans),...  12.4 us
    ppermute x4, starting transfers between devices, from_behind(): return lax.ppermute(shard, axis, pairs)  7.04 us
    pallas_call x1, Pallas kernels, on_device(): pl.pallas_call(functools.partial(final_kernel, group_width, pole_count, m...  4.58 us
    another operation x6, local copies, waits for them, and re-layouts, on_device(): jnp.stack([rates, residues]).reshape(2, nb, gpb, pole_count)  1.83 us
    slice x1, local copies, waits for them, and re-layouts, chip_scan(): prefix = prefix + prefix_flag * mine(decays[span_of[2 * offset - 2]]) * came  1.26 us
  transfers between devices with their start and end apart: 6, of which 6 were waited for; matrix products, arithmetic and copies ran while one was open for 8% of the time, Pallas kernels for 0%

profile of v17, /device:TPU:24, one launch (start us, length us, event | category | flops | bytes accessed | tf_op | source)
XLA Modules:
  0.0 58.0 jit_solution(13258119137529213362)
XLA Ops:
  0.0 0.9 %slice.56 = bf16[8,12288]{1,0:T(8,128)(2,1)S(1)} slice(bf16[128,12288]{1,0:T(8,128)(2,1)} %xv.1), slice={[120:128], [0:12288]} | slice | bytes 393216 | tf_op jit(solution)/shard_map/slice | solution.py:229
  0.9 0.7 %convert.4 = bf16[128]{0:T(256)(128)(2,1)S(1)} convert(s32[128]{0:T(128)} %param.6) | non-fusion elementwise | flops 128 | bytes 768 | tf_op jit(solution)/shard_map/convert.1
  1.6 0.1 slice.57
  1.7 0.1 broadcast_in_dim.36
  1.8 1.9 %collective-permute-start = (bf16[8,12416]{1,0:T(8,128)(2,1)S(1)}, bf16[8,12416]{1,0:T(8,128)(2,1)S(1)}, u32[]{:S(2)}, u32[]{:S(2)}) collective-permute-start(bf16[8,12416]{1,0:T(8,128)(2,1)S(1)} %pad_maximum_fusion), channel_id=1, source_target_pairs={{0,1},{1,2},{2,3},{3,4},{4,5},{5,6},{6,7},{7,8},{8,9},{9,10},{10,1... | collective-permute-start | bytes 595976 | tf_op jit(solution)/shard_map/ppermute | solution.py:20
  3.7 0.8 %stack.18 = f32[1,4,64,16]{2,1,3,0:T(4,128)S(1)} reshape(f32[256,16]{0,1:T(8,128)} %param.8) | data formatting | bytes 32768 | tf_op jit(solution)/shard_map/stack | solution.py:237
  4.5 0.8 %stack.19 = f32[1,4,64,16]{2,1,3,0:T(4,128)S(1)} reshape(f32[256,16]{0,1:T(8,128)} %param.9) | data formatting | bytes 32768 | tf_op jit(solution)/shard_map/stack | solution.py:237
  5.4 0.6 %slice_bitcast_fusion = (f32[4,16,64]{2,1,0:T(8,128)}, f32[4,16,64]{2,1,0:T(8,128)}) fusion(f32[2,4,16,64]{3,2,1,0:T(8,128)S(1)} %maximum_bitcast_fusion), kind=kLoop, calls=%fused_computation.20 | loop fusion | bytes 65536 | tf_op jit(solution)/shard_map/squeeze | solution.py:238
  6.0 3.7 %collective-permute-done.rq.rk.rv = bf16[8,12416]{1,0:T(8,128)(2,1)S(1)} collective-permute-done((bf16[8,12416]{1,0:T(8,128)(2,1)S(1)}, bf16[8,12416]{1,0:T(8,128)(2,1)S(1)}, u32[]{:S(2)}, u32[]{:S(2)}) %collective-permute-start) | collective-permute-done | bytes 198688 | tf_op jit(solution)/shard_map/ppermute | solution.py:20
  9.7 0.1 convert_reduce_fusion
  9.8 0.7 %add_convert_fusion = f32[256]{0:T(256)S(1)} fusion(s32[120]{0:T(128)S(1)} %broadcast_in_dim.37, s32[8]{0:T(128)S(1)} %convert_reduce_fusion, s32[128]{0:T(128)} %param.6), kind=kLoop, calls=%fused_computation.32 | loop fusion | flops 768 | bytes 2048 | tf_op jit(solution)/shard_map/convert_element_type | solution.py:234
  10.5 0.6 %broadcast_in_dim.38.e_ref = f32[8,256]{1,0:T(8,128)} broadcast(f32[256]{0:T(256)S(1)} %add_convert_fusion), dimensions={1} | broadcast | bytes 9216 | tf_op jit(solution)/shard_map/broadcast_in_dim | solution.py:235
  11.1 0.0 copy-done.2
  11.1 12.4 %shard_map.55 = (f32[128,4096]{1,0:T(8,128)}, f32[128,4096]{1,0:T(8,128)}, f32[16,4224]{1,0:T(8,128)}, f32[4,16,4096]{2,1,0:T(8,128)}, f32[128,128]{1,0:T(8,128)}) custom-call(bf16[128,12288]{1,0:T(8,128)(2,1)} %xv.1, bf16[128,12288]{1,0:T(8,128)(2,1)} %xv.1, bf16[128,12288]{1,0:T(8,128)(2,1)} %xv.1, bf16[8,12416]{1,0:T(8,128)(2,1)} %copy-done.2, ...), custom_call_target="tpu_custom_call" | custom-call | tf_op jit(solution)/shard_map/pallas_call | solution.py:246
  23.6 0.0 copy-start
  23.6 0.1 collective-permute-start.1
  23.7 1.3 %fusion.12 = (f32[1,16,4096]{2,1,0:T(8,128)S(1)}, f32[1,16,4096]{2,1,0:T(8,128)S(1)}, f32[1,16,4096]{2,1,0:T(8,128)S(1)}, f32[1,16,4096]{2,1,0:T(8,128)S(1)}) fusion(f32[4,16,4096]{2,1,0:T(8,128)} %get-tuple-element.13.d1_ref), kind=kLoop, calls=%fused_computation.34 | loop fusion | bytes 2097152 | tf_op jit(solution)/shard_map/slice | solution.py:193
  24.9 0.0 copy-done
  25.0 0.0 copy-start.5
  25.0 0.0 copy-start.6
  25.0 0.4 collective-permute-done.1.gt_ref.gf_ref
  25.5 0.1 fusion.11
  25.6 0.1 fusion.8
  25.7 0.1 broadcast_in_dim.40
  25.8 2.5 %collective-permute-start.2 = (f32[16,2176]{1,0:T(8,128)S(1)}, f32[16,2176]{1,0:T(8,128)S(1)}, u32[]{:S(2)}, u32[]{:S(2)}) collective-permute-start(f32[16,2176]{1,0:T(8,128)S(1)} %pad_maximum_fusion.1), channel_id=1, source_target_pairs={{0,2},{1,3},{2,4},{3,5},{4,6},{5,7},{6,8},{7,9},{8,10},{9,11},{10,... | collective-permute-start | bytes 417800 | tf_op jit(solution)/shard_map/ppermute | solution.py:20
  28.3 6.0 %collective-permute-done.2 = f32[16,2176]{1,0:T(8,128)S(1)} collective-permute-done((f32[16,2176]{1,0:T(8,128)S(1)}, f32[16,2176]{1,0:T(8,128)S(1)}, u32[]{:S(2)}, u32[]{:S(2)}) %collective-permute-start.2) | collective-permute-done | bytes 139296 | tf_op jit(solution)/shard_map/ppermute | solution.py:20
  34.3 0.1 fusion.6
  34.3 0.1 slice_reduce_fusion
  34.5 0.1 broadcast_in_dim.42
  34.6 1.3 %collective-permute-start.3 = (f32[16,2176]{1,0:T(8,128)S(1)}, f32[16,2176]{1,0:T(8,128)S(1)}, u32[]{:S(2)}, u32[]{:S(2)}) collective-permute-start(f32[16,2176]{1,0:T(8,128)S(1)} %pad_maximum_fusion.2), channel_id=1, source_target_pairs={{0,4},{1,5},{2,6},{3,7},{4,8},{5,9},{6,10},{7,11},{8,12},{9,13},{1... | collective-permute-start | bytes 417800 | tf_op jit(solution)/shard_map/ppermute | solution.py:20
  35.9 5.6 %collective-permute-done.3 = f32[16,2176]{1,0:T(8,128)S(1)} collective-permute-done((f32[16,2176]{1,0:T(8,128)S(1)}, f32[16,2176]{1,0:T(8,128)S(1)}, u32[]{:S(2)}, u32[]{:S(2)}) %collective-permute-start.3) | collective-permute-done | bytes 139296 | tf_op jit(solution)/shard_map/ppermute | solution.py:20
  41.5 0.1 multiply_reduce_fusion.1
  41.6 0.1 fusion.2
  41.7 0.1 broadcast_in_dim.44
  41.8 1.3 %collective-permute-start.4 = (f32[16,2176]{1,0:T(8,128)S(1)}, f32[16,2176]{1,0:T(8,128)S(1)}, u32[]{:S(2)}, u32[]{:S(2)}) collective-permute-start(f32[16,2176]{1,0:T(8,128)S(1)} %pad_maximum_fusion.3), channel_id=1, source_target_pairs={{0,8},{1,9},{2,10},{3,11},{4,12},{5,13},{6,14},{7,15},{16,24},{17,... | collective-permute-start | bytes 417800 | tf_op jit(solution)/shard_map/ppermute | solution.py:20
  43.1 0.0 copy-done.5
  43.1 0.1 copy.10
  43.2 0.1 copy.11
  43.3 0.1 stack.21
  43.4 0.1 stack.22
  43.6 7.6 %collective-permute-done.4 = f32[16,2176]{1,0:T(8,128)S(1)} collective-permute-done((f32[16,2176]{1,0:T(8,128)S(1)}, f32[16,2176]{1,0:T(8,128)S(1)}, u32[]{:S(2)}, u32[]{:S(2)}) %collective-permute-start.4) | collective-permute-done | bytes 139296 | tf_op jit(solution)/shard_map/ppermute | solution.py:20
  51.2 0.1 fusion.zo_ref
  51.3 0.1 collective-permute-start.5
  51.4 0.6 %pad_maximum_fusion.4.rr_ref = f32[2,1,4096]{2,1,0:T(1,128)} fusion(f32[1,1,4096]{2,1,0:T(1,128)S(1)} %stack.22, f32[1,1,4096]{2,1,0:T(1,128)S(1)} %stack.21), kind=kLoop, calls=%fused_computation.22 | loop fusion | flops 8192 | bytes 65536 | tf_op jit(solution)/shard_map/stack | solution.py:237
  52.0 0.7 %collective-permute-done.5.zp_ref = f32[16,2048]{1,0:T(8,128)S(1)} collective-permute-done((f32[16,2048]{1,0:T(8,128)S(1)}, f32[16,2048]{1,0:T(8,128)S(1)}, u32[]{:S(2)}, u32[]{:S(2)}) %collective-permute-start.5) | collective-permute-done | bytes 131104 | tf_op jit(solution)/shard_map/ppermute | solution.py:165
  52.7 0.0 copy-done.3
  52.7 0.6 %copy-done.4 = f32[16,2048]{1,0:T(8,128)} copy-done((f32[16,2048]{1,0:T(8,128)}, f32[16,2048]{1,0:T(8,128)S(1)}, u32[]{:S(2)}) %copy-start.4) | copy-done | bytes 131096
  53.4 4.6 %shard_map.56 = bf16[128,4096]{1,0:T(8,128)(2,1)} custom-call(f32[128,4096]{1,0:T(8,128)} %get-tuple-element.10.q_ref, f32[128,4096]{1,0:T(8,128)} %get-tuple-element.11.loc_ref, f32[16,2048]{1,0:T(8,128)} %copy-done.3, f32[16,2048]{1,0:T(8,128)} %copy-done.4, f32[16,4224]{1,0:T(8,128)} %get-tuple-element.12.pk_ref.pf_ref, f32[16,4224]{1,0:T(8,128)} %copy-done.1, ...), custom_call_target="tpu_custom_call" | custom-call | tf_op jit(solution)/shard_map/pallas_call | solution.py:294
  (16 shorter events, 0.1 us)
Async XLA Ops:
  1.8 7.9 %collective-permute-start = (bf16[8,12416]{1,0:T(8,128)(2,1)S(1)}, bf16[8,12416]{1,0:T(8,128)(2,1)S(1)}, u32[]{:S(2)}, u32[]{:S(2)}) collective-permute-start(bf16[8,12416]{1,0:T(8,128)(2,1)S(1)} %pad_maximum_fusion), channel_id=1, source_target_pairs={{0,1},{1,2},{2,3},{3,4},{4,5},{5,6},{6,7},{7,8},{8,9},{9,10},{10,1... | collective-permute-start | bytes 595976 | tf_op jit(solution)/shard_map/ppermute | solution.py:20
  9.7 1.5 %copy-start.2 = (bf16[8,12416]{1,0:T(8,128)(2,1)}, bf16[8,12416]{1,0:T(8,128)(2,1)S(1)}, u32[]{:S(2)}) copy-start(bf16[8,12416]{1,0:T(8,128)(2,1)S(1)} %collective-permute-done.rq.rk.rv) | copy-start | bytes 595972
  23.6 1.4 %copy-start = (f32[16,4224]{1,0:T(8,128)S(1)}, f32[16,4224]{1,0:T(8,128)}, u32[]{:S(2)}) copy-start(f32[16,4224]{1,0:T(8,128)} %get-tuple-element.12.pk_ref.pf_ref) | copy-start | bytes 811012
  23.6 1.8 %collective-permute-start.1 = (f32[16,4224]{1,0:T(8,128)}, f32[16,4224]{1,0:T(8,128)S(1)}, u32[]{:S(2)}, u32[]{:S(2)}) collective-permute-start(f32[16,4224]{1,0:T(8,128)} %get-tuple-element.12.pk_ref.pf_ref), channel_id=1, source_target_pairs={{0,1},{1,0},{2,3},{3,2},{4,5},{5,4},{6,7},{7,6},{8,9},{9,8},{10,11... | collective-permute-start | bytes 811016 | tf_op jit(solution)/shard_map/ppermute | solution.py:165
  25.0 18.2 %copy-start.5 = (f32[256,16]{0,1:T(8,128)S(1)}, f32[256,16]{0,1:T(8,128)}, u32[]{:S(2)}) copy-start(f32[256,16]{0,1:T(8,128)} %param.8) | copy-start | bytes 49156
  25.0 18.3 %copy-start.6 = (f32[256,16]{0,1:T(8,128)S(1)}, f32[256,16]{0,1:T(8,128)}, u32[]{:S(2)}) copy-start(f32[256,16]{0,1:T(8,128)} %param.9) | copy-start | bytes 49156
  25.4 25.9 %copy-start.1 = (f32[16,4224]{1,0:T(8,128)}, f32[16,4224]{1,0:T(8,128)S(1)}, u32[]{:S(2)}) copy-start(f32[16,4224]{1,0:T(8,128)S(1)} %collective-permute-done.1.gt_ref.gf_ref) | copy-start | bytes 811012
  25.8 8.5 %collective-permute-start.2 = (f32[16,2176]{1,0:T(8,128)S(1)}, f32[16,2176]{1,0:T(8,128)S(1)}, u32[]{:S(2)}, u32[]{:S(2)}) collective-permute-start(f32[16,2176]{1,0:T(8,128)S(1)} %pad_maximum_fusion.1), channel_id=1, source_target_pairs={{0,2},{1,3},{2,4},{3,5},{4,6},{5,7},{6,8},{7,9},{8,10},{9,11},{10,... | collective-permute-start | bytes 417800 | tf_op jit(solution)/shard_map/ppermute | solution.py:20
  34.6 6.9 %collective-permute-start.3 = (f32[16,2176]{1,0:T(8,128)S(1)}, f32[16,2176]{1,0:T(8,128)S(1)}, u32[]{:S(2)}, u32[]{:S(2)}) collective-permute-start(f32[16,2176]{1,0:T(8,128)S(1)} %pad_maximum_fusion.2), channel_id=1, source_target_pairs={{0,4},{1,5},{2,6},{3,7},{4,8},{5,9},{6,10},{7,11},{8,12},{9,13},{1... | collective-permute-start | bytes 417800 | tf_op jit(solution)/shard_map/ppermute | solution.py:20
  41.8 9.4 %collective-permute-start.4 = (f32[16,2176]{1,0:T(8,128)S(1)}, f32[16,2176]{1,0:T(8,128)S(1)}, u32[]{:S(2)}, u32[]{:S(2)}) collective-permute-start(f32[16,2176]{1,0:T(8,128)S(1)} %pad_maximum_fusion.3), channel_id=1, source_target_pairs={{0,8},{1,9},{2,10},{3,11},{4,12},{5,13},{6,14},{7,15},{16,24},{17,... | collective-permute-start | bytes 417800 | tf_op jit(solution)/shard_map/ppermute | solution.py:20
  51.3 1.4 %copy-start.3 = (f32[16,2048]{1,0:T(8,128)}, f32[16,2048]{1,0:T(8,128)S(1)}, u32[]{:S(2)}) copy-start(f32[16,2048]{1,0:T(8,128)S(1)} %fusion.zo_ref) | copy-start | bytes 393220
  51.3 1.4 %collective-permute-start.5 = (f32[16,2048]{1,0:T(8,128)S(1)}, f32[16,2048]{1,0:T(8,128)S(1)}, u32[]{:S(2)}, u32[]{:S(2)}) collective-permute-start(f32[16,2048]{1,0:T(8,128)S(1)} %fusion.zo_ref), channel_id=1, source_target_pairs={{0,1},{1,0},{2,3},{3,2},{4,5},{5,4},{6,7},{7,6},{8,9},{9,8},{10,11... | collective-permute-start | bytes 393224 | tf_op jit(solution)/shard_map/ppermute | solution.py:165
  52.7 0.7 %copy-start.4 = (f32[16,2048]{1,0:T(8,128)}, f32[16,2048]{1,0:T(8,128)S(1)}, u32[]{:S(2)}) copy-start(f32[16,2048]{1,0:T(8,128)S(1)} %collective-permute-done.5.zp_ref) | copy-start | bytes 393220

commit v18 on v17

--- a/solution.py
+++ b/solution.py
@@ -72,8 +72,8 @@
         ext_s[length:length + RIM, :] = r_ref[...]
         w = w_ref[...]
         outs = []
-        for c0 in range(0, width, 2 * SUB):
-            cols = slice(c0, c0 + 2 * SUB)
+        for c0 in range(0, width, SUB):
+            cols = slice(c0, c0 + SUB)
             ext = ext_s[:, cols]
             acc = w[0:1, cols] * x_ref[:, cols].astype(jnp.float32)
             for j in range(1, taps):

time: 58.7 us -> 58.3 us (level)
  no operation moved by 1% of the time
where the time goes in v18:
time: 58.3 us; the launch traced here: 57.6 us
  waiting for transfers between devices  24 us (41%)
  Pallas kernels  16.7 us (29%)
  starting transfers between devices  7.18 us (12%)
  local copies, waits for them, and re-layouts  6.54 us (11%)
  other arithmetic  2.93 us (5%)
    ppermute x4, waiting for transfers between devices, from_behind(): return lax.ppermute(shard, axis, pairs)  22.9 us
    pallas_call x1, Pallas kernels, on_device(): pl.pallas_call(functools.partial(local_kernel, taps, group_width, spans),...  12.1 us
    ppermute x4, starting transfers between devices, from_behind(): return lax.ppermute(shard, axis, pairs)  7.04 us
    pallas_call x1, Pallas kernels, on_device(): pl.pallas_call(functools.partial(final_kernel, group_width, pole_count, m...  4.59 us
    another operation x6, local copies, waits for them, and re-layouts, on_device(): jnp.stack([rates, residues]).reshape(2, nb, gpb, pole_count)  1.83 us
    slice x1, local copies, waits for them, and re-layouts, chip_scan(): prefix = prefix + prefix_flag * mine(decays[span_of[2 * offset - 2]]) * came  1.26 us
  transfers between devices with their start and end apart: 6, of which 6 were waited for; matrix products, arithmetic and copies ran while one was open for 8% of the time, Pallas kernels for 0%

profile of v18, /device:TPU:24, one launch (start us, length us, event | category | flops | bytes accessed | tf_op | source)
XLA Modules:
  0.0 57.6 jit_solution(17449043937113407346)
XLA Ops:
  0.0 0.9 %slice.56 = bf16[8,12288]{1,0:T(8,128)(2,1)S(1)} slice(bf16[128,12288]{1,0:T(8,128)(2,1)} %xv.1), slice={[120:128], [0:12288]} | slice | bytes 393216 | tf_op jit(solution)/shard_map/slice | solution.py:229
  0.9 0.7 %convert.4 = bf16[128]{0:T(256)(128)(2,1)S(1)} convert(s32[128]{0:T(128)} %param.6) | non-fusion elementwise | flops 128 | bytes 768 | tf_op jit(solution)/shard_map/convert.1
  1.6 0.1 slice.57
  1.7 0.1 broadcast_in_dim.36
  1.8 1.9 %collective-permute-start = (bf16[8,12416]{1,0:T(8,128)(2,1)S(1)}, bf16[8,12416]{1,0:T(8,128)(2,1)S(1)}, u32[]{:S(2)}, u32[]{:S(2)}) collective-permute-start(bf16[8,12416]{1,0:T(8,128)(2,1)S(1)} %pad_maximum_fusion), channel_id=1, source_target_pairs={{0,1},{1,2},{2,3},{3,4},{4,5},{5,6},{6,7},{7,8},{8,9},{9,10},{10,1... | collective-permute-start | bytes 595976 | tf_op jit(solution)/shard_map/ppermute | solution.py:20
  3.7 0.8 %stack.18 = f32[1,4,64,16]{2,1,3,0:T(4,128)S(1)} reshape(f32[256,16]{0,1:T(8,128)} %param.8) | data formatting | bytes 32768 | tf_op jit(solution)/shard_map/stack | solution.py:237
  4.5 0.8 %stack.19 = f32[1,4,64,16]{2,1,3,0:T(4,128)S(1)} reshape(f32[256,16]{0,1:T(8,128)} %param.9) | data formatting | bytes 32768 | tf_op jit(solution)/shard_map/stack | solution.py:237
  5.4 0.6 %slice_bitcast_fusion = (f32[4,16,64]{2,1,0:T(8,128)}, f32[4,16,64]{2,1,0:T(8,128)}) fusion(f32[2,4,16,64]{3,2,1,0:T(8,128)S(1)} %maximum_bitcast_fusion), kind=kLoop, calls=%fused_computation.20 | loop fusion | bytes 65536 | tf_op jit(solution)/shard_map/squeeze | solution.py:238
  6.0 3.7 %collective-permute-done.rq.rk.rv = bf16[8,12416]{1,0:T(8,128)(2,1)S(1)} collective-permute-done((bf16[8,12416]{1,0:T(8,128)(2,1)S(1)}, bf16[8,12416]{1,0:T(8,128)(2,1)S(1)}, u32[]{:S(2)}, u32[]{:S(2)}) %collective-permute-start) | collective-permute-done | bytes 198688 | tf_op jit(solution)/shard_map/ppermute | solution.py:20
  9.7 0.1 convert_reduce_fusion
  9.8 0.7 %add_convert_fusion = f32[256]{0:T(256)S(1)} fusion(s32[120]{0:T(128)S(1)} %broadcast_in_dim.37, s32[8]{0:T(128)S(1)} %convert_reduce_fusion, s32[128]{0:T(128)} %param.6), kind=kLoop, calls=%fused_computation.32 | loop fusion | flops 768 | bytes 2048 | tf_op jit(solution)/shard_map/convert_element_type | solution.py:234
  10.5 0.6 %broadcast_in_dim.38.e_ref = f32[8,256]{1,0:T(8,128)} broadcast(f32[256]{0:T(256)S(1)} %add_convert_fusion), dimensions={1} | broadcast | bytes 9216 | tf_op jit(solution)/shard_map/broadcast_in_dim | solution.py:235
  11.1 0.0 copy-done.2
  11.1 12.1 %shard_map.55 = (f32[128,4096]{1,0:T(8,128)}, f32[128,4096]{1,0:T(8,128)}, f32[16,4224]{1,0:T(8,128)}, f32[4,16,4096]{2,1,0:T(8,128)}, f32[128,128]{1,0:T(8,128)}) custom-call(bf16[128,12288]{1,0:T(8,128)(2,1)} %xv.1, bf16[128,12288]{1,0:T(8,128)(2,1)} %xv.1, bf16[128,12288]{1,0:T(8,128)(2,1)} %xv.1, bf16[8,12416]{1,0:T(8,128)(2,1)} %copy-done.2, ...), custom_call_target="tpu_custom_call" | custom-call | tf_op jit(solution)/shard_map/pallas_call | solution.py:246
  23.2 0.0 copy-start
  23.2 0.1 collective-permute-start.1
  23.3 1.3 %fusion.12 = (f32[1,16,4096]{2,1,0:T(8,128)S(1)}, f32[1,16,4096]{2,1,0:T(8,128)S(1)}, f32[1,16,4096]{2,1,0:T(8,128)S(1)}, f32[1,16,4096]{2,1,0:T(8,128)S(1)}) fusion(f32[4,16,4096]{2,1,0:T(8,128)} %get-tuple-element.13.d1_ref), kind=kLoop, calls=%fused_computation.34 | loop fusion | bytes 2097152 | tf_op jit(solution)/shard_map/slice | solution.py:193
  24.6 0.0 copy-done
  24.6 0.0 copy-start.5
  24.6 0.0 copy-start.6
  24.6 0.4 collective-permute-done.1.gt_ref.gf_ref
  25.1 0.1 fusion.11
  25.2 0.1 fusion.8
  25.3 0.1 broadcast_in_dim.40
  25.4 2.5 %collective-permute-start.2 = (f32[16,2176]{1,0:T(8,128)S(1)}, f32[16,2176]{1,0:T(8,128)S(1)}, u32[]{:S(2)}, u32[]{:S(2)}) collective-permute-start(f32[16,2176]{1,0:T(8,128)S(1)} %pad_maximum_fusion.1), channel_id=1, source_target_pairs={{0,2},{1,3},{2,4},{3,5},{4,6},{5,7},{6,8},{7,9},{8,10},{9,11},{10,... | collective-permute-start | bytes 417800 | tf_op jit(solution)/shard_map/ppermute | solution.py:20
  27.9 6.0 %collective-permute-done.2 = f32[16,2176]{1,0:T(8,128)S(1)} collective-permute-done((f32[16,2176]{1,0:T(8,128)S(1)}, f32[16,2176]{1,0:T(8,128)S(1)}, u32[]{:S(2)}, u32[]{:S(2)}) %collective-permute-start.2) | collective-permute-done | bytes 139296 | tf_op jit(solution)/shard_map/ppermute | solution.py:20
  33.9 0.1 fusion.6
  34.0 0.1 slice_reduce_fusion
  34.1 0.1 broadcast_in_dim.42
  34.2 1.3 %collective-permute-start.3 = (f32[16,2176]{1,0:T(8,128)S(1)}, f32[16,2176]{1,0:T(8,128)S(1)}, u32[]{:S(2)}, u32[]{:S(2)}) collective-permute-start(f32[16,2176]{1,0:T(8,128)S(1)} %pad_maximum_fusion.2), channel_id=1, source_target_pairs={{0,4},{1,5},{2,6},{3,7},{4,8},{5,9},{6,10},{7,11},{8,12},{9,13},{1... | collective-permute-start | bytes 417800 | tf_op jit(solution)/shard_map/ppermute | solution.py:20
  35.5 5.6 %collective-permute-done.3 = f32[16,2176]{1,0:T(8,128)S(1)} collective-permute-done((f32[16,2176]{1,0:T(8,128)S(1)}, f32[16,2176]{1,0:T(8,128)S(1)}, u32[]{:S(2)}, u32[]{:S(2)}) %collective-permute-start.3) | collective-permute-done | bytes 139296 | tf_op jit(solution)/shard_map/ppermute | solution.py:20
  41.1 0.1 multiply_reduce_fusion.1
  41.3 0.1 fusion.2
  41.4 0.1 broadcast_in_dim.44
  41.4 1.3 %collective-permute-start.4 = (f32[16,2176]{1,0:T(8,128)S(1)}, f32[16,2176]{1,0:T(8,128)S(1)}, u32[]{:S(2)}, u32[]{:S(2)}) collective-permute-start(f32[16,2176]{1,0:T(8,128)S(1)} %pad_maximum_fusion.3), channel_id=1, source_target_pairs={{0,8},{1,9},{2,10},{3,11},{4,12},{5,13},{6,14},{7,15},{16,24},{17,... | collective-permute-start | bytes 417800 | tf_op jit(solution)/shard_map/ppermute | solution.py:20
  42.7 0.0 copy-done.5
  42.8 0.1 copy.10
  42.9 0.0 copy-done.6
  42.9 0.1 copy.11
  43.0 0.1 stack.21
  43.1 0.1 stack.22
  43.2 7.6 %collective-permute-done.4 = f32[16,2176]{1,0:T(8,128)S(1)} collective-permute-done((f32[16,2176]{1,0:T(8,128)S(1)}, f32[16,2176]{1,0:T(8,128)S(1)}, u32[]{:S(2)}, u32[]{:S(2)}) %collective-permute-start.4) | collective-permute-done | bytes 139296 | tf_op jit(solution)/shard_map/ppermute | solution.py:20
  50.8 0.1 fusion.zo_ref
  51.0 0.1 collective-permute-start.5
  51.0 0.6 %pad_maximum_fusion.4.rr_ref = f32[2,1,4096]{2,1,0:T(1,128)} fusion(f32[1,1,4096]{2,1,0:T(1,128)S(1)} %stack.22, f32[1,1,4096]{2,1,0:T(1,128)S(1)} %stack.21), kind=kLoop, calls=%fused_computation.22 | loop fusion | flops 8192 | bytes 65536 | tf_op jit(solution)/shard_map/stack | solution.py:237
  51.7 0.7 %collective-permute-done.5.zp_ref = f32[16,2048]{1,0:T(8,128)S(1)} collective-permute-done((f32[16,2048]{1,0:T(8,128)S(1)}, f32[16,2048]{1,0:T(8,128)S(1)}, u32[]{:S(2)}, u32[]{:S(2)}) %collective-permute-start.5) | collective-permute-done | bytes 131104 | tf_op jit(solution)/shard_map/ppermute | solution.py:165
  52.4 0.6 %copy-done.4 = f32[16,2048]{1,0:T(8,128)} copy-done((f32[16,2048]{1,0:T(8,128)}, f32[16,2048]{1,0:T(8,128)S(1)}, u32[]{:S(2)}) %copy-start.4) | copy-done | bytes 131096
  53.0 4.6 %shard_map.56 = bf16[128,4096]{1,0:T(8,128)(2,1)} custom-call(f32[128,4096]{1,0:T(8,128)} %get-tuple-element.10.q_ref, f32[128,4096]{1,0:T(8,128)} %get-tuple-element.11.loc_ref, f32[16,2048]{1,0:T(8,128)} %copy-done.3, f32[16,2048]{1,0:T(8,128)} %copy-done.4, f32[16,4224]{1,0:T(8,128)} %get-tuple-element.12.pk_ref.pf_ref, f32[16,4224]{1,0:T(8,128)} %copy-done.1, ...), custom_call_target="tpu_custom_call" | custom-call | tf_op jit(solution)/shard_map/pallas_call | solution.py:294
  (16 shorter events, 0.1 us)
Async XLA Ops:
  1.8 7.9 %collective-permute-start = (bf16[8,12416]{1,0:T(8,128)(2,1)S(1)}, bf16[8,12416]{1,0:T(8,128)(2,1)S(1)}, u32[]{:S(2)}, u32[]{:S(2)}) collective-permute-start(bf16[8,12416]{1,0:T(8,128)(2,1)S(1)} %pad_maximum_fusion), channel_id=1, source_target_pairs={{0,1},{1,2},{2,3},{3,4},{4,5},{5,6},{6,7},{7,8},{8,9},{9,10},{10,1... | collective-permute-start | bytes 595976 | tf_op jit(solution)/shard_map/ppermute | solution.py:20
  9.7 1.5 %copy-start.2 = (bf16[8,12416]{1,0:T(8,128)(2,1)}, bf16[8,12416]{1,0:T(8,128)(2,1)S(1)}, u32[]{:S(2)}) copy-start(bf16[8,12416]{1,0:T(8,128)(2,1)S(1)} %collective-permute-done.rq.rk.rv) | copy-start | bytes 595972
  23.2 1.4 %copy-start = (f32[16,4224]{1,0:T(8,128)S(1)}, f32[16,4224]{1,0:T(8,128)}, u32[]{:S(2)}) copy-start(f32[16,4224]{1,0:T(8,128)} %get-tuple-element.12.pk_ref.pf_ref) | copy-start | bytes 811012
  23.2 1.8 %collective-permute-start.1 = (f32[16,4224]{1,0:T(8,128)}, f32[16,4224]{1,0:T(8,128)S(1)}, u32[]{:S(2)}, u32[]{:S(2)}) collective-permute-start(f32[16,4224]{1,0:T(8,128)} %get-tuple-element.12.pk_ref.pf_ref), channel_id=1, source_target_pairs={{0,1},{1,0},{2,3},{3,2},{4,5},{5,4},{6,7},{7,6},{8,9},{9,8},{10,11... | collective-permute-start | bytes 811016 | tf_op jit(solution)/shard_map/ppermute | solution.py:165
  24.6 18.2 %copy-start.5 = (f32[256,16]{0,1:T(8,128)S(1)}, f32[256,16]{0,1:T(8,128)}, u32[]{:S(2)}) copy-start(f32[256,16]{0,1:T(8,128)} %param.8) | copy-start | bytes 49156
  24.6 18.3 %copy-start.6 = (f32[256,16]{0,1:T(8,128)S(1)}, f32[256,16]{0,1:T(8,128)}, u32[]{:S(2)}) copy-start(f32[256,16]{0,1:T(8,128)} %param.9) | copy-start | bytes 49156
  25.1 25.9 %copy-start.1 = (f32[16,4224]{1,0:T(8,128)}, f32[16,4224]{1,0:T(8,128)S(1)}, u32[]{:S(2)}) copy-start(f32[16,4224]{1,0:T(8,128)S(1)} %collective-permute-done.1.gt_ref.gf_ref) | copy-start | bytes 811012
  25.4 8.5 %collective-permute-start.2 = (f32[16,2176]{1,0:T(8,128)S(1)}, f32[16,2176]{1,0:T(8,128)S(1)}, u32[]{:S(2)}, u32[]{:S(2)}) collective-permute-start(f32[16,2176]{1,0:T(8,128)S(1)} %pad_maximum_fusion.1), channel_id=1, source_target_pairs={{0,2},{1,3},{2,4},{3,5},{4,6},{5,7},{6,8},{7,9},{8,10},{9,11},{10,... | collective-permute-start | bytes 417800 | tf_op jit(solution)/shard_map/ppermute | solution.py:20
  34.2 6.9 %collective-permute-start.3 = (f32[16,2176]{1,0:T(8,128)S(1)}, f32[16,2176]{1,0:T(8,128)S(1)}, u32[]{:S(2)}, u32[]{:S(2)}) collective-permute-start(f32[16,2176]{1,0:T(8,128)S(1)} %pad_maximum_fusion.2), channel_id=1, source_target_pairs={{0,4},{1,5},{2,6},{3,7},{4,8},{5,9},{6,10},{7,11},{8,12},{9,13},{1... | collective-permute-start | bytes 417800 | tf_op jit(solution)/shard_map/ppermute | solution.py:20
  41.4 9.4 %collective-permute-start.4 = (f32[16,2176]{1,0:T(8,128)S(1)}, f32[16,2176]{1,0:T(8,128)S(1)}, u32[]{:S(2)}, u32[]{:S(2)}) collective-permute-start(f32[16,2176]{1,0:T(8,128)S(1)} %pad_maximum_fusion.3), channel_id=1, source_target_pairs={{0,8},{1,9},{2,10},{3,11},{4,12},{5,13},{6,14},{7,15},{16,24},{17,... | collective-permute-start | bytes 417800 | tf_op jit(solution)/shard_map/ppermute | solution.py:20
  50.9 1.4 %copy-start.3 = (f32[16,2048]{1,0:T(8,128)}, f32[16,2048]{1,0:T(8,128)S(1)}, u32[]{:S(2)}) copy-start(f32[16,2048]{1,0:T(8,128)S(1)} %fusion.zo_ref) | copy-start | bytes 393220
  51.0 1.4 %collective-permute-start.5 = (f32[16,2048]{1,0:T(8,128)S(1)}, f32[16,2048]{1,0:T(8,128)S(1)}, u32[]{:S(2)}, u32[]{:S(2)}) collective-permute-start(f32[16,2048]{1,0:T(8,128)S(1)} %fusion.zo_ref), channel_id=1, source_target_pairs={{0,1},{1,0},{2,3},{3,2},{4,5},{5,4},{6,7},{7,6},{8,9},{9,8},{10,11... | collective-permute-start | bytes 393224 | tf_op jit(solution)/shard_map/ppermute | solution.py:165
  52.4 0.7 %copy-start.4 = (f32[16,2048]{1,0:T(8,128)}, f32[16,2048]{1,0:T(8,128)S(1)}, u32[]{:S(2)}) copy-start(f32[16,2048]{1,0:T(8,128)S(1)} %collective-permute-done.5.zp_ref) | copy-start | bytes 393220
